TPU v7x, 32 devices: a whole 2x2x4 slice. The times are simulated.
32 devices in a mesh: ctx: 16 (over z, y, x), tp: 2 (over core).
Axes of the slice: x: 2, y: 2, z: 4, core: 2. Of those that a mesh axis runs over, the one named last changes fastest.
Arguments:
- tokens: bfloat16 [12288, 4096], P('ctx', 'tp'), may hold values from -6 to 6
- norm_gain: float32 [4096], replicated, may hold values from 0.1 to 1.9
- w_in: bfloat16 [4096, 3, 4096], P('ctx', None, 'tp'), may hold values from -0.09375 to 0.09375
- short_filter: float32 [3, 3, 4096], P(None, None, 'tp'), may hold values from -3.5 to 3.5
- long_filter: bfloat16 [128, 256], P(None, 'tp'), may hold values from -0.5 to 0.5
- w_out: bfloat16 [4096, 4096], P('tp', 'ctx'), may hold values from -0.125 to 0.125
Outputs:
- block_out: bfloat16 [12288, 4096], P('ctx', 'tp')
All inputs are finite; a program needn't handle non-finite values.
Results may differ from a plain program's by a relative error of at most 0.008.
Values may be sent and summed in bfloat16 or wider, within the bound.
No kernel may reach another device: no remote copies, remote signals or barrier semaphores. Data moves between devices by JAX's collectives and lax.ppermute only.
A program may use at most 192 MiB of HBM per device.

v0:
```python
import jax
import jax.numpy as jnp
from jax import lax
from jax.sharding import PartitionSpec as P


def shifted(value, axis, steps):
    count = lax.axis_size(axis)
    first, last = (max(0, -steps), min(count, count - steps))
    return lax.ppermute(value, axis, [(source, source + steps) for source in range(first, last)])


def toeplitz_pair(long_filter):
    filter_len = long_filter.shape[0]
    offsets = jnp.arange(filter_len)[:, None] - jnp.arange(filter_len)[None, :]
    table = long_filter.T
    nothing = jnp.zeros((), jnp.bfloat16)
    current = jnp.where(offsets >= 0, table[:, jnp.clip(offsets, 0, filter_len - 1)], nothing)
    previous = jnp.where(
        offsets < 0, table[:, jnp.clip(offsets + filter_len, 0, filter_len - 1)], nothing
    )
    return (current, previous)


def featurize(extended, short_filter, count):
    short_taps = short_filter.shape[0]
    ext_float = extended.astype(jnp.float32)
    featured = jnp.zeros((count,) + extended.shape[1:], jnp.float32)
    for tap in range(short_taps):
        featured = (
            featured
            + short_filter[tap] * ext_float[short_taps - 1 - tap : short_taps - 1 - tap + count]
        )
    return featured


def local(tokens, norm_gain, w_in, short_filter, long_filter, w_out):
    row_count = tokens.shape[0]
    local_width = short_filter.shape[2]
    short_taps = short_filter.shape[0]
    filter_len = long_filter.shape[0]
    groups_here = long_filter.shape[1]
    group_size = local_width // groups_here
    gathered = lax.all_gather(tokens, "tp", axis=1, tiled=True)
    wide_float = gathered.astype(jnp.float32)
    scale = lax.rsqrt(jnp.mean(wide_float * wide_float, axis=-1, keepdims=True) + 1e-06)
    normed = (wide_float * scale * norm_gain).astype(jnp.bfloat16)
    piece = lax.all_gather(w_in, "ctx", axis=0, tiled=True)
    projected = jnp.dot(
        normed, piece.reshape(piece.shape[0], 3 * local_width), preferred_element_type=jnp.float32
    )
    projected = projected.astype(jnp.bfloat16).reshape(row_count, 3, local_width)
    prior_rows = shifted(projected[row_count - (short_taps - 1) :], "ctx", 1)
    featured = featurize(jnp.concatenate([prior_rows, projected], axis=0), short_filter, row_count)
    mixed = (featured[:, 1] * featured[:, 2]).astype(jnp.bfloat16)
    mixed_prior = shifted(mixed[row_count - (filter_len - 1) :], "ctx", 1)
    query = featured[:, 0]
    zero_row = jnp.zeros((1, local_width), jnp.bfloat16)
    extended_mix = jnp.concatenate([zero_row, mixed_prior, mixed], axis=0)
    mix_blocks = extended_mix.reshape(
        row_count // filter_len + 1, filter_len, groups_here, group_size
    )
    current, previous = toeplitz_pair(long_filter)
    filtered = jnp.einsum(
        "gts,bsgc->btgc", current, mix_blocks[1:], preferred_element_type=jnp.float32
    )
    filtered = filtered + jnp.einsum(
        "gts,bsgc->btgc", previous, mix_blocks[:-1], preferred_element_type=jnp.float32
    )
    gated = (query * filtered.reshape(row_count, local_width)).astype(jnp.bfloat16)
    terms = jnp.dot(
        gated, lax.all_gather(w_out, "ctx", axis=1, tiled=True), preferred_element_type=jnp.float32
    )
    summed = lax.psum_scatter(
        terms.astype(jnp.bfloat16), "tp", scatter_dimension=1, tiled=True
    ).astype(jnp.float32)
    return (tokens.astype(jnp.float32) + summed).astype(jnp.bfloat16)


def solution(mesh):
    placed = (
        P("ctx", "tp"),
        P(),
        P("ctx", None, "tp"),
        P(None, None, "tp"),
        P(None, "tp"),
        P("tp", "ctx"),
    )
    return jax.shard_map(
        local, mesh=mesh, in_specs=placed, out_specs=P("ctx", "tp"), check_vma=False
    )
```

profile of v0, /device:TPU:0, one launch (start us, length us, event | category | flops | bytes accessed | tf_op | source)
XLA Modules:
  0.0 1397.2 jit_solution(7312715811662702378)
XLA Ops:
  6.5 0.7 all-gather.4.cloned.1.call-update
  7.3 4.6 copy.10
  12.0 0.7 all-gather.8.cloned.1.call-update
  13.5 14.9 %all-gather.4.cloned.1.call-done = bf16[768,4096]{1,0:T(8,128)(2,1)} async-done(((bf16[768,2048]{1,0:T(8,128)(2,1)}), bf16[768,4096]{1,0:T(8,128)(2,1)}) %all-gather.4.cloned.1.call-update) | async-done | bytes 6291472 | tf_op jit(solution)/shard_map/all_gather | solution.py:44
  28.4 4.1 fusion.2
  32.5 1019.6 %all-gather.6.cloned.1.call-done = bf16[4096,3,2048]{0,2,1:T(8,128)(2,1)} async-done(((bf16[256,3,2048]{0,2,1:T(8,128)(2,1)}), bf16[4096,3,2048]{0,2,1:T(8,128)(2,1)}) %all-gather.6.cloned.1.call-update) | async-done | bytes 50331664 | tf_op jit(solution)/shard_map/all_gather | solution.py:48
  1052.1 46.7 %convolution_convert_fusion = bf16[768,6144]{1,0:T(8,128)(2,1)} fusion(bf16[4096,6144]{0,1:T(8,128)(2,1)} %bitcast.70, bf16[768,4096]{1,0:T(8,128)(2,1)} %all-gather.4.cloned.1.call-done, f32[4096]{0:T(1024)S(1)} %copy-done.8, f32[768]{0:T(1024)S(1)} %add_rsqrt_fusion), kind=kOutput, calls=%fused_computation.13 | convolution fusion | flops 38672007168 | bytes 66079744 | tf_op jit(solution)/shard_map/dot_general | solution.py:49
  1098.9 0.9 slice.66
  1099.8 4.6 collective-permute-start
  1104.5 57.8 %gather_fusion = bf16[16384,128]{1,0:T(8,128)(2,1)} fusion(bf16[128,128]{0,1:T(8,128)(2,1)S(1)} %bitcast.62, s32[16384]{0:T(1024)S(1)} %fusion.28), kind=kCustom, calls=%fused_computation | custom fusion | bytes 8454144 | tf_op jit(solution)/shard_map/gather | solution.py:18
  1162.2 6.8 copy.13
  1169.0 57.8 %gather_fusion.1 = bf16[16384,128]{1,0:T(8,128)(2,1)} fusion(bf16[128,128]{0,1:T(8,128)(2,1)S(1)} %bitcast.63, s32[16384]{0:T(1024)S(1)} %fusion.30), kind=kCustom, calls=%fused_computation.1 | custom fusion | bytes 8454144 | tf_op jit(solution)/shard_map/gather | solution.py:20
  1226.7 6.7 copy.18
  1233.5 12.5 copy.11
  1246.0 0.9 copy.12
  1246.9 12.7 maximum_convert_fusion
  1259.6 23.0 %fusion = f32[768,3,2048]{0,2,1:T(8,128)S(1)} fusion(f32[770,3,2048]{0,2,1:T(8,128)} %maximum_convert_fusion, f32[3,2048]{1,0:T(4,128)S(1)} %get-tuple-element.6, f32[3,2048]{1,0:T(4,128)S(1)} %get-tuple-element.7, f32[3,2048]{1,0:T(4,128)S(1)} %get-tuple-element.5), kind=kLoop, calls=%fused_computation.3 | loop fusion | flops 23592960 | bytes 75571200 | tf_op jit(solution)/shard_map/add | solution.py:31
  1282.6 6.5 copy-done.2
  1289.0 2.3 fusion.7
  1291.4 4.9 copy.15
  1296.3 4.7 convert_element_type.43
  1301.2 3.0 collective-permute-start.1
  1304.2 9.1 fusion.12
  1313.9 2.1 copy.16
  1316.0 3.4 pad_maximum_fusion
  1319.4 3.2 copy.17
  1322.6 4.7 slice.61
  1327.3 8.3 add_bitcast_fusion
  1335.6 6.4 copy.20
  1342.0 25.2 %convolution_convert_fusion.1 = bf16[768,4096]{1,0:T(8,128)(2,1)} fusion(bf16[2048,4096]{1,0:T(8,128)(2,1)} %all-gather.8.cloned.1.call-done, f32[256,8,6,128]{3,2,1,0:T(8,128)} %bitcast.68, f32[768,3,2048]{0,2,1:T(8,128)} %copy-done.2), kind=kOutput, calls=%fused_computation.14 | convolution fusion | flops 12891193344 | bytes 37748736 | tf_op jit(solution)/shard_map/dot_general | solution.py:71
  1367.2 18.6 %reduce-scatter.2.cloned.1.call-done = bf16[768,2048]{1,0:T(8,128)(2,1)} async-done(((bf16[768,4096]{1,0:T(8,128)(2,1)}), bf16[768,2048]{1,0:T(8,128)(2,1)}) %reduce-scatter.2.cloned.1.call-update) | async-done | bytes 3145744 | tf_op jit(solution)/shard_map/reduce_scatter | solution.py:74
  1385.8 4.9 add_convert_fusion
  (35 shorter events, 1.7 us)
Async XLA Ops:
  6.5 1097.9 %copy-start = (bf16[128,128]{1,0:T(8,128)(2,1)S(1)}, bf16[128,128]{1,0:T(8,128)(2,1)}, u32[]{:S(2)}) copy-start(bf16[128,128]{1,0:T(8,128)(2,1)} %param.10) | copy-start | bytes 98308
  6.5 6.9 copy-start.6
  6.5 21.9 %all-gather.4.cloned.1.call-start = ((), (), s32[]{:S(2)}) async-start(), calls=%async_computation.1 | async-start | bytes 9437184 | tf_op jit(solution)/shard_map/all_gather | solution.py:44
  7.3 1044.9 %all-gather.6.cloned.1.call-start = ((), (), s32[]{:S(2)}) async-start(), calls=%async_computation.2 | async-start | bytes 53477376 | tf_op jit(solution)/shard_map/all_gather | solution.py:48
  11.9 1040.2 %copy-start.8 = (f32[4096]{0:T(1024)S(1)}, f32[4096]{0:T(1024)}, u32[]{:S(2)}) copy-start(f32[4096]{0:T(1024)} %param.7) | copy-start | bytes 49156
  12.0 1330.0 %all-gather.8.cloned.1.call-start = ((), (), s32[]{:S(2)}) async-start(), calls=%async_computation.3 | async-start | bytes 17825792 | tf_op jit(solution)/shard_map/all_gather | solution.py:72
  12.7 1373.1 %reduce-scatter.2.cloned.1.call-start = ((), (), s32[]{:S(2)}) async-start(), calls=%async_computation.4 | async-start | bytes 9437184 | tf_op jit(solution)/shard_map/reduce_scatter | solution.py:74
  1099.8 146.2 %collective-permute-start = (bf16[2,3,2048]{2,1,0:T(4,128)(2,1)S(1)}, bf16[2,3,2048]{2,1,0:T(4,128)(2,1)S(1)}, u32[]{:S(2)}, u32[]{:S(2)}) collective-permute-start(bf16[2,3,2048]{2,1,0:T(4,128)(2,1)S(1)} %slice.49), channel_id=1, source_target_pairs={{0,2},{2,4},{4,6},{6,8},{8,10},{10,12},{12,14},{14,16},{16,18},{18... | collective-permute-start | bytes 73736 | tf_op jit(solution)/shard_map/ppermute | solution.py:10
  1282.6 6.5 copy-start.2
  1291.4 4.9 copy-start.3
  1291.4 12.8 copy-start.7
  1301.2 14.8 %copy-start.4 = (bf16[768,1,2048]{2,0,1:T(8,128)(2,1)S(1)}, bf16[768,1,2048]{2,0,1:T(8,128)(2,1)}, u32[]{:S(2)}) copy-start(bf16[768,1,2048]{2,0,1:T(8,128)(2,1)} %copy.15) | copy-start | bytes 9437188
  1301.2 12.7 collective-permute-start.1
  1367.2 18.6 %copy-start.5 = (bf16[768,2048]{1,0:T(8,128)(2,1)S(1)}, bf16[768,2048]{1,0:T(8,128)(2,1)}, u32[]{:S(2)}) copy-start(bf16[768,2048]{1,0:T(8,128)(2,1)} %param.6) | copy-start | bytes 9437188
  1367.2 23.5 %copy-start.1 = (bf16[128,128]{1,0:T(8,128)(2,1)S(1)}, bf16[128,128]{1,0:T(8,128)(2,1)}, u32[]{:S(2)}) copy-start(bf16[128,128]{1,0:T(8,128)(2,1)} %param.10) | copy-start | bytes 98308
Sparse Core Ops, SparseCore 0:
  8.9 19.4 all-gather.3
  29.9 1022.2 all-gather.5
  1054.9 237.0 all-gather.7
  1367.3 18.4 reduce-scatter.1
where the time goes:
time: 1400 us
  waiting for transfers between devices  1060 us (76%)
  local copies, waits for them, and re-layouts  181 us (13%)
  matrix products  89.3 us (6%)
  other arithmetic  51 us (4%)
    all_gather x1, waiting for transfers between devices, local(): piece = lax.all_gather(w_in, 'ctx', axis=0, tiled=True)  1020 us
    gather x2, local copies, waits for them, and re-layouts, toeplitz_pair(): table[:, jnp.clip(offsets, 0, filter_len - 1)]  64.5 us
    gather x2, local copies, waits for them, and re-layouts, toeplitz_pair(): table[:, jnp.clip(offsets + filter_len, 0, filter_len - 1)]  64.5 us
    dot_general x1, matrix products, local(): jnp.dot(normed, piece.reshape(piece.shape[0], 3 * local_width), preferred...  46.7 us
  transfers between devices with their start and end apart: 6, of which 4 were waited for; matrix products, arithmetic and copies ran while one was open for 20% of the time, Pallas kernels for 0%

commit v1 on v0

v1 whole, which is shorter than its diff:
```python
import jax
import jax.numpy as jnp
from jax import lax
from jax.sharding import Mesh
from jax.sharding import PartitionSpec as P


def shifted(value, axis, steps):
    count = lax.axis_size(axis)
    first, last = (max(0, -steps), min(count, count - steps))
    return lax.ppermute(value, axis, [(source, source + steps) for source in range(first, last)])


def swap_pair(value):
    return lax.ppermute(value, "lo", [(0, 1), (1, 0)])


def toeplitz_pair(long_filter):
    filter_len, groups = long_filter.shape
    table = long_filter.T
    zeros = jnp.zeros((groups, filter_len), long_filter.dtype)

    def skew(edge):
        reverse = edge[:, ::-1]
        tiled = jnp.tile(reverse, (1, filter_len + 1))
        flat = tiled[:, filter_len - 1 : filter_len - 1 + filter_len * (2 * filter_len - 1)]
        return flat.reshape(groups, filter_len, 2 * filter_len - 1)[:, :, :filter_len]

    current = skew(jnp.concatenate([zeros, table], axis=1))
    previous = skew(jnp.concatenate([table, zeros], axis=1))
    return (current, previous)


def featurize(extended, short_filter, count):
    short_taps = short_filter.shape[0]
    ext_float = extended.astype(jnp.float32)
    featured = jnp.zeros((count,) + extended.shape[1:], jnp.float32)
    for tap in range(short_taps):
        featured = (
            featured
            + short_filter[tap] * ext_float[short_taps - 1 - tap : short_taps - 1 - tap + count]
        )
    return featured


def half_of(value, axis, half):
    size = value.shape[axis] // 2
    return lax.dynamic_slice_in_dim(value, half * size, size, axis)


def pair_ordered(mine, theirs, half, axis):
    first = jnp.where(half == 0, mine, theirs)
    second = jnp.where(half == 0, theirs, mine)
    return jnp.concatenate([first, second], axis=axis)


def local(tokens, norm_gain, w_in, short_filter, long_filter, w_out):
    own_rows, local_width = tokens.shape
    n_tp = lax.axis_size("tp")
    model_width = local_width * n_tp
    short_taps = short_filter.shape[0]
    filter_len = long_filter.shape[0]
    half = lax.axis_index("lo")
    other = 1 - half
    half_width = local_width // 2

    w_keep = half_of(w_in, 2, half)
    w_recv = swap_pair(half_of(w_in, 2, other))
    w_pair = pair_ordered(w_keep, w_recv, half, 0)
    w_full = lax.all_gather(w_pair, "hi", axis=0, tiled=True)

    o_keep = half_of(w_out, 0, half)
    o_recv = swap_pair(half_of(w_out, 0, other))
    o_pair = pair_ordered(o_keep, o_recv, half, 1)
    o_full = lax.all_gather(o_pair, "hi", axis=1, tiled=True)

    gathered = lax.all_gather(tokens, "tp", axis=1, tiled=True)
    pair_tokens = lax.all_gather(gathered, "lo", axis=0, tiled=True)
    row_count = pair_tokens.shape[0]
    wide_float = pair_tokens.astype(jnp.float32)
    scale = lax.rsqrt(jnp.mean(wide_float * wide_float, axis=-1, keepdims=True) + 1e-06)
    normed = (wide_float * scale * norm_gain).astype(jnp.bfloat16)

    projected = jnp.dot(
        normed, w_full.reshape(model_width, 3 * half_width), preferred_element_type=jnp.float32
    )
    projected = projected.astype(jnp.bfloat16).reshape(row_count, 3, half_width)

    taps = half_of(short_filter, 2, half)
    prior_rows = shifted(projected[row_count - (short_taps - 1) :], "hi", 1)
    featured = featurize(jnp.concatenate([prior_rows, projected], axis=0), taps, row_count)
    mixed = (featured[:, 1] * featured[:, 2]).astype(jnp.bfloat16)
    mixed_prior = shifted(mixed[row_count - (filter_len - 1) :], "hi", 1)
    query = featured[:, 0]
    zero_row = jnp.zeros((1, half_width), jnp.bfloat16)
    extended_mix = jnp.concatenate([zero_row, mixed_prior, mixed], axis=0)
    groups_here = long_filter.shape[1] // 2
    group_size = half_width // groups_here
    mix_blocks = extended_mix.reshape(
        row_count // filter_len + 1, filter_len, groups_here, group_size
    )
    current, previous = toeplitz_pair(half_of(long_filter, 1, half))
    filtered = jnp.einsum(
        "gts,bsgc->btgc", current, mix_blocks[1:], preferred_element_type=jnp.float32
    )
    filtered = filtered + jnp.einsum(
        "gts,bsgc->btgc", previous, mix_blocks[:-1], preferred_element_type=jnp.float32
    )
    gated = (query * filtered.reshape(row_count, half_width)).astype(jnp.bfloat16)

    terms = jnp.dot(gated, o_full, preferred_element_type=jnp.float32).astype(jnp.bfloat16)
    terms = terms.reshape(2, own_rows, n_tp, local_width).transpose(0, 2, 1, 3)
    terms = terms.reshape(2 * n_tp, own_rows, local_width)
    summed = lax.psum_scatter(terms, ("lo", "tp"), scatter_dimension=0, tiled=True)
    summed = summed.reshape(own_rows, local_width).astype(jnp.float32)
    return (tokens.astype(jnp.float32) + summed).astype(jnp.bfloat16)


def solution(mesh):
    n_ctx, n_tp = mesh.devices.shape
    paired = Mesh(mesh.devices.reshape(n_ctx // 2, 2, n_tp), ("hi", "lo", "tp"))
    ctx = ("hi", "lo")
    placed = (
        P(ctx, "tp"),
        P(),
        P(ctx, None, "tp"),
        P(None, None, "tp"),
        P(None, "tp"),
        P("tp", ctx),
    )
    return jax.shard_map(
        local, mesh=paired, in_specs=placed, out_specs=P(ctx, "tp"), check_vma=False
    )
```

time: 1400 us -> 1080 us (0.77)
  waiting for transfers between devices: 1060 us -> 771 us
  local copies, waits for them, and re-layouts: 181 us -> 139 us
    all_gather x2 -> x3, waiting for transfers between devices: 1020 us -> 570 us  [the longest x1 476 us: local(): w_full = lax.all_gather(w_pair, 'hi', axis=0, tiled=True)]
    gather x4 -> x0, local copies, waits for them, and re-layouts: 129 us -> none  [the longest x2 64.5 us: toeplitz_pair(): table[:, jnp.clip(offsets, 0, filter_len - 1)]]
    reduce_scatter x1, waiting for transfers between devices: 18.6 us -> 100 us  [local(): lax.psum_scatter(terms, ('lo', 'tp'), scatter_dimension=0, tiled=True)]
    ppermute x0 -> x2, waiting for transfers between devices: none -> 79.2 us  [swap_pair(): return lax.ppermute(value, 'lo', [(0, 1), (1, 0)])]
    reshape x0 -> x3, local copies, waits for them, and re-layouts: none -> 52.8 us  [the longest x2 31.7 us: skew(): flat.reshape(groups, filter_len, 2 * filter_len - 1)[:, :, :filter_len]]
  transfers between devices with their start and end apart: 6 -> 9, of which waited for: 4 -> 6; matrix products, arithmetic and copies ran while one was open for 20% -> 19% of each run, Pallas kernels for 0% -> 0%
where the time goes in v1:
time: 1080 us; the launch traced here: 1070 us
  waiting for transfers between devices  771 us (71%)
  local copies, waits for them, and re-layouts  139 us (13%)
  matrix products  82.2 us (8%)
  other arithmetic  56.2 us (5%)
  between operations  13.6 us (1%)
  starting transfers between devices  11.7 us (1%)
    all_gather x1, waiting for transfers between devices, local(): w_full = lax.all_gather(w_pair, 'hi', axis=0, tiled=True)  476 us
    reduce_scatter x1, waiting for transfers between devices, local(): lax.psum_scatter(terms, ('lo', 'tp'), scatter_dimension=0, tiled=True)  100 us
    all_gather x1, waiting for transfers between devices, local(): pair_tokens = lax.all_gather(gathered, 'lo', axis=0, tiled=True)  93.8 us
    ppermute x2, waiting for transfers between devices, swap_pair(): return lax.ppermute(value, 'lo', [(0, 1), (1, 0)])  79.2 us
    dot_general x1, matrix products, local(): jnp.dot(normed, w_full.reshape(model_width, 3 * half_width), preferred_el...  48.7 us
    reshape x2, local copies, waits for them, and re-layouts, skew(): flat.reshape(groups, filter_len, 2 * filter_len - 1)[:, :, :filter_len]  31.7 us
    dot_general x1, matrix products, local(): jnp.dot(gated, o_full, preferred_element_type=jnp.float32)  27.5 us
    add x1, other arithmetic, featurize(): featured + short_filter[tap] * ext_float[short_taps - 1 - tap:short_taps...  21.7 us
  transfers between devices with their start and end apart: 9, of which 6 were waited for; matrix products, arithmetic and copies ran while one was open for 19% of the time, Pallas kernels for 0%

profile of v1, /device:TPU:0, one launch (start us, length us, event | category | flops | bytes accessed | tf_op | source)
XLA Modules:
  0.0 1073.7 jit_solution(14046879931309871952)
XLA Ops:
  7.3 21.1 %all-gather.5.cloned.1.call-done = bf16[768,4096]{1,0:T(8,128)(2,1)} async-done(((bf16[768,2048]{1,0:T(8,128)(2,1)}), bf16[768,4096]{1,0:T(8,128)(2,1)}) %all-gather.5.cloned.1.call-update) | async-done | bytes 6291472 | tf_op jit(solution)/shard_map/all_gather | solution.py:77
  28.5 2.2 constant_dynamic-slice_fusion.2
  34.7 56.1 %collective-permute-done = bf16[256,3,1024]{0,2,1:T(8,128)(2,1)} collective-permute-done((bf16[256,3,1024]{0,2,1:T(8,128)(2,1)}, bf16[256,3,1024]{0,2,1:T(8,128)(2,1)}, u32[]{:S(2)}, u32[]{:S(2)}) %collective-permute-start) | collective-permute-done | bytes 1572896 | tf_op jit(solution)/shard_map/ppermute | solution.py:15
  94.5 2.5 collective-permute-start.3
  97.0 23.2 %collective-permute-done.3 = bf16[1024,256]{1,0:T(8,128)(2,1)S(1)} collective-permute-done((bf16[1024,256]{1,0:T(8,128)(2,1)S(1)}, bf16[1024,256]{1,0:T(8,128)(2,1)S(1)}, u32[]{:S(2)}, u32[]{:S(2)}) %collective-permute-start.3) | collective-permute-done | bytes 524320 | tf_op jit(solution)/shard_map/ppermute | solution.py:15
  121.5 93.8 %all-gather.7.cloned.1.call-done = bf16[1536,4096]{1,0:T(8,128)(2,1)} async-done(((bf16[768,4096]{1,0:T(8,128)(2,1)}), bf16[1536,4096]{1,0:T(8,128)(2,1)}) %all-gather.7.cloned.1.call-update) | async-done | bytes 12582928 | tf_op jit(solution)/shard_map/all_gather | solution.py:78
  215.3 7.1 fusion
  222.4 476.1 %all-gather.9.cloned.1.call-done = bf16[4096,3,1024]{0,2,1:T(8,128)(2,1)} async-done(((bf16[512,3,1024]{0,2,1:T(8,128)(2,1)}), bf16[4096,3,1024]{0,2,1:T(8,128)(2,1)}) %all-gather.9.cloned.1.call-update) | async-done | bytes 25165840 | tf_op jit(solution)/shard_map/all_gather | solution.py:70
  698.6 48.7 %fusion.9 = bf16[1536,3072]{1,0:T(8,128)(2,1)} fusion(bf16[4096,3072]{0,1:T(8,128)(2,1)} %bitcast.63, bf16[1536,4096]{1,0:T(8,128)(2,1)} %all-gather.7.cloned.1.call-done, f32[4096]{0:T(1024)S(1)} %copy-done.8, f32[1536]{0:T(1024)S(1)} %add_rsqrt_fusion), kind=kOutput, calls=%fused_computation.14 | convolution fusion | flops 38684590080 | bytes 47208448 | tf_op jit(solution)/shard_map/dot_general | solution.py:84
  748.1 2.4 collective-permute-start.1
  750.6 12.8 %copy.13 = bf16[1536,3072]{0,1:T(8,128)(2,1)} copy(bf16[1536,3072]{1,0:T(8,128)(2,1)} %fusion.9) | data formatting | bytes 18874368 | tf_op jit(solution)/shard_map/convert_element_type | solution.py:87
  763.8 15.1 %maximum_convert_fusion = f32[1538,3,1024]{0,2,1:T(8,128)} fusion(bf16[1536,3,1024]{0,2,1:T(8,128)(2,1)} %bitcast.56, bf16[2,3,1024]{0,2,1:T(8,128)(2,1)S(1)} %copy.14), kind=kLoop, calls=%fused_computation.15 | loop fusion | flops 18898944 | bytes 28348416 | tf_op jit(solution)/shard_map/convert_element_type | solution.py:36
  778.9 21.7 %fusion.3 = f32[1536,3,1024]{0,2,1:T(8,128)S(1)} fusion(f32[1538,3,1024]{0,2,1:T(8,128)} %maximum_convert_fusion, f32[3,1024]{1,0:T(4,128)S(1)} %get-tuple-element.13, f32[3,1024]{1,0:T(4,128)S(1)} %get-tuple-element.12, f32[3,1024]{1,0:T(4,128)S(1)} %get-tuple-element.11), kind=kLoop, calls=%fused_computation.6 | loop fusion | flops 23592960 | bytes 75534336 | tf_op jit(solution)/shard_map/add | solution.py:40
  800.6 6.5 copy-done.1
  807.1 2.7 fusion.13
  811.6 4.8 collective-permute-start.2
  818.0 3.3 slice.89
  821.3 15.8 %reshape.55 = bf16[64,128,255]{2,1,0:T(8,128)(2,1)} reshape(bf16[64,32640]{1,0:T(8,128)(2,1)} %slice.89) | data formatting | bytes 8355840 | tf_op jit(solution)/shard_map/reshape | solution.py:27
  838.5 3.3 slice.85
  841.8 15.8 %reshape.54 = bf16[64,128,255]{2,1,0:T(8,128)(2,1)} reshape(bf16[64,32640]{1,0:T(8,128)(2,1)} %slice.85) | data formatting | bytes 8355840 | tf_op jit(solution)/shard_map/reshape | solution.py:27
  857.7 2.8 copy.17
  860.5 3.6 convert_element_type.46
  865.0 13.2 %concatenate.21 = bf16[1664,1024]{1,0:T(8,128)(2,1)S(1)} concatenate(bf16[1,1024]{1,0:T(2,128)(2,1)S(1)} %broadcast_in_dim.2, bf16[127,1024]{1,0:T(8,128)(2,1)} %copy.18, bf16[1536,1024]{1,0:T(8,128)(2,1)} %bitcast.61), dimensions={0} | concatenate | bytes 6815744 | tf_op jit(solution)/shard_map/concatenate | solution.py:96
  880.2 3.2 copy.19
  883.3 3.8 slice.75
  887.2 4.5 fusion.16
  893.9 6.1 copy.22
  900.1 27.5 %convolution_convert_fusion = bf16[1536,4096]{1,0:T(8,128)(2,1)} fusion(bf16[1024,4096]{1,0:T(8,128)(2,1)} %all-gather.11.cloned.1.call-done, f32[128,8,12,128]{3,2,1,0:T(8,128)} %bitcast.62, f32[1536,3,1024]{0,2,1:T(8,128)} %copy-done.1), kind=kOutput, calls=%fused_computation.10 | convolution fusion | flops 12894339072 | bytes 35651584 | tf_op jit(solution)/shard_map/dot_general | solution.py:111
  927.6 21.1 %reshape.57 = bf16[2,768,2,2048]{3,2,1,0:T(2,128)(2,1)} reshape(bf16[1536,4096]{1,0:T(8,128)(2,1)} %convolution_convert_fusion) | data formatting | bytes 25165824 | tf_op jit(solution)/shard_map/reshape | solution.py:112
  948.7 13.4 %copy.23 = bf16[2,2,768,2048]{3,2,1,0:T(8,128)(2,1)} copy(bf16[2,2,768,2048]{3,1,2,0:T(2,128)(2,1)} %bitcast.55) | data formatting | bytes 25165824 | tf_op jit(solution)/shard_map/transpose | solution.py:112
  962.1 100.0 %reduce-scatter.2.cloned.1.call-done = bf16[1,768,2048]{2,1,0:T(8,128)(2,1)} async-done(((bf16[4,768,2048]{2,1,0:T(8,128)(2,1)}), bf16[1,768,2048]{2,1,0:T(8,128)(2,1)}) %reduce-scatter.2.cloned.1.call-update) | async-done | bytes 3145744 | tf_op jit(solution)/shard_map/reduce_scatter | solution.py:114
  1062.1 4.9 fusion.14
  (58 shorter events, 20.9 us)
Async XLA Ops:
  6.5 809.9 %copy-start = (bf16[128,128]{1,0:T(8,128)(2,1)S(1)}, bf16[128,128]{1,0:T(8,128)(2,1)}, u32[]{:S(2)}) copy-start(bf16[128,128]{1,0:T(8,128)(2,1)} %param.10) | copy-start | bytes 98308
  6.5 21.9 %all-gather.5.cloned.1.call-start = ((), (), s32[]{:S(2)}) async-start(), calls=%async_computation.1 | async-start | bytes 9437184 | tf_op jit(solution)/shard_map/all_gather | solution.py:77
  7.3 208.1 %all-gather.7.cloned.1.call-start = ((), (), s32[]{:S(2)}) async-start(), calls=%async_computation.2 | async-start | bytes 18874368 | tf_op jit(solution)/shard_map/all_gather | solution.py:78
  28.4 670.1 %all-gather.9.cloned.1.call-start = ((), (), s32[]{:S(2)}) async-start(), calls=%async_computation.3 | async-start | bytes 28311552 | tf_op jit(solution)/shard_map/all_gather | solution.py:70
  32.2 58.5 %collective-permute-start = (bf16[256,3,1024]{0,2,1:T(8,128)(2,1)}, bf16[256,3,1024]{0,2,1:T(8,128)(2,1)}, u32[]{:S(2)}, u32[]{:S(2)}) collective-permute-start(bf16[256,3,1024]{0,2,1:T(8,128)(2,1)} %copy.27), channel_id=1, source_target_pairs={{0,2},{2,0},{1,3},{3,1},{4,6},{6,4},{5,7},{7,5},{8,10},{10,8},{9,1... | collective-permute-start | bytes 4718600 | tf_op jit(solution)/shard_map/ppermute | solution.py:15
  92.4 2.0 copy-start.6
  94.3 805.7 %all-gather.11.cloned.1.call-start = ((), (), s32[]{:S(2)}) async-start(), calls=%async_computation.4 | async-start | bytes 9437184 | tf_op jit(solution)/shard_map/all_gather | solution.py:75
  94.5 25.7 %collective-permute-start.3 = (bf16[1024,256]{1,0:T(8,128)(2,1)S(1)}, bf16[1024,256]{1,0:T(8,128)(2,1)S(1)}, u32[]{:S(2)}, u32[]{:S(2)}) collective-permute-start(bf16[1024,256]{1,0:T(8,128)(2,1)S(1)} %constant_dynamic-slice_fusion), channel_id=1, source_target_pairs={{0,2},{2,0},{1,3},{3,1},{4,6},{6,4},{5,7},{7,5},{8,10},{10,8},{9,1... | collective-permute-start | bytes 1572872 | tf_op jit(solution)/shard_map/ppermute | solution.py:15
  121.5 940.7 %reduce-scatter.2.cloned.1.call-start = ((), (), s32[]{:S(2)}) async-start(), calls=%async_computation.5 | async-start | bytes 15728640 | tf_op jit(solution)/shard_map/reduce_scatter | solution.py:114
  121.5 577.0 %copy-start.8 = (f32[4096]{0:T(1024)S(1)}, f32[4096]{0:T(1024)}, u32[]{:S(2)}) copy-start(f32[4096]{0:T(1024)} %param.7) | copy-start | bytes 49156
  698.5 52.0 %copy-start.7 = (f32[3,3,2048]{2,1,0:T(4,128)S(1)}, f32[3,3,2048]{2,1,0:T(4,128)}, u32[]{:S(2)}) copy-start(f32[3,3,2048]{2,1,0:T(4,128)} %param.9) | copy-start | bytes 221188
  748.1 15.3 %collective-permute-start.1 = (bf16[2,3,1024]{2,1,0:T(4,128)(2,1)S(1)}, bf16[2,3,1024]{2,1,0:T(4,128)(2,1)S(1)}, u32[]{:S(2)}, u32[]{:S(2)}) collective-permute-start(bf16[2,3,1024]{2,1,0:T(4,128)(2,1)S(1)} %slice.61), channel_id=1, source_target_pairs={{0,4},{4,8},{8,12},{12,16},{16,20},{20,24},{24,28},{1,5},{5,9},{9,... | collective-permute-start | bytes 36872 | tf_op jit(solution)/shard_map/ppermute | solution.py:11
  800.6 6.6 copy-start.1
  811.6 52.5 %collective-permute-start.2 = (bf16[127,1024]{0,1:T(8,128)(2,1)}, bf16[127,1024]{0,1:T(8,128)(2,1)S(1)}, u32[]{:S(2)}, u32[]{:S(2)}) collective-permute-start(bf16[127,1024]{0,1:T(8,128)(2,1)} %slice_bitcast_fusion.5), channel_id=1, source_target_pairs={{0,4},{4,8},{8,12},{12,16},{16,20},{20,24},{24,28},{1,5},{5,9},{9,... | collective-permute-start | bytes 780296 | tf_op jit(solution)/shard_map/ppermute | solution.py:11
  838.5 19.2 %copy-start.2 = (bf16[1536,1,1024]{0,2,1:T(8,128)(2,1)S(1)}, bf16[1536,1,1024]{0,2,1:T(8,128)(2,1)}, u32[]{:S(2)}) copy-start(bf16[1536,1,1024]{0,2,1:T(8,128)(2,1)} %fusion.13) | copy-start | bytes 9437188
  887.2 4.5 copy-start.3
  887.2 5.3 copy-start.5
  962.1 100.0 %copy-start.4 = (bf16[768,2048]{1,0:T(8,128)(2,1)S(1)}, bf16[768,2048]{1,0:T(8,128)(2,1)}, u32[]{:S(2)}) copy-start(bf16[768,2048]{1,0:T(8,128)(2,1)} %param.6) | copy-start | bytes 9437188
Sparse Core Ops, SparseCore 0:
  8.9 19.4 all-gather.4
  30.0 185.3 all-gather.6
  216.9 481.6 all-gather.8
  700.4 125.5 all-gather.10
  962.3 99.8 reduce-scatter.1

commit v2 on v1

--- a/solution.py
+++ b/solution.py
@@ -54,37 +54,69 @@
     return jnp.concatenate([first, second], axis=axis)
 
 
+def ring_order(count):
+    return list(range(0, count, 2)) + list(range(count - 1 - count % 2, 0, -2))
+
+
 def local(tokens, norm_gain, w_in, short_filter, long_filter, w_out):
     own_rows, local_width = tokens.shape
     n_tp = lax.axis_size("tp")
+    n_hi = lax.axis_size("hi")
     model_width = local_width * n_tp
     short_taps = short_filter.shape[0]
     filter_len = long_filter.shape[0]
+    w_rows = w_in.shape[0]
     half = lax.axis_index("lo")
     other = 1 - half
     half_width = local_width // 2
 
-    w_keep = half_of(w_in, 2, half)
-    w_recv = swap_pair(half_of(w_in, 2, other))
-    w_pair = pair_ordered(w_keep, w_recv, half, 0)
-    w_full = lax.all_gather(w_pair, "hi", axis=0, tiled=True)
+    pair_tokens = pair_ordered(tokens, swap_pair(tokens), half, 0)
+    pair_tokens = lax.all_gather(pair_tokens, "tp", axis=1, tiled=True)
+    row_count = pair_tokens.shape[0]
+    wide_float = pair_tokens.astype(jnp.float32)
+    scale = lax.rsqrt(jnp.mean(wide_float * wide_float, axis=-1, keepdims=True) + 1e-06)
+    normed = (wide_float * scale * norm_gain).astype(jnp.bfloat16)
+
+    own_piece = half_of(w_in, 2, half).reshape(w_rows, 3 * half_width)
+    partner_piece = swap_pair(half_of(w_in, 2, other)).reshape(w_rows, 3 * half_width)
+    order = ring_order(n_hi)
+    place = [0] * n_hi
+    for index, member in enumerate(order):
+        place[member] = index
+    order_table = jnp.array(order, jnp.int32)
+    here = jnp.array(place, jnp.int32)[lax.axis_index("hi")]
+    forward = [(order[i], order[(i + 1) % n_hi]) for i in range(n_hi)]
+    backward = [(order[(i + 1) % n_hi], order[i]) for i in range(n_hi)]
+
+    def contribution(piece, ctx_index):
+        columns = lax.dynamic_slice_in_dim(normed, ctx_index * w_rows, w_rows, axis=1)
+        return jnp.dot(columns, piece, preferred_element_type=jnp.float32)
+
+    def ring_step(step, carry):
+        own, partner, total = carry
+        own_from = order_table[(here - step) % n_hi]
+        partner_from = order_table[(here + step) % n_hi]
+        total = total + contribution(own, 2 * own_from + half)
+        total = total + contribution(partner, 2 * partner_from + other)
+        own = lax.ppermute(own, "hi", forward)
+        partner = lax.ppermute(partner, "hi", backward)
+        return own, partner, total
+
+    total = jnp.zeros((row_count, 3 * half_width), jnp.float32)
+    own_piece, partner_piece, total = lax.fori_loop(
+        0, n_hi - 1, ring_step, (own_piece, partner_piece, total)
+    )
+    last = n_hi - 1
+    total = total + contribution(own_piece, 2 * order_table[(here - last) % n_hi] + half)
+    projected = total + contribution(
+        partner_piece, 2 * order_table[(here + last) % n_hi] + other
+    )
+    projected = projected.astype(jnp.bfloat16).reshape(row_count, 3, half_width)
 
     o_keep = half_of(w_out, 0, half)
     o_recv = swap_pair(half_of(w_out, 0, other))
     o_pair = pair_ordered(o_keep, o_recv, half, 1)
     o_full = lax.all_gather(o_pair, "hi", axis=1, tiled=True)
-
-    gathered = lax.all_gather(tokens, "tp", axis=1, tiled=True)
-    pair_tokens = lax.all_gather(gathered, "lo", axis=0, tiled=True)
-    row_count = pair_tokens.shape[0]
-    wide_float = pair_tokens.astype(jnp.float32)
-    scale = lax.rsqrt(jnp.mean(wide_float * wide_float, axis=-1, keepdims=True) + 1e-06)
-    normed = (wide_float * scale * norm_gain).astype(jnp.bfloat16)
-
-    projected = jnp.dot(
-        normed, w_full.reshape(model_width, 3 * half_width), preferred_element_type=jnp.float32
-    )
-    projected = projected.astype(jnp.bfloat16).reshape(row_count, 3, half_width)
 
     taps = half_of(short_filter, 2, half)
     prior_rows = shifted(projected[row_count - (short_taps - 1) :], "hi", 1)
@@ -109,11 +141,9 @@
     gated = (query * filtered.reshape(row_count, half_width)).astype(jnp.bfloat16)
 
     terms = jnp.dot(gated, o_full, preferred_element_type=jnp.float32).astype(jnp.bfloat16)
-    terms = terms.reshape(2, own_rows, n_tp, local_width).transpose(0, 2, 1, 3)
-    terms = terms.reshape(2 * n_tp, own_rows, local_width)
-    summed = lax.psum_scatter(terms, ("lo", "tp"), scatter_dimension=0, tiled=True)
-    summed = summed.reshape(own_rows, local_width).astype(jnp.float32)
-    return (tokens.astype(jnp.float32) + summed).astype(jnp.bfloat16)
+    summed = lax.psum_scatter(terms, "tp", scatter_dimension=1, tiled=True)
+    summed = lax.psum_scatter(summed, "lo", scatter_dimension=0, tiled=True)
+    return (tokens.astype(jnp.float32) + summed.astype(jnp.float32)).astype(jnp.bfloat16)
 
 
 def solution(mesh):

time: 1080 us -> 837 us (0.78)
  waiting for transfers between devices: 771 us -> 290 us
  matrix products: 82.2 us -> 261 us
  starting transfers between devices: 11.7 us -> 39.4 us
  loops' own time: 0 us -> 17.8 us
  other arithmetic: 56.2 us -> 72 us
    all_gather x3 -> x1, waiting for transfers between devices: 591 us -> 0.01 us  [local(): pair_tokens = lax.all_gather(pair_tokens, 'tp', axis=1, tiled=True)]
    dot_general x1 -> x16, matrix products: 48.7 us -> 227 us  [contribution(): return jnp.dot(columns, piece, preferred_element_type=jnp.float32)]
    ppermute x0 -> x14, waiting for transfers between devices: none -> 84.9 us  [the longest x7 60.2 us: ring_step(): own = lax.ppermute(own, 'hi', forward)]
    ppermute x0 -> x14, starting transfers between devices: none -> 27.1 us  [the longest x7 23.7 us: ring_step(): own = lax.ppermute(own, 'hi', forward)]
    ppermute x2 -> x3, waiting for transfers between devices: 79.2 us -> 105 us  [swap_pair(): return lax.ppermute(value, 'lo', [(0, 1), (1, 0)])]
    reshape x1 -> x0, local copies, waits for them, and re-layouts: 21.1 us -> none  [local(): terms = terms.reshape(2, own_rows, n_tp, local_width).transpose(0, 2, 1, 3)]
    while x0 -> x14, local copies, waits for them, and re-layouts: none -> 19.7 us
    another operation x0 -> x1, loops' own time: none -> 17.8 us  [local(): lax.fori_loop(0, n_hi - 1, ring_step, (own_piece, partner_piece, total))]
  transfers between devices with their start and end apart: 9 -> 23, of which waited for: 6 -> 11; matrix products, arithmetic and copies ran while one was open for 19% -> 51% of each run, Pallas kernels for 0% -> 0%
where the time goes in v2:
time: 837 us; the launch traced here: 832 us
  waiting for transfers between devices  290 us (35%)
  matrix products  261 us (31%)
  local copies, waits for them, and re-layouts  136 us (16%)
  other arithmetic  72 us (9%)
  starting transfers between devices  39.4 us (5%)
  loops' own time  17.8 us (2%)
  between operations  16 us (2%)
    dot_general x16, matrix products, contribution(): return jnp.dot(columns, piece, preferred_element_type=jnp.float32)  227 us
    ppermute x3, waiting for transfers between devices, swap_pair(): return lax.ppermute(value, 'lo', [(0, 1), (1, 0)])  105 us
    reduce_scatter x1, waiting for transfers between devices, local(): summed = lax.psum_scatter(summed, 'lo', scatter_dimension=0, tiled=True)  80.4 us
    ppermute x7, waiting for transfers between devices, ring_step(): own = lax.ppermute(own, 'hi', forward)  60.2 us
    reshape x2, local copies, waits for them, and re-layouts, skew(): flat.reshape(groups, filter_len, 2 * filter_len - 1)[:, :, :filter_len]  31.7 us
    dot_general x1, matrix products, local(): jnp.dot(gated, o_full, preferred_element_type=jnp.float32)  27.7 us
    ppermute x7, waiting for transfers between devices, ring_step(): partner = lax.ppermute(partner, 'hi', backward)  24.8 us
    ppermute x7, starting transfers between devices, ring_step(): own = lax.ppermute(own, 'hi', forward)  23.7 us
  transfers between devices with their start and end apart: 23, of which 11 were waited for; matrix products, arithmetic and copies ran while one was open for 51% of the time, Pallas kernels for 0%

profile of v2, /device:TPU:0, one launch (start us, length us, event | category | flops | bytes accessed | tf_op | source)
XLA Modules:
  0.0 831.9 jit_solution(14478085673087479549)
XLA Ops:
  9.5 68.3 %collective-permute-done.3 = bf16[768,2048]{1,0:T(8,128)(2,1)S(1)} collective-permute-done((bf16[768,2048]{1,0:T(8,128)(2,1)}, bf16[768,2048]{1,0:T(8,128)(2,1)S(1)}, u32[]{:S(2)}, u32[]{:S(2)}) %collective-permute-start.3) | collective-permute-done | bytes 3145760 | tf_op jit(solution)/shard_map/ppermute | solution.py:15
  97.8 37.1 %collective-permute-done.6 = bf16[1024,256]{1,0:T(8,128)(2,1)} collective-permute-done((bf16[1024,256]{1,0:T(8,128)(2,1)}, bf16[1024,256]{1,0:T(8,128)(2,1)}, u32[]{:S(2)}, u32[]{:S(2)}) %collective-permute-start.6) | collective-permute-done | bytes 524320 | tf_op jit(solution)/shard_map/ppermute | solution.py:15
  147.7 11.9 %fusion.8 = bf16[1536,4096]{1,0:T(8,128)(2,1)} fusion(bf16[1536,4096]{1,0:T(8,128)(2,1)} %all-gather.3.cloned.1.call-done, f32[4096]{0:T(1024)S(1)} %copy-done.8, f32[1536]{0:T(1024)S(1)} %add_rsqrt_fusion), kind=kLoop, calls=%fused_computation.11 | loop fusion | flops 25165824 | bytes 25188352 | tf_op jit(solution)/shard_map/convert_element_type | solution.py:78
  159.5 353.2 %while.21 = (s32[]{:T(128)}, bf16[256,3072]{1,0:T(8,128)(2,1)}, bf16[256,3072]{1,0:T(8,128)(2,1)}, f32[1536,3072]{1,0:T(8,128)}, s32[]{:T(128)}, /*index=5*/s32[...) while((s32[]{:T(128)}, bf16[256,3072]{1,0:T(8,128)(2,1)}, ...), condition=%wide.region_2.3_spmd.clone.clone, body=%wide.region_1.2_spmd.sunk.clone.clone.sunk | while | flops 4845993984 | bytes 99091128 | solution.py:106
  167.6 9.1 %fusion.48 = f32[1536,3072]{1,0:T(8,128)} fusion(bf16[256,3072]{1,0:T(8,128)(2,1)S(1)} %copy.48, bf16[1536,4096]{1,0:T(8,128)(2,1)} %get-tuple-element.415, s32[]{:T(128)S(6)} %select_n.182), kind=kOutput, calls=%fused_computation.3.clone.1 | convolution fusion | flops 2415919104 | bytes 21233668 | tf_op jit(solution)/shard_map/while/body/eval_jaxpr/dot_general | solution.py:93
  176.7 12.8 %fusion.49 = f32[1536,3072]{1,0:T(8,128)} fusion(f32[1536,3072]{1,0:T(8,128)} %fusion.48, f32[1536,3072]{1,0:T(8,128)} %get-tuple-element.396, bf16[256,3072]{1,0:T(8,128)(2,1)S(1)} %copy.49, pred[]{:T(512)S(6)} %compare.9, bf16[1536,4096]{1,0:T(8,128)(2,1)} %get-tuple-element.415, s32[]{:T(128)S(6)} %select_n.183), kind=kOutput, calls=%fused_computation.1.clone.1 | convolution fusion | flops 2430074880 | bytes 58982404 | tf_op jit(solution)/shard_map/while/body/eval_jaxpr/dot_general | solution.py:93
  189.4 33.0 %collective-permute-done = bf16[256,3072]{1,0:T(8,128)(2,1)} collective-permute-done((bf16[256,3072]{1,0:T(8,128)(2,1)S(1)}, bf16[256,3072]{1,0:T(8,128)(2,1)}, u32[]{:S(2)}, u32[]{:S(2)}) %collective-permute-start) | collective-permute-done | bytes 1572896 | tf_op jit(solution)/shard_map/while/body/eval_jaxpr/ppermute | solution.py:101
  229.6 10.6 %collective-permute-start = (bf16[256,3072]{1,0:T(8,128)(2,1)S(1)}, bf16[256,3072]{1,0:T(8,128)(2,1)}, u32[]{:S(2)}, u32[]{:S(2)}) collective-permute-start(bf16[256,3072]{1,0:T(8,128)(2,1)S(1)} %copy.48), channel_id=1, source_target_pairs={{0,8},{8,16},{16,24},{24,28},{28,20},{20,12},{12,4},{4,0},{1,9},{9... | collective-permute-start | bytes 4718600 | tf_op jit(solution)/shard_map/while/body/eval_jaxpr/ppermute | solution.py:101
  244.9 9.1 %fusion.48 = f32[1536,3072]{1,0:T(8,128)} fusion(bf16[256,3072]{1,0:T(8,128)(2,1)S(1)} %copy.48, bf16[1536,4096]{1,0:T(8,128)(2,1)} %get-tuple-element.415, s32[]{:T(128)S(6)} %select_n.182), kind=kOutput, calls=%fused_computation.3.clone.1 | convolution fusion | flops 2415919104 | bytes 21233668 | tf_op jit(solution)/shard_map/while/body/eval_jaxpr/dot_general | solution.py:93
  254.0 20.4 %fusion.49 = f32[1536,3072]{1,0:T(8,128)} fusion(f32[1536,3072]{1,0:T(8,128)} %fusion.48, f32[1536,3072]{1,0:T(8,128)} %get-tuple-element.396, bf16[256,3072]{1,0:T(8,128)(2,1)S(1)} %copy.49, pred[]{:T(512)S(6)} %compare.9, bf16[1536,4096]{1,0:T(8,128)(2,1)} %get-tuple-element.415, s32[]{:T(128)S(6)} %select_n.183), kind=kOutput, calls=%fused_computation.1.clone.1 | convolution fusion | flops 2430074880 | bytes 58982404 | tf_op jit(solution)/shard_map/while/body/eval_jaxpr/dot_general | solution.py:93
  274.4 27.1 %collective-permute-done = bf16[256,3072]{1,0:T(8,128)(2,1)} collective-permute-done((bf16[256,3072]{1,0:T(8,128)(2,1)S(1)}, bf16[256,3072]{1,0:T(8,128)(2,1)}, u32[]{:S(2)}, u32[]{:S(2)}) %collective-permute-start) | collective-permute-done | bytes 1572896 | tf_op jit(solution)/shard_map/while/body/eval_jaxpr/ppermute | solution.py:101
  301.6 14.7 %collective-permute-done.1 = bf16[256,3072]{1,0:T(8,128)(2,1)} collective-permute-done((bf16[256,3072]{1,0:T(8,128)(2,1)S(1)}, bf16[256,3072]{1,0:T(8,128)(2,1)}, u32[]{:S(2)}, u32[]{:S(2)}) %collective-permute-start.1) | collective-permute-done | bytes 1572896 | tf_op jit(solution)/shard_map/while/body/eval_jaxpr/ppermute | solution.py:102
  326.7 9.1 %fusion.48 = f32[1536,3072]{1,0:T(8,128)} fusion(bf16[256,3072]{1,0:T(8,128)(2,1)S(1)} %copy.48, bf16[1536,4096]{1,0:T(8,128)(2,1)} %get-tuple-element.415, s32[]{:T(128)S(6)} %select_n.182), kind=kOutput, calls=%fused_computation.3.clone.1 | convolution fusion | flops 2415919104 | bytes 21233668 | tf_op jit(solution)/shard_map/while/body/eval_jaxpr/dot_general | solution.py:93
  335.8 20.4 %fusion.49 = f32[1536,3072]{1,0:T(8,128)} fusion(f32[1536,3072]{1,0:T(8,128)} %fusion.48, f32[1536,3072]{1,0:T(8,128)} %get-tuple-element.396, bf16[256,3072]{1,0:T(8,128)(2,1)S(1)} %copy.49, pred[]{:T(512)S(6)} %compare.9, bf16[1536,4096]{1,0:T(8,128)(2,1)} %get-tuple-element.415, s32[]{:T(128)S(6)} %select_n.183), kind=kOutput, calls=%fused_computation.1.clone.1 | convolution fusion | flops 2430074880 | bytes 58982404 | tf_op jit(solution)/shard_map/while/body/eval_jaxpr/dot_general | solution.py:93
  367.2 9.1 %fusion.48 = f32[1536,3072]{1,0:T(8,128)} fusion(bf16[256,3072]{1,0:T(8,128)(2,1)S(1)} %copy.48, bf16[1536,4096]{1,0:T(8,128)(2,1)} %get-tuple-element.415, s32[]{:T(128)S(6)} %select_n.182), kind=kOutput, calls=%fused_computation.3.clone.1 | convolution fusion | flops 2415919104 | bytes 21233668 | tf_op jit(solution)/shard_map/while/body/eval_jaxpr/dot_general | solution.py:93
  376.3 20.4 %fusion.49 = f32[1536,3072]{1,0:T(8,128)} fusion(f32[1536,3072]{1,0:T(8,128)} %fusion.48, f32[1536,3072]{1,0:T(8,128)} %get-tuple-element.396, bf16[256,3072]{1,0:T(8,128)(2,1)S(1)} %copy.49, pred[]{:T(512)S(6)} %compare.9, bf16[1536,4096]{1,0:T(8,128)(2,1)} %get-tuple-element.415, s32[]{:T(128)S(6)} %select_n.183), kind=kOutput, calls=%fused_computation.1.clone.1 | convolution fusion | flops 2430074880 | bytes 58982404 | tf_op jit(solution)/shard_map/while/body/eval_jaxpr/dot_general | solution.py:93
  407.5 9.1 %fusion.48 = f32[1536,3072]{1,0:T(8,128)} fusion(bf16[256,3072]{1,0:T(8,128)(2,1)S(1)} %copy.48, bf16[1536,4096]{1,0:T(8,128)(2,1)} %get-tuple-element.415, s32[]{:T(128)S(6)} %select_n.182), kind=kOutput, calls=%fused_computation.3.clone.1 | convolution fusion | flops 2415919104 | bytes 21233668 | tf_op jit(solution)/shard_map/while/body/eval_jaxpr/dot_general | solution.py:93
  416.5 20.5 %fusion.49 = f32[1536,3072]{1,0:T(8,128)} fusion(f32[1536,3072]{1,0:T(8,128)} %fusion.48, f32[1536,3072]{1,0:T(8,128)} %get-tuple-element.396, bf16[256,3072]{1,0:T(8,128)(2,1)S(1)} %copy.49, pred[]{:T(512)S(6)} %compare.9, bf16[1536,4096]{1,0:T(8,128)(2,1)} %get-tuple-element.415, s32[]{:T(128)S(6)} %select_n.183), kind=kOutput, calls=%fused_computation.1.clone.1 | convolution fusion | flops 2430074880 | bytes 58982404 | tf_op jit(solution)/shard_map/while/body/eval_jaxpr/dot_general | solution.py:93
  454.6 20.4 %fusion.49 = f32[1536,3072]{1,0:T(8,128)} fusion(f32[1536,3072]{1,0:T(8,128)} %fusion.48, f32[1536,3072]{1,0:T(8,128)} %get-tuple-element.396, bf16[256,3072]{1,0:T(8,128)(2,1)S(1)} %copy.49, pred[]{:T(512)S(6)} %compare.9, bf16[1536,4096]{1,0:T(8,128)(2,1)} %get-tuple-element.415, s32[]{:T(128)S(6)} %select_n.183), kind=kOutput, calls=%fused_computation.1.clone.1 | convolution fusion | flops 2430074880 | bytes 58982404 | tf_op jit(solution)/shard_map/while/body/eval_jaxpr/dot_general | solution.py:93
  483.2 9.1 %fusion.48 = f32[1536,3072]{1,0:T(8,128)} fusion(bf16[256,3072]{1,0:T(8,128)(2,1)S(1)} %copy.48, bf16[1536,4096]{1,0:T(8,128)(2,1)} %get-tuple-element.415, s32[]{:T(128)S(6)} %select_n.182), kind=kOutput, calls=%fused_computation.3.clone.1 | convolution fusion | flops 2415919104 | bytes 21233668 | tf_op jit(solution)/shard_map/while/body/eval_jaxpr/dot_general | solution.py:93
  492.2 20.4 %fusion.49 = f32[1536,3072]{1,0:T(8,128)} fusion(f32[1536,3072]{1,0:T(8,128)} %fusion.48, f32[1536,3072]{1,0:T(8,128)} %get-tuple-element.396, bf16[256,3072]{1,0:T(8,128)(2,1)S(1)} %copy.49, pred[]{:T(512)S(6)} %compare.9, bf16[1536,4096]{1,0:T(8,128)(2,1)} %get-tuple-element.415, s32[]{:T(128)S(6)} %select_n.183), kind=kOutput, calls=%fused_computation.1.clone.1 | convolution fusion | flops 2430074880 | bytes 58982404 | tf_op jit(solution)/shard_map/while/body/eval_jaxpr/dot_general | solution.py:93
  512.7 10.8 %fusion.24 = f32[1536,3072]{1,0:T(8,128)} fusion(bf16[256,3072]{1,0:T(8,128)(2,1)} %get-tuple-element.229, bf16[1536,4096]{1,0:T(8,128)(2,1)} %get-tuple-element.432, s32[]{:T(128)S(6)} %select_n.138), kind=kOutput, calls=%fused_computation.39 | convolution fusion | flops 2415919104 | bytes 21233668 | tf_op jit(solution)/shard_map/dot_general | solution.py:93
  523.5 17.5 %add_convert_fusion = bf16[1536,3072]{1,0:T(8,128)(2,1)} fusion(f32[1536,3072]{1,0:T(8,128)} %get-tuple-element.228, f32[1536,3072]{1,0:T(8,128)} %fusion.24, bf16[256,3072]{1,0:T(8,128)(2,1)} %get-tuple-element.230, bf16[1536,4096]{1,0:T(8,128)(2,1)} %get-tuple-element.432, s32[]{:T(128)S(6)} %select_n.141), kind=kOutput, calls=%fused_computation.17 | convolution fusion | flops 2430074880 | bytes 49545220 | tf_op jit(solution)/shard_map/dot_general | solution.py:93
  544.9 12.7 %copy.18 = bf16[1536,3072]{0,1:T(8,128)(2,1)} copy(bf16[1536,3072]{1,0:T(8,128)(2,1)} %add_convert_fusion) | data formatting | bytes 18874368 | tf_op jit(solution)/shard_map/convert_element_type | solution.py:114
  558.0 15.1 %maximum_convert_fusion = f32[1538,3,1024]{0,2,1:T(8,128)} fusion(bf16[1536,3,1024]{0,2,1:T(8,128)(2,1)} %bitcast.66, bf16[2,3,1024]{0,2,1:T(8,128)(2,1)S(1)} %copy.19), kind=kLoop, calls=%fused_computation.19 | loop fusion | flops 18898944 | bytes 28348416 | tf_op jit(solution)/shard_map/convert_element_type | solution.py:36
  573.1 21.8 %fusion.9 = f32[1536,3,1024]{0,2,1:T(8,128)S(1)} fusion(f32[1538,3,1024]{0,2,1:T(8,128)} %maximum_convert_fusion, f32[3,1024]{1,0:T(4,128)S(1)} %get-tuple-element.319, f32[3,1024]{1,0:T(4,128)S(1)} %get-tuple-element.318, f32[3,1024]{1,0:T(4,128)S(1)} %get-tuple-element.317), kind=kLoop, calls=%fused_computation.13 | loop fusion | flops 23592960 | bytes 75534336 | tf_op jit(solution)/shard_map/add | solution.py:40
  614.5 15.8 %reshape.58 = bf16[64,128,255]{2,1,0:T(8,128)(2,1)} reshape(bf16[64,32640]{1,0:T(8,128)(2,1)} %slice.89) | data formatting | bytes 8355840 | tf_op jit(solution)/shard_map/reshape | solution.py:27
  635.1 15.9 %reshape.57 = bf16[64,128,255]{2,1,0:T(8,128)(2,1)} reshape(bf16[64,32640]{1,0:T(8,128)(2,1)} %slice.85) | data formatting | bytes 8355840 | tf_op jit(solution)/shard_map/reshape | solution.py:27
  658.3 13.2 %concatenate.21 = bf16[1664,1024]{1,0:T(8,128)(2,1)S(1)} concatenate(bf16[1,1024]{1,0:T(2,128)(2,1)S(1)} %broadcast_in_dim.10, bf16[127,1024]{1,0:T(8,128)(2,1)} %copy.23, bf16[1536,1024]{1,0:T(8,128)(2,1)} %bitcast.71), dimensions={0} | concatenate | bytes 6815744 | tf_op jit(solution)/shard_map/concatenate | solution.py:128
  693.4 27.7 %convolution_convert_fusion = bf16[1536,4096]{1,0:T(8,128)(2,1)} fusion(bf16[1024,4096]{1,0:T(8,128)(2,1)} %all-gather.5.cloned.1.call-done, f32[128,8,12,128]{3,2,1,0:T(8,128)} %bitcast.72, f32[1536,3,1024]{0,2,1:T(8,128)} %copy-done.1), kind=kOutput, calls=%fused_computation.18 | convolution fusion | flops 12894339072 | bytes 35651584 | tf_op jit(solution)/shard_map/dot_general | solution.py:143
  721.1 18.8 %reduce-scatter.3.cloned.1.call-done = bf16[1536,2048]{1,0:T(8,128)(2,1)} async-done(((bf16[1536,4096]{1,0:T(8,128)(2,1)}), bf16[1536,2048]{1,0:T(8,128)(2,1)}) %reduce-scatter.3.cloned.1.call-update) | async-done | bytes 6291472 | tf_op jit(solution)/shard_map/reduce_scatter | solution.py:144
  740.0 80.4 %reduce-scatter.5.cloned.1.call-done = bf16[768,2048]{1,0:T(8,128)(2,1)} async-done(((bf16[1536,2048]{1,0:T(8,128)(2,1)}), bf16[768,2048]{1,0:T(8,128)(2,1)}) %reduce-scatter.5.cloned.1.call-update) | async-done | bytes 3145744 | tf_op jit(solution)/shard_map/reduce_scatter | solution.py:145
  (128 shorter events, 155.9 us)
Async XLA Ops:
  6.5 603.2 %copy-start = (bf16[128,128]{1,0:T(8,128)(2,1)S(1)}, bf16[128,128]{1,0:T(8,128)(2,1)}, u32[]{:S(2)}) copy-start(bf16[128,128]{1,0:T(8,128)(2,1)} %param.14) | copy-start | bytes 98308
  6.5 134.0 %all-gather.3.cloned.1.call-start = ((), (), s32[]{:S(2)}) async-start(), calls=%async_computation.2 | async-start | bytes 18874368 | tf_op jit(solution)/shard_map/all_gather | solution.py:74
  6.5 71.2 %collective-permute-start.3 = (bf16[768,2048]{1,0:T(8,128)(2,1)}, bf16[768,2048]{1,0:T(8,128)(2,1)S(1)}, u32[]{:S(2)}, u32[]{:S(2)}) collective-permute-start(bf16[768,2048]{1,0:T(8,128)(2,1)} %param.10), channel_id=1, source_target_pairs={{0,2},{2,0},{1,3},{3,1},{4,6},{6,4},{5,7},{7,5},{8,10},{10,8},{9,1... | collective-permute-start | bytes 9437192 | tf_op jit(solution)/shard_map/ppermute | solution.py:15
  84.0 7.8 copy-start.9
  84.0 9.5 %copy-start.6 = (s32[8]{0:T(128)S(1)}, s32[8]{0:T(128)}, u32[]{:S(2)}) copy-start(s32[8]{0:T(128)} %constant.142.clone) | copy-start | bytes 100
  84.0 609.4 %all-gather.5.cloned.1.call-start = ((), (), s32[]{:S(2)}) async-start(), calls=%async_computation.3 | async-start | bytes 9437184 | tf_op jit(solution)/shard_map/all_gather | solution.py:119
  87.8 50.1 %collective-permute-start.2 = (bf16[256,3,1024]{0,2,1:T(8,128)(2,1)}, bf16[256,3,1024]{0,2,1:T(8,128)(2,1)}, u32[]{:S(2)}, u32[]{:S(2)}) collective-permute-start(bf16[256,3,1024]{0,2,1:T(8,128)(2,1)} %copy.31), channel_id=1, source_target_pairs={{0,2},{2,0},{1,3},{3,1},{4,6},{6,4},{5,7},{7,5},{8,10},{10,8},{9,1... | collective-permute-start | bytes 4718600 | tf_op jit(solution)/shard_map/ppermute | solution.py:15
  91.4 43.5 %collective-permute-start.6 = (bf16[1024,256]{1,0:T(8,128)(2,1)}, bf16[1024,256]{1,0:T(8,128)(2,1)}, u32[]{:S(2)}, u32[]{:S(2)}) collective-permute-start(bf16[1024,256]{1,0:T(8,128)(2,1)} %constant_dynamic-slice_fusion), channel_id=1, source_target_pairs={{0,2},{2,0},{1,3},{3,1},{4,6},{6,4},{5,7},{7,5},{8,10},{10,8},{9,1... | collective-permute-start | bytes 1572872 | tf_op jit(solution)/shard_map/ppermute | solution.py:15
  137.4 602.5 %reduce-scatter.3.cloned.1.call-start = ((), (), s32[]{:S(2)}) async-start(), calls=%async_computation.4 | async-start | bytes 18874368 | tf_op jit(solution)/shard_map/reduce_scatter | solution.py:144
  140.6 7.1 copy-start.8
  160.9 61.5 %collective-permute-start = (bf16[256,3072]{1,0:T(8,128)(2,1)S(1)}, bf16[256,3072]{1,0:T(8,128)(2,1)}, u32[]{:S(2)}, u32[]{:S(2)}) collective-permute-start(bf16[256,3072]{1,0:T(8,128)(2,1)S(1)} %copy.48), channel_id=1, source_target_pairs={{0,8},{8,16},{16,24},{24,28},{28,20},{20,12},{12,4},{4,0},{1,9},{9... | collective-permute-start | bytes 4718600 | tf_op jit(solution)/shard_map/while/body/eval_jaxpr/ppermute | solution.py:101
  163.9 64.3 %collective-permute-start.1 = (bf16[256,3072]{1,0:T(8,128)(2,1)S(1)}, bf16[256,3072]{1,0:T(8,128)(2,1)}, u32[]{:S(2)}, u32[]{:S(2)}) collective-permute-start(bf16[256,3072]{1,0:T(8,128)(2,1)S(1)} %copy.49), channel_id=1, source_target_pairs={{8,0},{16,8},{24,16},{28,24},{20,28},{12,20},{4,12},{0,4},{9,1},{1... | collective-permute-start | bytes 4718600 | tf_op jit(solution)/shard_map/while/body/eval_jaxpr/ppermute | solution.py:102
  229.6 72.0 %collective-permute-start = (bf16[256,3072]{1,0:T(8,128)(2,1)S(1)}, bf16[256,3072]{1,0:T(8,128)(2,1)}, u32[]{:S(2)}, u32[]{:S(2)}) collective-permute-start(bf16[256,3072]{1,0:T(8,128)(2,1)S(1)} %copy.48), channel_id=1, source_target_pairs={{0,8},{8,16},{16,24},{24,28},{28,20},{20,12},{12,4},{4,0},{1,9},{9... | collective-permute-start | bytes 4718600 | tf_op jit(solution)/shard_map/while/body/eval_jaxpr/ppermute | solution.py:101
  241.7 74.6 %collective-permute-start.1 = (bf16[256,3072]{1,0:T(8,128)(2,1)S(1)}, bf16[256,3072]{1,0:T(8,128)(2,1)}, u32[]{:S(2)}, u32[]{:S(2)}) collective-permute-start(bf16[256,3072]{1,0:T(8,128)(2,1)S(1)} %copy.49), channel_id=1, source_target_pairs={{8,0},{16,8},{24,16},{28,24},{20,28},{12,20},{4,12},{0,4},{9,1},{1... | collective-permute-start | bytes 4718600 | tf_op jit(solution)/shard_map/while/body/eval_jaxpr/ppermute | solution.py:102
  317.6 38.6 %collective-permute-start = (bf16[256,3072]{1,0:T(8,128)(2,1)S(1)}, bf16[256,3072]{1,0:T(8,128)(2,1)}, u32[]{:S(2)}, u32[]{:S(2)}) collective-permute-start(bf16[256,3072]{1,0:T(8,128)(2,1)S(1)} %copy.48), channel_id=1, source_target_pairs={{0,8},{8,16},{16,24},{24,28},{28,20},{20,12},{12,4},{4,0},{1,9},{9... | collective-permute-start | bytes 4718600 | tf_op jit(solution)/shard_map/while/body/eval_jaxpr/ppermute | solution.py:101
  323.5 33.9 %collective-permute-start.1 = (bf16[256,3072]{1,0:T(8,128)(2,1)S(1)}, bf16[256,3072]{1,0:T(8,128)(2,1)}, u32[]{:S(2)}, u32[]{:S(2)}) collective-permute-start(bf16[256,3072]{1,0:T(8,128)(2,1)S(1)} %copy.49), channel_id=1, source_target_pairs={{8,0},{16,8},{24,16},{28,24},{20,28},{12,20},{4,12},{0,4},{9,1},{1... | collective-permute-start | bytes 4718600 | tf_op jit(solution)/shard_map/while/body/eval_jaxpr/ppermute | solution.py:102
  358.8 37.9 %collective-permute-start = (bf16[256,3072]{1,0:T(8,128)(2,1)S(1)}, bf16[256,3072]{1,0:T(8,128)(2,1)}, u32[]{:S(2)}, u32[]{:S(2)}) collective-permute-start(bf16[256,3072]{1,0:T(8,128)(2,1)S(1)} %copy.48), channel_id=1, source_target_pairs={{0,8},{8,16},{16,24},{24,28},{28,20},{20,12},{12,4},{4,0},{1,9},{9... | collective-permute-start | bytes 4718600 | tf_op jit(solution)/shard_map/while/body/eval_jaxpr/ppermute | solution.py:101
  364.0 35.4 %collective-permute-start.1 = (bf16[256,3072]{1,0:T(8,128)(2,1)S(1)}, bf16[256,3072]{1,0:T(8,128)(2,1)}, u32[]{:S(2)}, u32[]{:S(2)}) collective-permute-start(bf16[256,3072]{1,0:T(8,128)(2,1)S(1)} %copy.49), channel_id=1, source_target_pairs={{8,0},{16,8},{24,16},{28,24},{20,28},{12,20},{4,12},{0,4},{9,1},{1... | collective-permute-start | bytes 4718600 | tf_op jit(solution)/shard_map/while/body/eval_jaxpr/ppermute | solution.py:102
  400.8 36.2 %collective-permute-start = (bf16[256,3072]{1,0:T(8,128)(2,1)S(1)}, bf16[256,3072]{1,0:T(8,128)(2,1)}, u32[]{:S(2)}, u32[]{:S(2)}) collective-permute-start(bf16[256,3072]{1,0:T(8,128)(2,1)S(1)} %copy.48), channel_id=1, source_target_pairs={{0,8},{8,16},{16,24},{24,28},{28,20},{20,12},{12,4},{4,0},{1,9},{9... | collective-permute-start | bytes 4718600 | tf_op jit(solution)/shard_map/while/body/eval_jaxpr/ppermute | solution.py:101
  403.6 33.9 %collective-permute-start.1 = (bf16[256,3072]{1,0:T(8,128)(2,1)S(1)}, bf16[256,3072]{1,0:T(8,128)(2,1)}, u32[]{:S(2)}, u32[]{:S(2)}) collective-permute-start(bf16[256,3072]{1,0:T(8,128)(2,1)S(1)} %copy.49), channel_id=1, source_target_pairs={{8,0},{16,8},{24,16},{28,24},{20,28},{12,20},{4,12},{0,4},{9,1},{1... | collective-permute-start | bytes 4718600 | tf_op jit(solution)/shard_map/while/body/eval_jaxpr/ppermute | solution.py:102
  438.9 36.2 %collective-permute-start = (bf16[256,3072]{1,0:T(8,128)(2,1)S(1)}, bf16[256,3072]{1,0:T(8,128)(2,1)}, u32[]{:S(2)}, u32[]{:S(2)}) collective-permute-start(bf16[256,3072]{1,0:T(8,128)(2,1)S(1)} %copy.48), channel_id=1, source_target_pairs={{0,8},{8,16},{16,24},{24,28},{28,20},{20,12},{12,4},{4,0},{1,9},{9... | collective-permute-start | bytes 4718600 | tf_op jit(solution)/shard_map/while/body/eval_jaxpr/ppermute | solution.py:101
  441.2 33.9 %collective-permute-start.1 = (bf16[256,3072]{1,0:T(8,128)(2,1)S(1)}, bf16[256,3072]{1,0:T(8,128)(2,1)}, u32[]{:S(2)}, u32[]{:S(2)}) collective-permute-start(bf16[256,3072]{1,0:T(8,128)(2,1)S(1)} %copy.49), channel_id=1, source_target_pairs={{8,0},{16,8},{24,16},{28,24},{20,28},{12,20},{4,12},{0,4},{9,1},{1... | collective-permute-start | bytes 4718600 | tf_op jit(solution)/shard_map/while/body/eval_jaxpr/ppermute | solution.py:102
  476.5 36.2 %collective-permute-start = (bf16[256,3072]{1,0:T(8,128)(2,1)S(1)}, bf16[256,3072]{1,0:T(8,128)(2,1)}, u32[]{:S(2)}, u32[]{:S(2)}) collective-permute-start(bf16[256,3072]{1,0:T(8,128)(2,1)S(1)} %copy.48), channel_id=1, source_target_pairs={{0,8},{8,16},{16,24},{24,28},{28,20},{20,12},{12,4},{4,0},{1,9},{9... | collective-permute-start | bytes 4718600 | tf_op jit(solution)/shard_map/while/body/eval_jaxpr/ppermute | solution.py:101
  478.8 33.9 %collective-permute-start.1 = (bf16[256,3072]{1,0:T(8,128)(2,1)S(1)}, bf16[256,3072]{1,0:T(8,128)(2,1)}, u32[]{:S(2)}, u32[]{:S(2)}) collective-permute-start(bf16[256,3072]{1,0:T(8,128)(2,1)S(1)} %copy.49), channel_id=1, source_target_pairs={{8,0},{16,8},{24,16},{28,24},{20,28},{12,20},{4,12},{0,4},{9,1},{1... | collective-permute-start | bytes 4718600 | tf_op jit(solution)/shard_map/while/body/eval_jaxpr/ppermute | solution.py:102
  523.5 21.4 %copy-start.7 = (f32[3,3,2048]{2,1,0:T(4,128)S(1)}, f32[3,3,2048]{2,1,0:T(4,128)}, u32[]{:S(2)}) copy-start(f32[3,3,2048]{2,1,0:T(4,128)} %param.13) | copy-start | bytes 221188
  541.8 15.8 %collective-permute-start.4 = (bf16[2,3,1024]{2,1,0:T(4,128)(2,1)S(1)}, bf16[2,3,1024]{2,1,0:T(4,128)(2,1)S(1)}, u32[]{:S(2)}, u32[]{:S(2)}) collective-permute-start(bf16[2,3,1024]{2,1,0:T(4,128)(2,1)S(1)} %slice.61), channel_id=1, source_target_pairs={{0,4},{4,8},{8,12},{12,16},{16,20},{20,24},{24,28},{1,5},{5,9},{9,... | collective-permute-start | bytes 36872 | tf_op jit(solution)/shard_map/ppermute | solution.py:11
  595.0 6.4 copy-start.1
  605.9 51.5 %collective-permute-start.5 = (bf16[127,1024]{0,1:T(8,128)(2,1)}, bf16[127,1024]{0,1:T(8,128)(2,1)S(1)}, u32[]{:S(2)}, u32[]{:S(2)}) collective-permute-start(bf16[127,1024]{0,1:T(8,128)(2,1)} %slice_bitcast_fusion.5), channel_id=1, source_target_pairs={{0,4},{4,8},{8,12},{12,16},{16,20},{20,24},{24,28},{1,5},{5,9},{9,... | collective-permute-start | bytes 780296 | tf_op jit(solution)/shard_map/ppermute | solution.py:11
  631.8 19.2 %copy-start.2 = (bf16[1536,1,1024]{0,2,1:T(8,128)(2,1)S(1)}, bf16[1536,1,1024]{0,2,1:T(8,128)(2,1)}, u32[]{:S(2)}) copy-start(bf16[1536,1,1024]{0,2,1:T(8,128)(2,1)} %fusion.12) | copy-start | bytes 9437188
  680.5 5.3 copy-start.5
  721.1 99.2 %copy-start.4 = (bf16[768,2048]{1,0:T(8,128)(2,1)S(1)}, bf16[768,2048]{1,0:T(8,128)(2,1)}, u32[]{:S(2)}) copy-start(bf16[768,2048]{1,0:T(8,128)(2,1)} %param.10) | copy-start | bytes 9437188
  721.1 99.2 %reduce-scatter.5.cloned.1.call-start = ((), (), s32[]{:S(2)}) async-start(), calls=%async_computation.5 | async-start | bytes 9437184 | tf_op jit(solution)/shard_map/reduce_scatter | solution.py:145
  (1 other events, 4.5 us)
Sparse Core Ops, SparseCore 0:
  84.1 26.3 all-gather.2
  137.6 185.1 all-gather.4
  721.2 18.6 reduce-scatter.2
  742.1 78.1 reduce-scatter.4

commit v3 on v2

--- a/solution.py
+++ b/solution.py
@@ -88,28 +88,24 @@
     forward = [(order[i], order[(i + 1) % n_hi]) for i in range(n_hi)]
     backward = [(order[(i + 1) % n_hi], order[i]) for i in range(n_hi)]
 
-    def contribution(piece, ctx_index):
-        columns = lax.dynamic_slice_in_dim(normed, ctx_index * w_rows, w_rows, axis=1)
-        return jnp.dot(columns, piece, preferred_element_type=jnp.float32)
+    n_ctx = 2 * n_hi
+    gathered_w = jnp.zeros((n_ctx, w_rows, 3 * half_width), jnp.bfloat16)
 
-    def ring_step(step, carry):
-        own, partner, total = carry
+    def store(buffer, piece, ctx_index):
+        return lax.dynamic_update_slice_in_dim(buffer, piece[None], ctx_index, axis=0)
+
+    for step in range(n_hi):
+        if step > 0:
+            own_piece = lax.ppermute(own_piece, "hi", forward)
+            partner_piece = lax.ppermute(partner_piece, "hi", backward)
         own_from = order_table[(here - step) % n_hi]
         partner_from = order_table[(here + step) % n_hi]
-        total = total + contribution(own, 2 * own_from + half)
-        total = total + contribution(partner, 2 * partner_from + other)
-        own = lax.ppermute(own, "hi", forward)
-        partner = lax.ppermute(partner, "hi", backward)
-        return own, partner, total
-
-    total = jnp.zeros((row_count, 3 * half_width), jnp.float32)
-    own_piece, partner_piece, total = lax.fori_loop(
-        0, n_hi - 1, ring_step, (own_piece, partner_piece, total)
-    )
-    last = n_hi - 1
-    total = total + contribution(own_piece, 2 * order_table[(here - last) % n_hi] + half)
-    projected = total + contribution(
-        partner_piece, 2 * order_table[(here + last) % n_hi] + other
+        gathered_w = store(gathered_w, own_piece, 2 * own_from + half)
+        gathered_w = store(gathered_w, partner_piece, 2 * partner_from + other)
+    projected = jnp.dot(
+        normed,
+        gathered_w.reshape(n_ctx * w_rows, 3 * half_width),
+        preferred_element_type=jnp.float32,
     )
     projected = projected.astype(jnp.bfloat16).reshape(row_count, 3, half_width)
 

time: 837 us -> 828 us (0.989)
  matrix products: 261 us -> 81.1 us
  waiting for transfers between devices: 290 us -> 444 us
  local copies, waits for them, and re-layouts: 136 us -> 168 us
  between operations: 16 us -> 34.3 us
  loops' own time: 17.8 us -> 0 us
  other arithmetic: 72 us -> 59.9 us
    dot_general x16 -> x1, matrix products: 227 us -> 47.6 us  [local(): jnp.dot(normed, gathered_w.reshape(n_ctx * w_rows, 3 * half_width), prefe...]
    ppermute x14, waiting for transfers between devices: 84.9 us -> 240 us  [the longest x7 238 us: local(): partner_piece = lax.ppermute(partner_piece, 'hi', backward)]
    broadcast_in_dim x0 -> x15, local copies, waits for them, and re-layouts: none -> 32.1 us  [the longest x14 23.4 us: store(): piece[None]]
    dynamic_update_slice x0 -> x16, local copies, waits for them, and re-layouts: none -> 20.6 us  [store(): lax.dynamic_update_slice_in_dim(buffer, piece[None], ctx_index, axis=0)]
    while x14 -> x0, local copies, waits for them, and re-layouts: 19.7 us -> none
    another operation x1 -> x0, loops' own time: 17.8 us -> none  [local(): lax.fori_loop(0, n_hi - 1, ring_step, (own_piece, partner_piece, total))]
    convert_element_type x1 -> x0, other arithmetic: 11.9 us -> none  [local(): normed = (wide_float * scale * norm_gain).astype(jnp.bfloat16)]
    ppermute x14, starting transfers between devices: 27.1 us -> 16.7 us  [the longest x7 9.35 us: local(): own_piece = lax.ppermute(own_piece, 'hi', forward)]
  transfers between devices with their start and end apart: 23 -> 23, of which waited for: 11 -> 12; matrix products, arithmetic and copies ran while one was open for 51% -> 31% of each run, Pallas kernels for 0% -> 0%
where the time goes in v3:
time: 828 us; the launch traced here: 819 us
  waiting for transfers between devices  444 us (54%)
  local copies, waits for them, and re-layouts  168 us (20%)
  matrix products  81.1 us (10%)
  other arithmetic  59.9 us (7%)
  between operations  34.3 us (4%)
  starting transfers between devices  31.8 us (4%)
    ppermute x7, waiting for transfers between devices, local(): partner_piece = lax.ppermute(partner_piece, 'hi', backward)  238 us
    ppermute x3, waiting for transfers between devices, swap_pair(): return lax.ppermute(value, 'lo', [(0, 1), (1, 0)])  100 us
    reduce_scatter x1, waiting for transfers between devices, local(): summed = lax.psum_scatter(summed, 'lo', scatter_dimension=0, tiled=True)  80.4 us
    dot_general x1, matrix products, local(): jnp.dot(normed, gathered_w.reshape(n_ctx * w_rows, 3 * half_width), prefe...  47.6 us
    reshape x2, local copies, waits for them, and re-layouts, skew(): flat.reshape(groups, filter_len, 2 * filter_len - 1)[:, :, :filter_len]  31.7 us
    dot_general x1, matrix products, local(): jnp.dot(gated, o_full, preferred_element_type=jnp.float32)  27.6 us
    reduce_scatter x1, waiting for transfers between devices, local(): summed = lax.psum_scatter(terms, 'tp', scatter_dimension=1, tiled=True)  24 us
    broadcast_in_dim x14, local copies, waits for them, and re-layouts, store(): piece[None]  23.4 us
  transfers between devices with their start and end apart: 23, of which 12 were waited for; matrix products, arithmetic and copies ran while one was open for 31% of the time, Pallas kernels for 0%

profile of v3, /device:TPU:0, one launch (start us, length us, event | category | flops | bytes accessed | tf_op | source)
XLA Modules:
  0.0 819.2 jit_solution(6560323242261208198)
XLA Ops:
  9.5 68.3 %collective-permute-done = bf16[768,2048]{1,0:T(8,128)(2,1)S(1)} collective-permute-done((bf16[768,2048]{1,0:T(8,128)(2,1)}, bf16[768,2048]{1,0:T(8,128)(2,1)S(1)}, u32[]{:S(2)}, u32[]{:S(2)}) %collective-permute-start) | collective-permute-done | bytes 3145760 | tf_op jit(solution)/shard_map/ppermute | solution.py:15
  80.1 3.7 pad_maximum_fusion
  91.7 31.8 %collective-permute-done.1 = bf16[256,3,1024]{0,2,1:T(8,128)(2,1)} collective-permute-done((bf16[256,3,1024]{0,2,1:T(8,128)(2,1)}, bf16[256,3,1024]{0,2,1:T(8,128)(2,1)}, u32[]{:S(2)}, u32[]{:S(2)}) %collective-permute-start.1) | collective-permute-done | bytes 1572896 | tf_op jit(solution)/shard_map/ppermute | solution.py:15
  126.7 31.7 %collective-permute-done.3 = bf16[256,3072]{0,1:T(8,128)(2,1)S(1)} collective-permute-done((bf16[256,3072]{0,1:T(8,128)(2,1)}, bf16[256,3072]{0,1:T(8,128)(2,1)S(1)}, u32[]{:S(2)}, u32[]{:S(2)}) %collective-permute-start.3) | collective-permute-done | bytes 1572896 | tf_op jit(solution)/shard_map/ppermute | solution.py:100
  161.3 31.7 %collective-permute-done.5 = bf16[256,3072]{0,1:T(8,128)(2,1)S(1)} collective-permute-done((bf16[256,3072]{0,1:T(8,128)(2,1)S(1)}, bf16[256,3072]{0,1:T(8,128)(2,1)S(1)}, u32[]{:S(2)}, u32[]{:S(2)}) %collective-permute-start.5) | collective-permute-done | bytes 1572896 | tf_op jit(solution)/shard_map/ppermute | solution.py:100
  196.3 31.0 %collective-permute-done.7 = bf16[256,3072]{0,1:T(8,128)(2,1)} collective-permute-done((bf16[256,3072]{0,1:T(8,128)(2,1)S(1)}, bf16[256,3072]{0,1:T(8,128)(2,1)}, u32[]{:S(2)}, u32[]{:S(2)}) %collective-permute-start.7) | collective-permute-done | bytes 1572896 | tf_op jit(solution)/shard_map/ppermute | solution.py:100
  255.2 8.7 %broadcast_in_dim.51 = bf16[16,256,3072]{2,1,0:T(8,128)(2,1)} broadcast(bf16[]{:T(256)} %constant.128.clone.1), dimensions={} | broadcast | bytes 25165826 | tf_op jit(solution)/shard_map/broadcast_in_dim | solution.py:92
  283.7 47.3 %collective-permute-done.11 = bf16[256,3072]{0,1:T(8,128)(2,1)} collective-permute-done((bf16[256,3072]{0,1:T(8,128)(2,1)}, bf16[256,3072]{0,1:T(8,128)(2,1)}, u32[]{:S(2)}, u32[]{:S(2)}) %collective-permute-start.11) | collective-permute-done | bytes 1572896 | tf_op jit(solution)/shard_map/ppermute | solution.py:100
  349.8 51.6 %collective-permute-done.13 = bf16[256,3072]{0,1:T(8,128)(2,1)} collective-permute-done((bf16[256,3072]{0,1:T(8,128)(2,1)}, bf16[256,3072]{0,1:T(8,128)(2,1)}, u32[]{:S(2)}, u32[]{:S(2)}) %collective-permute-start.13) | collective-permute-done | bytes 1572896 | tf_op jit(solution)/shard_map/ppermute | solution.py:100
  414.9 44.7 %collective-permute-done.15 = bf16[256,3072]{0,1:T(8,128)(2,1)} collective-permute-done((bf16[256,3072]{0,1:T(8,128)(2,1)}, bf16[256,3072]{0,1:T(8,128)(2,1)}, u32[]{:S(2)}, u32[]{:S(2)}) %collective-permute-start.15) | collective-permute-done | bytes 1572896 | tf_op jit(solution)/shard_map/ppermute | solution.py:100
  462.6 7.1 fusion
  469.7 47.6 %fusion.9 = bf16[1536,3072]{1,0:T(8,128)(2,1)S(1)} fusion(bf16[4096,3072]{1,0:T(8,128)(2,1)} %bitcast.35, bf16[1536,4096]{1,0:T(8,128)(2,1)} %all-gather.3.cloned.1.call-done, f32[4096]{0:T(1024)S(1)} %copy-done.16, f32[1536]{0:T(1024)S(1)} %add_rsqrt_fusion), kind=kOutput, calls=%fused_computation.14 | convolution fusion | flops 38684590080 | bytes 47208448 | tf_op jit(solution)/shard_map/dot_general | solution.py:105
  517.4 3.6 copy-done.5
  522.4 13.1 %copy.42 = bf16[1536,3072]{0,1:T(8,128)(2,1)} copy(bf16[1536,3072]{1,0:T(8,128)(2,1)} %copy-done.5) | data formatting | bytes 18874368 | tf_op jit(solution)/shard_map/convert_element_type | solution.py:110
  536.0 15.1 %maximum_convert_fusion = f32[1538,3,1024]{0,2,1:T(8,128)} fusion(bf16[1536,3,1024]{0,2,1:T(8,128)(2,1)} %bitcast.83, bf16[2,3,1024]{0,2,1:T(8,128)(2,1)S(1)} %copy.43), kind=kLoop, calls=%fused_computation.15 | loop fusion | flops 18898944 | bytes 28348416 | tf_op jit(solution)/shard_map/convert_element_type | solution.py:36
  551.1 21.9 %fusion.3 = f32[1536,3,1024]{0,2,1:T(8,128)S(1)} fusion(f32[1538,3,1024]{0,2,1:T(8,128)} %maximum_convert_fusion, f32[3,1024]{1,0:T(4,128)S(1)} %get-tuple-element.13, f32[3,1024]{1,0:T(4,128)S(1)} %get-tuple-element.12, f32[3,1024]{1,0:T(4,128)S(1)} %get-tuple-element.11), kind=kLoop, calls=%fused_computation.6 | loop fusion | flops 23592960 | bytes 75534336 | tf_op jit(solution)/shard_map/add | solution.py:40
  573.0 6.5 copy-done.1
  583.9 7.6 collective-permute-start.17
  593.2 3.3 slice.89
  596.5 15.8 %reshape.84 = bf16[64,128,255]{2,1,0:T(8,128)(2,1)} reshape(bf16[64,32640]{1,0:T(8,128)(2,1)} %slice.89) | data formatting | bytes 8355840 | tf_op jit(solution)/shard_map/reshape | solution.py:27
  613.7 3.3 slice.85
  617.0 15.8 %reshape.83 = bf16[64,128,255]{2,1,0:T(8,128)(2,1)} reshape(bf16[64,32640]{1,0:T(8,128)(2,1)} %slice.85) | data formatting | bytes 8355840 | tf_op jit(solution)/shard_map/reshape | solution.py:27
  635.7 3.6 convert_element_type.43
  640.2 13.2 %concatenate.21 = bf16[1664,1024]{1,0:T(8,128)(2,1)S(1)} concatenate(bf16[1,1024]{1,0:T(2,128)(2,1)S(1)} %broadcast_in_dim.66, bf16[127,1024]{1,0:T(8,128)(2,1)} %copy.47, bf16[1536,1024]{1,0:T(8,128)(2,1)} %bitcast.88), dimensions={0} | concatenate | bytes 6815744 | tf_op jit(solution)/shard_map/concatenate | solution.py:124
  655.4 3.2 copy.48
  658.5 3.9 slice.75
  662.4 4.5 fusion.15
  669.2 6.1 copy.51
  675.3 27.6 %convolution_convert_fusion = bf16[1536,4096]{1,0:T(8,128)(2,1)} fusion(bf16[1024,4096]{1,0:T(8,128)(2,1)} %all-gather.5.cloned.1.call-done, f32[128,8,12,128]{3,2,1,0:T(8,128)} %bitcast.89, f32[1536,3,1024]{0,2,1:T(8,128)} %copy-done.1), kind=kOutput, calls=%fused_computation.10 | convolution fusion | flops 12894339072 | bytes 35651584 | tf_op jit(solution)/shard_map/dot_general | solution.py:139
  703.0 24.0 %reduce-scatter.3.cloned.1.call-done = bf16[1536,2048]{1,0:T(8,128)(2,1)} async-done(((bf16[1536,4096]{1,0:T(8,128)(2,1)}), bf16[1536,2048]{1,0:T(8,128)(2,1)}) %reduce-scatter.3.cloned.1.call-update) | async-done | bytes 6291472 | tf_op jit(solution)/shard_map/reduce_scatter | solution.py:140
  727.0 80.4 %reduce-scatter.5.cloned.1.call-done = bf16[768,2048]{1,0:T(8,128)(2,1)} async-done(((bf16[1536,2048]{1,0:T(8,128)(2,1)}), bf16[768,2048]{1,0:T(8,128)(2,1)}) %reduce-scatter.5.cloned.1.call-update) | async-done | bytes 3145744 | tf_op jit(solution)/shard_map/reduce_scatter | solution.py:141
  807.4 4.9 add_convert_fusion
  (136 shorter events, 102.2 us)
Async XLA Ops:
  6.5 585.0 %copy-start = (bf16[128,128]{1,0:T(8,128)(2,1)S(1)}, bf16[128,128]{1,0:T(8,128)(2,1)}, u32[]{:S(2)}) copy-start(bf16[128,128]{1,0:T(8,128)(2,1)} %param.12) | copy-start | bytes 98308
  6.5 456.1 %all-gather.3.cloned.1.call-start = ((), (), s32[]{:S(2)}) async-start(), calls=%async_computation.2 | async-start | bytes 18874368 | tf_op jit(solution)/shard_map/all_gather | solution.py:74
  6.5 71.2 %collective-permute-start = (bf16[768,2048]{1,0:T(8,128)(2,1)}, bf16[768,2048]{1,0:T(8,128)(2,1)S(1)}, u32[]{:S(2)}, u32[]{:S(2)}) collective-permute-start(bf16[768,2048]{1,0:T(8,128)(2,1)} %param.8), channel_id=1, source_target_pairs={{0,2},{2,0},{1,3},{3,1},{4,6},{6,4},{5,7},{7,5},{8,10},{10,8},{9,1... | collective-permute-start | bytes 9437192 | tf_op jit(solution)/shard_map/ppermute | solution.py:15
  83.8 591.5 %all-gather.5.cloned.1.call-start = ((), (), s32[]{:S(2)}) async-start(), calls=%async_computation.3 | async-start | bytes 9437184 | tf_op jit(solution)/shard_map/all_gather | solution.py:115
  83.9 148.7 %copy-start.17 = (s32[8]{0:T(128)S(1)}, s32[8]{0:T(128)}, u32[]{:S(2)}) copy-start(s32[8]{0:T(128)} %constant.151.clone) | copy-start | bytes 100
  83.9 160.5 %copy-start.14 = (s32[8]{0:T(128)S(1)}, s32[8]{0:T(128)}, u32[]{:S(2)}) copy-start(s32[8]{0:T(128)} %constant.150.clone) | copy-start | bytes 100
  87.7 35.9 %collective-permute-start.1 = (bf16[256,3,1024]{0,2,1:T(8,128)(2,1)}, bf16[256,3,1024]{0,2,1:T(8,128)(2,1)}, u32[]{:S(2)}, u32[]{:S(2)}) collective-permute-start(bf16[256,3,1024]{0,2,1:T(8,128)(2,1)} %copy.55), channel_id=1, source_target_pairs={{0,2},{2,0},{1,3},{3,1},{4,6},{6,4},{5,7},{7,5},{8,10},{10,8},{9,1... | collective-permute-start | bytes 4718600 | tf_op jit(solution)/shard_map/ppermute | solution.py:15
  90.1 35.0 %collective-permute-start.2 = (bf16[256,3072]{0,1:T(8,128)(2,1)S(1)}, bf16[256,3072]{0,1:T(8,128)(2,1)S(1)}, u32[]{:S(2)}, u32[]{:S(2)}) collective-permute-start(bf16[256,3072]{0,1:T(8,128)(2,1)S(1)} %bitcast.90), channel_id=1, source_target_pairs={{0,8},{8,16},{16,24},{24,28},{28,20},{20,12},{12,4},{4,0},{1,9},{9... | collective-permute-start | bytes 4718600 | tf_op jit(solution)/shard_map/ppermute | solution.py:99
  123.6 34.9 %collective-permute-start.3 = (bf16[256,3072]{0,1:T(8,128)(2,1)}, bf16[256,3072]{0,1:T(8,128)(2,1)S(1)}, u32[]{:S(2)}, u32[]{:S(2)}) collective-permute-start(bf16[256,3072]{0,1:T(8,128)(2,1)} %bitcast.8), channel_id=1, source_target_pairs={{8,0},{16,8},{24,16},{28,24},{20,28},{12,20},{4,12},{0,4},{9,1},{1... | collective-permute-start | bytes 4718600 | tf_op jit(solution)/shard_map/ppermute | solution.py:100
  125.1 102.1 %copy-start.12 = (bf16[256,3072]{0,1:T(8,128)(2,1)}, bf16[256,3072]{0,1:T(8,128)(2,1)S(1)}, u32[]{:S(2)}) copy-start(bf16[256,3072]{0,1:T(8,128)(2,1)S(1)} %collective-permute-done.2) | copy-start | bytes 4718596
  125.1 34.6 %collective-permute-start.4 = (bf16[256,3072]{0,1:T(8,128)(2,1)S(1)}, bf16[256,3072]{0,1:T(8,128)(2,1)S(1)}, u32[]{:S(2)}, u32[]{:S(2)}) collective-permute-start(bf16[256,3072]{0,1:T(8,128)(2,1)S(1)} %collective-permute-done.2), channel_id=1, source_target_pairs={{0,8},{8,16},{16,24},{24,28},{28,20},{20,12},{12,4},{4,0},{1,9},{9... | collective-permute-start | bytes 4718600 | tf_op jit(solution)/shard_map/ppermute | solution.py:99
  158.4 68.9 %copy-start.11 = (bf16[256,3072]{0,1:T(8,128)(2,1)}, bf16[256,3072]{0,1:T(8,128)(2,1)S(1)}, u32[]{:S(2)}) copy-start(bf16[256,3072]{0,1:T(8,128)(2,1)S(1)} %collective-permute-done.3) | copy-start | bytes 4718596
  158.4 34.6 %collective-permute-start.5 = (bf16[256,3072]{0,1:T(8,128)(2,1)S(1)}, bf16[256,3072]{0,1:T(8,128)(2,1)S(1)}, u32[]{:S(2)}, u32[]{:S(2)}) collective-permute-start(bf16[256,3072]{0,1:T(8,128)(2,1)S(1)} %collective-permute-done.3), channel_id=1, source_target_pairs={{8,0},{16,8},{24,16},{28,24},{20,28},{12,20},{4,12},{0,4},{9,1},{1... | collective-permute-start | bytes 4718600 | tf_op jit(solution)/shard_map/ppermute | solution.py:100
  159.8 36.5 %copy-start.9 = (bf16[256,3072]{0,1:T(8,128)(2,1)}, bf16[256,3072]{0,1:T(8,128)(2,1)S(1)}, u32[]{:S(2)}) copy-start(bf16[256,3072]{0,1:T(8,128)(2,1)S(1)} %collective-permute-done.4) | copy-start | bytes 4718596
  159.8 34.6 %collective-permute-start.6 = (bf16[256,3072]{0,1:T(8,128)(2,1)S(1)}, bf16[256,3072]{0,1:T(8,128)(2,1)S(1)}, u32[]{:S(2)}, u32[]{:S(2)}) collective-permute-start(bf16[256,3072]{0,1:T(8,128)(2,1)S(1)} %collective-permute-done.4), channel_id=1, source_target_pairs={{0,8},{8,16},{16,24},{24,28},{28,20},{20,12},{12,4},{4,0},{1,9},{9... | collective-permute-start | bytes 4718600 | tf_op jit(solution)/shard_map/ppermute | solution.py:99
  193.0 34.3 %collective-permute-start.7 = (bf16[256,3072]{0,1:T(8,128)(2,1)S(1)}, bf16[256,3072]{0,1:T(8,128)(2,1)}, u32[]{:S(2)}, u32[]{:S(2)}) collective-permute-start(bf16[256,3072]{0,1:T(8,128)(2,1)S(1)} %collective-permute-done.5), channel_id=1, source_target_pairs={{8,0},{16,8},{24,16},{28,24},{20,28},{12,20},{4,12},{0,4},{9,1},{1... | collective-permute-start | bytes 4718600 | tf_op jit(solution)/shard_map/ppermute | solution.py:100
  195.6 36.5 %collective-permute-start.8 = (bf16[256,3072]{0,1:T(8,128)(2,1)S(1)}, bf16[256,3072]{0,1:T(8,128)(2,1)}, u32[]{:S(2)}, u32[]{:S(2)}) collective-permute-start(bf16[256,3072]{0,1:T(8,128)(2,1)S(1)} %collective-permute-done.6), channel_id=1, source_target_pairs={{0,8},{8,16},{16,24},{24,28},{28,20},{20,12},{12,4},{4,0},{1,9},{9... | collective-permute-start | bytes 4718600 | tf_op jit(solution)/shard_map/ppermute | solution.py:99
  227.3 39.2 %collective-permute-start.9 = (bf16[256,3072]{0,1:T(8,128)(2,1)}, bf16[256,3072]{0,1:T(8,128)(2,1)}, u32[]{:S(2)}, u32[]{:S(2)}) collective-permute-start(bf16[256,3072]{0,1:T(8,128)(2,1)} %collective-permute-done.7), channel_id=1, source_target_pairs={{8,0},{16,8},{24,16},{28,24},{20,28},{12,20},{4,12},{0,4},{9,1},{1... | collective-permute-start | bytes 4718600 | tf_op jit(solution)/shard_map/ppermute | solution.py:100
  230.6 34.6 %collective-permute-start.18 = (bf16[1024,256]{1,0:T(8,128)(2,1)}, bf16[1024,256]{1,0:T(8,128)(2,1)}, u32[]{:S(2)}, u32[]{:S(2)}) collective-permute-start(bf16[1024,256]{1,0:T(8,128)(2,1)} %constant_dynamic-slice_fusion), channel_id=1, source_target_pairs={{0,2},{2,0},{1,3},{3,1},{4,6},{6,4},{5,7},{7,5},{8,10},{10,8},{9,1... | collective-permute-start | bytes 1572872 | tf_op jit(solution)/shard_map/ppermute | solution.py:15
  232.1 44.9 %collective-permute-start.10 = (bf16[256,3072]{0,1:T(8,128)(2,1)}, bf16[256,3072]{0,1:T(8,128)(2,1)}, u32[]{:S(2)}, u32[]{:S(2)}) collective-permute-start(bf16[256,3072]{0,1:T(8,128)(2,1)} %collective-permute-done.8), channel_id=1, source_target_pairs={{0,8},{8,16},{16,24},{24,28},{28,20},{20,12},{12,4},{4,0},{1,9},{9... | collective-permute-start | bytes 4718600 | tf_op jit(solution)/shard_map/ppermute | solution.py:99
  266.5 64.5 %collective-permute-start.11 = (bf16[256,3072]{0,1:T(8,128)(2,1)}, bf16[256,3072]{0,1:T(8,128)(2,1)}, u32[]{:S(2)}, u32[]{:S(2)}) collective-permute-start(bf16[256,3072]{0,1:T(8,128)(2,1)} %collective-permute-done.9), channel_id=1, source_target_pairs={{8,0},{16,8},{24,16},{28,24},{20,28},{12,20},{4,12},{0,4},{9,1},{1... | collective-permute-start | bytes 4718600 | tf_op jit(solution)/shard_map/ppermute | solution.py:100
  269.1 457.9 %reduce-scatter.3.cloned.1.call-start = ((), (), s32[]{:S(2)}) async-start(), calls=%async_computation.4 | async-start | bytes 18874368 | tf_op jit(solution)/shard_map/reduce_scatter | solution.py:140
  277.0 63.7 %collective-permute-start.12 = (bf16[256,3072]{0,1:T(8,128)(2,1)}, bf16[256,3072]{0,1:T(8,128)(2,1)}, u32[]{:S(2)}, u32[]{:S(2)}) collective-permute-start(bf16[256,3072]{0,1:T(8,128)(2,1)} %collective-permute-done.10), channel_id=1, source_target_pairs={{0,8},{8,16},{16,24},{24,28},{28,20},{20,12},{12,4},{4,0},{1,9},{9... | collective-permute-start | bytes 4718600 | tf_op jit(solution)/shard_map/ppermute | solution.py:99
  278.9 53.4 %copy-start.8 = (bf16[256,3072]{0,1:T(8,128)(2,1)S(1)}, bf16[256,3072]{0,1:T(8,128)(2,1)}, u32[]{:S(2)}) copy-start(bf16[256,3072]{0,1:T(8,128)(2,1)} %copy-done.7) | copy-start | bytes 4718596
  331.0 70.4 %collective-permute-start.13 = (bf16[256,3072]{0,1:T(8,128)(2,1)}, bf16[256,3072]{0,1:T(8,128)(2,1)}, u32[]{:S(2)}, u32[]{:S(2)}) collective-permute-start(bf16[256,3072]{0,1:T(8,128)(2,1)} %collective-permute-done.11), channel_id=1, source_target_pairs={{8,0},{16,8},{24,16},{28,24},{20,28},{12,20},{4,12},{0,4},{9,1},{1... | collective-permute-start | bytes 4718600 | tf_op jit(solution)/shard_map/ppermute | solution.py:100
  340.7 69.8 %collective-permute-start.14 = (bf16[256,3072]{0,1:T(8,128)(2,1)}, bf16[256,3072]{0,1:T(8,128)(2,1)}, u32[]{:S(2)}, u32[]{:S(2)}) collective-permute-start(bf16[256,3072]{0,1:T(8,128)(2,1)} %collective-permute-done.12), channel_id=1, source_target_pairs={{0,8},{8,16},{16,24},{24,28},{28,20},{20,12},{12,4},{4,0},{1,9},{9... | collective-permute-start | bytes 4718600 | tf_op jit(solution)/shard_map/ppermute | solution.py:99
  401.4 58.2 %collective-permute-start.15 = (bf16[256,3072]{0,1:T(8,128)(2,1)}, bf16[256,3072]{0,1:T(8,128)(2,1)}, u32[]{:S(2)}, u32[]{:S(2)}) collective-permute-start(bf16[256,3072]{0,1:T(8,128)(2,1)} %collective-permute-done.13), channel_id=1, source_target_pairs={{8,0},{16,8},{24,16},{28,24},{20,28},{12,20},{4,12},{0,4},{9,1},{1... | collective-permute-start | bytes 4718600 | tf_op jit(solution)/shard_map/ppermute | solution.py:100
  469.7 52.6 %copy-start.15 = (f32[3,3,2048]{2,1,0:T(4,128)S(1)}, f32[3,3,2048]{2,1,0:T(4,128)}, u32[]{:S(2)}) copy-start(f32[3,3,2048]{2,1,0:T(4,128)} %param.11) | copy-start | bytes 221188
  521.1 14.5 %collective-permute-start.16 = (bf16[2,3,1024]{2,1,0:T(4,128)(2,1)S(1)}, bf16[2,3,1024]{2,1,0:T(4,128)(2,1)S(1)}, u32[]{:S(2)}, u32[]{:S(2)}) collective-permute-start(bf16[2,3,1024]{2,1,0:T(4,128)(2,1)S(1)} %slice.61), channel_id=1, source_target_pairs={{0,4},{4,8},{8,12},{12,16},{16,20},{20,24},{24,28},{1,5},{5,9},{9,... | collective-permute-start | bytes 36872 | tf_op jit(solution)/shard_map/ppermute | solution.py:11
  583.9 55.4 %collective-permute-start.17 = (bf16[127,1024]{0,1:T(8,128)(2,1)}, bf16[127,1024]{0,1:T(8,128)(2,1)S(1)}, u32[]{:S(2)}, u32[]{:S(2)}) collective-permute-start(bf16[127,1024]{0,1:T(8,128)(2,1)} %slice_bitcast_fusion.5), channel_id=1, source_target_pairs={{0,4},{4,8},{8,12},{12,16},{16,20},{20,24},{24,28},{1,5},{5,9},{9,... | collective-permute-start | bytes 780296 | tf_op jit(solution)/shard_map/ppermute | solution.py:11
  703.0 104.5 %copy-start.4 = (bf16[768,2048]{1,0:T(8,128)(2,1)S(1)}, bf16[768,2048]{1,0:T(8,128)(2,1)}, u32[]{:S(2)}) copy-start(bf16[768,2048]{1,0:T(8,128)(2,1)} %param.8) | copy-start | bytes 9437188
  703.0 104.5 %reduce-scatter.5.cloned.1.call-start = ((), (), s32[]{:S(2)}) async-start(), calls=%async_computation.5 | async-start | bytes 9437184 | tf_op jit(solution)/shard_map/reduce_scatter | solution.py:141
  (9 other events, 91.7 us)
Sparse Core Ops, SparseCore 0:
  83.9 26.3 all-gather.2
  269.3 196.6 all-gather.4
  703.1 23.8 reduce-scatter.2
  729.2 78.2 reduce-scatter.4

commit v4 on v3

--- a/solution.py
+++ b/solution.py
@@ -94,10 +94,15 @@
     def store(buffer, piece, ctx_index):
         return lax.dynamic_update_slice_in_dim(buffer, piece[None], ctx_index, axis=0)
 
+    current, previous = toeplitz_pair(half_of(long_filter, 1, half))
     for step in range(n_hi):
         if step > 0:
             own_piece = lax.ppermute(own_piece, "hi", forward)
             partner_piece = lax.ppermute(partner_piece, "hi", backward)
+        if step == 1:
+            own_piece, partner_piece, current, previous = lax.optimization_barrier(
+                (own_piece, partner_piece, current, previous)
+            )
         own_from = order_table[(here - step) % n_hi]
         partner_from = order_table[(here + step) % n_hi]
         gathered_w = store(gathered_w, own_piece, 2 * own_from + half)
@@ -127,7 +132,6 @@
     mix_blocks = extended_mix.reshape(
         row_count // filter_len + 1, filter_len, groups_here, group_size
     )
-    current, previous = toeplitz_pair(half_of(long_filter, 1, half))
     filtered = jnp.einsum(
         "gts,bsgc->btgc", current, mix_blocks[1:], preferred_element_type=jnp.float32
     )
@@ -136,10 +140,13 @@
     )
     gated = (query * filtered.reshape(row_count, half_width)).astype(jnp.bfloat16)
 
-    terms = jnp.dot(gated, o_full, preferred_element_type=jnp.float32).astype(jnp.bfloat16)
-    summed = lax.psum_scatter(terms, "tp", scatter_dimension=1, tiled=True)
-    summed = lax.psum_scatter(summed, "lo", scatter_dimension=0, tiled=True)
-    return (tokens.astype(jnp.float32) + summed.astype(jnp.float32)).astype(jnp.bfloat16)
+    def out_terms(rows):
+        terms = jnp.dot(rows, o_full, preferred_element_type=jnp.float32).astype(jnp.bfloat16)
+        return lax.psum_scatter(terms, "tp", scatter_dimension=1, tiled=True)
+
+    arrived = swap_pair(out_terms(half_of(gated, 0, other)))
+    summed = out_terms(half_of(gated, 0, half)).astype(jnp.float32) + arrived.astype(jnp.float32)
+    return (tokens.astype(jnp.float32) + summed).astype(jnp.bfloat16)
 
 
 def solution(mesh):

time: 828 us -> 748 us (0.903)
  waiting for transfers between devices: 444 us -> 365 us
    ppermute x7, waiting for transfers between devices: 238 us -> 10.8 us  [local(): partner_piece = lax.ppermute(partner_piece, 'hi', backward)]
    ppermute x7, waiting for transfers between devices: 1.71 us -> 172 us  [local(): own_piece = lax.ppermute(own_piece, 'hi', forward)]
    reduce_scatter x2, waiting for transfers between devices: 104 us -> 29.2 us  [out_terms(): return lax.psum_scatter(terms, 'tp', scatter_dimension=1, tiled=True)]
    ppermute x3 -> x4, waiting for transfers between devices: 100 us -> 153 us  [swap_pair(): return lax.ppermute(value, 'lo', [(0, 1), (1, 0)])]
    dot_general x1 -> x2, matrix products: 27.6 us -> 24.5 us  [out_terms(): jnp.dot(rows, o_full, preferred_element_type=jnp.float32)]
  transfers between devices with their start and end apart: 23 -> 24, of which waited for: 12 -> 14; matrix products, arithmetic and copies ran while one was open for 31% -> 37% of each run, Pallas kernels for 0% -> 0%
where the time goes in v4:
time: 748 us; the launch traced here: 744 us
  waiting for transfers between devices  365 us (49%)
  local copies, waits for them, and re-layouts  168 us (22%)
  matrix products  78.4 us (10%)
  other arithmetic  66.7 us (9%)
  between operations  32.9 us (4%)
  starting transfers between devices  32.8 us (4%)
    ppermute x7, waiting for transfers between devices, local(): own_piece = lax.ppermute(own_piece, 'hi', forward)  172 us
    ppermute x4, waiting for transfers between devices, swap_pair(): return lax.ppermute(value, 'lo', [(0, 1), (1, 0)])  153 us
    dot_general x1, matrix products, local(): jnp.dot(normed, gathered_w.reshape(n_ctx * w_rows, 3 * half_width), prefe...  47.9 us
    reshape x2, local copies, waits for them, and re-layouts, skew(): flat.reshape(groups, filter_len, 2 * filter_len - 1)[:, :, :filter_len]  31.7 us
    reduce_scatter x2, waiting for transfers between devices, out_terms(): return lax.psum_scatter(terms, 'tp', scatter_dimension=1, tiled=True)  29.2 us
    dot_general x2, matrix products, out_terms(): jnp.dot(rows, o_full, preferred_element_type=jnp.float32)  24.5 us
    broadcast_in_dim x14, local copies, waits for them, and re-layouts, store(): piece[None]  23.2 us
    add x1, other arithmetic, featurize(): featured + short_filter[tap] * ext_float[short_taps - 1 - tap:short_taps...  22 us
  transfers between devices with their start and end apart: 24, of which 14 were waited for; matrix products, arithmetic and copies ran while one was open for 37% of the time, Pallas kernels for 0%

profile of v4, /device:TPU:0, one launch (start us, length us, event | category | flops | bytes accessed | tf_op | source)
XLA Modules:
  0.0 743.6 jit_solution(3692547557208650454)
XLA Ops:
  9.5 68.3 %collective-permute-done = bf16[768,2048]{1,0:T(8,128)(2,1)S(1)} collective-permute-done((bf16[768,2048]{1,0:T(8,128)(2,1)}, bf16[768,2048]{1,0:T(8,128)(2,1)S(1)}, u32[]{:S(2)}, u32[]{:S(2)}) %collective-permute-start) | collective-permute-done | bytes 3145760 | tf_op jit(solution)/shard_map/ppermute | solution.py:15
  80.1 3.7 pad_maximum_fusion
  91.7 31.8 %collective-permute-done.1 = bf16[256,3,1024]{0,2,1:T(8,128)(2,1)} collective-permute-done((bf16[256,3,1024]{0,2,1:T(8,128)(2,1)}, bf16[256,3,1024]{0,2,1:T(8,128)(2,1)}, u32[]{:S(2)}, u32[]{:S(2)}) %collective-permute-start.1) | collective-permute-done | bytes 1572896 | tf_op jit(solution)/shard_map/ppermute | solution.py:15
  129.9 15.9 %reshape.81 = bf16[64,128,255]{2,1,0:T(8,128)(2,1)} reshape(bf16[64,32640]{1,0:T(8,128)(2,1)} %slice.78) | data formatting | bytes 8355840 | tf_op jit(solution)/shard_map/reshape | solution.py:27
  150.4 15.9 %reshape.82 = bf16[64,128,255]{2,1,0:T(8,128)(2,1)} reshape(bf16[64,32640]{1,0:T(8,128)(2,1)} %slice.80) | data formatting | bytes 8355840 | tf_op jit(solution)/shard_map/reshape | solution.py:27
  171.6 32.5 %collective-permute-done.4 = bf16[256,3072]{0,1:T(8,128)(2,1)S(1)} collective-permute-done((bf16[256,3072]{0,1:T(8,128)(2,1)S(1)}, bf16[256,3072]{0,1:T(8,128)(2,1)S(1)}, u32[]{:S(2)}, u32[]{:S(2)}) %collective-permute-start.4) | collective-permute-done | bytes 1572896 | tf_op jit(solution)/shard_map/ppermute | solution.py:100
  207.3 31.1 %collective-permute-done.6 = bf16[256,3072]{0,1:T(8,128)(2,1)} collective-permute-done((bf16[256,3072]{0,1:T(8,128)(2,1)S(1)}, bf16[256,3072]{0,1:T(8,128)(2,1)}, u32[]{:S(2)}, u32[]{:S(2)}) %collective-permute-start.6) | collective-permute-done | bytes 1572896 | tf_op jit(solution)/shard_map/ppermute | solution.py:100
  257.9 15.1 %collective-permute-done.8 = bf16[256,3072]{0,1:T(8,128)(2,1)} collective-permute-done((bf16[256,3072]{0,1:T(8,128)(2,1)}, bf16[256,3072]{0,1:T(8,128)(2,1)}, u32[]{:S(2)}, u32[]{:S(2)}) %collective-permute-start.8) | collective-permute-done | bytes 1572896 | tf_op jit(solution)/shard_map/ppermute | solution.py:100
  276.2 8.8 %broadcast_in_dim.51 = bf16[16,256,3072]{2,1,0:T(8,128)(2,1)} broadcast(bf16[]{:T(256)} %constant.130.clone.1), dimensions={} | broadcast | bytes 25165826 | tf_op jit(solution)/shard_map/broadcast_in_dim | solution.py:92
  325.5 48.4 %collective-permute-done.12 = bf16[256,3072]{0,1:T(8,128)(2,1)} collective-permute-done((bf16[256,3072]{0,1:T(8,128)(2,1)}, bf16[256,3072]{0,1:T(8,128)(2,1)}, u32[]{:S(2)}, u32[]{:S(2)}) %collective-permute-start.12) | collective-permute-done | bytes 1572896 | tf_op jit(solution)/shard_map/ppermute | solution.py:100
  390.0 44.5 %collective-permute-done.14 = bf16[256,3072]{0,1:T(8,128)(2,1)} collective-permute-done((bf16[256,3072]{0,1:T(8,128)(2,1)}, bf16[256,3072]{0,1:T(8,128)(2,1)}, u32[]{:S(2)}, u32[]{:S(2)}) %collective-permute-start.14) | collective-permute-done | bytes 1572896 | tf_op jit(solution)/shard_map/ppermute | solution.py:100
  436.3 8.5 %collective-permute-done.15 = bf16[256,3072]{0,1:T(8,128)(2,1)} collective-permute-done((bf16[256,3072]{0,1:T(8,128)(2,1)}, bf16[256,3072]{0,1:T(8,128)(2,1)}, u32[]{:S(2)}, u32[]{:S(2)}) %collective-permute-start.15) | collective-permute-done | bytes 1572896 | tf_op jit(solution)/shard_map/ppermute | solution.py:101
  449.0 7.1 fusion
  456.2 47.9 %fusion.9 = bf16[1536,3072]{1,0:T(8,128)(2,1)S(1)} fusion(bf16[4096,3072]{1,0:T(8,128)(2,1)} %bitcast.36, bf16[1536,4096]{1,0:T(8,128)(2,1)} %all-gather.3.cloned.1.call-done, f32[4096]{0:T(1024)S(1)} %copy-done.14, f32[1536]{0:T(1024)S(1)} %add_rsqrt_fusion), kind=kOutput, calls=%fused_computation.13 | convolution fusion | flops 38684590080 | bytes 47208448 | tf_op jit(solution)/shard_map/dot_general | solution.py:110
  504.2 3.6 copy-done.6
  510.8 12.9 %copy.44 = bf16[1536,3072]{0,1:T(8,128)(2,1)} copy(bf16[1536,3072]{1,0:T(8,128)(2,1)} %copy-done.6) | data formatting | bytes 18874368 | tf_op jit(solution)/shard_map/convert_element_type | solution.py:115
  524.1 15.1 %maximum_convert_fusion = f32[1538,3,1024]{0,2,1:T(8,128)} fusion(bf16[1536,3,1024]{0,2,1:T(8,128)(2,1)} %bitcast.82, bf16[2,3,1024]{0,2,1:T(8,128)(2,1)S(1)} %copy.45), kind=kLoop, calls=%fused_computation.14 | loop fusion | flops 18898944 | bytes 28348416 | tf_op jit(solution)/shard_map/convert_element_type | solution.py:36
  539.2 22.0 %fusion.3 = f32[1536,3,1024]{0,2,1:T(8,128)S(1)} fusion(f32[1538,3,1024]{0,2,1:T(8,128)} %maximum_convert_fusion, f32[3,1024]{1,0:T(4,128)S(1)} %get-tuple-element.21, f32[3,1024]{1,0:T(4,128)S(1)} %get-tuple-element.20, f32[3,1024]{1,0:T(4,128)S(1)} %get-tuple-element.19), kind=kLoop, calls=%fused_computation.6 | loop fusion | flops 23592960 | bytes 75534336 | tf_op jit(solution)/shard_map/add | solution.py:40
  561.2 6.5 copy-done.2
  572.3 4.4 collective-permute-start.17
  576.7 4.9 copy.47
  581.6 3.6 convert_element_type.49
  586.1 13.2 %concatenate.22 = bf16[1664,1024]{1,0:T(8,128)(2,1)S(1)} concatenate(bf16[1,1024]{1,0:T(2,128)(2,1)S(1)} %broadcast_in_dim.66, bf16[127,1024]{1,0:T(8,128)(2,1)} %copy.48, bf16[1536,1024]{1,0:T(8,128)(2,1)} %bitcast.88), dimensions={0} | concatenate | bytes 6815744 | tf_op jit(solution)/shard_map/concatenate | solution.py:129
  604.5 3.6 slice.77
  608.1 4.5 fusion.14
  617.1 4.8 fusion.12
  622.0 12.4 %convolution_convert_fusion = bf16[768,4096]{1,0:T(8,128)(2,1)} fusion(bf16[1024,4096]{1,0:T(8,128)(2,1)} %all-gather.5.cloned.1.call-done, bf16[1536,1024]{0,1:T(8,128)(2,1)S(1)} %fusion.12, s32[]{:T(128)S(6)} %select_n.261), kind=kOutput, calls=%fused_computation.15 | convolution fusion | flops 6445596672 | bytes 16252932 | tf_op jit(solution)/shard_map/dot_general | solution.py:144
  634.4 12.1 %convolution_convert_fusion.1 = bf16[768,4096]{1,0:T(8,128)(2,1)} fusion(bf16[1024,4096]{1,0:T(8,128)(2,1)} %all-gather.5.cloned.1.call-done, bf16[1536,1024]{0,1:T(8,128)(2,1)S(1)} %fusion.12, s32[]{:T(128)S(6)} %select_n.257), kind=kOutput, calls=%fused_computation.16 | convolution fusion | flops 6445596672 | bytes 16252932 | tf_op jit(solution)/shard_map/dot_general | solution.py:144
  646.6 12.9 %reduce-scatter.5.cloned.1.call-done = bf16[768,2048]{1,0:T(8,128)(2,1)} async-done(((bf16[768,4096]{1,0:T(8,128)(2,1)}), bf16[768,2048]{1,0:T(8,128)(2,1)}) %reduce-scatter.5.cloned.1.call-update) | async-done | bytes 3145744 | tf_op jit(solution)/shard_map/reduce_scatter | solution.py:145
  661.3 16.2 %reduce-scatter.3.cloned.1.call-done = bf16[768,2048]{1,0:T(8,128)(2,1)} async-done(((bf16[768,4096]{1,0:T(8,128)(2,1)}), bf16[768,2048]{1,0:T(8,128)(2,1)}) %reduce-scatter.3.cloned.1.call-update) | async-done | bytes 3145744 | tf_op jit(solution)/shard_map/reduce_scatter | solution.py:145
  677.5 52.7 %collective-permute-done.19 = bf16[768,2048]{1,0:T(8,128)(2,1)} collective-permute-done((bf16[768,2048]{1,0:T(8,128)(2,1)}, bf16[768,2048]{1,0:T(8,128)(2,1)}, u32[]{:S(2)}, u32[]{:S(2)}) %collective-permute-start.19) | collective-permute-done | bytes 3145760 | tf_op jit(solution)/shard_map/ppermute | solution.py:15
  730.2 6.6 add_convert_fusion
  (139 shorter events, 119.0 us)
Async XLA Ops:
  6.5 118.6 %copy-start = (bf16[128,128]{1,0:T(8,128)(2,1)S(1)}, bf16[128,128]{1,0:T(8,128)(2,1)}, u32[]{:S(2)}) copy-start(bf16[128,128]{1,0:T(8,128)(2,1)} %param.12) | copy-start | bytes 98308
  6.5 442.5 %all-gather.3.cloned.1.call-start = ((), (), s32[]{:S(2)}) async-start(), calls=%async_computation.2 | async-start | bytes 18874368 | tf_op jit(solution)/shard_map/all_gather | solution.py:74
  6.5 71.2 %collective-permute-start = (bf16[768,2048]{1,0:T(8,128)(2,1)}, bf16[768,2048]{1,0:T(8,128)(2,1)S(1)}, u32[]{:S(2)}, u32[]{:S(2)}) collective-permute-start(bf16[768,2048]{1,0:T(8,128)(2,1)} %param.8), channel_id=1, source_target_pairs={{0,2},{2,0},{1,3},{3,1},{4,6},{6,4},{5,7},{7,5},{8,10},{10,8},{9,1... | collective-permute-start | bytes 9437192 | tf_op jit(solution)/shard_map/ppermute | solution.py:15
  83.8 538.2 %all-gather.5.cloned.1.call-start = ((), (), s32[]{:S(2)}) async-start(), calls=%async_computation.3 | async-start | bytes 9437184 | tf_op jit(solution)/shard_map/all_gather | solution.py:120
  87.6 35.9 %collective-permute-start.1 = (bf16[256,3,1024]{0,2,1:T(8,128)(2,1)}, bf16[256,3,1024]{0,2,1:T(8,128)(2,1)}, u32[]{:S(2)}, u32[]{:S(2)}) collective-permute-start(bf16[256,3,1024]{0,2,1:T(8,128)(2,1)} %copy.55), channel_id=1, source_target_pairs={{0,2},{2,0},{1,3},{3,1},{4,6},{6,4},{5,7},{7,5},{8,10},{10,8},{9,1... | collective-permute-start | bytes 4718600 | tf_op jit(solution)/shard_map/ppermute | solution.py:15
  90.1 79.4 %collective-permute-start.2 = (bf16[256,3072]{0,1:T(8,128)(2,1)S(1)}, bf16[256,3072]{0,1:T(8,128)(2,1)S(1)}, u32[]{:S(2)}, u32[]{:S(2)}) collective-permute-start(bf16[256,3072]{0,1:T(8,128)(2,1)S(1)} %bitcast.89), channel_id=1, source_target_pairs={{0,8},{8,16},{16,24},{24,28},{28,20},{20,12},{12,4},{4,0},{1,9},{9... | collective-permute-start | bytes 4718600 | tf_op jit(solution)/shard_map/ppermute | solution.py:100
  123.5 46.0 %collective-permute-start.3 = (bf16[256,3072]{0,1:T(8,128)(2,1)}, bf16[256,3072]{0,1:T(8,128)(2,1)}, u32[]{:S(2)}, u32[]{:S(2)}) collective-permute-start(bf16[256,3072]{0,1:T(8,128)(2,1)} %bitcast.6), channel_id=1, source_target_pairs={{8,0},{16,8},{24,16},{28,24},{20,28},{12,20},{4,12},{0,4},{9,1},{1... | collective-permute-start | bytes 4718600 | tf_op jit(solution)/shard_map/ppermute | solution.py:101
  150.4 94.7 %copy-start.15 = (s32[8]{0:T(128)S(1)}, s32[8]{0:T(128)}, u32[]{:S(2)}) copy-start(s32[8]{0:T(128)} %constant.155.clone) | copy-start | bytes 100
  150.4 105.2 %copy-start.12 = (s32[8]{0:T(128)S(1)}, s32[8]{0:T(128)}, u32[]{:S(2)}) copy-start(s32[8]{0:T(128)} %constant.154.clone) | copy-start | bytes 100
  169.5 87.5 %copy-start.7 = (bf16[256,3072]{0,1:T(8,128)(2,1)}, bf16[256,3072]{0,1:T(8,128)(2,1)S(1)}, u32[]{:S(2)}) copy-start(bf16[256,3072]{0,1:T(8,128)(2,1)S(1)} %collective-permute-done.2) | copy-start | bytes 4718596
  169.5 34.6 %collective-permute-start.4 = (bf16[256,3072]{0,1:T(8,128)(2,1)S(1)}, bf16[256,3072]{0,1:T(8,128)(2,1)S(1)}, u32[]{:S(2)}, u32[]{:S(2)}) collective-permute-start(bf16[256,3072]{0,1:T(8,128)(2,1)S(1)} %collective-permute-done.2), channel_id=1, source_target_pairs={{0,8},{8,16},{16,24},{24,28},{28,20},{20,12},{12,4},{4,0},{1,9},{9... | collective-permute-start | bytes 4718600 | tf_op jit(solution)/shard_map/ppermute | solution.py:100
  170.1 34.6 %collective-permute-start.5 = (bf16[256,3072]{0,1:T(8,128)(2,1)}, bf16[256,3072]{0,1:T(8,128)(2,1)S(1)}, u32[]{:S(2)}, u32[]{:S(2)}) collective-permute-start(bf16[256,3072]{0,1:T(8,128)(2,1)} %collective-permute-done.3), channel_id=1, source_target_pairs={{8,0},{16,8},{24,16},{28,24},{20,28},{12,20},{4,12},{0,4},{9,1},{1... | collective-permute-start | bytes 4718600 | tf_op jit(solution)/shard_map/ppermute | solution.py:101
  204.1 34.3 %collective-permute-start.6 = (bf16[256,3072]{0,1:T(8,128)(2,1)S(1)}, bf16[256,3072]{0,1:T(8,128)(2,1)}, u32[]{:S(2)}, u32[]{:S(2)}) collective-permute-start(bf16[256,3072]{0,1:T(8,128)(2,1)S(1)} %collective-permute-done.4), channel_id=1, source_target_pairs={{0,8},{8,16},{16,24},{24,28},{28,20},{20,12},{12,4},{4,0},{1,9},{9... | collective-permute-start | bytes 4718600 | tf_op jit(solution)/shard_map/ppermute | solution.py:100
  205.9 34.3 %collective-permute-start.7 = (bf16[256,3072]{0,1:T(8,128)(2,1)S(1)}, bf16[256,3072]{0,1:T(8,128)(2,1)}, u32[]{:S(2)}, u32[]{:S(2)}) collective-permute-start(bf16[256,3072]{0,1:T(8,128)(2,1)S(1)} %collective-permute-done.5), channel_id=1, source_target_pairs={{8,0},{16,8},{24,16},{28,24},{20,28},{12,20},{4,12},{0,4},{9,1},{1... | collective-permute-start | bytes 4718600 | tf_op jit(solution)/shard_map/ppermute | solution.py:101
  238.4 34.6 %collective-permute-start.8 = (bf16[256,3072]{0,1:T(8,128)(2,1)}, bf16[256,3072]{0,1:T(8,128)(2,1)}, u32[]{:S(2)}, u32[]{:S(2)}) collective-permute-start(bf16[256,3072]{0,1:T(8,128)(2,1)} %collective-permute-done.6), channel_id=1, source_target_pairs={{0,8},{8,16},{16,24},{24,28},{28,20},{20,12},{12,4},{4,0},{1,9},{9... | collective-permute-start | bytes 4718600 | tf_op jit(solution)/shard_map/ppermute | solution.py:100
  240.2 34.4 %collective-permute-start.9 = (bf16[256,3072]{0,1:T(8,128)(2,1)}, bf16[256,3072]{0,1:T(8,128)(2,1)}, u32[]{:S(2)}, u32[]{:S(2)}) collective-permute-start(bf16[256,3072]{0,1:T(8,128)(2,1)} %collective-permute-done.7), channel_id=1, source_target_pairs={{8,0},{16,8},{24,16},{28,24},{20,28},{12,20},{4,12},{0,4},{9,1},{1... | collective-permute-start | bytes 4718600 | tf_op jit(solution)/shard_map/ppermute | solution.py:101
  243.6 51.2 %collective-permute-start.18 = (bf16[1024,256]{1,0:T(8,128)(2,1)}, bf16[1024,256]{1,0:T(8,128)(2,1)}, u32[]{:S(2)}, u32[]{:S(2)}) collective-permute-start(bf16[1024,256]{1,0:T(8,128)(2,1)} %constant_dynamic-slice_fusion), channel_id=1, source_target_pairs={{0,2},{2,0},{1,3},{3,1},{4,6},{6,4},{5,7},{7,5},{8,10},{10,8},{9,1... | collective-permute-start | bytes 1572872 | tf_op jit(solution)/shard_map/ppermute | solution.py:15
  257.9 36.9 %copy-start.11 = (bf16[2048,256]{1,0:T(8,128)(2,1)S(1)}, bf16[2048,256]{1,0:T(8,128)(2,1)}, u32[]{:S(2)}) copy-start(bf16[2048,256]{1,0:T(8,128)(2,1)} %param.13) | copy-start | bytes 3145732
  273.0 35.0 %collective-permute-start.10 = (bf16[256,3072]{0,1:T(8,128)(2,1)}, bf16[256,3072]{0,1:T(8,128)(2,1)}, u32[]{:S(2)}, u32[]{:S(2)}) collective-permute-start(bf16[256,3072]{0,1:T(8,128)(2,1)} %collective-permute-done.8), channel_id=1, source_target_pairs={{0,8},{8,16},{16,24},{24,28},{28,20},{20,12},{12,4},{4,0},{1,9},{9... | collective-permute-start | bytes 4718600 | tf_op jit(solution)/shard_map/ppermute | solution.py:100
  274.6 34.4 %collective-permute-start.11 = (bf16[256,3072]{0,1:T(8,128)(2,1)}, bf16[256,3072]{0,1:T(8,128)(2,1)}, u32[]{:S(2)}, u32[]{:S(2)}) collective-permute-start(bf16[256,3072]{0,1:T(8,128)(2,1)} %collective-permute-done.9), channel_id=1, source_target_pairs={{8,0},{16,8},{24,16},{28,24},{20,28},{12,20},{4,12},{0,4},{9,1},{1... | collective-permute-start | bytes 4718600 | tf_op jit(solution)/shard_map/ppermute | solution.py:101
  297.2 362.4 %reduce-scatter.5.cloned.1.call-start = ((), (), s32[]{:S(2)}) async-start(), calls=%async_computation.5 | async-start | bytes 9437184 | tf_op jit(solution)/shard_map/reduce_scatter | solution.py:145
  308.0 66.0 %collective-permute-start.12 = (bf16[256,3072]{0,1:T(8,128)(2,1)}, bf16[256,3072]{0,1:T(8,128)(2,1)}, u32[]{:S(2)}, u32[]{:S(2)}) collective-permute-start(bf16[256,3072]{0,1:T(8,128)(2,1)} %collective-permute-done.10), channel_id=1, source_target_pairs={{0,8},{8,16},{16,24},{24,28},{28,20},{20,12},{12,4},{4,0},{1,9},{9... | collective-permute-start | bytes 4718600 | tf_op jit(solution)/shard_map/ppermute | solution.py:100
  308.9 67.5 %collective-permute-start.13 = (bf16[256,3072]{0,1:T(8,128)(2,1)}, bf16[256,3072]{0,1:T(8,128)(2,1)}, u32[]{:S(2)}, u32[]{:S(2)}) collective-permute-start(bf16[256,3072]{0,1:T(8,128)(2,1)} %collective-permute-done.11), channel_id=1, source_target_pairs={{8,0},{16,8},{24,16},{28,24},{20,28},{12,20},{4,12},{0,4},{9,1},{1... | collective-permute-start | bytes 4718600 | tf_op jit(solution)/shard_map/ppermute | solution.py:101
  374.0 60.6 %collective-permute-start.14 = (bf16[256,3072]{0,1:T(8,128)(2,1)}, bf16[256,3072]{0,1:T(8,128)(2,1)}, u32[]{:S(2)}, u32[]{:S(2)}) collective-permute-start(bf16[256,3072]{0,1:T(8,128)(2,1)} %collective-permute-done.12), channel_id=1, source_target_pairs={{0,8},{8,16},{16,24},{24,28},{28,20},{20,12},{12,4},{4,0},{1,9},{9... | collective-permute-start | bytes 4718600 | tf_op jit(solution)/shard_map/ppermute | solution.py:100
  376.5 68.3 %collective-permute-start.15 = (bf16[256,3072]{0,1:T(8,128)(2,1)}, bf16[256,3072]{0,1:T(8,128)(2,1)}, u32[]{:S(2)}, u32[]{:S(2)}) collective-permute-start(bf16[256,3072]{0,1:T(8,128)(2,1)} %collective-permute-done.13), channel_id=1, source_target_pairs={{8,0},{16,8},{24,16},{28,24},{20,28},{12,20},{4,12},{0,4},{9,1},{1... | collective-permute-start | bytes 4718600 | tf_op jit(solution)/shard_map/ppermute | solution.py:101
  456.2 54.6 %copy-start.13 = (f32[3,3,2048]{2,1,0:T(4,128)S(1)}, f32[3,3,2048]{2,1,0:T(4,128)}, u32[]{:S(2)}) copy-start(f32[3,3,2048]{2,1,0:T(4,128)} %param.11) | copy-start | bytes 221188
  507.8 15.8 %collective-permute-start.16 = (bf16[2,3,1024]{2,1,0:T(4,128)(2,1)S(1)}, bf16[2,3,1024]{2,1,0:T(4,128)(2,1)S(1)}, u32[]{:S(2)}, u32[]{:S(2)}) collective-permute-start(bf16[2,3,1024]{2,1,0:T(4,128)(2,1)S(1)} %slice.65), channel_id=1, source_target_pairs={{0,4},{4,8},{8,12},{12,16},{16,20},{20,24},{24,28},{1,5},{5,9},{9,... | collective-permute-start | bytes 36872 | tf_op jit(solution)/shard_map/ppermute | solution.py:11
  572.3 12.9 %collective-permute-start.17 = (bf16[127,1024]{0,1:T(8,128)(2,1)}, bf16[127,1024]{0,1:T(8,128)(2,1)S(1)}, u32[]{:S(2)}, u32[]{:S(2)}) collective-permute-start(bf16[127,1024]{0,1:T(8,128)(2,1)} %slice_bitcast_fusion.1), channel_id=1, source_target_pairs={{0,4},{4,8},{8,12},{12,16},{16,20},{20,24},{24,28},{1,5},{5,9},{9,... | collective-permute-start | bytes 780296 | tf_op jit(solution)/shard_map/ppermute | solution.py:11
  634.4 43.1 %reduce-scatter.3.cloned.1.call-start = ((), (), s32[]{:S(2)}) async-start(), calls=%async_computation.4 | async-start | bytes 9437184 | tf_op jit(solution)/shard_map/reduce_scatter | solution.py:145
  646.6 83.6 %copy-start.5 = (bf16[768,2048]{1,0:T(8,128)(2,1)S(1)}, bf16[768,2048]{1,0:T(8,128)(2,1)}, u32[]{:S(2)}) copy-start(bf16[768,2048]{1,0:T(8,128)(2,1)} %param.8) | copy-start | bytes 9437188
  646.6 90.2 %copy-start.1 = (bf16[128,128]{1,0:T(8,128)(2,1)S(1)}, bf16[128,128]{1,0:T(8,128)(2,1)}, u32[]{:S(2)}) copy-start(bf16[128,128]{1,0:T(8,128)(2,1)} %param.12) | copy-start | bytes 98308
  659.6 70.6 %collective-permute-start.19 = (bf16[768,2048]{1,0:T(8,128)(2,1)}, bf16[768,2048]{1,0:T(8,128)(2,1)}, u32[]{:S(2)}, u32[]{:S(2)}) collective-permute-start(bf16[768,2048]{1,0:T(8,128)(2,1)} %reduce-scatter.5.cloned.1.call-done), channel_id=1, source_target_pairs={{0,2},{2,0},{1,3},{3,1},{4,6},{6,4},{5,7},{7,5},{8,10},{10,8},{9,1... | collective-permute-start | bytes 9437192 | tf_op jit(solution)/shard_map/ppermute | solution.py:15
  (9 other events, 82.7 us)
Sparse Core Ops, SparseCore 0:
  83.9 26.3 all-gather.2
  297.3 179.5 all-gather.4
  634.5 24.9 reduce-scatter.4
  661.8 15.6 reduce-scatter.2

commit v5 on v4

--- a/solution.py
+++ b/solution.py
@@ -70,13 +70,6 @@
     other = 1 - half
     half_width = local_width // 2
 
-    pair_tokens = pair_ordered(tokens, swap_pair(tokens), half, 0)
-    pair_tokens = lax.all_gather(pair_tokens, "tp", axis=1, tiled=True)
-    row_count = pair_tokens.shape[0]
-    wide_float = pair_tokens.astype(jnp.float32)
-    scale = lax.rsqrt(jnp.mean(wide_float * wide_float, axis=-1, keepdims=True) + 1e-06)
-    normed = (wide_float * scale * norm_gain).astype(jnp.bfloat16)
-
     own_piece = half_of(w_in, 2, half).reshape(w_rows, 3 * half_width)
     partner_piece = swap_pair(half_of(w_in, 2, other)).reshape(w_rows, 3 * half_width)
     order = ring_order(n_hi)
@@ -99,25 +92,36 @@
         if step > 0:
             own_piece = lax.ppermute(own_piece, "hi", forward)
             partner_piece = lax.ppermute(partner_piece, "hi", backward)
+        own_stored, partner_stored = own_piece, partner_piece
         if step == 1:
-            own_piece, partner_piece, current, previous = lax.optimization_barrier(
-                (own_piece, partner_piece, current, previous)
+            own_stored, partner_stored, current, previous, tokens_late = lax.optimization_barrier(
+                (own_piece, partner_piece, current, previous, tokens)
             )
+        if step == n_hi - 1:
+            w_out_late, own_stored = lax.optimization_barrier((w_out, own_piece))
         own_from = order_table[(here - step) % n_hi]
         partner_from = order_table[(here + step) % n_hi]
-        gathered_w = store(gathered_w, own_piece, 2 * own_from + half)
-        gathered_w = store(gathered_w, partner_piece, 2 * partner_from + other)
+        gathered_w = store(gathered_w, own_stored, 2 * own_from + half)
+        gathered_w = store(gathered_w, partner_stored, 2 * partner_from + other)
+
+    pair_tokens = pair_ordered(tokens_late, swap_pair(tokens_late), half, 0)
+    pair_tokens = lax.all_gather(pair_tokens, "tp", axis=1, tiled=True)
+    row_count = pair_tokens.shape[0]
+    wide_float = pair_tokens.astype(jnp.float32)
+    scale = lax.rsqrt(jnp.mean(wide_float * wide_float, axis=-1, keepdims=True) + 1e-06)
+    normed = (wide_float * scale * norm_gain).astype(jnp.bfloat16)
+
+    o_keep = half_of(w_out_late, 0, half)
+    o_recv = swap_pair(half_of(w_out_late, 0, other))
+    o_pair = pair_ordered(o_keep, o_recv, half, 1)
+    o_full = lax.all_gather(o_pair, "hi", axis=1, tiled=True)
+
     projected = jnp.dot(
         normed,
         gathered_w.reshape(n_ctx * w_rows, 3 * half_width),
         preferred_element_type=jnp.float32,
     )
     projected = projected.astype(jnp.bfloat16).reshape(row_count, 3, half_width)
-
-    o_keep = half_of(w_out, 0, half)
-    o_recv = swap_pair(half_of(w_out, 0, other))
-    o_pair = pair_ordered(o_keep, o_recv, half, 1)
-    o_full = lax.all_gather(o_pair, "hi", axis=1, tiled=True)
 
     taps = half_of(short_filter, 2, half)
     prior_rows = shifted(projected[row_count - (short_taps - 1) :], "hi", 1)

time: 748 us -> 767 us (1.025)
  waiting for transfers between devices: 365 us -> 379 us
    ppermute x7, waiting for transfers between devices: 10.8 us -> 70.3 us  [local(): partner_piece = lax.ppermute(partner_piece, 'hi', backward)]
    ppermute x7, waiting for transfers between devices: 172 us -> 130 us  [local(): own_piece = lax.ppermute(own_piece, 'hi', forward)]
    unnamed x36 -> x40, local copies, waits for them, and re-layouts: 15.4 us -> 16.1 us
  transfers between devices with their start and end apart: 24 -> 24, of which waited for: 14 -> 12; matrix products, arithmetic and copies ran while one was open for 37% -> 36% of each run, Pallas kernels for 0% -> 0%
where the time goes in v5:
time: 767 us; the launch traced here: 756 us
  waiting for transfers between devices  379 us (49%)
  local copies, waits for them, and re-layouts  168 us (22%)
  matrix products  78.2 us (10%)
  other arithmetic  66.6 us (9%)
  between operations  33.5 us (4%)
  starting transfers between devices  30.4 us (4%)
    ppermute x4, waiting for transfers between devices, swap_pair(): return lax.ppermute(value, 'lo', [(0, 1), (1, 0)])  152 us
    ppermute x7, waiting for transfers between devices, local(): own_piece = lax.ppermute(own_piece, 'hi', forward)  130 us
    ppermute x7, waiting for transfers between devices, local(): partner_piece = lax.ppermute(partner_piece, 'hi', backward)  70.3 us
    dot_general x1, matrix products, local(): jnp.dot(normed, gathered_w.reshape(n_ctx * w_rows, 3 * half_width), prefe...  47.9 us
    reshape x2, local copies, waits for them, and re-layouts, skew(): flat.reshape(groups, filter_len, 2 * filter_len - 1)[:, :, :filter_len]  31.8 us
    reduce_scatter x2, waiting for transfers between devices, out_terms(): return lax.psum_scatter(terms, 'tp', scatter_dimension=1, tiled=True)  26.4 us
    dot_general x2, matrix products, out_terms(): jnp.dot(rows, o_full, preferred_element_type=jnp.float32)  24.4 us
    broadcast_in_dim x14, local copies, waits for them, and re-layouts, store(): piece[None]  23.9 us
  transfers between devices with their start and end apart: 24, of which 12 were waited for; matrix products, arithmetic and copies ran while one was open for 36% of the time, Pallas kernels for 0%

profile of v5, /device:TPU:0, one launch (start us, length us, event | category | flops | bytes accessed | tf_op | source)
XLA Modules:
  0.0 755.5 jit_solution(1256245058816417018)
XLA Ops:
  16.4 31.6 %collective-permute-done.1 = bf16[256,3,1024]{0,2,1:T(8,128)(2,1)} collective-permute-done((bf16[256,3,1024]{0,2,1:T(8,128)(2,1)}, bf16[256,3,1024]{0,2,1:T(8,128)(2,1)}, u32[]{:S(2)}, u32[]{:S(2)}) %collective-permute-start.1) | collective-permute-done | bytes 1572896 | tf_op jit(solution)/shard_map/ppermute | solution.py:15
  54.5 15.8 %reshape.81 = bf16[64,128,255]{2,1,0:T(8,128)(2,1)} reshape(bf16[64,32640]{1,0:T(8,128)(2,1)} %slice.78) | data formatting | bytes 8355840 | tf_op jit(solution)/shard_map/reshape | solution.py:27
  75.0 16.0 %reshape.82 = bf16[64,128,255]{2,1,0:T(8,128)(2,1)} reshape(bf16[64,32640]{1,0:T(8,128)(2,1)} %slice.80) | data formatting | bytes 8355840 | tf_op jit(solution)/shard_map/reshape | solution.py:27
  95.7 67.3 %collective-permute-done.3 = bf16[768,2048]{1,0:T(8,128)(2,1)} collective-permute-done((bf16[768,2048]{1,0:T(8,128)(2,1)S(1)}, bf16[768,2048]{1,0:T(8,128)(2,1)}, u32[]{:S(2)}, u32[]{:S(2)}) %collective-permute-start.3) | collective-permute-done | bytes 3145760 | tf_op jit(solution)/shard_map/ppermute | solution.py:15
  165.4 3.8 pad_maximum_fusion
  169.8 34.2 %collective-permute-done.4 = bf16[256,3072]{0,1:T(8,128)(2,1)S(1)} collective-permute-done((bf16[256,3072]{0,1:T(8,128)(2,1)}, bf16[256,3072]{0,1:T(8,128)(2,1)S(1)}, u32[]{:S(2)}, u32[]{:S(2)}) %collective-permute-start.4) | collective-permute-done | bytes 1572896 | tf_op jit(solution)/shard_map/ppermute | solution.py:93
  206.1 32.5 %collective-permute-done.6 = bf16[256,3072]{0,1:T(8,128)(2,1)S(1)} collective-permute-done((bf16[256,3072]{0,1:T(8,128)(2,1)S(1)}, bf16[256,3072]{0,1:T(8,128)(2,1)S(1)}, u32[]{:S(2)}, u32[]{:S(2)}) %collective-permute-start.6) | collective-permute-done | bytes 1572896 | tf_op jit(solution)/shard_map/ppermute | solution.py:93
  240.6 31.4 %collective-permute-done.8 = bf16[256,3072]{0,1:T(8,128)(2,1)S(1)} collective-permute-done((bf16[256,3072]{0,1:T(8,128)(2,1)S(1)}, bf16[256,3072]{0,1:T(8,128)(2,1)S(1)}, u32[]{:S(2)}, u32[]{:S(2)}) %collective-permute-start.8) | collective-permute-done | bytes 1572896 | tf_op jit(solution)/shard_map/ppermute | solution.py:93
  275.2 32.1 %collective-permute-done.10 = bf16[256,3072]{0,1:T(8,128)(2,1)} collective-permute-done((bf16[256,3072]{0,1:T(8,128)(2,1)S(1)}, bf16[256,3072]{0,1:T(8,128)(2,1)}, u32[]{:S(2)}, u32[]{:S(2)}) %collective-permute-start.10) | collective-permute-done | bytes 1572896 | tf_op jit(solution)/shard_map/ppermute | solution.py:93
  330.6 8.6 %broadcast_in_dim.51 = bf16[16,256,3072]{2,1,0:T(8,128)(2,1)} broadcast(bf16[]{:T(256)} %constant.130.clone.1), dimensions={} | broadcast | bytes 25165826 | tf_op jit(solution)/shard_map/broadcast_in_dim | solution.py:85
  364.0 15.8 %collective-permute-done.11 = bf16[256,3072]{0,1:T(8,128)(2,1)} collective-permute-done((bf16[256,3072]{0,1:T(8,128)(2,1)}, bf16[256,3072]{0,1:T(8,128)(2,1)}, u32[]{:S(2)}, u32[]{:S(2)}) %collective-permute-start.11) | collective-permute-done | bytes 1572896 | tf_op jit(solution)/shard_map/ppermute | solution.py:94
  393.0 21.3 %collective-permute-done.13 = bf16[256,3072]{0,1:T(8,128)(2,1)} collective-permute-done((bf16[256,3072]{0,1:T(8,128)(2,1)}, bf16[256,3072]{0,1:T(8,128)(2,1)}, u32[]{:S(2)}, u32[]{:S(2)}) %collective-permute-start.13) | collective-permute-done | bytes 1572896 | tf_op jit(solution)/shard_map/ppermute | solution.py:94
  428.3 33.2 %collective-permute-done.15 = bf16[256,3072]{0,1:T(8,128)(2,1)} collective-permute-done((bf16[256,3072]{0,1:T(8,128)(2,1)}, bf16[256,3072]{0,1:T(8,128)(2,1)}, u32[]{:S(2)}, u32[]{:S(2)}) %collective-permute-start.15) | collective-permute-done | bytes 1572896 | tf_op jit(solution)/shard_map/ppermute | solution.py:94
  464.4 7.2 fusion
  471.6 47.9 %fusion.9 = bf16[1536,3072]{1,0:T(8,128)(2,1)S(1)} fusion(bf16[4096,3072]{1,0:T(8,128)(2,1)} %bitcast.36, bf16[1536,4096]{1,0:T(8,128)(2,1)} %all-gather.3.cloned.1.call-done, f32[4096]{0:T(1024)S(1)} %copy-done.16, f32[1536]{0:T(1024)S(1)} %add_rsqrt_fusion), kind=kOutput, calls=%fused_computation.13 | convolution fusion | flops 38684590080 | bytes 47208448 | tf_op jit(solution)/shard_map/dot_general | solution.py:119
  524.5 12.9 %copy.44 = bf16[1536,3072]{0,1:T(8,128)(2,1)} copy(bf16[1536,3072]{1,0:T(8,128)(2,1)} %copy-done.7) | data formatting | bytes 18874368 | tf_op jit(solution)/shard_map/convert_element_type | solution.py:124
  537.8 15.1 %maximum_convert_fusion = f32[1538,3,1024]{0,2,1:T(8,128)} fusion(bf16[1536,3,1024]{0,2,1:T(8,128)(2,1)} %bitcast.82, bf16[2,3,1024]{0,2,1:T(8,128)(2,1)S(1)} %copy.45), kind=kLoop, calls=%fused_computation.14 | loop fusion | flops 18898944 | bytes 28348416 | tf_op jit(solution)/shard_map/convert_element_type | solution.py:36
  552.9 21.8 %fusion.3 = f32[1536,3,1024]{0,2,1:T(8,128)S(1)} fusion(f32[1538,3,1024]{0,2,1:T(8,128)} %maximum_convert_fusion, f32[3,1024]{1,0:T(4,128)S(1)} %get-tuple-element.27, f32[3,1024]{1,0:T(4,128)S(1)} %get-tuple-element.26, f32[3,1024]{1,0:T(4,128)S(1)} %get-tuple-element.25), kind=kLoop, calls=%fused_computation.6 | loop fusion | flops 23592960 | bytes 75534336 | tf_op jit(solution)/shard_map/add | solution.py:40
  574.7 6.4 copy-done.2
  585.8 5.5 collective-permute-start.17
  591.3 4.9 copy.47
  596.2 3.7 convert_element_type.49
  600.8 13.2 %concatenate.22 = bf16[1664,1024]{1,0:T(8,128)(2,1)S(1)} concatenate(bf16[1,1024]{1,0:T(2,128)(2,1)S(1)} %broadcast_in_dim.66, bf16[127,1024]{1,0:T(8,128)(2,1)} %copy.48, bf16[1536,1024]{1,0:T(8,128)(2,1)} %bitcast.88), dimensions={0} | concatenate | bytes 6815744 | tf_op jit(solution)/shard_map/concatenate | solution.py:133
  619.1 3.6 slice.77
  622.7 4.5 fusion.14
  631.8 4.8 fusion.12
  636.7 12.4 %convolution_convert_fusion = bf16[768,4096]{1,0:T(8,128)(2,1)} fusion(bf16[1024,4096]{1,0:T(8,128)(2,1)} %all-gather.5.cloned.1.call-done, bf16[1536,1024]{0,1:T(8,128)(2,1)S(1)} %fusion.12, s32[]{:T(128)S(6)} %select_n.261), kind=kOutput, calls=%fused_computation.15 | convolution fusion | flops 6445596672 | bytes 16252932 | tf_op jit(solution)/shard_map/dot_general | solution.py:148
  649.1 12.0 %convolution_convert_fusion.1 = bf16[768,4096]{1,0:T(8,128)(2,1)} fusion(bf16[1024,4096]{1,0:T(8,128)(2,1)} %all-gather.5.cloned.1.call-done, bf16[1536,1024]{0,1:T(8,128)(2,1)S(1)} %fusion.12, s32[]{:T(128)S(6)} %select_n.257), kind=kOutput, calls=%fused_computation.16 | convolution fusion | flops 6445596672 | bytes 16252932 | tf_op jit(solution)/shard_map/dot_general | solution.py:148
  661.2 10.1 %reduce-scatter.5.cloned.1.call-done = bf16[768,2048]{1,0:T(8,128)(2,1)} async-done(((bf16[768,4096]{1,0:T(8,128)(2,1)}), bf16[768,2048]{1,0:T(8,128)(2,1)}) %reduce-scatter.5.cloned.1.call-update) | async-done | bytes 3145744 | tf_op jit(solution)/shard_map/reduce_scatter | solution.py:149
  673.1 16.2 %reduce-scatter.3.cloned.1.call-done = bf16[768,2048]{1,0:T(8,128)(2,1)} async-done(((bf16[768,4096]{1,0:T(8,128)(2,1)}), bf16[768,2048]{1,0:T(8,128)(2,1)}) %reduce-scatter.3.cloned.1.call-update) | async-done | bytes 3145744 | tf_op jit(solution)/shard_map/reduce_scatter | solution.py:149
  689.3 52.7 %collective-permute-done.19 = bf16[768,2048]{1,0:T(8,128)(2,1)} collective-permute-done((bf16[768,2048]{1,0:T(8,128)(2,1)}, bf16[768,2048]{1,0:T(8,128)(2,1)}, u32[]{:S(2)}, u32[]{:S(2)}) %collective-permute-start.19) | collective-permute-done | bytes 3145760 | tf_op jit(solution)/shard_map/ppermute | solution.py:15
  742.0 6.6 add_convert_fusion
  (143 shorter events, 117.0 us)
Async XLA Ops:
  6.5 457.9 %all-gather.3.cloned.1.call-start = ((), (), s32[]{:S(2)}) async-start(), calls=%async_computation.2 | async-start | bytes 18874368 | tf_op jit(solution)/shard_map/all_gather | solution.py:108
  10.3 37.6 %collective-permute-start.1 = (bf16[256,3,1024]{0,2,1:T(8,128)(2,1)}, bf16[256,3,1024]{0,2,1:T(8,128)(2,1)}, u32[]{:S(2)}, u32[]{:S(2)}) collective-permute-start(bf16[256,3,1024]{0,2,1:T(8,128)(2,1)} %copy.55), channel_id=1, source_target_pairs={{0,2},{2,0},{1,3},{3,1},{4,6},{6,4},{5,7},{7,5},{8,10},{10,8},{9,1... | collective-permute-start | bytes 4718600 | tf_op jit(solution)/shard_map/ppermute | solution.py:15
  14.8 79.4 %collective-permute-start = (bf16[256,3072]{0,1:T(8,128)(2,1)}, bf16[256,3072]{0,1:T(8,128)(2,1)}, u32[]{:S(2)}, u32[]{:S(2)}) collective-permute-start(bf16[256,3072]{0,1:T(8,128)(2,1)} %bitcast.1), channel_id=1, source_target_pairs={{0,8},{8,16},{16,24},{24,28},{28,20},{20,12},{12,4},{4,0},{1,9},{9... | collective-permute-start | bytes 4718600 | tf_op jit(solution)/shard_map/ppermute | solution.py:93
  48.0 46.2 %collective-permute-start.2 = (bf16[256,3072]{0,1:T(8,128)(2,1)}, bf16[256,3072]{0,1:T(8,128)(2,1)}, u32[]{:S(2)}, u32[]{:S(2)}) collective-permute-start(bf16[256,3072]{0,1:T(8,128)(2,1)} %bitcast.2), channel_id=1, source_target_pairs={{8,0},{16,8},{24,16},{28,24},{20,28},{12,20},{4,12},{0,4},{9,1},{1... | collective-permute-start | bytes 4718600 | tf_op jit(solution)/shard_map/ppermute | solution.py:94
  94.2 68.9 %collective-permute-start.3 = (bf16[768,2048]{1,0:T(8,128)(2,1)S(1)}, bf16[768,2048]{1,0:T(8,128)(2,1)}, u32[]{:S(2)}, u32[]{:S(2)}) collective-permute-start(bf16[768,2048]{1,0:T(8,128)(2,1)S(1)} %copy-done.5), channel_id=1, source_target_pairs={{0,2},{2,0},{1,3},{3,1},{4,6},{6,4},{5,7},{7,5},{8,10},{10,8},{9,1... | collective-permute-start | bytes 9437192 | tf_op jit(solution)/shard_map/ppermute | solution.py:15
  169.1 138.9 %copy-start.17 = (s32[8]{0:T(128)S(1)}, s32[8]{0:T(128)}, u32[]{:S(2)}) copy-start(s32[8]{0:T(128)} %constant.155.clone) | copy-start | bytes 100
  169.1 149.4 %copy-start.14 = (s32[8]{0:T(128)S(1)}, s32[8]{0:T(128)}, u32[]{:S(2)}) copy-start(s32[8]{0:T(128)} %constant.154.clone) | copy-start | bytes 100
  169.2 467.5 %all-gather.5.cloned.1.call-start = ((), (), s32[]{:S(2)}) async-start(), calls=%async_computation.3 | async-start | bytes 9437184 | tf_op jit(solution)/shard_map/all_gather | solution.py:117
  169.2 34.8 %collective-permute-start.4 = (bf16[256,3072]{0,1:T(8,128)(2,1)}, bf16[256,3072]{0,1:T(8,128)(2,1)S(1)}, u32[]{:S(2)}, u32[]{:S(2)}) collective-permute-start(bf16[256,3072]{0,1:T(8,128)(2,1)} %collective-permute-done), channel_id=1, source_target_pairs={{0,8},{8,16},{16,24},{24,28},{28,20},{20,12},{12,4},{4,0},{1,9},{9... | collective-permute-start | bytes 4718600 | tf_op jit(solution)/shard_map/ppermute | solution.py:93
  204.0 34.6 %collective-permute-start.6 = (bf16[256,3072]{0,1:T(8,128)(2,1)S(1)}, bf16[256,3072]{0,1:T(8,128)(2,1)S(1)}, u32[]{:S(2)}, u32[]{:S(2)}) collective-permute-start(bf16[256,3072]{0,1:T(8,128)(2,1)S(1)} %collective-permute-done.4), channel_id=1, source_target_pairs={{0,8},{8,16},{16,24},{24,28},{28,20},{20,12},{12,4},{4,0},{1,9},{9... | collective-permute-start | bytes 4718600 | tf_op jit(solution)/shard_map/ppermute | solution.py:93
  204.6 34.6 %collective-permute-start.5 = (bf16[256,3072]{0,1:T(8,128)(2,1)}, bf16[256,3072]{0,1:T(8,128)(2,1)S(1)}, u32[]{:S(2)}, u32[]{:S(2)}) collective-permute-start(bf16[256,3072]{0,1:T(8,128)(2,1)} %collective-permute-done.2), channel_id=1, source_target_pairs={{8,0},{16,8},{24,16},{28,24},{20,28},{12,20},{4,12},{0,4},{9,1},{1... | collective-permute-start | bytes 4718600 | tf_op jit(solution)/shard_map/ppermute | solution.py:94
  238.6 68.7 %copy-start.9 = (bf16[256,3072]{0,1:T(8,128)(2,1)}, bf16[256,3072]{0,1:T(8,128)(2,1)S(1)}, u32[]{:S(2)}) copy-start(bf16[256,3072]{0,1:T(8,128)(2,1)S(1)} %collective-permute-done.6) | copy-start | bytes 4718596
  238.6 33.4 %collective-permute-start.8 = (bf16[256,3072]{0,1:T(8,128)(2,1)S(1)}, bf16[256,3072]{0,1:T(8,128)(2,1)S(1)}, u32[]{:S(2)}, u32[]{:S(2)}) collective-permute-start(bf16[256,3072]{0,1:T(8,128)(2,1)S(1)} %collective-permute-done.6), channel_id=1, source_target_pairs={{0,8},{8,16},{16,24},{24,28},{28,20},{20,12},{12,4},{4,0},{1,9},{9... | collective-permute-start | bytes 4718600 | tf_op jit(solution)/shard_map/ppermute | solution.py:93
  239.2 68.1 %copy-start.10 = (bf16[256,3072]{0,1:T(8,128)(2,1)}, bf16[256,3072]{0,1:T(8,128)(2,1)S(1)}, u32[]{:S(2)}) copy-start(bf16[256,3072]{0,1:T(8,128)(2,1)S(1)} %collective-permute-done.5) | copy-start | bytes 4718596
  239.2 34.6 %collective-permute-start.7 = (bf16[256,3072]{0,1:T(8,128)(2,1)S(1)}, bf16[256,3072]{0,1:T(8,128)(2,1)S(1)}, u32[]{:S(2)}, u32[]{:S(2)}) collective-permute-start(bf16[256,3072]{0,1:T(8,128)(2,1)S(1)} %collective-permute-done.5), channel_id=1, source_target_pairs={{8,0},{16,8},{24,16},{28,24},{20,28},{12,20},{4,12},{0,4},{9,1},{1... | collective-permute-start | bytes 4718600 | tf_op jit(solution)/shard_map/ppermute | solution.py:94
  273.2 34.1 %collective-permute-start.10 = (bf16[256,3072]{0,1:T(8,128)(2,1)S(1)}, bf16[256,3072]{0,1:T(8,128)(2,1)}, u32[]{:S(2)}, u32[]{:S(2)}) collective-permute-start(bf16[256,3072]{0,1:T(8,128)(2,1)S(1)} %collective-permute-done.8), channel_id=1, source_target_pairs={{0,8},{8,16},{16,24},{24,28},{28,20},{20,12},{12,4},{4,0},{1,9},{9... | collective-permute-start | bytes 4718600 | tf_op jit(solution)/shard_map/ppermute | solution.py:93
  273.7 65.5 %copy-start.11 = (bf16[256,3072]{0,1:T(8,128)(2,1)}, bf16[256,3072]{0,1:T(8,128)(2,1)S(1)}, u32[]{:S(2)}) copy-start(bf16[256,3072]{0,1:T(8,128)(2,1)S(1)} %collective-permute-done.7) | copy-start | bytes 4718596
  273.7 71.4 %collective-permute-start.9 = (bf16[256,3072]{0,1:T(8,128)(2,1)S(1)}, bf16[256,3072]{0,1:T(8,128)(2,1)}, u32[]{:S(2)}, u32[]{:S(2)}) collective-permute-start(bf16[256,3072]{0,1:T(8,128)(2,1)S(1)} %collective-permute-done.7), channel_id=1, source_target_pairs={{8,0},{16,8},{24,16},{28,24},{20,28},{12,20},{4,12},{0,4},{9,1},{1... | collective-permute-start | bytes 4718600 | tf_op jit(solution)/shard_map/ppermute | solution.py:94
  307.3 45.4 %collective-permute-start.12 = (bf16[256,3072]{0,1:T(8,128)(2,1)}, bf16[256,3072]{0,1:T(8,128)(2,1)}, u32[]{:S(2)}, u32[]{:S(2)}) collective-permute-start(bf16[256,3072]{0,1:T(8,128)(2,1)} %collective-permute-done.10), channel_id=1, source_target_pairs={{0,8},{8,16},{16,24},{24,28},{28,20},{20,12},{12,4},{4,0},{1,9},{9... | collective-permute-start | bytes 4718600 | tf_op jit(solution)/shard_map/ppermute | solution.py:93
  345.2 34.6 %collective-permute-start.11 = (bf16[256,3072]{0,1:T(8,128)(2,1)}, bf16[256,3072]{0,1:T(8,128)(2,1)}, u32[]{:S(2)}, u32[]{:S(2)}) collective-permute-start(bf16[256,3072]{0,1:T(8,128)(2,1)} %collective-permute-done.9), channel_id=1, source_target_pairs={{8,0},{16,8},{24,16},{28,24},{20,28},{12,20},{4,12},{0,4},{9,1},{1... | collective-permute-start | bytes 4718600 | tf_op jit(solution)/shard_map/ppermute | solution.py:94
  352.6 32.8 %collective-permute-start.14 = (bf16[256,3072]{0,1:T(8,128)(2,1)}, bf16[256,3072]{0,1:T(8,128)(2,1)}, u32[]{:S(2)}, u32[]{:S(2)}) collective-permute-start(bf16[256,3072]{0,1:T(8,128)(2,1)} %collective-permute-done.12), channel_id=1, source_target_pairs={{0,8},{8,16},{16,24},{24,28},{28,20},{20,12},{12,4},{4,0},{1,9},{9... | collective-permute-start | bytes 4718600 | tf_op jit(solution)/shard_map/ppermute | solution.py:93
  379.8 34.6 %collective-permute-start.13 = (bf16[256,3072]{0,1:T(8,128)(2,1)}, bf16[256,3072]{0,1:T(8,128)(2,1)}, u32[]{:S(2)}, u32[]{:S(2)}) collective-permute-start(bf16[256,3072]{0,1:T(8,128)(2,1)} %collective-permute-done.11), channel_id=1, source_target_pairs={{8,0},{16,8},{24,16},{28,24},{20,28},{12,20},{4,12},{0,4},{9,1},{1... | collective-permute-start | bytes 4718600 | tf_op jit(solution)/shard_map/ppermute | solution.py:94
  385.5 30.2 %collective-permute-start.18 = (bf16[1024,256]{1,0:T(8,128)(2,1)S(1)}, bf16[1024,256]{1,0:T(8,128)(2,1)}, u32[]{:S(2)}, u32[]{:S(2)}) collective-permute-start(bf16[1024,256]{1,0:T(8,128)(2,1)S(1)} %constant_dynamic-slice_fusion), channel_id=1, source_target_pairs={{0,2},{2,0},{1,3},{3,1},{4,6},{6,4},{5,7},{7,5},{8,10},{10,8},{9,1... | collective-permute-start | bytes 1572872 | tf_op jit(solution)/shard_map/ppermute | solution.py:15
  414.4 47.1 %collective-permute-start.15 = (bf16[256,3072]{0,1:T(8,128)(2,1)}, bf16[256,3072]{0,1:T(8,128)(2,1)}, u32[]{:S(2)}, u32[]{:S(2)}) collective-permute-start(bf16[256,3072]{0,1:T(8,128)(2,1)} %collective-permute-done.13), channel_id=1, source_target_pairs={{8,0},{16,8},{24,16},{28,24},{20,28},{12,20},{4,12},{0,4},{9,1},{1... | collective-permute-start | bytes 4718600 | tf_op jit(solution)/shard_map/ppermute | solution.py:94
  418.0 253.3 %reduce-scatter.5.cloned.1.call-start = ((), (), s32[]{:S(2)}) async-start(), calls=%async_computation.5 | async-start | bytes 9437184 | tf_op jit(solution)/shard_map/reduce_scatter | solution.py:149
  471.6 52.8 %copy-start.15 = (f32[3,3,2048]{2,1,0:T(4,128)S(1)}, f32[3,3,2048]{2,1,0:T(4,128)}, u32[]{:S(2)}) copy-start(f32[3,3,2048]{2,1,0:T(4,128)} %param.11) | copy-start | bytes 221188
  523.1 14.2 %collective-permute-start.16 = (bf16[2,3,1024]{2,1,0:T(4,128)(2,1)S(1)}, bf16[2,3,1024]{2,1,0:T(4,128)(2,1)S(1)}, u32[]{:S(2)}, u32[]{:S(2)}) collective-permute-start(bf16[2,3,1024]{2,1,0:T(4,128)(2,1)S(1)} %slice.65), channel_id=1, source_target_pairs={{0,4},{4,8},{8,12},{12,16},{16,20},{20,24},{24,28},{1,5},{5,9},{9,... | collective-permute-start | bytes 36872 | tf_op jit(solution)/shard_map/ppermute | solution.py:11
  585.8 14.1 %collective-permute-start.17 = (bf16[127,1024]{0,1:T(8,128)(2,1)}, bf16[127,1024]{0,1:T(8,128)(2,1)S(1)}, u32[]{:S(2)}, u32[]{:S(2)}) collective-permute-start(bf16[127,1024]{0,1:T(8,128)(2,1)} %slice_bitcast_fusion.1), channel_id=1, source_target_pairs={{0,4},{4,8},{8,12},{12,16},{16,20},{20,24},{24,28},{1,5},{5,9},{9,... | collective-permute-start | bytes 780296 | tf_op jit(solution)/shard_map/ppermute | solution.py:11
  649.1 40.2 %reduce-scatter.3.cloned.1.call-start = ((), (), s32[]{:S(2)}) async-start(), calls=%async_computation.4 | async-start | bytes 9437184 | tf_op jit(solution)/shard_map/reduce_scatter | solution.py:149
  661.2 80.8 %copy-start.6 = (bf16[768,2048]{1,0:T(8,128)(2,1)S(1)}, bf16[768,2048]{1,0:T(8,128)(2,1)}, u32[]{:S(2)}) copy-start(bf16[768,2048]{1,0:T(8,128)(2,1)} %param.8) | copy-start | bytes 9437188
  661.2 87.4 %copy-start.1 = (bf16[128,128]{1,0:T(8,128)(2,1)S(1)}, bf16[128,128]{1,0:T(8,128)(2,1)}, u32[]{:S(2)}) copy-start(bf16[128,128]{1,0:T(8,128)(2,1)} %param.12) | copy-start | bytes 98308
  671.4 70.6 %collective-permute-start.19 = (bf16[768,2048]{1,0:T(8,128)(2,1)}, bf16[768,2048]{1,0:T(8,128)(2,1)}, u32[]{:S(2)}, u32[]{:S(2)}) collective-permute-start(bf16[768,2048]{1,0:T(8,128)(2,1)} %reduce-scatter.5.cloned.1.call-done), channel_id=1, source_target_pairs={{0,2},{2,0},{1,3},{3,1},{4,6},{6,4},{5,7},{7,5},{8,10},{10,8},{9,1... | collective-permute-start | bytes 9437192 | tf_op jit(solution)/shard_map/ppermute | solution.py:15
  (11 other events, 107.3 us)
Sparse Core Ops, SparseCore 0:
  169.3 25.1 all-gather.2
  418.1 136.4 all-gather.4
  649.2 22.1 reduce-scatter.4
  673.6 15.6 reduce-scatter.2

commit v6 on v4

--- a/solution.py
+++ b/solution.py
@@ -16,19 +16,20 @@
 
 
 def toeplitz_pair(long_filter):
-    filter_len, groups = long_filter.shape
+    filter_len = long_filter.shape[0]
+    tap = lax.broadcasted_iota(jnp.int32, (filter_len, filter_len, filter_len), 0)
+    offset = lax.broadcasted_iota(jnp.int32, (filter_len, filter_len, filter_len), 1) - (
+        lax.broadcasted_iota(jnp.int32, (filter_len, filter_len, filter_len), 2)
+    )
     table = long_filter.T
-    zeros = jnp.zeros((groups, filter_len), long_filter.dtype)
 
-    def skew(edge):
-        reverse = edge[:, ::-1]
-        tiled = jnp.tile(reverse, (1, filter_len + 1))
-        flat = tiled[:, filter_len - 1 : filter_len - 1 + filter_len * (2 * filter_len - 1)]
-        return flat.reshape(groups, filter_len, 2 * filter_len - 1)[:, :, :filter_len]
+    def spread(hot):
+        dense = jnp.einsum(
+            "gm,mts->gts", table, hot.astype(table.dtype), preferred_element_type=jnp.float32
+        )
+        return dense.astype(table.dtype)
 
-    current = skew(jnp.concatenate([zeros, table], axis=1))
-    previous = skew(jnp.concatenate([table, zeros], axis=1))
-    return (current, previous)
+    return (spread(offset == tap), spread(offset + filter_len == tap))
 
 
 def featurize(extended, short_filter, count):
@@ -99,10 +100,6 @@
         if step > 0:
             own_piece = lax.ppermute(own_piece, "hi", forward)
             partner_piece = lax.ppermute(partner_piece, "hi", backward)
-        if step == 1:
-            own_piece, partner_piece, current, previous = lax.optimization_barrier(
-                (own_piece, partner_piece, current, previous)
-            )
         own_from = order_table[(here - step) % n_hi]
         partner_from = order_table[(here + step) % n_hi]
         gathered_w = store(gathered_w, own_piece, 2 * own_from + half)

time: 748 us -> 764 us (1.021)
  waiting for transfers between devices: 365 us -> 414 us
  local copies, waits for them, and re-layouts: 168 us -> 122 us
    ppermute x7, waiting for transfers between devices: 10.8 us -> 238 us  [local(): partner_piece = lax.ppermute(partner_piece, 'hi', backward)]
    ppermute x7, waiting for transfers between devices: 172 us -> 1.71 us  [local(): own_piece = lax.ppermute(own_piece, 'hi', forward)]
    reshape x2 -> x0, local copies, waits for them, and re-layouts: 31.7 us -> none  [skew(): flat.reshape(groups, filter_len, 2 * filter_len - 1)[:, :, :filter_len]]
    slice x5 -> x0, local copies, waits for them, and re-layouts: 9.96 us -> none  [the longest x2 6.46 us: skew(): tiled[:, filter_len - 1:filter_len - 1 + filter_len * (2 * filter_len - 1)]]
    reduce_scatter x2, waiting for transfers between devices: 29.2 us -> 20.8 us  [out_terms(): return lax.psum_scatter(terms, 'tp', scatter_dimension=1, tiled=True)]
    unnamed x36 -> x38, local copies, waits for them, and re-layouts: 15.4 us -> 13.6 us
  transfers between devices with their start and end apart: 24 -> 24, of which waited for: 14 -> 13; matrix products, arithmetic and copies ran while one was open for 37% -> 32% of each run, Pallas kernels for 0% -> 0%
where the time goes in v6:
time: 764 us; the launch traced here: 756 us
  waiting for transfers between devices  414 us (54%)
  local copies, waits for them, and re-layouts  122 us (16%)
  matrix products  85.7 us (11%)
  other arithmetic  66.5 us (9%)
  between operations  34.1 us (4%)
  starting transfers between devices  33.5 us (4%)
    ppermute x7, waiting for transfers between devices, local(): partner_piece = lax.ppermute(partner_piece, 'hi', backward)  238 us
    ppermute x4, waiting for transfers between devices, swap_pair(): return lax.ppermute(value, 'lo', [(0, 1), (1, 0)])  153 us
    dot_general x1, matrix products, local(): jnp.dot(normed, gathered_w.reshape(n_ctx * w_rows, 3 * half_width), prefe...  47.7 us
    dot_general x2, matrix products, out_terms(): jnp.dot(rows, o_full, preferred_element_type=jnp.float32)  24.7 us
    broadcast_in_dim x14, local copies, waits for them, and re-layouts, store(): piece[None]  23.4 us
    add x1, other arithmetic, featurize(): featured + short_filter[tap] * ext_float[short_taps - 1 - tap:short_taps...  21.9 us
    reduce_scatter x2, waiting for transfers between devices, out_terms(): return lax.psum_scatter(terms, 'tp', scatter_dimension=1, tiled=True)  20.8 us
    dynamic_update_slice x16, local copies, waits for them, and re-layouts, store(): lax.dynamic_update_slice_in_dim(buffer, piece[None], ctx_index, axis=0)  20.6 us
  transfers between devices with their start and end apart: 24, of which 13 were waited for; matrix products, arithmetic and copies ran while one was open for 32% of the time, Pallas kernels for 0%

profile of v6, /device:TPU:0, one launch (start us, length us, event | category | flops | bytes accessed | tf_op | source)
XLA Modules:
  0.0 755.7 jit_solution(9753642534010056877)
XLA Ops:
  9.5 68.3 %collective-permute-done = bf16[768,2048]{1,0:T(8,128)(2,1)S(1)} collective-permute-done((bf16[768,2048]{1,0:T(8,128)(2,1)}, bf16[768,2048]{1,0:T(8,128)(2,1)S(1)}, u32[]{:S(2)}, u32[]{:S(2)}) %collective-permute-start) | collective-permute-done | bytes 3145760 | tf_op jit(solution)/shard_map/ppermute | solution.py:15
  80.1 3.7 pad_maximum_fusion
  91.7 31.8 %collective-permute-done.1 = bf16[256,3,1024]{0,2,1:T(8,128)(2,1)} collective-permute-done((bf16[256,3,1024]{0,2,1:T(8,128)(2,1)}, bf16[256,3,1024]{0,2,1:T(8,128)(2,1)}, u32[]{:S(2)}, u32[]{:S(2)}) %collective-permute-start.1) | collective-permute-done | bytes 1572896 | tf_op jit(solution)/shard_map/ppermute | solution.py:15
  126.7 31.7 %collective-permute-done.3 = bf16[256,3072]{0,1:T(8,128)(2,1)S(1)} collective-permute-done((bf16[256,3072]{0,1:T(8,128)(2,1)}, bf16[256,3072]{0,1:T(8,128)(2,1)S(1)}, u32[]{:S(2)}, u32[]{:S(2)}) %collective-permute-start.3) | collective-permute-done | bytes 1572896 | tf_op jit(solution)/shard_map/ppermute | solution.py:102
  161.3 31.7 %collective-permute-done.5 = bf16[256,3072]{0,1:T(8,128)(2,1)S(1)} collective-permute-done((bf16[256,3072]{0,1:T(8,128)(2,1)S(1)}, bf16[256,3072]{0,1:T(8,128)(2,1)S(1)}, u32[]{:S(2)}, u32[]{:S(2)}) %collective-permute-start.5) | collective-permute-done | bytes 1572896 | tf_op jit(solution)/shard_map/ppermute | solution.py:102
  196.3 31.0 %collective-permute-done.7 = bf16[256,3072]{0,1:T(8,128)(2,1)} collective-permute-done((bf16[256,3072]{0,1:T(8,128)(2,1)S(1)}, bf16[256,3072]{0,1:T(8,128)(2,1)}, u32[]{:S(2)}, u32[]{:S(2)}) %collective-permute-start.7) | collective-permute-done | bytes 1572896 | tf_op jit(solution)/shard_map/ppermute | solution.py:102
  255.2 8.7 %broadcast_in_dim.50 = bf16[16,256,3072]{2,1,0:T(8,128)(2,1)} broadcast(bf16[]{:T(256)} %constant.130.clone.1), dimensions={} | broadcast | bytes 25165826 | tf_op jit(solution)/shard_map/broadcast_in_dim | solution.py:93
  283.7 47.3 %collective-permute-done.11 = bf16[256,3072]{0,1:T(8,128)(2,1)} collective-permute-done((bf16[256,3072]{0,1:T(8,128)(2,1)}, bf16[256,3072]{0,1:T(8,128)(2,1)}, u32[]{:S(2)}, u32[]{:S(2)}) %collective-permute-start.11) | collective-permute-done | bytes 1572896 | tf_op jit(solution)/shard_map/ppermute | solution.py:102
  340.7 3.0 collective-permute-start.14
  349.8 51.7 %collective-permute-done.13 = bf16[256,3072]{0,1:T(8,128)(2,1)} collective-permute-done((bf16[256,3072]{0,1:T(8,128)(2,1)}, bf16[256,3072]{0,1:T(8,128)(2,1)}, u32[]{:S(2)}, u32[]{:S(2)}) %collective-permute-start.13) | collective-permute-done | bytes 1572896 | tf_op jit(solution)/shard_map/ppermute | solution.py:102
  414.9 44.7 %collective-permute-done.15 = bf16[256,3072]{0,1:T(8,128)(2,1)} collective-permute-done((bf16[256,3072]{0,1:T(8,128)(2,1)}, bf16[256,3072]{0,1:T(8,128)(2,1)}, u32[]{:S(2)}, u32[]{:S(2)}) %collective-permute-start.15) | collective-permute-done | bytes 1572896 | tf_op jit(solution)/shard_map/ppermute | solution.py:102
  462.6 7.1 fusion
  469.7 47.7 %fusion.9 = bf16[1536,3072]{1,0:T(8,128)(2,1)S(1)} fusion(bf16[4096,3072]{1,0:T(8,128)(2,1)} %bitcast.35, bf16[1536,4096]{1,0:T(8,128)(2,1)} %all-gather.3.cloned.1.call-done, f32[4096]{0:T(1024)S(1)} %copy-done.16, f32[1536]{0:T(1024)S(1)} %add_rsqrt_fusion), kind=kOutput, calls=%fused_computation.13 | convolution fusion | flops 38684590080 | bytes 47208448 | tf_op jit(solution)/shard_map/dot_general | solution.py:107
  517.4 3.6 copy-done.5
  522.4 13.1 %copy.38 = bf16[1536,3072]{0,1:T(8,128)(2,1)} copy(bf16[1536,3072]{1,0:T(8,128)(2,1)} %copy-done.5) | data formatting | bytes 18874368 | tf_op jit(solution)/shard_map/convert_element_type | solution.py:112
  535.9 15.1 %maximum_convert_fusion = f32[1538,3,1024]{0,2,1:T(8,128)} fusion(bf16[1536,3,1024]{0,2,1:T(8,128)(2,1)} %bitcast.77, bf16[2,3,1024]{0,2,1:T(8,128)(2,1)S(1)} %copy.39), kind=kLoop, calls=%fused_computation.14 | loop fusion | flops 18898944 | bytes 28348416 | tf_op jit(solution)/shard_map/convert_element_type | solution.py:37
  551.0 21.9 %fusion.3 = f32[1536,3,1024]{0,2,1:T(8,128)S(1)} fusion(f32[1538,3,1024]{0,2,1:T(8,128)} %maximum_convert_fusion, f32[3,1024]{1,0:T(4,128)S(1)} %get-tuple-element.13, f32[3,1024]{1,0:T(4,128)S(1)} %get-tuple-element.12, f32[3,1024]{1,0:T(4,128)S(1)} %get-tuple-element.11), kind=kLoop, calls=%fused_computation.6 | loop fusion | flops 23592960 | bytes 75534336 | tf_op jit(solution)/shard_map/add | solution.py:41
  573.0 6.5 copy-done.1
  584.1 7.6 %collective-permute-start.17 = (bf16[127,1024]{0,1:T(8,128)(2,1)}, bf16[127,1024]{0,1:T(8,128)(2,1)S(1)}, u32[]{:S(2)}, u32[]{:S(2)}) collective-permute-start(bf16[127,1024]{0,1:T(8,128)(2,1)} %slice_bitcast_fusion.1), channel_id=1, source_target_pairs={{0,4},{4,8},{8,12},{12,16},{16,20},{20,24},{24,28},{1,5},{5,9},{9,... | collective-permute-start | bytes 780296 | tf_op jit(solution)/shard_map/ppermute | solution.py:11
  597.1 3.0 copy.43
  600.1 3.6 convert_element_type.57
  604.6 13.2 %concatenate.14 = bf16[1664,1024]{1,0:T(8,128)(2,1)S(1)} concatenate(bf16[1,1024]{1,0:T(2,128)(2,1)S(1)} %broadcast_in_dim.65, bf16[127,1024]{1,0:T(8,128)(2,1)} %copy.44, bf16[1536,1024]{1,0:T(8,128)(2,1)} %bitcast.79), dimensions={0} | concatenate | bytes 6815744 | tf_op jit(solution)/shard_map/concatenate | solution.py:126
  619.8 3.2 copy.45
  623.0 3.7 slice.61
  626.6 5.4 fusion.17
  637.4 4.8 fusion.14
  642.3 12.3 %convolution_convert_fusion = bf16[768,4096]{1,0:T(8,128)(2,1)} fusion(bf16[1024,4096]{1,0:T(8,128)(2,1)} %all-gather.5.cloned.1.call-done, bf16[1536,1024]{0,1:T(8,128)(2,1)S(1)} %fusion.14, s32[]{:T(128)S(6)} %select_n.261), kind=kOutput, calls=%fused_computation.20 | convolution fusion | flops 6445596672 | bytes 16252932 | tf_op jit(solution)/shard_map/dot_general | solution.py:141
  654.7 12.4 %convolution_convert_fusion.1 = bf16[768,4096]{1,0:T(8,128)(2,1)} fusion(bf16[1024,4096]{1,0:T(8,128)(2,1)} %all-gather.5.cloned.1.call-done, bf16[1536,1024]{0,1:T(8,128)(2,1)S(1)} %fusion.14, s32[]{:T(128)S(6)} %select_n.257), kind=kOutput, calls=%fused_computation.21 | convolution fusion | flops 6445596672 | bytes 16252932 | tf_op jit(solution)/shard_map/dot_general | solution.py:141
  667.1 4.6 reduce-scatter.5.cloned.1.call-done
  673.4 16.2 %reduce-scatter.3.cloned.1.call-done = bf16[768,2048]{1,0:T(8,128)(2,1)} async-done(((bf16[768,4096]{1,0:T(8,128)(2,1)}), bf16[768,2048]{1,0:T(8,128)(2,1)}) %reduce-scatter.3.cloned.1.call-update) | async-done | bytes 3145744 | tf_op jit(solution)/shard_map/reduce_scatter | solution.py:142
  689.7 52.7 %collective-permute-done.19 = bf16[768,2048]{1,0:T(8,128)(2,1)} collective-permute-done((bf16[768,2048]{1,0:T(8,128)(2,1)}, bf16[768,2048]{1,0:T(8,128)(2,1)}, u32[]{:S(2)}, u32[]{:S(2)}) %collective-permute-start.19) | collective-permute-done | bytes 3145760 | tf_op jit(solution)/shard_map/ppermute | solution.py:15
  742.3 6.6 add_convert_fusion
  (128 shorter events, 103.8 us)
Async XLA Ops:
  6.5 585.1 %copy-start = (bf16[128,128]{1,0:T(8,128)(2,1)S(1)}, bf16[128,128]{1,0:T(8,128)(2,1)}, u32[]{:S(2)}) copy-start(bf16[128,128]{1,0:T(8,128)(2,1)} %param.12) | copy-start | bytes 98308
  6.5 456.1 %all-gather.3.cloned.1.call-start = ((), (), s32[]{:S(2)}) async-start(), calls=%async_computation.2 | async-start | bytes 18874368 | tf_op jit(solution)/shard_map/all_gather | solution.py:75
  6.5 71.2 %collective-permute-start = (bf16[768,2048]{1,0:T(8,128)(2,1)}, bf16[768,2048]{1,0:T(8,128)(2,1)S(1)}, u32[]{:S(2)}, u32[]{:S(2)}) collective-permute-start(bf16[768,2048]{1,0:T(8,128)(2,1)} %param.8), channel_id=1, source_target_pairs={{0,2},{2,0},{1,3},{3,1},{4,6},{6,4},{5,7},{7,5},{8,10},{10,8},{9,1... | collective-permute-start | bytes 9437192 | tf_op jit(solution)/shard_map/ppermute | solution.py:15
  83.8 558.5 %all-gather.5.cloned.1.call-start = ((), (), s32[]{:S(2)}) async-start(), calls=%async_computation.3 | async-start | bytes 9437184 | tf_op jit(solution)/shard_map/all_gather | solution.py:117
  83.9 148.7 %copy-start.17 = (s32[8]{0:T(128)S(1)}, s32[8]{0:T(128)}, u32[]{:S(2)}) copy-start(s32[8]{0:T(128)} %constant.155.clone) | copy-start | bytes 100
  83.9 160.5 %copy-start.14 = (s32[8]{0:T(128)S(1)}, s32[8]{0:T(128)}, u32[]{:S(2)}) copy-start(s32[8]{0:T(128)} %constant.154.clone) | copy-start | bytes 100
  87.7 35.9 %collective-permute-start.1 = (bf16[256,3,1024]{0,2,1:T(8,128)(2,1)}, bf16[256,3,1024]{0,2,1:T(8,128)(2,1)}, u32[]{:S(2)}, u32[]{:S(2)}) collective-permute-start(bf16[256,3,1024]{0,2,1:T(8,128)(2,1)} %copy.56), channel_id=1, source_target_pairs={{0,2},{2,0},{1,3},{3,1},{4,6},{6,4},{5,7},{7,5},{8,10},{10,8},{9,1... | collective-permute-start | bytes 4718600 | tf_op jit(solution)/shard_map/ppermute | solution.py:15
  90.1 35.0 %collective-permute-start.2 = (bf16[256,3072]{0,1:T(8,128)(2,1)S(1)}, bf16[256,3072]{0,1:T(8,128)(2,1)S(1)}, u32[]{:S(2)}, u32[]{:S(2)}) collective-permute-start(bf16[256,3072]{0,1:T(8,128)(2,1)S(1)} %bitcast.80), channel_id=1, source_target_pairs={{0,8},{8,16},{16,24},{24,28},{28,20},{20,12},{12,4},{4,0},{1,9},{9... | collective-permute-start | bytes 4718600 | tf_op jit(solution)/shard_map/ppermute | solution.py:101
  123.6 34.9 %collective-permute-start.3 = (bf16[256,3072]{0,1:T(8,128)(2,1)}, bf16[256,3072]{0,1:T(8,128)(2,1)S(1)}, u32[]{:S(2)}, u32[]{:S(2)}) collective-permute-start(bf16[256,3072]{0,1:T(8,128)(2,1)} %bitcast.8), channel_id=1, source_target_pairs={{8,0},{16,8},{24,16},{28,24},{20,28},{12,20},{4,12},{0,4},{9,1},{1... | collective-permute-start | bytes 4718600 | tf_op jit(solution)/shard_map/ppermute | solution.py:102
  125.1 102.1 %copy-start.12 = (bf16[256,3072]{0,1:T(8,128)(2,1)}, bf16[256,3072]{0,1:T(8,128)(2,1)S(1)}, u32[]{:S(2)}) copy-start(bf16[256,3072]{0,1:T(8,128)(2,1)S(1)} %collective-permute-done.2) | copy-start | bytes 4718596
  125.1 34.6 %collective-permute-start.4 = (bf16[256,3072]{0,1:T(8,128)(2,1)S(1)}, bf16[256,3072]{0,1:T(8,128)(2,1)S(1)}, u32[]{:S(2)}, u32[]{:S(2)}) collective-permute-start(bf16[256,3072]{0,1:T(8,128)(2,1)S(1)} %collective-permute-done.2), channel_id=1, source_target_pairs={{0,8},{8,16},{16,24},{24,28},{28,20},{20,12},{12,4},{4,0},{1,9},{9... | collective-permute-start | bytes 4718600 | tf_op jit(solution)/shard_map/ppermute | solution.py:101
  158.4 68.9 %copy-start.11 = (bf16[256,3072]{0,1:T(8,128)(2,1)}, bf16[256,3072]{0,1:T(8,128)(2,1)S(1)}, u32[]{:S(2)}) copy-start(bf16[256,3072]{0,1:T(8,128)(2,1)S(1)} %collective-permute-done.3) | copy-start | bytes 4718596
  158.4 34.6 %collective-permute-start.5 = (bf16[256,3072]{0,1:T(8,128)(2,1)S(1)}, bf16[256,3072]{0,1:T(8,128)(2,1)S(1)}, u32[]{:S(2)}, u32[]{:S(2)}) collective-permute-start(bf16[256,3072]{0,1:T(8,128)(2,1)S(1)} %collective-permute-done.3), channel_id=1, source_target_pairs={{8,0},{16,8},{24,16},{28,24},{20,28},{12,20},{4,12},{0,4},{9,1},{1... | collective-permute-start | bytes 4718600 | tf_op jit(solution)/shard_map/ppermute | solution.py:102
  159.8 34.6 %collective-permute-start.6 = (bf16[256,3072]{0,1:T(8,128)(2,1)S(1)}, bf16[256,3072]{0,1:T(8,128)(2,1)S(1)}, u32[]{:S(2)}, u32[]{:S(2)}) collective-permute-start(bf16[256,3072]{0,1:T(8,128)(2,1)S(1)} %collective-permute-done.4), channel_id=1, source_target_pairs={{0,8},{8,16},{16,24},{24,28},{28,20},{20,12},{12,4},{4,0},{1,9},{9... | collective-permute-start | bytes 4718600 | tf_op jit(solution)/shard_map/ppermute | solution.py:101
  193.0 34.3 %collective-permute-start.7 = (bf16[256,3072]{0,1:T(8,128)(2,1)S(1)}, bf16[256,3072]{0,1:T(8,128)(2,1)}, u32[]{:S(2)}, u32[]{:S(2)}) collective-permute-start(bf16[256,3072]{0,1:T(8,128)(2,1)S(1)} %collective-permute-done.5), channel_id=1, source_target_pairs={{8,0},{16,8},{24,16},{28,24},{20,28},{12,20},{4,12},{0,4},{9,1},{1... | collective-permute-start | bytes 4718600 | tf_op jit(solution)/shard_map/ppermute | solution.py:102
  195.6 36.5 %collective-permute-start.8 = (bf16[256,3072]{0,1:T(8,128)(2,1)S(1)}, bf16[256,3072]{0,1:T(8,128)(2,1)}, u32[]{:S(2)}, u32[]{:S(2)}) collective-permute-start(bf16[256,3072]{0,1:T(8,128)(2,1)S(1)} %collective-permute-done.6), channel_id=1, source_target_pairs={{0,8},{8,16},{16,24},{24,28},{28,20},{20,12},{12,4},{4,0},{1,9},{9... | collective-permute-start | bytes 4718600 | tf_op jit(solution)/shard_map/ppermute | solution.py:101
  227.3 39.2 %collective-permute-start.9 = (bf16[256,3072]{0,1:T(8,128)(2,1)}, bf16[256,3072]{0,1:T(8,128)(2,1)}, u32[]{:S(2)}, u32[]{:S(2)}) collective-permute-start(bf16[256,3072]{0,1:T(8,128)(2,1)} %collective-permute-done.7), channel_id=1, source_target_pairs={{8,0},{16,8},{24,16},{28,24},{20,28},{12,20},{4,12},{0,4},{9,1},{1... | collective-permute-start | bytes 4718600 | tf_op jit(solution)/shard_map/ppermute | solution.py:102
  230.6 34.6 %collective-permute-start.18 = (bf16[1024,256]{1,0:T(8,128)(2,1)}, bf16[1024,256]{1,0:T(8,128)(2,1)}, u32[]{:S(2)}, u32[]{:S(2)}) collective-permute-start(bf16[1024,256]{1,0:T(8,128)(2,1)} %constant_dynamic-slice_fusion), channel_id=1, source_target_pairs={{0,2},{2,0},{1,3},{3,1},{4,6},{6,4},{5,7},{7,5},{8,10},{10,8},{9,1... | collective-permute-start | bytes 1572872 | tf_op jit(solution)/shard_map/ppermute | solution.py:15
  232.1 44.9 %collective-permute-start.10 = (bf16[256,3072]{0,1:T(8,128)(2,1)}, bf16[256,3072]{0,1:T(8,128)(2,1)}, u32[]{:S(2)}, u32[]{:S(2)}) collective-permute-start(bf16[256,3072]{0,1:T(8,128)(2,1)} %collective-permute-done.8), channel_id=1, source_target_pairs={{0,8},{8,16},{16,24},{24,28},{28,20},{20,12},{12,4},{4,0},{1,9},{9... | collective-permute-start | bytes 4718600 | tf_op jit(solution)/shard_map/ppermute | solution.py:101
  266.5 64.5 %collective-permute-start.11 = (bf16[256,3072]{0,1:T(8,128)(2,1)}, bf16[256,3072]{0,1:T(8,128)(2,1)}, u32[]{:S(2)}, u32[]{:S(2)}) collective-permute-start(bf16[256,3072]{0,1:T(8,128)(2,1)} %collective-permute-done.9), channel_id=1, source_target_pairs={{8,0},{16,8},{24,16},{28,24},{20,28},{12,20},{4,12},{0,4},{9,1},{1... | collective-permute-start | bytes 4718600 | tf_op jit(solution)/shard_map/ppermute | solution.py:102
  269.1 402.6 %reduce-scatter.5.cloned.1.call-start = ((), (), s32[]{:S(2)}) async-start(), calls=%async_computation.5 | async-start | bytes 9437184 | tf_op jit(solution)/shard_map/reduce_scatter | solution.py:142
  277.0 63.7 %collective-permute-start.12 = (bf16[256,3072]{0,1:T(8,128)(2,1)}, bf16[256,3072]{0,1:T(8,128)(2,1)}, u32[]{:S(2)}, u32[]{:S(2)}) collective-permute-start(bf16[256,3072]{0,1:T(8,128)(2,1)} %collective-permute-done.10), channel_id=1, source_target_pairs={{0,8},{8,16},{16,24},{24,28},{28,20},{20,12},{12,4},{4,0},{1,9},{9... | collective-permute-start | bytes 4718600 | tf_op jit(solution)/shard_map/ppermute | solution.py:101
  278.9 53.4 %copy-start.8 = (bf16[256,3072]{0,1:T(8,128)(2,1)S(1)}, bf16[256,3072]{0,1:T(8,128)(2,1)}, u32[]{:S(2)}) copy-start(bf16[256,3072]{0,1:T(8,128)(2,1)} %copy-done.7) | copy-start | bytes 4718596
  331.0 70.4 %collective-permute-start.13 = (bf16[256,3072]{0,1:T(8,128)(2,1)}, bf16[256,3072]{0,1:T(8,128)(2,1)}, u32[]{:S(2)}, u32[]{:S(2)}) collective-permute-start(bf16[256,3072]{0,1:T(8,128)(2,1)} %collective-permute-done.11), channel_id=1, source_target_pairs={{8,0},{16,8},{24,16},{28,24},{20,28},{12,20},{4,12},{0,4},{9,1},{1... | collective-permute-start | bytes 4718600 | tf_op jit(solution)/shard_map/ppermute | solution.py:102
  340.7 69.8 %collective-permute-start.14 = (bf16[256,3072]{0,1:T(8,128)(2,1)}, bf16[256,3072]{0,1:T(8,128)(2,1)}, u32[]{:S(2)}, u32[]{:S(2)}) collective-permute-start(bf16[256,3072]{0,1:T(8,128)(2,1)} %collective-permute-done.12), channel_id=1, source_target_pairs={{0,8},{8,16},{16,24},{24,28},{28,20},{20,12},{12,4},{4,0},{1,9},{9... | collective-permute-start | bytes 4718600 | tf_op jit(solution)/shard_map/ppermute | solution.py:101
  401.4 58.2 %collective-permute-start.15 = (bf16[256,3072]{0,1:T(8,128)(2,1)}, bf16[256,3072]{0,1:T(8,128)(2,1)}, u32[]{:S(2)}, u32[]{:S(2)}) collective-permute-start(bf16[256,3072]{0,1:T(8,128)(2,1)} %collective-permute-done.13), channel_id=1, source_target_pairs={{8,0},{16,8},{24,16},{28,24},{20,28},{12,20},{4,12},{0,4},{9,1},{1... | collective-permute-start | bytes 4718600 | tf_op jit(solution)/shard_map/ppermute | solution.py:102
  469.7 52.6 %copy-start.15 = (f32[3,3,2048]{2,1,0:T(4,128)S(1)}, f32[3,3,2048]{2,1,0:T(4,128)}, u32[]{:S(2)}) copy-start(f32[3,3,2048]{2,1,0:T(4,128)} %param.11) | copy-start | bytes 221188
  521.1 14.5 %collective-permute-start.16 = (bf16[2,3,1024]{2,1,0:T(4,128)(2,1)S(1)}, bf16[2,3,1024]{2,1,0:T(4,128)(2,1)S(1)}, u32[]{:S(2)}, u32[]{:S(2)}) collective-permute-start(bf16[2,3,1024]{2,1,0:T(4,128)(2,1)S(1)} %slice.49), channel_id=1, source_target_pairs={{0,4},{4,8},{8,12},{12,16},{16,20},{20,24},{24,28},{1,5},{5,9},{9,... | collective-permute-start | bytes 36872 | tf_op jit(solution)/shard_map/ppermute | solution.py:11
  584.1 19.6 %collective-permute-start.17 = (bf16[127,1024]{0,1:T(8,128)(2,1)}, bf16[127,1024]{0,1:T(8,128)(2,1)S(1)}, u32[]{:S(2)}, u32[]{:S(2)}) collective-permute-start(bf16[127,1024]{0,1:T(8,128)(2,1)} %slice_bitcast_fusion.1), channel_id=1, source_target_pairs={{0,4},{4,8},{8,12},{12,16},{16,20},{20,24},{24,28},{1,5},{5,9},{9,... | collective-permute-start | bytes 780296 | tf_op jit(solution)/shard_map/ppermute | solution.py:11
  654.7 35.0 %reduce-scatter.3.cloned.1.call-start = ((), (), s32[]{:S(2)}) async-start(), calls=%async_computation.4 | async-start | bytes 9437184 | tf_op jit(solution)/shard_map/reduce_scatter | solution.py:142
  667.1 75.2 %copy-start.4 = (bf16[768,2048]{1,0:T(8,128)(2,1)S(1)}, bf16[768,2048]{1,0:T(8,128)(2,1)}, u32[]{:S(2)}) copy-start(bf16[768,2048]{1,0:T(8,128)(2,1)} %param.8) | copy-start | bytes 9437188
  671.7 70.6 %collective-permute-start.19 = (bf16[768,2048]{1,0:T(8,128)(2,1)}, bf16[768,2048]{1,0:T(8,128)(2,1)}, u32[]{:S(2)}, u32[]{:S(2)}) collective-permute-start(bf16[768,2048]{1,0:T(8,128)(2,1)} %reduce-scatter.5.cloned.1.call-done), channel_id=1, source_target_pairs={{0,2},{2,0},{1,3},{3,1},{4,6},{6,4},{5,7},{7,5},{8,10},{10,8},{9,1... | collective-permute-start | bytes 9437192 | tf_op jit(solution)/shard_map/ppermute | solution.py:15
  (10 other events, 124.9 us)
Sparse Core Ops, SparseCore 0:
  83.9 26.3 all-gather.2
  269.3 196.6 all-gather.4
  654.8 16.9 reduce-scatter.4
  674.0 15.6 reduce-scatter.2

commit v7 on v6

--- a/solution.py
+++ b/solution.py
@@ -24,10 +24,7 @@
     table = long_filter.T
 
     def spread(hot):
-        dense = jnp.einsum(
-            "gm,mts->gts", table, hot.astype(table.dtype), preferred_element_type=jnp.float32
-        )
-        return dense.astype(table.dtype)
+        return jnp.einsum("gm,mts->gts", table, hot.astype(table.dtype))
 
     return (spread(offset == tap), spread(offset + filter_len == tap))
 
@@ -71,7 +68,7 @@
     other = 1 - half
     half_width = local_width // 2
 
-    pair_tokens = pair_ordered(tokens, swap_pair(tokens), half, 0)
+    pair_tokens = lax.all_gather(tokens, "lo", axis=0, tiled=True)
     pair_tokens = lax.all_gather(pair_tokens, "tp", axis=1, tiled=True)
     row_count = pair_tokens.shape[0]
     wide_float = pair_tokens.astype(jnp.float32)
@@ -89,32 +86,41 @@
     forward = [(order[i], order[(i + 1) % n_hi]) for i in range(n_hi)]
     backward = [(order[(i + 1) % n_hi], order[i]) for i in range(n_hi)]
 
+    e_cols = w_out.shape[1]
+    own_out = half_of(w_out, 0, half)
+    partner_out = swap_pair(half_of(w_out, 0, other))
+
     n_ctx = 2 * n_hi
     gathered_w = jnp.zeros((n_ctx, w_rows, 3 * half_width), jnp.bfloat16)
+    gathered_o = jnp.zeros((half_width, n_ctx, e_cols), jnp.bfloat16)
 
     def store(buffer, piece, ctx_index):
         return lax.dynamic_update_slice_in_dim(buffer, piece[None], ctx_index, axis=0)
+
+    def store_out(buffer, piece, ctx_index):
+        return lax.dynamic_update_slice_in_dim(buffer, piece[:, None], ctx_index, axis=1)
 
     current, previous = toeplitz_pair(half_of(long_filter, 1, half))
     for step in range(n_hi):
         if step > 0:
             own_piece = lax.ppermute(own_piece, "hi", forward)
             partner_piece = lax.ppermute(partner_piece, "hi", backward)
-        own_from = order_table[(here - step) % n_hi]
-        partner_from = order_table[(here + step) % n_hi]
-        gathered_w = store(gathered_w, own_piece, 2 * own_from + half)
-        gathered_w = store(gathered_w, partner_piece, 2 * partner_from + other)
+            own_out = lax.ppermute(own_out, "hi", forward)
+            partner_out = lax.ppermute(partner_out, "hi", backward)
+        own_at = 2 * order_table[(here - step) % n_hi] + half
+        partner_at = 2 * order_table[(here + step) % n_hi] + other
+        gathered_w = store(gathered_w, own_piece, own_at)
+        gathered_w = store(gathered_w, partner_piece, partner_at)
+        gathered_o = store_out(gathered_o, own_out, own_at)
+        gathered_o = store_out(gathered_o, partner_out, partner_at)
+    o_full = gathered_o.reshape(half_width, n_ctx * e_cols)
+
     projected = jnp.dot(
         normed,
         gathered_w.reshape(n_ctx * w_rows, 3 * half_width),
         preferred_element_type=jnp.float32,
     )
     projected = projected.astype(jnp.bfloat16).reshape(row_count, 3, half_width)
-
-    o_keep = half_of(w_out, 0, half)
-    o_recv = swap_pair(half_of(w_out, 0, other))
-    o_pair = pair_ordered(o_keep, o_recv, half, 1)
-    o_full = lax.all_gather(o_pair, "hi", axis=1, tiled=True)
 
     taps = half_of(short_filter, 2, half)
     prior_rows = shifted(projected[row_count - (short_taps - 1) :], "hi", 1)

time: 764 us -> 742 us (0.971)
  waiting for transfers between devices: 414 us -> 352 us
  local copies, waits for them, and re-layouts: 122 us -> 154 us
  starting transfers between devices: 33.5 us -> 47.1 us
  other arithmetic: 66.5 us -> 58.4 us
    ppermute x7, waiting for transfers between devices: 238 us -> 48 us  [local(): partner_piece = lax.ppermute(partner_piece, 'hi', backward)]
    ppermute x0 -> x14, waiting for transfers between devices: none -> 101 us  [the longest x7 72.2 us: local(): own_out = lax.ppermute(own_out, 'hi', forward)]
    ppermute x4 -> x3, waiting for transfers between devices: 153 us -> 52.7 us  [swap_pair(): return lax.ppermute(value, 'lo', [(0, 1), (1, 0)])]
    all_gather x1, waiting for transfers between devices: 0.02 us -> 99.9 us  [local(): pair_tokens = lax.all_gather(tokens, 'lo', axis=0, tiled=True)]
    ppermute x7, waiting for transfers between devices: 1.71 us -> 31.3 us  [local(): own_piece = lax.ppermute(own_piece, 'hi', forward)]
    dynamic_update_slice x0 -> x16, local copies, waits for them, and re-layouts: none -> 24.8 us  [store_out(): lax.dynamic_update_slice_in_dim(buffer, piece[:, None], ctx_index, axis=1)]
    ppermute x0 -> x14, starting transfers between devices: none -> 15.2 us  [the longest x7 10.5 us: local(): partner_out = lax.ppermute(partner_out, 'hi', backward)]
  transfers between devices with their start and end apart: 24 -> 37, of which waited for: 13 -> 21; matrix products, arithmetic and copies ran while one was open for 32% -> 31% of each run, Pallas kernels for 0% -> 0%
where the time goes in v7:
time: 742 us; the launch traced here: 732 us
  waiting for transfers between devices  352 us (47%)
  local copies, waits for them, and re-layouts  154 us (21%)
  matrix products  86 us (12%)
  other arithmetic  58.4 us (8%)
  starting transfers between devices  47.1 us (6%)
  between operations  34.6 us (5%)
    all_gather x1, waiting for transfers between devices, local(): pair_tokens = lax.all_gather(tokens, 'lo', axis=0, tiled=True)  99.9 us
    ppermute x7, waiting for transfers between devices, local(): own_out = lax.ppermute(own_out, 'hi', forward)  72.2 us
    ppermute x3, waiting for transfers between devices, swap_pair(): return lax.ppermute(value, 'lo', [(0, 1), (1, 0)])  52.7 us
    ppermute x7, waiting for transfers between devices, local(): partner_piece = lax.ppermute(partner_piece, 'hi', backward)  48 us
    dot_general x1, matrix products, local(): jnp.dot(normed, gathered_w.reshape(n_ctx * w_rows, 3 * half_width), prefe...  47.9 us
    ppermute x7, waiting for transfers between devices, local(): own_piece = lax.ppermute(own_piece, 'hi', forward)  31.3 us
    ppermute x7, waiting for transfers between devices, local(): partner_out = lax.ppermute(partner_out, 'hi', backward)  28.5 us
    dynamic_update_slice x16, local copies, waits for them, and re-layouts, store_out(): lax.dynamic_update_slice_in_dim(buffer, piece[:, None], ctx_index, axis=1)  24.8 us
  transfers between devices with their start and end apart: 37, of which 21 were waited for; matrix products, arithmetic and copies ran while one was open for 31% of the time, Pallas kernels for 0%

profile of v7, /device:TPU:0, one launch (start us, length us, event | category | flops | bytes accessed | tf_op | source)
XLA Modules:
  0.0 731.8 jit_solution(15343022460564055280)
XLA Ops:
  16.4 99.9 %all-gather.3.cloned.1.call-done = bf16[1536,2048]{1,0:T(8,128)(2,1)} async-done(((bf16[768,2048]{1,0:T(8,128)(2,1)}), bf16[1536,2048]{1,0:T(8,128)(2,1)}) %all-gather.3.cloned.1.call-update) | async-done | bytes 6291472 | tf_op jit(solution)/shard_map/all_gather | solution.py:71
  118.5 34.7 %collective-permute-done.2 = bf16[256,3072]{0,1:T(8,128)(2,1)} collective-permute-done((bf16[256,3072]{0,1:T(8,128)(2,1)}, bf16[256,3072]{0,1:T(8,128)(2,1)}, u32[]{:S(2)}, u32[]{:S(2)}) %collective-permute-start.2) | collective-permute-done | bytes 1572896 | tf_op jit(solution)/shard_map/ppermute | solution.py:107
  175.5 8.8 %broadcast_in_dim.101 = bf16[16,256,3072]{2,1,0:T(8,128)(2,1)} broadcast(bf16[]{:T(256)} %constant.131.clone.1), dimensions={} | broadcast | bytes 25165826 | tf_op jit(solution)/shard_map/broadcast_in_dim | solution.py:94
  195.0 6.7 collective-permute-done.18
  214.0 4.3 broadcast_in_dim.117
  222.1 13.2 %collective-permute-done.19 = bf16[1024,256]{0,1:T(8,128)(2,1)S(1)} collective-permute-done((bf16[1024,256]{0,1:T(8,128)(2,1)}, bf16[1024,256]{0,1:T(8,128)(2,1)S(1)}, u32[]{:S(2)}, u32[]{:S(2)}) %collective-permute-start.19) | collective-permute-done | bytes 524320 | tf_op jit(solution)/shard_map/ppermute | solution.py:109
  242.4 4.7 collective-permute-done.21
  263.8 29.8 %collective-permute-done.24 = bf16[1024,256]{0,1:T(8,128)(2,1)} collective-permute-done((bf16[1024,256]{0,1:T(8,128)(2,1)}, bf16[1024,256]{0,1:T(8,128)(2,1)}, u32[]{:S(2)}, u32[]{:S(2)}) %collective-permute-start.24) | collective-permute-done | bytes 524320 | tf_op jit(solution)/shard_map/ppermute | solution.py:108
  298.8 5.6 collective-permute-done.25
  320.7 29.9 %collective-permute-done.28 = bf16[1024,256]{0,1:T(8,128)(2,1)} collective-permute-done((bf16[1024,256]{0,1:T(8,128)(2,1)S(1)}, bf16[1024,256]{0,1:T(8,128)(2,1)}, u32[]{:S(2)}, u32[]{:S(2)}) %collective-permute-start.28) | collective-permute-done | bytes 524320 | tf_op jit(solution)/shard_map/ppermute | solution.py:108
  375.2 21.2 %collective-permute-done.11 = bf16[256,3072]{0,1:T(8,128)(2,1)} collective-permute-done((bf16[256,3072]{0,1:T(8,128)(2,1)}, bf16[256,3072]{0,1:T(8,128)(2,1)}, u32[]{:S(2)}, u32[]{:S(2)}) %collective-permute-start.11) | collective-permute-done | bytes 1572896 | tf_op jit(solution)/shard_map/ppermute | solution.py:106
  403.0 4.0 collective-permute-done.12
  417.4 10.2 %collective-permute-done.13 = bf16[256,3072]{0,1:T(8,128)(2,1)} collective-permute-done((bf16[256,3072]{0,1:T(8,128)(2,1)}, bf16[256,3072]{0,1:T(8,128)(2,1)}, u32[]{:S(2)}, u32[]{:S(2)}) %collective-permute-start.13) | collective-permute-done | bytes 1572896 | tf_op jit(solution)/shard_map/ppermute | solution.py:106
  431.9 5.7 collective-permute-done.14
  440.7 7.1 fusion
  447.8 47.9 %fusion.9 = bf16[1536,3072]{1,0:T(8,128)(2,1)S(1)} fusion(bf16[4096,3072]{1,0:T(8,128)(2,1)} %bitcast.35, bf16[1536,4096]{1,0:T(8,128)(2,1)} %all-gather.5.cloned.1.call-done, f32[4096]{0:T(1024)S(1)} %copy-done.11, f32[1536]{0:T(1024)S(1)} %add_rsqrt_fusion), kind=kOutput, calls=%fused_computation.13 | convolution fusion | flops 38684590080 | bytes 47208448 | tf_op jit(solution)/shard_map/dot_general | solution.py:118
  495.7 3.6 copy-done.6
  504.6 12.8 %copy.40 = bf16[1536,3072]{0,1:T(8,128)(2,1)} copy(bf16[1536,3072]{1,0:T(8,128)(2,1)} %copy-done.6) | data formatting | bytes 18874368 | tf_op jit(solution)/shard_map/convert_element_type | solution.py:123
  517.9 15.1 %maximum_convert_fusion = f32[1538,3,1024]{0,2,1:T(8,128)} fusion(bf16[1536,3,1024]{0,2,1:T(8,128)(2,1)} %bitcast.110, bf16[2,3,1024]{0,2,1:T(8,128)(2,1)S(1)} %copy.41), kind=kLoop, calls=%fused_computation.14 | loop fusion | flops 18898944 | bytes 28348416 | tf_op jit(solution)/shard_map/convert_element_type | solution.py:34
  533.0 22.1 %fusion.3 = f32[1536,3,1024]{0,2,1:T(8,128)S(1)} fusion(f32[1538,3,1024]{0,2,1:T(8,128)} %maximum_convert_fusion, f32[3,1024]{1,0:T(4,128)S(1)} %get-tuple-element.11, f32[3,1024]{1,0:T(4,128)S(1)} %get-tuple-element.10, f32[3,1024]{1,0:T(4,128)S(1)} %get-tuple-element.9), kind=kLoop, calls=%fused_computation.6 | loop fusion | flops 23592960 | bytes 75534336 | tf_op jit(solution)/shard_map/add | solution.py:38
  555.1 6.5 copy-done.2
  573.3 4.6 copy.45
  577.9 3.6 convert_element_type.51
  582.4 13.2 %concatenate.7 = bf16[1664,1024]{1,0:T(8,128)(2,1)S(1)} concatenate(bf16[1,1024]{1,0:T(2,128)(2,1)S(1)} %broadcast_in_dim.116, bf16[127,1024]{1,0:T(8,128)(2,1)} %copy.46, bf16[1536,1024]{1,0:T(8,128)(2,1)} %bitcast.112), dimensions={0} | concatenate | bytes 6815744 | tf_op jit(solution)/shard_map/concatenate | solution.py:132
  600.8 3.8 slice.61
  604.6 5.4 fusion.17
  615.4 4.8 fusion.14
  620.3 12.5 %convolution_convert_fusion = bf16[768,4096]{1,0:T(8,128)(2,1)} fusion(bf16[1024,4096]{0,1:T(8,128)(2,1)} %bitcast.62, bf16[1536,1024]{0,1:T(8,128)(2,1)S(1)} %fusion.14, s32[]{:T(128)S(6)} %select_n.247), kind=kOutput, calls=%fused_computation.20 | convolution fusion | flops 6445596672 | bytes 16252932 | tf_op jit(solution)/shard_map/dot_general | solution.py:147
  632.9 12.3 %convolution_convert_fusion.1 = bf16[768,4096]{1,0:T(8,128)(2,1)} fusion(bf16[1024,4096]{0,1:T(8,128)(2,1)} %bitcast.62, bf16[1536,1024]{0,1:T(8,128)(2,1)S(1)} %fusion.14, s32[]{:T(128)S(6)} %select_n.246), kind=kOutput, calls=%fused_computation.21 | convolution fusion | flops 6445596672 | bytes 16252932 | tf_op jit(solution)/shard_map/dot_general | solution.py:147
  649.3 16.2 %reduce-scatter.3.cloned.1.call-done = bf16[768,2048]{1,0:T(8,128)(2,1)} async-done(((bf16[768,4096]{1,0:T(8,128)(2,1)}), bf16[768,2048]{1,0:T(8,128)(2,1)}) %reduce-scatter.3.cloned.1.call-update) | async-done | bytes 3145744 | tf_op jit(solution)/shard_map/reduce_scatter | solution.py:148
  665.6 52.7 %collective-permute-done.32 = bf16[768,2048]{1,0:T(8,128)(2,1)} collective-permute-done((bf16[768,2048]{1,0:T(8,128)(2,1)}, bf16[768,2048]{1,0:T(8,128)(2,1)}, u32[]{:S(2)}, u32[]{:S(2)}) %collective-permute-start.32) | collective-permute-done | bytes 3145760 | tf_op jit(solution)/shard_map/ppermute | solution.py:15
  718.2 6.6 add_convert_fusion
  (159 shorter events, 167.8 us)
Async XLA Ops:
  6.5 109.8 %all-gather.3.cloned.1.call-start = ((), (), s32[]{:S(2)}) async-start(), calls=%async_computation.2 | async-start | bytes 9437184 | tf_op jit(solution)/shard_map/all_gather | solution.py:71
  7.3 433.4 %all-gather.5.cloned.1.call-start = ((), (), s32[]{:S(2)}) async-start(), calls=%async_computation.3 | async-start | bytes 18874368 | tf_op jit(solution)/shard_map/all_gather | solution.py:72
  11.1 105.3 %collective-permute-start = (bf16[256,3,1024]{0,2,1:T(8,128)(2,1)}, bf16[256,3,1024]{0,2,1:T(8,128)(2,1)}, u32[]{:S(2)}, u32[]{:S(2)}) collective-permute-start(bf16[256,3,1024]{0,2,1:T(8,128)(2,1)} %copy.60), channel_id=1, source_target_pairs={{0,2},{2,0},{1,3},{3,1},{4,6},{6,4},{5,7},{7,5},{8,10},{10,8},{9,1... | collective-permute-start | bytes 4718600 | tf_op jit(solution)/shard_map/ppermute | solution.py:15
  14.7 103.5 %collective-permute-start.1 = (bf16[256,3072]{0,1:T(8,128)(2,1)S(1)}, bf16[256,3072]{0,1:T(8,128)(2,1)S(1)}, u32[]{:S(2)}, u32[]{:S(2)}) collective-permute-start(bf16[256,3072]{0,1:T(8,128)(2,1)S(1)} %bitcast.113), channel_id=1, source_target_pairs={{0,8},{8,16},{16,24},{24,28},{28,20},{20,12},{12,4},{4,0},{1,9},{9... | collective-permute-start | bytes 4718600 | tf_op jit(solution)/shard_map/ppermute | solution.py:106
  116.3 531.3 %reduce-scatter.5.cloned.1.call-start = ((), (), s32[]{:S(2)}) async-start(), calls=%async_computation.5 | async-start | bytes 9437184 | tf_op jit(solution)/shard_map/reduce_scatter | solution.py:148
  116.4 36.8 %collective-permute-start.2 = (bf16[256,3072]{0,1:T(8,128)(2,1)}, bf16[256,3072]{0,1:T(8,128)(2,1)}, u32[]{:S(2)}, u32[]{:S(2)}) collective-permute-start(bf16[256,3072]{0,1:T(8,128)(2,1)} %bitcast.8), channel_id=1, source_target_pairs={{8,0},{16,8},{24,16},{28,24},{20,28},{12,20},{4,12},{0,4},{9,1},{1... | collective-permute-start | bytes 4718600 | tf_op jit(solution)/shard_map/ppermute | solution.py:107
  118.2 36.7 %collective-permute-start.3 = (bf16[256,3072]{0,1:T(8,128)(2,1)S(1)}, bf16[256,3072]{0,1:T(8,128)(2,1)}, u32[]{:S(2)}, u32[]{:S(2)}) collective-permute-start(bf16[256,3072]{0,1:T(8,128)(2,1)S(1)} %collective-permute-done.1), channel_id=1, source_target_pairs={{0,8},{8,16},{16,24},{24,28},{28,20},{20,12},{12,4},{4,0},{1,9},{9... | collective-permute-start | bytes 4718600 | tf_op jit(solution)/shard_map/ppermute | solution.py:106
  153.2 35.9 %collective-permute-start.4 = (bf16[256,3072]{0,1:T(8,128)(2,1)}, bf16[256,3072]{0,1:T(8,128)(2,1)}, u32[]{:S(2)}, u32[]{:S(2)}) collective-permute-start(bf16[256,3072]{0,1:T(8,128)(2,1)} %collective-permute-done.2), channel_id=1, source_target_pairs={{8,0},{16,8},{24,16},{28,24},{20,28},{12,20},{4,12},{0,4},{9,1},{1... | collective-permute-start | bytes 4718600 | tf_op jit(solution)/shard_map/ppermute | solution.py:107
  154.9 84.3 %collective-permute-start.5 = (bf16[256,3072]{0,1:T(8,128)(2,1)}, bf16[256,3072]{0,1:T(8,128)(2,1)}, u32[]{:S(2)}, u32[]{:S(2)}) collective-permute-start(bf16[256,3072]{0,1:T(8,128)(2,1)} %collective-permute-done.3), channel_id=1, source_target_pairs={{0,8},{8,16},{16,24},{24,28},{28,20},{20,12},{12,4},{4,0},{1,9},{9... | collective-permute-start | bytes 4718600 | tf_op jit(solution)/shard_map/ppermute | solution.py:106
  157.5 35.9 %collective-permute-start.17 = (bf16[1024,256]{0,1:T(8,128)(2,1)}, bf16[1024,256]{0,1:T(8,128)(2,1)}, u32[]{:S(2)}, u32[]{:S(2)}) collective-permute-start(bf16[1024,256]{0,1:T(8,128)(2,1)} %copy.63), channel_id=1, source_target_pairs={{0,2},{2,0},{1,3},{3,1},{4,6},{6,4},{5,7},{7,5},{8,10},{10,8},{9,1... | collective-permute-start | bytes 1572872 | tf_op jit(solution)/shard_map/ppermute | solution.py:15
  160.2 41.5 %collective-permute-start.18 = (bf16[1024,256]{0,1:T(8,128)(2,1)}, bf16[1024,256]{0,1:T(8,128)(2,1)}, u32[]{:S(2)}, u32[]{:S(2)}) collective-permute-start(bf16[1024,256]{0,1:T(8,128)(2,1)} %copy.62), channel_id=1, source_target_pairs={{0,8},{8,16},{16,24},{24,28},{28,20},{20,12},{12,4},{4,0},{1,9},{9... | collective-permute-start | bytes 1572872 | tf_op jit(solution)/shard_map/ppermute | solution.py:108
  189.1 63.1 %collective-permute-start.6 = (bf16[256,3072]{0,1:T(8,128)(2,1)}, bf16[256,3072]{0,1:T(8,128)(2,1)}, u32[]{:S(2)}, u32[]{:S(2)}) collective-permute-start(bf16[256,3072]{0,1:T(8,128)(2,1)} %collective-permute-done.4), channel_id=1, source_target_pairs={{8,0},{16,8},{24,16},{28,24},{20,28},{12,20},{4,12},{0,4},{9,1},{1... | collective-permute-start | bytes 4718600 | tf_op jit(solution)/shard_map/ppermute | solution.py:107
  193.4 41.8 %collective-permute-start.19 = (bf16[1024,256]{0,1:T(8,128)(2,1)}, bf16[1024,256]{0,1:T(8,128)(2,1)S(1)}, u32[]{:S(2)}, u32[]{:S(2)}) collective-permute-start(bf16[1024,256]{0,1:T(8,128)(2,1)} %collective-permute-done.17), channel_id=1, source_target_pairs={{8,0},{16,8},{24,16},{28,24},{20,28},{12,20},{4,12},{0,4},{9,1},{1... | collective-permute-start | bytes 1572872 | tf_op jit(solution)/shard_map/ppermute | solution.py:109
  201.7 35.1 %collective-permute-start.20 = (bf16[1024,256]{0,1:T(8,128)(2,1)}, bf16[1024,256]{0,1:T(8,128)(2,1)S(1)}, u32[]{:S(2)}, u32[]{:S(2)}) collective-permute-start(bf16[1024,256]{0,1:T(8,128)(2,1)} %collective-permute-done.18), channel_id=1, source_target_pairs={{0,8},{8,16},{16,24},{24,28},{28,20},{20,12},{12,4},{4,0},{1,9},{9... | collective-permute-start | bytes 1572872 | tf_op jit(solution)/shard_map/ppermute | solution.py:108
  239.2 56.2 %collective-permute-start.7 = (bf16[256,3072]{0,1:T(8,128)(2,1)}, bf16[256,3072]{0,1:T(8,128)(2,1)}, u32[]{:S(2)}, u32[]{:S(2)}) collective-permute-start(bf16[256,3072]{0,1:T(8,128)(2,1)} %collective-permute-done.5), channel_id=1, source_target_pairs={{0,8},{8,16},{16,24},{24,28},{28,20},{20,12},{12,4},{4,0},{1,9},{9... | collective-permute-start | bytes 4718600 | tf_op jit(solution)/shard_map/ppermute | solution.py:106
  251.7 41.9 %collective-permute-start.24 = (bf16[1024,256]{0,1:T(8,128)(2,1)}, bf16[1024,256]{0,1:T(8,128)(2,1)}, u32[]{:S(2)}, u32[]{:S(2)}) collective-permute-start(bf16[1024,256]{0,1:T(8,128)(2,1)} %collective-permute-done.22), channel_id=1, source_target_pairs={{0,8},{8,16},{16,24},{24,28},{28,20},{20,12},{12,4},{4,0},{1,9},{9... | collective-permute-start | bytes 1572872 | tf_op jit(solution)/shard_map/ppermute | solution.py:108
  252.3 58.8 %collective-permute-start.8 = (bf16[256,3072]{0,1:T(8,128)(2,1)}, bf16[256,3072]{0,1:T(8,128)(2,1)}, u32[]{:S(2)}, u32[]{:S(2)}) collective-permute-start(bf16[256,3072]{0,1:T(8,128)(2,1)} %collective-permute-done.6), channel_id=1, source_target_pairs={{8,0},{16,8},{24,16},{28,24},{20,28},{12,20},{4,12},{0,4},{9,1},{1... | collective-permute-start | bytes 4718600 | tf_op jit(solution)/shard_map/ppermute | solution.py:107
  262.3 42.1 %collective-permute-start.25 = (bf16[1024,256]{0,1:T(8,128)(2,1)}, bf16[1024,256]{0,1:T(8,128)(2,1)S(1)}, u32[]{:S(2)}, u32[]{:S(2)}) collective-permute-start(bf16[1024,256]{0,1:T(8,128)(2,1)} %collective-permute-done.23), channel_id=1, source_target_pairs={{8,0},{16,8},{24,16},{28,24},{20,28},{12,20},{4,12},{0,4},{9,1},{1... | collective-permute-start | bytes 1572872 | tf_op jit(solution)/shard_map/ppermute | solution.py:109
  295.4 57.9 %collective-permute-start.9 = (bf16[256,3072]{0,1:T(8,128)(2,1)}, bf16[256,3072]{0,1:T(8,128)(2,1)}, u32[]{:S(2)}, u32[]{:S(2)}) collective-permute-start(bf16[256,3072]{0,1:T(8,128)(2,1)} %collective-permute-done.7), channel_id=1, source_target_pairs={{0,8},{8,16},{16,24},{24,28},{28,20},{20,12},{12,4},{4,0},{1,9},{9... | collective-permute-start | bytes 4718600 | tf_op jit(solution)/shard_map/ppermute | solution.py:106
  308.6 42.0 %collective-permute-start.28 = (bf16[1024,256]{0,1:T(8,128)(2,1)S(1)}, bf16[1024,256]{0,1:T(8,128)(2,1)}, u32[]{:S(2)}, u32[]{:S(2)}) collective-permute-start(bf16[1024,256]{0,1:T(8,128)(2,1)S(1)} %collective-permute-done.26), channel_id=1, source_target_pairs={{0,8},{8,16},{16,24},{24,28},{28,20},{20,12},{12,4},{4,0},{1,9},{9... | collective-permute-start | bytes 1572872 | tf_op jit(solution)/shard_map/ppermute | solution.py:108
  311.1 53.3 %collective-permute-start.10 = (bf16[256,3072]{0,1:T(8,128)(2,1)}, bf16[256,3072]{0,1:T(8,128)(2,1)}, u32[]{:S(2)}, u32[]{:S(2)}) collective-permute-start(bf16[256,3072]{0,1:T(8,128)(2,1)} %collective-permute-done.8), channel_id=1, source_target_pairs={{8,0},{16,8},{24,16},{28,24},{20,28},{12,20},{4,12},{0,4},{9,1},{1... | collective-permute-start | bytes 4718600 | tf_op jit(solution)/shard_map/ppermute | solution.py:107
  319.2 42.0 %collective-permute-start.29 = (bf16[1024,256]{0,1:T(8,128)(2,1)S(1)}, bf16[1024,256]{0,1:T(8,128)(2,1)}, u32[]{:S(2)}, u32[]{:S(2)}) collective-permute-start(bf16[1024,256]{0,1:T(8,128)(2,1)S(1)} %collective-permute-done.27), channel_id=1, source_target_pairs={{8,0},{16,8},{24,16},{28,24},{20,28},{12,20},{4,12},{0,4},{9,1},{1... | collective-permute-start | bytes 1572872 | tf_op jit(solution)/shard_map/ppermute | solution.py:109
  350.6 218.9 %collective-permute-start.30 = (bf16[1024,256]{0,1:T(8,128)(2,1)}, bf16[1024,256]{0,1:T(8,128)(2,1)}, u32[]{:S(2)}, u32[]{:S(2)}) collective-permute-start(bf16[1024,256]{0,1:T(8,128)(2,1)} %collective-permute-done.28), channel_id=1, source_target_pairs={{0,8},{8,16},{16,24},{24,28},{28,20},{20,12},{12,4},{4,0},{1,9},{9... | collective-permute-start | bytes 1572872 | tf_op jit(solution)/shard_map/ppermute | solution.py:108
  353.3 43.1 %collective-permute-start.11 = (bf16[256,3072]{0,1:T(8,128)(2,1)}, bf16[256,3072]{0,1:T(8,128)(2,1)}, u32[]{:S(2)}, u32[]{:S(2)}) collective-permute-start(bf16[256,3072]{0,1:T(8,128)(2,1)} %collective-permute-done.9), channel_id=1, source_target_pairs={{0,8},{8,16},{16,24},{24,28},{28,20},{20,12},{12,4},{4,0},{1,9},{9... | collective-permute-start | bytes 4718600 | tf_op jit(solution)/shard_map/ppermute | solution.py:106
  361.2 210.2 %collective-permute-start.31 = (bf16[1024,256]{0,1:T(8,128)(2,1)}, bf16[1024,256]{0,1:T(8,128)(2,1)}, u32[]{:S(2)}, u32[]{:S(2)}) collective-permute-start(bf16[1024,256]{0,1:T(8,128)(2,1)} %collective-permute-done.29), channel_id=1, source_target_pairs={{8,0},{16,8},{24,16},{28,24},{20,28},{12,20},{4,12},{0,4},{9,1},{1... | collective-permute-start | bytes 1572872 | tf_op jit(solution)/shard_map/ppermute | solution.py:109
  364.4 42.6 %collective-permute-start.12 = (bf16[256,3072]{0,1:T(8,128)(2,1)}, bf16[256,3072]{0,1:T(8,128)(2,1)}, u32[]{:S(2)}, u32[]{:S(2)}) collective-permute-start(bf16[256,3072]{0,1:T(8,128)(2,1)} %collective-permute-done.10), channel_id=1, source_target_pairs={{8,0},{16,8},{24,16},{28,24},{20,28},{12,20},{4,12},{0,4},{9,1},{1... | collective-permute-start | bytes 4718600 | tf_op jit(solution)/shard_map/ppermute | solution.py:107
  396.4 31.1 %collective-permute-start.13 = (bf16[256,3072]{0,1:T(8,128)(2,1)}, bf16[256,3072]{0,1:T(8,128)(2,1)}, u32[]{:S(2)}, u32[]{:S(2)}) collective-permute-start(bf16[256,3072]{0,1:T(8,128)(2,1)} %collective-permute-done.11), channel_id=1, source_target_pairs={{0,8},{8,16},{16,24},{24,28},{28,20},{20,12},{12,4},{4,0},{1,9},{9... | collective-permute-start | bytes 4718600 | tf_op jit(solution)/shard_map/ppermute | solution.py:106
  407.0 30.7 %collective-permute-start.14 = (bf16[256,3072]{0,1:T(8,128)(2,1)}, bf16[256,3072]{0,1:T(8,128)(2,1)}, u32[]{:S(2)}, u32[]{:S(2)}) collective-permute-start(bf16[256,3072]{0,1:T(8,128)(2,1)} %collective-permute-done.12), channel_id=1, source_target_pairs={{8,0},{16,8},{24,16},{28,24},{20,28},{12,20},{4,12},{0,4},{9,1},{1... | collective-permute-start | bytes 4718600 | tf_op jit(solution)/shard_map/ppermute | solution.py:107
  499.3 18.1 %collective-permute-start.15 = (bf16[2,3,1024]{2,1,0:T(4,128)(2,1)S(1)}, bf16[2,3,1024]{2,1,0:T(4,128)(2,1)S(1)}, u32[]{:S(2)}, u32[]{:S(2)}) collective-permute-start(bf16[2,3,1024]{2,1,0:T(4,128)(2,1)S(1)} %slice.49), channel_id=1, source_target_pairs={{0,4},{4,8},{8,12},{12,16},{16,20},{20,24},{24,28},{1,5},{5,9},{9,... | collective-permute-start | bytes 36872 | tf_op jit(solution)/shard_map/ppermute | solution.py:11
  566.2 15.3 %collective-permute-start.16 = (bf16[127,1024]{0,1:T(8,128)(2,1)}, bf16[127,1024]{0,1:T(8,128)(2,1)S(1)}, u32[]{:S(2)}, u32[]{:S(2)}) collective-permute-start(bf16[127,1024]{0,1:T(8,128)(2,1)} %slice_bitcast_fusion.1), channel_id=1, source_target_pairs={{0,4},{4,8},{8,12},{12,16},{16,20},{20,24},{24,28},{1,5},{5,9},{9,... | collective-permute-start | bytes 780296 | tf_op jit(solution)/shard_map/ppermute | solution.py:11
  632.8 32.7 %reduce-scatter.3.cloned.1.call-start = ((), (), s32[]{:S(2)}) async-start(), calls=%async_computation.4 | async-start | bytes 9437184 | tf_op jit(solution)/shard_map/reduce_scatter | solution.py:148
  647.6 70.6 %collective-permute-start.32 = (bf16[768,2048]{1,0:T(8,128)(2,1)}, bf16[768,2048]{1,0:T(8,128)(2,1)}, u32[]{:S(2)}, u32[]{:S(2)}) collective-permute-start(bf16[768,2048]{1,0:T(8,128)(2,1)} %reduce-scatter.5.cloned.1.call-done), channel_id=1, source_target_pairs={{0,2},{2,0},{1,3},{3,1},{4,6},{6,4},{5,7},{7,5},{8,10},{10,8},{9,1... | collective-permute-start | bytes 9437192 | tf_op jit(solution)/shard_map/ppermute | solution.py:15
  (18 other events, 819.6 us)
Sparse Core Ops, SparseCore 0:
  8.9 107.3 all-gather.2
  117.9 26.3 all-gather.4
  632.9 14.6 reduce-scatter.4
  649.9 15.6 reduce-scatter.2

commit v8 on v7

--- a/solution.py
+++ b/solution.py
@@ -68,9 +68,10 @@
     other = 1 - half
     half_width = local_width // 2
 
-    pair_tokens = lax.all_gather(tokens, "lo", axis=0, tiled=True)
-    pair_tokens = lax.all_gather(pair_tokens, "tp", axis=1, tiled=True)
-    row_count = pair_tokens.shape[0]
+    pair_tokens = lax.all_gather(tokens, ("lo", "tp"), axis=0, tiled=False)
+    pair_tokens = pair_tokens.reshape(2, n_tp, own_rows, local_width).transpose(0, 2, 1, 3)
+    row_count = 2 * own_rows
+    pair_tokens = pair_tokens.reshape(row_count, model_width)
     wide_float = pair_tokens.astype(jnp.float32)
     scale = lax.rsqrt(jnp.mean(wide_float * wide_float, axis=-1, keepdims=True) + 1e-06)
     normed = (wide_float * scale * norm_gain).astype(jnp.bfloat16)

time: 742 us -> 774 us (1.043)
  other arithmetic: 58.4 us -> 122 us
  waiting for transfers between devices: 352 us -> 305 us
  local copies, waits for them, and re-layouts: 154 us -> 170 us
    all_gather x2 -> x1, waiting for transfers between devices: 99.9 us -> 0.01 us  [local(): pair_tokens = lax.all_gather(tokens, ('lo', 'tp'), axis=0, tiled=False)]
    convert_element_type x0 -> x2, other arithmetic: none -> 63.2 us  [the longest x1 48.8 us: local(): normed = (wide_float * scale * norm_gain).astype(jnp.bfloat16)]
    ppermute x3, waiting for transfers between devices: 52.7 us -> 111 us  [swap_pair(): return lax.ppermute(value, 'lo', [(0, 1), (1, 0)])]
    ppermute x7, waiting for transfers between devices: 31.3 us -> 22.3 us  [local(): own_piece = lax.ppermute(own_piece, 'hi', forward)]
    convert_element_type x1, local copies, waits for them, and re-layouts: 12.8 us -> 21.1 us  [local(): projected = projected.astype(jnp.bfloat16).reshape(row_count, 3, half_width)]
    unnamed x30 -> x37, local copies, waits for them, and re-layouts: 14.4 us -> 22.6 us
  transfers between devices with their start and end apart: 37 -> 36, of which waited for: 21 -> 21; matrix products, arithmetic and copies ran while one was open for 31% -> 40% of each run, Pallas kernels for 0% -> 0%
where the time goes in v8:
time: 774 us; the launch traced here: 763 us
  waiting for transfers between devices  305 us (39%)
  local copies, waits for them, and re-layouts  170 us (22%)
  other arithmetic  122 us (16%)
  matrix products  84.6 us (11%)
  starting transfers between devices  47.3 us (6%)
  between operations  34.1 us (4%)
    ppermute x3, waiting for transfers between devices, swap_pair(): return lax.ppermute(value, 'lo', [(0, 1), (1, 0)])  111 us
    ppermute x7, waiting for transfers between devices, local(): own_out = lax.ppermute(own_out, 'hi', forward)  66.5 us
    ppermute x7, waiting for transfers between devices, local(): partner_piece = lax.ppermute(partner_piece, 'hi', backward)  50 us
    convert_element_type x1, other arithmetic, local(): normed = (wide_float * scale * norm_gain).astype(jnp.bfloat16)  48.8 us
    dot_general x1, matrix products, local(): jnp.dot(normed, gathered_w.reshape(n_ctx * w_rows, 3 * half_width), prefe...  46.2 us
    ppermute x7, waiting for transfers between devices, local(): partner_out = lax.ppermute(partner_out, 'hi', backward)  35.3 us
    dot_general x2, matrix products, out_terms(): jnp.dot(rows, o_full, preferred_element_type=jnp.float32)  25 us
    dynamic_update_slice x16, local copies, waits for them, and re-layouts, store_out(): lax.dynamic_update_slice_in_dim(buffer, piece[:, None], ctx_index, axis=1)  24.8 us
  transfers between devices with their start and end apart: 36, of which 21 were waited for; matrix products, arithmetic and copies ran while one was open for 40% of the time, Pallas kernels for 0%

profile of v8, /device:TPU:0, one launch (start us, length us, event | category | flops | bytes accessed | tf_op | source)
XLA Modules:
  0.0 763.4 jit_solution(5275695154163535040)
XLA Ops:
  16.4 58.4 %collective-permute-done = bf16[256,3,1024]{0,2,1:T(8,128)(2,1)} collective-permute-done((bf16[256,3,1024]{0,2,1:T(8,128)(2,1)}, bf16[256,3,1024]{0,2,1:T(8,128)(2,1)}, u32[]{:S(2)}, u32[]{:S(2)}) %collective-permute-start) | collective-permute-done | bytes 1572896 | tf_op jit(solution)/shard_map/ppermute | solution.py:15
  76.8 32.5 %collective-permute-done.2 = bf16[256,3072]{0,1:T(8,128)(2,1)} collective-permute-done((bf16[256,3072]{0,1:T(8,128)(2,1)}, bf16[256,3072]{0,1:T(8,128)(2,1)}, u32[]{:S(2)}, u32[]{:S(2)}) %collective-permute-start.2) | collective-permute-done | bytes 1572896 | tf_op jit(solution)/shard_map/ppermute | solution.py:108
  132.0 8.7 %broadcast_in_dim.101 = bf16[16,256,3072]{2,1,0:T(8,128)(2,1)} broadcast(bf16[]{:T(256)} %constant.131.clone.1), dimensions={} | broadcast | bytes 25165826 | tf_op jit(solution)/shard_map/broadcast_in_dim | solution.py:95
  150.3 6.2 collective-permute-done.18
  168.8 4.3 broadcast_in_dim.117
  176.8 12.9 %collective-permute-done.19 = bf16[1024,256]{0,1:T(8,128)(2,1)S(1)} collective-permute-done((bf16[1024,256]{0,1:T(8,128)(2,1)}, bf16[1024,256]{0,1:T(8,128)(2,1)S(1)}, u32[]{:S(2)}, u32[]{:S(2)}) %collective-permute-start.19) | collective-permute-done | bytes 524320 | tf_op jit(solution)/shard_map/ppermute | solution.py:110
  196.8 6.2 collective-permute-done.21
  219.6 28.4 %collective-permute-done.24 = bf16[1024,256]{0,1:T(8,128)(2,1)} collective-permute-done((bf16[1024,256]{0,1:T(8,128)(2,1)}, bf16[1024,256]{0,1:T(8,128)(2,1)}, u32[]{:S(2)}, u32[]{:S(2)}) %collective-permute-start.24) | collective-permute-done | bytes 524320 | tf_op jit(solution)/shard_map/ppermute | solution.py:109
  253.2 6.9 collective-permute-done.25
  270.3 4.7 collective-permute-done.27
  276.4 28.6 %collective-permute-done.28 = bf16[1024,256]{0,1:T(8,128)(2,1)} collective-permute-done((bf16[1024,256]{0,1:T(8,128)(2,1)S(1)}, bf16[1024,256]{0,1:T(8,128)(2,1)}, u32[]{:S(2)}, u32[]{:S(2)}) %collective-permute-start.28) | collective-permute-done | bytes 524320 | tf_op jit(solution)/shard_map/ppermute | solution.py:109
  331.0 19.8 %collective-permute-done.11 = bf16[256,3072]{0,1:T(8,128)(2,1)} collective-permute-done((bf16[256,3072]{0,1:T(8,128)(2,1)}, bf16[256,3072]{0,1:T(8,128)(2,1)}, u32[]{:S(2)}, u32[]{:S(2)}) %collective-permute-start.11) | collective-permute-done | bytes 1572896 | tf_op jit(solution)/shard_map/ppermute | solution.py:107
  357.4 5.4 collective-permute-done.12
  379.8 10.3 %collective-permute-done.14 = bf16[256,3072]{0,1:T(8,128)(2,1)} collective-permute-done((bf16[256,3072]{0,1:T(8,128)(2,1)}, bf16[256,3072]{0,1:T(8,128)(2,1)}, u32[]{:S(2)}, u32[]{:S(2)}) %collective-permute-start.14) | collective-permute-done | bytes 1572896 | tf_op jit(solution)/shard_map/ppermute | solution.py:108
  393.0 14.4 %convert.1 = f32[2,2,768,2048]{3,2,1,0:T(8,128)} convert(bf16[2,2,768,2048]{3,2,1,0:T(8,128)(2,1)} %bitcast.117) | non-fusion elementwise | flops 6291456 | bytes 37748736 | tf_op jit(solution)/shard_map/convert_element_type | solution.py:75
  407.4 7.1 multiply_reduce_fusion
  414.5 48.8 %fusion.1 = bf16[2,2,768,2048]{3,1,2,0:T(2,128)(2,1)S(1)} fusion(f32[2,2,768,2048]{3,2,1,0:T(8,128)} %convert.1, f32[2,2048]{1,0:T(2,128)S(1)} %mul.181, f32[2,768]{1,0:T(2,128)S(1)} %add_rsqrt_fusion), kind=kLoop, calls=%fused_computation.2 | loop fusion | flops 18874368 | bytes 37771264 | tf_op jit(solution)/shard_map/convert_element_type | solution.py:77
  463.3 8.1 %copy.66 = bf16[192,8,2,2048]{3,1,2,0:T(8,128)(2,1)} copy(bf16[192,8,2,2048]{3,2,1,0:T(2,128)(2,1)S(1)} %bitcast.119) | data formatting | bytes 25165824
  471.5 46.2 %convolution_convert_fusion = bf16[1536,3072]{1,0:T(8,128)(2,1)S(1)} fusion(bf16[1536,4096]{1,0:T(8,128)(2,1)} %bitcast.122, bf16[4096,3072]{1,0:T(8,128)(2,1)} %bitcast.38), kind=kOutput, calls=%fused_computation.9 | convolution fusion | flops 38659424256 | bytes 47185920 | tf_op jit(solution)/shard_map/dot_general | solution.py:119
  526.6 21.1 %copy.42 = bf16[1536,3072]{0,1:T(8,128)(2,1)} copy(bf16[1536,3072]{1,0:T(8,128)(2,1)} %copy-done.6) | data formatting | bytes 18874368 | tf_op jit(solution)/shard_map/convert_element_type | solution.py:124
  548.2 15.1 %maximum_convert_fusion = f32[1538,3,1024]{0,2,1:T(8,128)} fusion(bf16[1536,3,1024]{0,2,1:T(8,128)(2,1)} %bitcast.120, bf16[2,3,1024]{0,2,1:T(8,128)(2,1)S(1)} %copy.43), kind=kLoop, calls=%fused_computation.10 | loop fusion | flops 18898944 | bytes 28348416 | tf_op jit(solution)/shard_map/convert_element_type | solution.py:34
  563.3 22.1 %fusion.2 = f32[1536,3,1024]{0,2,1:T(8,128)S(1)} fusion(f32[1538,3,1024]{0,2,1:T(8,128)} %maximum_convert_fusion, f32[3,1024]{1,0:T(4,128)S(1)} %copy-done.12, f32[3,1024]{1,0:T(4,128)S(1)} %copy-done.11, f32[3,1024]{1,0:T(4,128)S(1)} %copy-done.10), kind=kLoop, calls=%fused_computation.5 | loop fusion | flops 23592960 | bytes 75534336 | tf_op jit(solution)/shard_map/add | solution.py:38
  585.4 6.5 copy-done.2
  603.7 4.6 copy.47
  612.8 13.2 %concatenate.7 = bf16[1664,1024]{1,0:T(8,128)(2,1)S(1)} concatenate(bf16[1,1024]{1,0:T(2,128)(2,1)S(1)} %broadcast_in_dim.116, bf16[127,1024]{1,0:T(8,128)(2,1)} %copy.48, bf16[1536,1024]{1,0:T(8,128)(2,1)} %bitcast.123), dimensions={0} | concatenate | bytes 6815744 | tf_op jit(solution)/shard_map/concatenate | solution.py:133
  635.0 5.4 fusion.9
  645.9 4.8 fusion.6
  650.7 12.5 %convolution_convert_fusion.1 = bf16[768,4096]{1,0:T(8,128)(2,1)} fusion(bf16[1024,4096]{0,1:T(8,128)(2,1)} %bitcast.65, bf16[1536,1024]{0,1:T(8,128)(2,1)S(1)} %fusion.6, s32[]{:T(128)S(6)} %select_n.247), kind=kOutput, calls=%fused_computation.16 | convolution fusion | flops 6445596672 | bytes 16252932 | tf_op jit(solution)/shard_map/dot_general | solution.py:148
  663.3 12.5 %convolution_convert_fusion.2 = bf16[768,4096]{1,0:T(8,128)(2,1)} fusion(bf16[1024,4096]{0,1:T(8,128)(2,1)} %bitcast.65, bf16[1536,1024]{0,1:T(8,128)(2,1)S(1)} %fusion.6, s32[]{:T(128)S(6)} %select_n.246), kind=kOutput, calls=%fused_computation.17 | convolution fusion | flops 6445596672 | bytes 16252932 | tf_op jit(solution)/shard_map/dot_general | solution.py:148
  680.9 16.4 %reduce-scatter.3.cloned.1.call-done = bf16[768,2048]{1,0:T(8,128)(2,1)} async-done(((bf16[768,4096]{1,0:T(8,128)(2,1)}), bf16[768,2048]{1,0:T(8,128)(2,1)}) %reduce-scatter.3.cloned.1.call-update) | async-done | bytes 3145744 | tf_op jit(solution)/shard_map/reduce_scatter | solution.py:149
  697.3 52.5 %collective-permute-done.32 = bf16[768,2048]{1,0:T(8,128)(2,1)} collective-permute-done((bf16[768,2048]{1,0:T(8,128)(2,1)}, bf16[768,2048]{1,0:T(8,128)(2,1)}, u32[]{:S(2)}, u32[]{:S(2)}) %collective-permute-start.32) | collective-permute-done | bytes 3145760 | tf_op jit(solution)/shard_map/ppermute | solution.py:15
  749.8 6.6 add_convert_fusion
  (166 shorter events, 178.0 us)
Async XLA Ops:
  6.5 386.5 %all-gather.3.cloned.1.call-start = ((), (), s32[]{:S(2)}) async-start(), calls=%async_computation.4 | async-start | bytes 15728640 | tf_op jit(solution)/shard_map/all_gather | solution.py:71
  7.3 671.9 %reduce-scatter.5.cloned.1.call-start = ((), (), s32[]{:S(2)}) async-start(), calls=%async_computation.3 | async-start | bytes 9437184 | tf_op jit(solution)/shard_map/reduce_scatter | solution.py:149
  11.1 63.6 %collective-permute-start = (bf16[256,3,1024]{0,2,1:T(8,128)(2,1)}, bf16[256,3,1024]{0,2,1:T(8,128)(2,1)}, u32[]{:S(2)}, u32[]{:S(2)}) collective-permute-start(bf16[256,3,1024]{0,2,1:T(8,128)(2,1)} %copy.62), channel_id=1, source_target_pairs={{0,2},{2,0},{1,3},{3,1},{4,6},{6,4},{5,7},{7,5},{8,10},{10,8},{9,1... | collective-permute-start | bytes 4718600 | tf_op jit(solution)/shard_map/ppermute | solution.py:15
  14.7 61.4 %collective-permute-start.1 = (bf16[256,3072]{0,1:T(8,128)(2,1)S(1)}, bf16[256,3072]{0,1:T(8,128)(2,1)S(1)}, u32[]{:S(2)}, u32[]{:S(2)}) collective-permute-start(bf16[256,3072]{0,1:T(8,128)(2,1)S(1)} %bitcast.124), channel_id=1, source_target_pairs={{0,8},{8,16},{16,24},{24,28},{28,20},{20,12},{12,4},{4,0},{1,9},{9... | collective-permute-start | bytes 4718600 | tf_op jit(solution)/shard_map/ppermute | solution.py:107
  74.7 34.6 %collective-permute-start.2 = (bf16[256,3072]{0,1:T(8,128)(2,1)}, bf16[256,3072]{0,1:T(8,128)(2,1)}, u32[]{:S(2)}, u32[]{:S(2)}) collective-permute-start(bf16[256,3072]{0,1:T(8,128)(2,1)} %bitcast.11), channel_id=1, source_target_pairs={{8,0},{16,8},{24,16},{28,24},{20,28},{12,20},{4,12},{0,4},{9,1},{1... | collective-permute-start | bytes 4718600 | tf_op jit(solution)/shard_map/ppermute | solution.py:108
  76.1 34.6 %collective-permute-start.3 = (bf16[256,3072]{0,1:T(8,128)(2,1)S(1)}, bf16[256,3072]{0,1:T(8,128)(2,1)}, u32[]{:S(2)}, u32[]{:S(2)}) collective-permute-start(bf16[256,3072]{0,1:T(8,128)(2,1)S(1)} %collective-permute-done.1), channel_id=1, source_target_pairs={{0,8},{8,16},{16,24},{24,28},{28,20},{20,12},{12,4},{4,0},{1,9},{9... | collective-permute-start | bytes 4718600 | tf_op jit(solution)/shard_map/ppermute | solution.py:107
  109.3 34.6 %collective-permute-start.4 = (bf16[256,3072]{0,1:T(8,128)(2,1)}, bf16[256,3072]{0,1:T(8,128)(2,1)}, u32[]{:S(2)}, u32[]{:S(2)}) collective-permute-start(bf16[256,3072]{0,1:T(8,128)(2,1)} %collective-permute-done.2), channel_id=1, source_target_pairs={{8,0},{16,8},{24,16},{28,24},{20,28},{12,20},{4,12},{0,4},{9,1},{1... | collective-permute-start | bytes 4718600 | tf_op jit(solution)/shard_map/ppermute | solution.py:108
  110.7 83.0 %collective-permute-start.5 = (bf16[256,3072]{0,1:T(8,128)(2,1)}, bf16[256,3072]{0,1:T(8,128)(2,1)}, u32[]{:S(2)}, u32[]{:S(2)}) collective-permute-start(bf16[256,3072]{0,1:T(8,128)(2,1)} %collective-permute-done.3), channel_id=1, source_target_pairs={{0,8},{8,16},{16,24},{24,28},{28,20},{20,12},{12,4},{4,0},{1,9},{9... | collective-permute-start | bytes 4718600 | tf_op jit(solution)/shard_map/ppermute | solution.py:107
  113.6 35.0 %collective-permute-start.17 = (bf16[1024,256]{0,1:T(8,128)(2,1)}, bf16[1024,256]{0,1:T(8,128)(2,1)}, u32[]{:S(2)}, u32[]{:S(2)}) collective-permute-start(bf16[1024,256]{0,1:T(8,128)(2,1)} %copy.65), channel_id=1, source_target_pairs={{0,2},{2,0},{1,3},{3,1},{4,6},{6,4},{5,7},{7,5},{8,10},{10,8},{9,1... | collective-permute-start | bytes 1572872 | tf_op jit(solution)/shard_map/ppermute | solution.py:15
  117.1 39.4 %collective-permute-start.18 = (bf16[1024,256]{0,1:T(8,128)(2,1)}, bf16[1024,256]{0,1:T(8,128)(2,1)}, u32[]{:S(2)}, u32[]{:S(2)}) collective-permute-start(bf16[1024,256]{0,1:T(8,128)(2,1)} %copy.64), channel_id=1, source_target_pairs={{0,8},{8,16},{16,24},{24,28},{28,20},{20,12},{12,4},{4,0},{1,9},{9... | collective-permute-start | bytes 1572872 | tf_op jit(solution)/shard_map/ppermute | solution.py:109
  143.8 62.9 %collective-permute-start.6 = (bf16[256,3072]{0,1:T(8,128)(2,1)}, bf16[256,3072]{0,1:T(8,128)(2,1)}, u32[]{:S(2)}, u32[]{:S(2)}) collective-permute-start(bf16[256,3072]{0,1:T(8,128)(2,1)} %collective-permute-done.4), channel_id=1, source_target_pairs={{8,0},{16,8},{24,16},{28,24},{20,28},{12,20},{4,12},{0,4},{9,1},{1... | collective-permute-start | bytes 4718600 | tf_op jit(solution)/shard_map/ppermute | solution.py:108
  148.6 41.2 %collective-permute-start.19 = (bf16[1024,256]{0,1:T(8,128)(2,1)}, bf16[1024,256]{0,1:T(8,128)(2,1)S(1)}, u32[]{:S(2)}, u32[]{:S(2)}) collective-permute-start(bf16[1024,256]{0,1:T(8,128)(2,1)} %collective-permute-done.17), channel_id=1, source_target_pairs={{8,0},{16,8},{24,16},{28,24},{20,28},{12,20},{4,12},{0,4},{9,1},{1... | collective-permute-start | bytes 1572872 | tf_op jit(solution)/shard_map/ppermute | solution.py:110
  156.5 34.7 %collective-permute-start.20 = (bf16[1024,256]{0,1:T(8,128)(2,1)}, bf16[1024,256]{0,1:T(8,128)(2,1)S(1)}, u32[]{:S(2)}, u32[]{:S(2)}) collective-permute-start(bf16[1024,256]{0,1:T(8,128)(2,1)} %collective-permute-done.18), channel_id=1, source_target_pairs={{0,8},{8,16},{16,24},{24,28},{28,20},{20,12},{12,4},{4,0},{1,9},{9... | collective-permute-start | bytes 1572872 | tf_op jit(solution)/shard_map/ppermute | solution.py:109
  193.7 56.3 %collective-permute-start.7 = (bf16[256,3072]{0,1:T(8,128)(2,1)}, bf16[256,3072]{0,1:T(8,128)(2,1)}, u32[]{:S(2)}, u32[]{:S(2)}) collective-permute-start(bf16[256,3072]{0,1:T(8,128)(2,1)} %collective-permute-done.5), channel_id=1, source_target_pairs={{0,8},{8,16},{16,24},{24,28},{28,20},{20,12},{12,4},{4,0},{1,9},{9... | collective-permute-start | bytes 4718600 | tf_op jit(solution)/shard_map/ppermute | solution.py:107
  203.0 15.2 %collective-permute-start.23 = (bf16[1024,256]{0,1:T(8,128)(2,1)}, bf16[1024,256]{0,1:T(8,128)(2,1)}, u32[]{:S(2)}, u32[]{:S(2)}) collective-permute-start(bf16[1024,256]{0,1:T(8,128)(2,1)} %collective-permute-done.21), channel_id=1, source_target_pairs={{8,0},{16,8},{24,16},{28,24},{20,28},{12,20},{4,12},{0,4},{9,1},{1... | collective-permute-start | bytes 1572872 | tf_op jit(solution)/shard_map/ppermute | solution.py:110
  206.1 41.9 %collective-permute-start.24 = (bf16[1024,256]{0,1:T(8,128)(2,1)}, bf16[1024,256]{0,1:T(8,128)(2,1)}, u32[]{:S(2)}, u32[]{:S(2)}) collective-permute-start(bf16[1024,256]{0,1:T(8,128)(2,1)} %collective-permute-done.22), channel_id=1, source_target_pairs={{0,8},{8,16},{16,24},{24,28},{28,20},{20,12},{12,4},{4,0},{1,9},{9... | collective-permute-start | bytes 1572872 | tf_op jit(solution)/shard_map/ppermute | solution.py:109
  206.8 58.8 %collective-permute-start.8 = (bf16[256,3072]{0,1:T(8,128)(2,1)}, bf16[256,3072]{0,1:T(8,128)(2,1)}, u32[]{:S(2)}, u32[]{:S(2)}) collective-permute-start(bf16[256,3072]{0,1:T(8,128)(2,1)} %collective-permute-done.6), channel_id=1, source_target_pairs={{8,0},{16,8},{24,16},{28,24},{20,28},{12,20},{4,12},{0,4},{9,1},{1... | collective-permute-start | bytes 4718600 | tf_op jit(solution)/shard_map/ppermute | solution.py:108
  218.2 42.0 %collective-permute-start.25 = (bf16[1024,256]{0,1:T(8,128)(2,1)}, bf16[1024,256]{0,1:T(8,128)(2,1)S(1)}, u32[]{:S(2)}, u32[]{:S(2)}) collective-permute-start(bf16[1024,256]{0,1:T(8,128)(2,1)} %collective-permute-done.23), channel_id=1, source_target_pairs={{8,0},{16,8},{24,16},{28,24},{20,28},{12,20},{4,12},{0,4},{9,1},{1... | collective-permute-start | bytes 1572872 | tf_op jit(solution)/shard_map/ppermute | solution.py:110
  249.9 57.8 %collective-permute-start.9 = (bf16[256,3072]{0,1:T(8,128)(2,1)}, bf16[256,3072]{0,1:T(8,128)(2,1)}, u32[]{:S(2)}, u32[]{:S(2)}) collective-permute-start(bf16[256,3072]{0,1:T(8,128)(2,1)} %collective-permute-done.7), channel_id=1, source_target_pairs={{0,8},{8,16},{16,24},{24,28},{28,20},{20,12},{12,4},{4,0},{1,9},{9... | collective-permute-start | bytes 4718600 | tf_op jit(solution)/shard_map/ppermute | solution.py:107
  263.0 42.0 %collective-permute-start.28 = (bf16[1024,256]{0,1:T(8,128)(2,1)S(1)}, bf16[1024,256]{0,1:T(8,128)(2,1)}, u32[]{:S(2)}, u32[]{:S(2)}) collective-permute-start(bf16[1024,256]{0,1:T(8,128)(2,1)S(1)} %collective-permute-done.26), channel_id=1, source_target_pairs={{0,8},{8,16},{16,24},{24,28},{28,20},{20,12},{12,4},{4,0},{1,9},{9... | collective-permute-start | bytes 1572872 | tf_op jit(solution)/shard_map/ppermute | solution.py:109
  265.5 54.5 %collective-permute-start.10 = (bf16[256,3072]{0,1:T(8,128)(2,1)}, bf16[256,3072]{0,1:T(8,128)(2,1)}, u32[]{:S(2)}, u32[]{:S(2)}) collective-permute-start(bf16[256,3072]{0,1:T(8,128)(2,1)} %collective-permute-done.8), channel_id=1, source_target_pairs={{8,0},{16,8},{24,16},{28,24},{20,28},{12,20},{4,12},{0,4},{9,1},{1... | collective-permute-start | bytes 4718600 | tf_op jit(solution)/shard_map/ppermute | solution.py:108
  275.0 42.0 %collective-permute-start.29 = (bf16[1024,256]{0,1:T(8,128)(2,1)S(1)}, bf16[1024,256]{0,1:T(8,128)(2,1)}, u32[]{:S(2)}, u32[]{:S(2)}) collective-permute-start(bf16[1024,256]{0,1:T(8,128)(2,1)S(1)} %collective-permute-done.27), channel_id=1, source_target_pairs={{8,0},{16,8},{24,16},{28,24},{20,28},{12,20},{4,12},{0,4},{9,1},{1... | collective-permute-start | bytes 1572872 | tf_op jit(solution)/shard_map/ppermute | solution.py:110
  305.0 295.0 %collective-permute-start.30 = (bf16[1024,256]{0,1:T(8,128)(2,1)}, bf16[1024,256]{0,1:T(8,128)(2,1)}, u32[]{:S(2)}, u32[]{:S(2)}) collective-permute-start(bf16[1024,256]{0,1:T(8,128)(2,1)} %collective-permute-done.28), channel_id=1, source_target_pairs={{0,8},{8,16},{16,24},{24,28},{28,20},{20,12},{12,4},{4,0},{1,9},{9... | collective-permute-start | bytes 1572872 | tf_op jit(solution)/shard_map/ppermute | solution.py:109
  307.7 43.1 %collective-permute-start.11 = (bf16[256,3072]{0,1:T(8,128)(2,1)}, bf16[256,3072]{0,1:T(8,128)(2,1)}, u32[]{:S(2)}, u32[]{:S(2)}) collective-permute-start(bf16[256,3072]{0,1:T(8,128)(2,1)} %collective-permute-done.9), channel_id=1, source_target_pairs={{0,8},{8,16},{16,24},{24,28},{28,20},{20,12},{12,4},{4,0},{1,9},{9... | collective-permute-start | bytes 4718600 | tf_op jit(solution)/shard_map/ppermute | solution.py:107
  317.0 284.9 %collective-permute-start.31 = (bf16[1024,256]{0,1:T(8,128)(2,1)}, bf16[1024,256]{0,1:T(8,128)(2,1)}, u32[]{:S(2)}, u32[]{:S(2)}) collective-permute-start(bf16[1024,256]{0,1:T(8,128)(2,1)} %collective-permute-done.29), channel_id=1, source_target_pairs={{8,0},{16,8},{24,16},{28,24},{20,28},{12,20},{4,12},{0,4},{9,1},{1... | collective-permute-start | bytes 1572872 | tf_op jit(solution)/shard_map/ppermute | solution.py:110
  320.1 42.7 %collective-permute-start.12 = (bf16[256,3072]{0,1:T(8,128)(2,1)}, bf16[256,3072]{0,1:T(8,128)(2,1)}, u32[]{:S(2)}, u32[]{:S(2)}) collective-permute-start(bf16[256,3072]{0,1:T(8,128)(2,1)} %collective-permute-done.10), channel_id=1, source_target_pairs={{8,0},{16,8},{24,16},{28,24},{20,28},{12,20},{4,12},{0,4},{9,1},{1... | collective-permute-start | bytes 4718600 | tf_op jit(solution)/shard_map/ppermute | solution.py:108
  350.8 24.7 %collective-permute-start.13 = (bf16[256,3072]{0,1:T(8,128)(2,1)}, bf16[256,3072]{0,1:T(8,128)(2,1)}, u32[]{:S(2)}, u32[]{:S(2)}) collective-permute-start(bf16[256,3072]{0,1:T(8,128)(2,1)} %collective-permute-done.11), channel_id=1, source_target_pairs={{0,8},{8,16},{16,24},{24,28},{28,20},{20,12},{12,4},{4,0},{1,9},{9... | collective-permute-start | bytes 4718600 | tf_op jit(solution)/shard_map/ppermute | solution.py:107
  362.8 27.3 %collective-permute-start.14 = (bf16[256,3072]{0,1:T(8,128)(2,1)}, bf16[256,3072]{0,1:T(8,128)(2,1)}, u32[]{:S(2)}, u32[]{:S(2)}) collective-permute-start(bf16[256,3072]{0,1:T(8,128)(2,1)} %collective-permute-done.12), channel_id=1, source_target_pairs={{8,0},{16,8},{24,16},{28,24},{20,28},{12,20},{4,12},{0,4},{9,1},{1... | collective-permute-start | bytes 4718600 | tf_op jit(solution)/shard_map/ppermute | solution.py:108
  521.4 26.3 %collective-permute-start.15 = (bf16[2,3,1024]{2,1,0:T(4,128)(2,1)S(1)}, bf16[2,3,1024]{2,1,0:T(4,128)(2,1)S(1)}, u32[]{:S(2)}, u32[]{:S(2)}) collective-permute-start(bf16[2,3,1024]{2,1,0:T(4,128)(2,1)S(1)} %slice.49), channel_id=1, source_target_pairs={{0,4},{4,8},{8,12},{12,16},{16,20},{20,24},{24,28},{1,5},{5,9},{9,... | collective-permute-start | bytes 36872 | tf_op jit(solution)/shard_map/ppermute | solution.py:11
  596.5 15.4 %collective-permute-start.16 = (bf16[127,1024]{0,1:T(8,128)(2,1)}, bf16[127,1024]{0,1:T(8,128)(2,1)S(1)}, u32[]{:S(2)}, u32[]{:S(2)}) collective-permute-start(bf16[127,1024]{0,1:T(8,128)(2,1)} %slice_bitcast_fusion.1), channel_id=1, source_target_pairs={{0,4},{4,8},{8,12},{12,16},{16,20},{20,24},{24,28},{1,5},{5,9},{9,... | collective-permute-start | bytes 780296 | tf_op jit(solution)/shard_map/ppermute | solution.py:11
  663.2 34.1 %reduce-scatter.3.cloned.1.call-start = ((), (), s32[]{:S(2)}) async-start(), calls=%async_computation.2 | async-start | bytes 9437184 | tf_op jit(solution)/shard_map/reduce_scatter | solution.py:149
  679.2 70.6 %collective-permute-start.32 = (bf16[768,2048]{1,0:T(8,128)(2,1)}, bf16[768,2048]{1,0:T(8,128)(2,1)}, u32[]{:S(2)}, u32[]{:S(2)}) collective-permute-start(bf16[768,2048]{1,0:T(8,128)(2,1)} %reduce-scatter.5.cloned.1.call-done), channel_id=1, source_target_pairs={{0,2},{2,0},{1,3},{3,1},{4,6},{6,4},{5,7},{7,5},{8,10},{10,8},{9,1... | collective-permute-start | bytes 9437192 | tf_op jit(solution)/shard_map/ppermute | solution.py:15
  (20 other events, 741.4 us)
Sparse Core Ops, SparseCore 0:
  8.9 111.8 all-gather.2
  663.4 15.7 reduce-scatter.4
  681.6 15.6 reduce-scatter.2

commit v9 on v7

--- a/solution.py
+++ b/solution.py
@@ -68,7 +68,7 @@
     other = 1 - half
     half_width = local_width // 2
 
-    pair_tokens = lax.all_gather(tokens, "lo", axis=0, tiled=True)
+    pair_tokens = pair_ordered(tokens, swap_pair(tokens), half, 0)
     pair_tokens = lax.all_gather(pair_tokens, "tp", axis=1, tiled=True)
     row_count = pair_tokens.shape[0]
     wide_float = pair_tokens.astype(jnp.float32)

time: 742 us -> 734 us (0.989)
  waiting for transfers between devices: 352 us -> 337 us
    all_gather x1 -> x0, waiting for transfers between devices: 99.9 us -> none  [local(): pair_tokens = lax.all_gather(tokens, 'lo', axis=0, tiled=True)]
    ppermute x3 -> x4, waiting for transfers between devices: 52.7 us -> 137 us  [swap_pair(): return lax.ppermute(value, 'lo', [(0, 1), (1, 0)])]
    unnamed x30 -> x32, local copies, waits for them, and re-layouts: 14.4 us -> 17.4 us
  transfers between devices with their start and end apart: 37 -> 37, of which waited for: 21 -> 22; matrix products, arithmetic and copies ran while one was open for 31% -> 33% of each run, Pallas kernels for 0% -> 0%
where the time goes in v9:
time: 734 us; the launch traced here: 723 us
  waiting for transfers between devices  337 us (46%)
  local copies, waits for them, and re-layouts  158 us (22%)
  matrix products  86.1 us (12%)
  other arithmetic  64.4 us (9%)
  starting transfers between devices  43.2 us (6%)
  between operations  34.5 us (5%)
    ppermute x4, waiting for transfers between devices, swap_pair(): return lax.ppermute(value, 'lo', [(0, 1), (1, 0)])  137 us
    ppermute x7, waiting for transfers between devices, local(): own_out = lax.ppermute(own_out, 'hi', forward)  72.5 us
    ppermute x7, waiting for transfers between devices, local(): partner_piece = lax.ppermute(partner_piece, 'hi', backward)  48.3 us
    dot_general x1, matrix products, local(): jnp.dot(normed, gathered_w.reshape(n_ctx * w_rows, 3 * half_width), prefe...  47.9 us
    ppermute x7, waiting for transfers between devices, local(): partner_out = lax.ppermute(partner_out, 'hi', backward)  30.9 us
    ppermute x7, waiting for transfers between devices, local(): own_piece = lax.ppermute(own_piece, 'hi', forward)  29.4 us
    dynamic_update_slice x16, local copies, waits for them, and re-layouts, store_out(): lax.dynamic_update_slice_in_dim(buffer, piece[:, None], ctx_index, axis=1)  24.8 us
    dot_general x2, matrix products, out_terms(): jnp.dot(rows, o_full, preferred_element_type=jnp.float32)  24.8 us
  transfers between devices with their start and end apart: 37, of which 22 were waited for; matrix products, arithmetic and copies ran while one was open for 33% of the time, Pallas kernels for 0%

profile of v9, /device:TPU:0, one launch (start us, length us, event | category | flops | bytes accessed | tf_op | source)
XLA Modules:
  0.0 723.5 jit_solution(17629884091873634490)
XLA Ops:
  9.5 4.1 constant_dynamic-slice_fusion.2
  21.2 57.6 %collective-permute-done = bf16[768,2048]{1,0:T(8,128)(2,1)} collective-permute-done((bf16[768,2048]{1,0:T(8,128)(2,1)}, bf16[768,2048]{1,0:T(8,128)(2,1)}, u32[]{:S(2)}, u32[]{:S(2)}) %collective-permute-start) | collective-permute-done | bytes 3145760 | tf_op jit(solution)/shard_map/ppermute | solution.py:15
  84.8 26.8 %collective-permute-done.1 = bf16[256,3,1024]{0,2,1:T(8,128)(2,1)} collective-permute-done((bf16[256,3,1024]{0,2,1:T(8,128)(2,1)}, bf16[256,3,1024]{0,2,1:T(8,128)(2,1)}, u32[]{:S(2)}, u32[]{:S(2)}) %collective-permute-start.1) | collective-permute-done | bytes 1572896 | tf_op jit(solution)/shard_map/ppermute | solution.py:15
  113.7 33.9 %collective-permute-done.3 = bf16[256,3072]{0,1:T(8,128)(2,1)} collective-permute-done((bf16[256,3072]{0,1:T(8,128)(2,1)}, bf16[256,3072]{0,1:T(8,128)(2,1)}, u32[]{:S(2)}, u32[]{:S(2)}) %collective-permute-start.3) | collective-permute-done | bytes 1572896 | tf_op jit(solution)/shard_map/ppermute | solution.py:107
  169.6 8.8 %broadcast_in_dim.101 = bf16[16,256,3072]{2,1,0:T(8,128)(2,1)} broadcast(bf16[]{:T(256)} %constant.131.clone.1), dimensions={} | broadcast | bytes 25165826 | tf_op jit(solution)/shard_map/broadcast_in_dim | solution.py:94
  187.9 6.8 collective-permute-done.19
  207.4 4.3 broadcast_in_dim.117
  215.5 13.0 %collective-permute-done.20 = bf16[1024,256]{0,1:T(8,128)(2,1)S(1)} collective-permute-done((bf16[1024,256]{0,1:T(8,128)(2,1)}, bf16[1024,256]{0,1:T(8,128)(2,1)S(1)}, u32[]{:S(2)}, u32[]{:S(2)}) %collective-permute-start.20) | collective-permute-done | bytes 524320 | tf_op jit(solution)/shard_map/ppermute | solution.py:109
  235.3 5.1 collective-permute-done.22
  256.7 29.8 %collective-permute-done.25 = bf16[1024,256]{0,1:T(8,128)(2,1)} collective-permute-done((bf16[1024,256]{0,1:T(8,128)(2,1)}, bf16[1024,256]{0,1:T(8,128)(2,1)}, u32[]{:S(2)}, u32[]{:S(2)}) %collective-permute-start.25) | collective-permute-done | bytes 524320 | tf_op jit(solution)/shard_map/ppermute | solution.py:108
  291.3 6.3 collective-permute-done.26
  313.5 30.0 %collective-permute-done.29 = bf16[1024,256]{0,1:T(8,128)(2,1)} collective-permute-done((bf16[1024,256]{0,1:T(8,128)(2,1)S(1)}, bf16[1024,256]{0,1:T(8,128)(2,1)}, u32[]{:S(2)}, u32[]{:S(2)}) %collective-permute-start.29) | collective-permute-done | bytes 524320 | tf_op jit(solution)/shard_map/ppermute | solution.py:108
  367.8 21.5 %collective-permute-done.12 = bf16[256,3072]{0,1:T(8,128)(2,1)} collective-permute-done((bf16[256,3072]{0,1:T(8,128)(2,1)}, bf16[256,3072]{0,1:T(8,128)(2,1)}, u32[]{:S(2)}, u32[]{:S(2)}) %collective-permute-start.12) | collective-permute-done | bytes 1572896 | tf_op jit(solution)/shard_map/ppermute | solution.py:106
  396.3 4.0 collective-permute-done.13
  410.1 8.0 %collective-permute-done.14 = bf16[256,3072]{0,1:T(8,128)(2,1)} collective-permute-done((bf16[256,3072]{0,1:T(8,128)(2,1)}, bf16[256,3072]{0,1:T(8,128)(2,1)}, u32[]{:S(2)}, u32[]{:S(2)}) %collective-permute-start.14) | collective-permute-done | bytes 1572896 | tf_op jit(solution)/shard_map/ppermute | solution.py:106
  422.5 7.5 %collective-permute-done.15 = bf16[256,3072]{0,1:T(8,128)(2,1)} collective-permute-done((bf16[256,3072]{0,1:T(8,128)(2,1)}, bf16[256,3072]{0,1:T(8,128)(2,1)}, u32[]{:S(2)}, u32[]{:S(2)}) %collective-permute-start.15) | collective-permute-done | bytes 1572896 | tf_op jit(solution)/shard_map/ppermute | solution.py:107
  433.0 7.1 fusion
  440.1 47.9 %fusion.9 = bf16[1536,3072]{1,0:T(8,128)(2,1)S(1)} fusion(bf16[4096,3072]{1,0:T(8,128)(2,1)} %bitcast.35, bf16[1536,4096]{1,0:T(8,128)(2,1)} %all-gather.2.cloned.1.call-done, f32[4096]{0:T(1024)S(1)} %copy-done.12, f32[1536]{0:T(1024)S(1)} %add_rsqrt_fusion), kind=kOutput, calls=%fused_computation.13 | convolution fusion | flops 38684590080 | bytes 47208448 | tf_op jit(solution)/shard_map/dot_general | solution.py:118
  496.4 12.8 %copy.40 = bf16[1536,3072]{0,1:T(8,128)(2,1)} copy(bf16[1536,3072]{1,0:T(8,128)(2,1)} %copy-done.7) | data formatting | bytes 18874368 | tf_op jit(solution)/shard_map/convert_element_type | solution.py:123
  509.6 15.1 %maximum_convert_fusion = f32[1538,3,1024]{0,2,1:T(8,128)} fusion(bf16[1536,3,1024]{0,2,1:T(8,128)(2,1)} %bitcast.110, bf16[2,3,1024]{0,2,1:T(8,128)(2,1)S(1)} %copy.41), kind=kLoop, calls=%fused_computation.14 | loop fusion | flops 18898944 | bytes 28348416 | tf_op jit(solution)/shard_map/convert_element_type | solution.py:34
  524.7 22.1 %fusion.3 = f32[1536,3,1024]{0,2,1:T(8,128)S(1)} fusion(f32[1538,3,1024]{0,2,1:T(8,128)} %maximum_convert_fusion, f32[3,1024]{1,0:T(4,128)S(1)} %get-tuple-element.13, f32[3,1024]{1,0:T(4,128)S(1)} %get-tuple-element.12, f32[3,1024]{1,0:T(4,128)S(1)} %get-tuple-element.11), kind=kLoop, calls=%fused_computation.6 | loop fusion | flops 23592960 | bytes 75534336 | tf_op jit(solution)/shard_map/add | solution.py:38
  546.8 6.5 copy-done.2
  565.0 4.6 copy.45
  574.1 13.2 %concatenate.11 = bf16[1664,1024]{1,0:T(8,128)(2,1)S(1)} concatenate(bf16[1,1024]{1,0:T(2,128)(2,1)S(1)} %broadcast_in_dim.116, bf16[127,1024]{1,0:T(8,128)(2,1)} %copy.46, bf16[1536,1024]{1,0:T(8,128)(2,1)} %bitcast.112), dimensions={0} | concatenate | bytes 6815744 | tf_op jit(solution)/shard_map/concatenate | solution.py:132
  592.5 3.8 slice.61
  596.3 5.4 fusion.17
  607.2 4.8 fusion.14
  612.0 12.5 %convolution_convert_fusion = bf16[768,4096]{1,0:T(8,128)(2,1)} fusion(bf16[1024,4096]{0,1:T(8,128)(2,1)} %bitcast.62, bf16[1536,1024]{0,1:T(8,128)(2,1)S(1)} %fusion.14, s32[]{:T(128)S(6)} %select_n.262), kind=kOutput, calls=%fused_computation.20 | convolution fusion | flops 6445596672 | bytes 16252932 | tf_op jit(solution)/shard_map/dot_general | solution.py:147
  624.6 12.3 %convolution_convert_fusion.1 = bf16[768,4096]{1,0:T(8,128)(2,1)} fusion(bf16[1024,4096]{0,1:T(8,128)(2,1)} %bitcast.62, bf16[1536,1024]{0,1:T(8,128)(2,1)S(1)} %fusion.14, s32[]{:T(128)S(6)} %select_n.261), kind=kOutput, calls=%fused_computation.21 | convolution fusion | flops 6445596672 | bytes 16252932 | tf_op jit(solution)/shard_map/dot_general | solution.py:147
  641.0 16.4 %reduce-scatter.3.cloned.1.call-done = bf16[768,2048]{1,0:T(8,128)(2,1)} async-done(((bf16[768,4096]{1,0:T(8,128)(2,1)}), bf16[768,2048]{1,0:T(8,128)(2,1)}) %reduce-scatter.3.cloned.1.call-update) | async-done | bytes 3145744 | tf_op jit(solution)/shard_map/reduce_scatter | solution.py:148
  657.4 52.5 %collective-permute-done.33 = bf16[768,2048]{1,0:T(8,128)(2,1)} collective-permute-done((bf16[768,2048]{1,0:T(8,128)(2,1)}, bf16[768,2048]{1,0:T(8,128)(2,1)}, u32[]{:S(2)}, u32[]{:S(2)}) %collective-permute-start.33) | collective-permute-done | bytes 3145760 | tf_op jit(solution)/shard_map/ppermute | solution.py:15
  709.9 6.6 add_convert_fusion
  (162 shorter events, 178.0 us)
Async XLA Ops:
  6.5 426.5 %all-gather.2.cloned.1.call-start = ((), (), s32[]{:S(2)}) async-start(), calls=%async_computation.2 | async-start | bytes 18874368 | tf_op jit(solution)/shard_map/all_gather | solution.py:72
  6.5 72.2 %collective-permute-start = (bf16[768,2048]{1,0:T(8,128)(2,1)}, bf16[768,2048]{1,0:T(8,128)(2,1)}, u32[]{:S(2)}, u32[]{:S(2)}) collective-permute-start(bf16[768,2048]{1,0:T(8,128)(2,1)} %param.8), channel_id=1, source_target_pairs={{0,2},{2,0},{1,3},{3,1},{4,6},{6,4},{5,7},{7,5},{8,10},{10,8},{9,1... | collective-permute-start | bytes 9437192 | tf_op jit(solution)/shard_map/ppermute | solution.py:15
  16.2 95.4 %collective-permute-start.1 = (bf16[256,3,1024]{0,2,1:T(8,128)(2,1)}, bf16[256,3,1024]{0,2,1:T(8,128)(2,1)}, u32[]{:S(2)}, u32[]{:S(2)}) collective-permute-start(bf16[256,3,1024]{0,2,1:T(8,128)(2,1)} %copy.60), channel_id=1, source_target_pairs={{0,2},{2,0},{1,3},{3,1},{4,6},{6,4},{5,7},{7,5},{8,10},{10,8},{9,1... | collective-permute-start | bytes 4718600 | tf_op jit(solution)/shard_map/ppermute | solution.py:15
  18.9 94.4 %collective-permute-start.2 = (bf16[256,3072]{0,1:T(8,128)(2,1)}, bf16[256,3072]{0,1:T(8,128)(2,1)}, u32[]{:S(2)}, u32[]{:S(2)}) collective-permute-start(bf16[256,3072]{0,1:T(8,128)(2,1)} %bitcast.113), channel_id=1, source_target_pairs={{0,8},{8,16},{16,24},{24,28},{28,20},{20,12},{12,4},{4,0},{1,9},{9... | collective-permute-start | bytes 4718600 | tf_op jit(solution)/shard_map/ppermute | solution.py:106
  84.8 554.5 %reduce-scatter.5.cloned.1.call-start = ((), (), s32[]{:S(2)}) async-start(), calls=%async_computation.4 | async-start | bytes 9437184 | tf_op jit(solution)/shard_map/reduce_scatter | solution.py:148
  111.6 35.9 %collective-permute-start.3 = (bf16[256,3072]{0,1:T(8,128)(2,1)}, bf16[256,3072]{0,1:T(8,128)(2,1)}, u32[]{:S(2)}, u32[]{:S(2)}) collective-permute-start(bf16[256,3072]{0,1:T(8,128)(2,1)} %bitcast.8), channel_id=1, source_target_pairs={{8,0},{16,8},{24,16},{28,24},{20,28},{12,20},{4,12},{0,4},{9,1},{1... | collective-permute-start | bytes 4718600 | tf_op jit(solution)/shard_map/ppermute | solution.py:107
  113.4 35.6 %collective-permute-start.4 = (bf16[256,3072]{0,1:T(8,128)(2,1)}, bf16[256,3072]{0,1:T(8,128)(2,1)}, u32[]{:S(2)}, u32[]{:S(2)}) collective-permute-start(bf16[256,3072]{0,1:T(8,128)(2,1)} %collective-permute-done.2), channel_id=1, source_target_pairs={{0,8},{8,16},{16,24},{24,28},{28,20},{20,12},{12,4},{4,0},{1,9},{9... | collective-permute-start | bytes 4718600 | tf_op jit(solution)/shard_map/ppermute | solution.py:106
  147.5 35.0 %collective-permute-start.5 = (bf16[256,3072]{0,1:T(8,128)(2,1)}, bf16[256,3072]{0,1:T(8,128)(2,1)}, u32[]{:S(2)}, u32[]{:S(2)}) collective-permute-start(bf16[256,3072]{0,1:T(8,128)(2,1)} %collective-permute-done.3), channel_id=1, source_target_pairs={{8,0},{16,8},{24,16},{28,24},{20,28},{12,20},{4,12},{0,4},{9,1},{1... | collective-permute-start | bytes 4718600 | tf_op jit(solution)/shard_map/ppermute | solution.py:107
  149.0 83.5 %collective-permute-start.6 = (bf16[256,3072]{0,1:T(8,128)(2,1)}, bf16[256,3072]{0,1:T(8,128)(2,1)}, u32[]{:S(2)}, u32[]{:S(2)}) collective-permute-start(bf16[256,3072]{0,1:T(8,128)(2,1)} %collective-permute-done.4), channel_id=1, source_target_pairs={{0,8},{8,16},{16,24},{24,28},{28,20},{20,12},{12,4},{4,0},{1,9},{9... | collective-permute-start | bytes 4718600 | tf_op jit(solution)/shard_map/ppermute | solution.py:106
  151.8 34.5 %collective-permute-start.18 = (bf16[1024,256]{0,1:T(8,128)(2,1)}, bf16[1024,256]{0,1:T(8,128)(2,1)}, u32[]{:S(2)}, u32[]{:S(2)}) collective-permute-start(bf16[1024,256]{0,1:T(8,128)(2,1)} %copy.63), channel_id=1, source_target_pairs={{0,2},{2,0},{1,3},{3,1},{4,6},{6,4},{5,7},{7,5},{8,10},{10,8},{9,1... | collective-permute-start | bytes 1572872 | tf_op jit(solution)/shard_map/ppermute | solution.py:15
  154.2 40.5 %collective-permute-start.19 = (bf16[1024,256]{0,1:T(8,128)(2,1)}, bf16[1024,256]{0,1:T(8,128)(2,1)}, u32[]{:S(2)}, u32[]{:S(2)}) collective-permute-start(bf16[1024,256]{0,1:T(8,128)(2,1)} %copy.62), channel_id=1, source_target_pairs={{0,8},{8,16},{16,24},{24,28},{28,20},{20,12},{12,4},{4,0},{1,9},{9... | collective-permute-start | bytes 1572872 | tf_op jit(solution)/shard_map/ppermute | solution.py:108
  182.5 63.0 %collective-permute-start.7 = (bf16[256,3072]{0,1:T(8,128)(2,1)}, bf16[256,3072]{0,1:T(8,128)(2,1)}, u32[]{:S(2)}, u32[]{:S(2)}) collective-permute-start(bf16[256,3072]{0,1:T(8,128)(2,1)} %collective-permute-done.5), channel_id=1, source_target_pairs={{8,0},{16,8},{24,16},{28,24},{20,28},{12,20},{4,12},{0,4},{9,1},{1... | collective-permute-start | bytes 4718600 | tf_op jit(solution)/shard_map/ppermute | solution.py:107
  186.3 42.2 %collective-permute-start.20 = (bf16[1024,256]{0,1:T(8,128)(2,1)}, bf16[1024,256]{0,1:T(8,128)(2,1)S(1)}, u32[]{:S(2)}, u32[]{:S(2)}) collective-permute-start(bf16[1024,256]{0,1:T(8,128)(2,1)} %collective-permute-done.18), channel_id=1, source_target_pairs={{8,0},{16,8},{24,16},{28,24},{20,28},{12,20},{4,12},{0,4},{9,1},{1... | collective-permute-start | bytes 1572872 | tf_op jit(solution)/shard_map/ppermute | solution.py:109
  194.7 34.9 %collective-permute-start.21 = (bf16[1024,256]{0,1:T(8,128)(2,1)}, bf16[1024,256]{0,1:T(8,128)(2,1)S(1)}, u32[]{:S(2)}, u32[]{:S(2)}) collective-permute-start(bf16[1024,256]{0,1:T(8,128)(2,1)} %collective-permute-done.19), channel_id=1, source_target_pairs={{0,8},{8,16},{16,24},{24,28},{28,20},{20,12},{12,4},{4,0},{1,9},{9... | collective-permute-start | bytes 1572872 | tf_op jit(solution)/shard_map/ppermute | solution.py:108
  232.4 56.2 %collective-permute-start.8 = (bf16[256,3072]{0,1:T(8,128)(2,1)}, bf16[256,3072]{0,1:T(8,128)(2,1)}, u32[]{:S(2)}, u32[]{:S(2)}) collective-permute-start(bf16[256,3072]{0,1:T(8,128)(2,1)} %collective-permute-done.6), channel_id=1, source_target_pairs={{0,8},{8,16},{16,24},{24,28},{28,20},{20,12},{12,4},{4,0},{1,9},{9... | collective-permute-start | bytes 4718600 | tf_op jit(solution)/shard_map/ppermute | solution.py:106
  244.6 41.9 %collective-permute-start.25 = (bf16[1024,256]{0,1:T(8,128)(2,1)}, bf16[1024,256]{0,1:T(8,128)(2,1)}, u32[]{:S(2)}, u32[]{:S(2)}) collective-permute-start(bf16[1024,256]{0,1:T(8,128)(2,1)} %collective-permute-done.23), channel_id=1, source_target_pairs={{0,8},{8,16},{16,24},{24,28},{28,20},{20,12},{12,4},{4,0},{1,9},{9... | collective-permute-start | bytes 1572872 | tf_op jit(solution)/shard_map/ppermute | solution.py:108
  245.5 58.8 %collective-permute-start.9 = (bf16[256,3072]{0,1:T(8,128)(2,1)}, bf16[256,3072]{0,1:T(8,128)(2,1)}, u32[]{:S(2)}, u32[]{:S(2)}) collective-permute-start(bf16[256,3072]{0,1:T(8,128)(2,1)} %collective-permute-done.7), channel_id=1, source_target_pairs={{8,0},{16,8},{24,16},{28,24},{20,28},{12,20},{4,12},{0,4},{9,1},{1... | collective-permute-start | bytes 4718600 | tf_op jit(solution)/shard_map/ppermute | solution.py:107
  255.6 42.1 %collective-permute-start.26 = (bf16[1024,256]{0,1:T(8,128)(2,1)}, bf16[1024,256]{0,1:T(8,128)(2,1)S(1)}, u32[]{:S(2)}, u32[]{:S(2)}) collective-permute-start(bf16[1024,256]{0,1:T(8,128)(2,1)} %collective-permute-done.24), channel_id=1, source_target_pairs={{8,0},{16,8},{24,16},{28,24},{20,28},{12,20},{4,12},{0,4},{9,1},{1... | collective-permute-start | bytes 1572872 | tf_op jit(solution)/shard_map/ppermute | solution.py:109
  288.6 57.9 %collective-permute-start.10 = (bf16[256,3072]{0,1:T(8,128)(2,1)}, bf16[256,3072]{0,1:T(8,128)(2,1)}, u32[]{:S(2)}, u32[]{:S(2)}) collective-permute-start(bf16[256,3072]{0,1:T(8,128)(2,1)} %collective-permute-done.8), channel_id=1, source_target_pairs={{0,8},{8,16},{16,24},{24,28},{28,20},{20,12},{12,4},{4,0},{1,9},{9... | collective-permute-start | bytes 4718600 | tf_op jit(solution)/shard_map/ppermute | solution.py:106
  301.5 42.0 %collective-permute-start.29 = (bf16[1024,256]{0,1:T(8,128)(2,1)S(1)}, bf16[1024,256]{0,1:T(8,128)(2,1)}, u32[]{:S(2)}, u32[]{:S(2)}) collective-permute-start(bf16[1024,256]{0,1:T(8,128)(2,1)S(1)} %collective-permute-done.27), channel_id=1, source_target_pairs={{0,8},{8,16},{16,24},{24,28},{28,20},{20,12},{12,4},{4,0},{1,9},{9... | collective-permute-start | bytes 1572872 | tf_op jit(solution)/shard_map/ppermute | solution.py:108
  304.3 52.9 %collective-permute-start.11 = (bf16[256,3072]{0,1:T(8,128)(2,1)}, bf16[256,3072]{0,1:T(8,128)(2,1)}, u32[]{:S(2)}, u32[]{:S(2)}) collective-permute-start(bf16[256,3072]{0,1:T(8,128)(2,1)} %collective-permute-done.9), channel_id=1, source_target_pairs={{8,0},{16,8},{24,16},{28,24},{20,28},{12,20},{4,12},{0,4},{9,1},{1... | collective-permute-start | bytes 4718600 | tf_op jit(solution)/shard_map/ppermute | solution.py:107
  312.5 42.0 %collective-permute-start.30 = (bf16[1024,256]{0,1:T(8,128)(2,1)S(1)}, bf16[1024,256]{0,1:T(8,128)(2,1)}, u32[]{:S(2)}, u32[]{:S(2)}) collective-permute-start(bf16[1024,256]{0,1:T(8,128)(2,1)S(1)} %collective-permute-done.28), channel_id=1, source_target_pairs={{8,0},{16,8},{24,16},{28,24},{20,28},{12,20},{4,12},{0,4},{9,1},{1... | collective-permute-start | bytes 1572872 | tf_op jit(solution)/shard_map/ppermute | solution.py:109
  343.5 217.8 %collective-permute-start.31 = (bf16[1024,256]{0,1:T(8,128)(2,1)}, bf16[1024,256]{0,1:T(8,128)(2,1)}, u32[]{:S(2)}, u32[]{:S(2)}) collective-permute-start(bf16[1024,256]{0,1:T(8,128)(2,1)} %collective-permute-done.29), channel_id=1, source_target_pairs={{0,8},{8,16},{16,24},{24,28},{28,20},{20,12},{12,4},{4,0},{1,9},{9... | collective-permute-start | bytes 1572872 | tf_op jit(solution)/shard_map/ppermute | solution.py:108
  346.5 42.7 %collective-permute-start.12 = (bf16[256,3072]{0,1:T(8,128)(2,1)}, bf16[256,3072]{0,1:T(8,128)(2,1)}, u32[]{:S(2)}, u32[]{:S(2)}) collective-permute-start(bf16[256,3072]{0,1:T(8,128)(2,1)} %collective-permute-done.10), channel_id=1, source_target_pairs={{0,8},{8,16},{16,24},{24,28},{28,20},{20,12},{12,4},{4,0},{1,9},{9... | collective-permute-start | bytes 4718600 | tf_op jit(solution)/shard_map/ppermute | solution.py:106
  354.5 208.7 %collective-permute-start.32 = (bf16[1024,256]{0,1:T(8,128)(2,1)}, bf16[1024,256]{0,1:T(8,128)(2,1)}, u32[]{:S(2)}, u32[]{:S(2)}) collective-permute-start(bf16[1024,256]{0,1:T(8,128)(2,1)} %collective-permute-done.30), channel_id=1, source_target_pairs={{8,0},{16,8},{24,16},{28,24},{20,28},{12,20},{4,12},{0,4},{9,1},{1... | collective-permute-start | bytes 1572872 | tf_op jit(solution)/shard_map/ppermute | solution.py:109
  357.2 43.1 %collective-permute-start.13 = (bf16[256,3072]{0,1:T(8,128)(2,1)}, bf16[256,3072]{0,1:T(8,128)(2,1)}, u32[]{:S(2)}, u32[]{:S(2)}) collective-permute-start(bf16[256,3072]{0,1:T(8,128)(2,1)} %collective-permute-done.11), channel_id=1, source_target_pairs={{8,0},{16,8},{24,16},{28,24},{20,28},{12,20},{4,12},{0,4},{9,1},{1... | collective-permute-start | bytes 4718600 | tf_op jit(solution)/shard_map/ppermute | solution.py:107
  389.3 28.8 %collective-permute-start.14 = (bf16[256,3072]{0,1:T(8,128)(2,1)}, bf16[256,3072]{0,1:T(8,128)(2,1)}, u32[]{:S(2)}, u32[]{:S(2)}) collective-permute-start(bf16[256,3072]{0,1:T(8,128)(2,1)} %collective-permute-done.12), channel_id=1, source_target_pairs={{0,8},{8,16},{16,24},{24,28},{28,20},{20,12},{12,4},{4,0},{1,9},{9... | collective-permute-start | bytes 4718600 | tf_op jit(solution)/shard_map/ppermute | solution.py:106
  400.3 29.8 %collective-permute-start.15 = (bf16[256,3072]{0,1:T(8,128)(2,1)}, bf16[256,3072]{0,1:T(8,128)(2,1)}, u32[]{:S(2)}, u32[]{:S(2)}) collective-permute-start(bf16[256,3072]{0,1:T(8,128)(2,1)} %collective-permute-done.13), channel_id=1, source_target_pairs={{8,0},{16,8},{24,16},{28,24},{20,28},{12,20},{4,12},{0,4},{9,1},{1... | collective-permute-start | bytes 4718600 | tf_op jit(solution)/shard_map/ppermute | solution.py:107
  491.7 17.5 %collective-permute-start.16 = (bf16[2,3,1024]{2,1,0:T(4,128)(2,1)S(1)}, bf16[2,3,1024]{2,1,0:T(4,128)(2,1)S(1)}, u32[]{:S(2)}, u32[]{:S(2)}) collective-permute-start(bf16[2,3,1024]{2,1,0:T(4,128)(2,1)S(1)} %slice.49), channel_id=1, source_target_pairs={{0,4},{4,8},{8,12},{12,16},{16,20},{20,24},{24,28},{1,5},{5,9},{9,... | collective-permute-start | bytes 36872 | tf_op jit(solution)/shard_map/ppermute | solution.py:11
  557.9 15.3 %collective-permute-start.17 = (bf16[127,1024]{0,1:T(8,128)(2,1)}, bf16[127,1024]{0,1:T(8,128)(2,1)S(1)}, u32[]{:S(2)}, u32[]{:S(2)}) collective-permute-start(bf16[127,1024]{0,1:T(8,128)(2,1)} %slice_bitcast_fusion.1), channel_id=1, source_target_pairs={{0,4},{4,8},{8,12},{12,16},{16,20},{20,24},{24,28},{1,5},{5,9},{9,... | collective-permute-start | bytes 780296 | tf_op jit(solution)/shard_map/ppermute | solution.py:11
  624.5 32.9 %reduce-scatter.3.cloned.1.call-start = ((), (), s32[]{:S(2)}) async-start(), calls=%async_computation.3 | async-start | bytes 9437184 | tf_op jit(solution)/shard_map/reduce_scatter | solution.py:148
  639.3 70.6 %collective-permute-start.33 = (bf16[768,2048]{1,0:T(8,128)(2,1)}, bf16[768,2048]{1,0:T(8,128)(2,1)}, u32[]{:S(2)}, u32[]{:S(2)}) collective-permute-start(bf16[768,2048]{1,0:T(8,128)(2,1)} %reduce-scatter.5.cloned.1.call-done), channel_id=1, source_target_pairs={{0,2},{2,0},{1,3},{3,1},{4,6},{6,4},{5,7},{7,5},{8,10},{10,8},{9,1... | collective-permute-start | bytes 9437192 | tf_op jit(solution)/shard_map/ppermute | solution.py:15
  (19 other events, 768.4 us)
Sparse Core Ops, SparseCore 0:
  84.9 26.6 all-gather.1
  624.7 14.6 reduce-scatter.4
  641.7 15.6 reduce-scatter.2

commit v10 on v9

--- a/solution.py
+++ b/solution.py
@@ -132,23 +132,26 @@
     extended_mix = jnp.concatenate([zero_row, mixed_prior, mixed], axis=0)
     groups_here = long_filter.shape[1] // 2
     group_size = half_width // groups_here
-    mix_blocks = extended_mix.reshape(
-        row_count // filter_len + 1, filter_len, groups_here, group_size
-    )
-    filtered = jnp.einsum(
-        "gts,bsgc->btgc", current, mix_blocks[1:], preferred_element_type=jnp.float32
-    )
-    filtered = filtered + jnp.einsum(
-        "gts,bsgc->btgc", previous, mix_blocks[:-1], preferred_element_type=jnp.float32
-    )
-    gated = (query * filtered.reshape(row_count, half_width)).astype(jnp.bfloat16)
+    block_count = own_rows // filter_len
+
+    def gated_rows(part):
+        window = lax.dynamic_slice_in_dim(extended_mix, part * own_rows, own_rows + filter_len, 0)
+        mix_blocks = window.reshape(block_count + 1, filter_len, groups_here, group_size)
+        filtered = jnp.einsum(
+            "gts,bsgc->btgc", current, mix_blocks[1:], preferred_element_type=jnp.float32
+        )
+        filtered = filtered + jnp.einsum(
+            "gts,bsgc->btgc", previous, mix_blocks[:-1], preferred_element_type=jnp.float32
+        )
+        rows = lax.dynamic_slice_in_dim(query, part * own_rows, own_rows, 0)
+        return (rows * filtered.reshape(own_rows, half_width)).astype(jnp.bfloat16)
 
     def out_terms(rows):
         terms = jnp.dot(rows, o_full, preferred_element_type=jnp.float32).astype(jnp.bfloat16)
         return lax.psum_scatter(terms, "tp", scatter_dimension=1, tiled=True)
 
-    arrived = swap_pair(out_terms(half_of(gated, 0, other)))
-    summed = out_terms(half_of(gated, 0, half)).astype(jnp.float32) + arrived.astype(jnp.float32)
+    arrived = swap_pair(out_terms(gated_rows(other)))
+    summed = out_terms(gated_rows(half)).astype(jnp.float32) + arrived.astype(jnp.float32)
     return (tokens.astype(jnp.float32) + summed).astype(jnp.bfloat16)
 
 

time: 734 us -> 745 us (1.015)
  local copies, waits for them, and re-layouts: 158 us -> 177 us
  waiting for transfers between devices: 337 us -> 326 us
    slice x3 -> x9, local copies, waits for them, and re-layouts: 8.99 us -> 28.6 us  [the longest x5 17 us: gated_rows(): mix_blocks[:-1]]
    reshape x0 -> x2, local copies, waits for them, and re-layouts: none -> 7.92 us  [gated_rows(): return (rows * filtered.reshape(own_rows, half_width)).astype(jnp.bfloat16)]
    convert_element_type x2 -> x0, other arithmetic: 7.52 us -> none  [the longest x1 4.83 us: local(): (query * filtered.reshape(row_count, half_width)).astype(jnp.bfloat16)]
    unnamed x32 -> x30, local copies, waits for them, and re-layouts: 17.4 us -> 10.9 us
  transfers between devices with their start and end apart: 37 -> 37, of which waited for: 22 -> 21; matrix products, arithmetic and copies ran while one was open for 33% -> 36% of each run, Pallas kernels for 0% -> 0%
where the time goes in v10:
time: 745 us; the launch traced here: 735 us
  waiting for transfers between devices  326 us (44%)
  local copies, waits for them, and re-layouts  177 us (24%)
  matrix products  92.7 us (12%)
  other arithmetic  60.4 us (8%)
  starting transfers between devices  43.4 us (6%)
  between operations  34.3 us (5%)
    ppermute x4, waiting for transfers between devices, swap_pair(): return lax.ppermute(value, 'lo', [(0, 1), (1, 0)])  132 us
    ppermute x7, waiting for transfers between devices, local(): own_out = lax.ppermute(own_out, 'hi', forward)  72.5 us
    ppermute x7, waiting for transfers between devices, local(): partner_piece = lax.ppermute(partner_piece, 'hi', backward)  48.5 us
    dot_general x1, matrix products, local(): jnp.dot(normed, gathered_w.reshape(n_ctx * w_rows, 3 * half_width), prefe...  47.7 us
    ppermute x7, waiting for transfers between devices, local(): partner_out = lax.ppermute(partner_out, 'hi', backward)  30.4 us
    ppermute x7, waiting for transfers between devices, local(): own_piece = lax.ppermute(own_piece, 'hi', forward)  29.4 us
    dot_general x2, matrix products, out_terms(): jnp.dot(rows, o_full, preferred_element_type=jnp.float32)  25.7 us
    dynamic_update_slice x16, local copies, waits for them, and re-layouts, store_out(): lax.dynamic_update_slice_in_dim(buffer, piece[:, None], ctx_index, axis=1)  24.8 us
  transfers between devices with their start and end apart: 37, of which 21 were waited for; matrix products, arithmetic and copies ran while one was open for 36% of the time, Pallas kernels for 0%

profile of v10, /device:TPU:0, one launch (start us, length us, event | category | flops | bytes accessed | tf_op | source)
XLA Modules:
  0.0 734.6 jit_solution(9269260732303424881)
XLA Ops:
  9.5 4.3 constant_dynamic-slice_fusion.6
  21.1 57.6 %collective-permute-done = bf16[768,2048]{1,0:T(8,128)(2,1)} collective-permute-done((bf16[768,2048]{1,0:T(8,128)(2,1)}, bf16[768,2048]{1,0:T(8,128)(2,1)}, u32[]{:S(2)}, u32[]{:S(2)}) %collective-permute-start) | collective-permute-done | bytes 3145760 | tf_op jit(solution)/shard_map/ppermute | solution.py:15
  84.8 26.8 %collective-permute-done.1 = bf16[256,3,1024]{0,2,1:T(8,128)(2,1)} collective-permute-done((bf16[256,3,1024]{0,2,1:T(8,128)(2,1)}, bf16[256,3,1024]{0,2,1:T(8,128)(2,1)}, u32[]{:S(2)}, u32[]{:S(2)}) %collective-permute-start.1) | collective-permute-done | bytes 1572896 | tf_op jit(solution)/shard_map/ppermute | solution.py:15
  113.6 33.9 %collective-permute-done.3 = bf16[256,3072]{0,1:T(8,128)(2,1)} collective-permute-done((bf16[256,3072]{0,1:T(8,128)(2,1)}, bf16[256,3072]{0,1:T(8,128)(2,1)}, u32[]{:S(2)}, u32[]{:S(2)}) %collective-permute-start.3) | collective-permute-done | bytes 1572896 | tf_op jit(solution)/shard_map/ppermute | solution.py:107
  169.5 8.6 %broadcast_in_dim.101 = bf16[16,256,3072]{2,1,0:T(8,128)(2,1)} broadcast(bf16[]{:T(256)} %constant.134.clone.1), dimensions={} | broadcast | bytes 25165826 | tf_op jit(solution)/shard_map/broadcast_in_dim | solution.py:94
  187.9 6.8 collective-permute-done.19
  207.4 4.3 broadcast_in_dim.117
  215.5 13.0 %collective-permute-done.20 = bf16[1024,256]{0,1:T(8,128)(2,1)S(1)} collective-permute-done((bf16[1024,256]{0,1:T(8,128)(2,1)}, bf16[1024,256]{0,1:T(8,128)(2,1)S(1)}, u32[]{:S(2)}, u32[]{:S(2)}) %collective-permute-start.20) | collective-permute-done | bytes 524320 | tf_op jit(solution)/shard_map/ppermute | solution.py:109
  235.3 5.1 collective-permute-done.22
  256.7 29.8 %collective-permute-done.25 = bf16[1024,256]{0,1:T(8,128)(2,1)} collective-permute-done((bf16[1024,256]{0,1:T(8,128)(2,1)}, bf16[1024,256]{0,1:T(8,128)(2,1)}, u32[]{:S(2)}, u32[]{:S(2)}) %collective-permute-start.25) | collective-permute-done | bytes 524320 | tf_op jit(solution)/shard_map/ppermute | solution.py:108
  291.3 6.3 collective-permute-done.26
  313.5 30.0 %collective-permute-done.29 = bf16[1024,256]{0,1:T(8,128)(2,1)} collective-permute-done((bf16[1024,256]{0,1:T(8,128)(2,1)S(1)}, bf16[1024,256]{0,1:T(8,128)(2,1)}, u32[]{:S(2)}, u32[]{:S(2)}) %collective-permute-start.29) | collective-permute-done | bytes 524320 | tf_op jit(solution)/shard_map/ppermute | solution.py:108
  367.8 21.5 %collective-permute-done.12 = bf16[256,3072]{0,1:T(8,128)(2,1)} collective-permute-done((bf16[256,3072]{0,1:T(8,128)(2,1)}, bf16[256,3072]{0,1:T(8,128)(2,1)}, u32[]{:S(2)}, u32[]{:S(2)}) %collective-permute-start.12) | collective-permute-done | bytes 1572896 | tf_op jit(solution)/shard_map/ppermute | solution.py:106
  410.1 8.0 %collective-permute-done.14 = bf16[256,3072]{0,1:T(8,128)(2,1)} collective-permute-done((bf16[256,3072]{0,1:T(8,128)(2,1)}, bf16[256,3072]{0,1:T(8,128)(2,1)}, u32[]{:S(2)}, u32[]{:S(2)}) %collective-permute-start.14) | collective-permute-done | bytes 1572896 | tf_op jit(solution)/shard_map/ppermute | solution.py:106
  422.5 7.5 %collective-permute-done.15 = bf16[256,3072]{0,1:T(8,128)(2,1)} collective-permute-done((bf16[256,3072]{0,1:T(8,128)(2,1)}, bf16[256,3072]{0,1:T(8,128)(2,1)}, u32[]{:S(2)}, u32[]{:S(2)}) %collective-permute-start.15) | collective-permute-done | bytes 1572896 | tf_op jit(solution)/shard_map/ppermute | solution.py:107
  433.0 7.1 fusion
  440.1 47.7 %fusion.9 = bf16[1536,3072]{1,0:T(8,128)(2,1)S(1)} fusion(bf16[4096,3072]{1,0:T(8,128)(2,1)} %bitcast.35, bf16[1536,4096]{1,0:T(8,128)(2,1)} %all-gather.2.cloned.1.call-done, f32[4096]{0:T(1024)S(1)} %copy-done.11, f32[1536]{0:T(1024)S(1)} %add_rsqrt_fusion), kind=kOutput, calls=%fused_computation.13 | convolution fusion | flops 38684590080 | bytes 47208448 | tf_op jit(solution)/shard_map/dot_general | solution.py:118
  496.1 12.9 %copy.58 = bf16[1536,3072]{0,1:T(8,128)(2,1)} copy(bf16[1536,3072]{1,0:T(8,128)(2,1)} %copy-done.4) | data formatting | bytes 18874368 | tf_op jit(solution)/shard_map/convert_element_type | solution.py:123
  509.4 15.1 %maximum_convert_fusion = f32[1538,3,1024]{0,2,1:T(8,128)} fusion(bf16[1536,3,1024]{0,2,1:T(8,128)(2,1)} %bitcast.118, bf16[2,3,1024]{0,2,1:T(8,128)(2,1)S(1)} %copy.59), kind=kLoop, calls=%fused_computation.14 | loop fusion | flops 18898944 | bytes 28348416 | tf_op jit(solution)/shard_map/convert_element_type | solution.py:34
  524.6 22.2 %fusion.3 = f32[1536,3,1024]{0,2,1:T(8,128)S(1)} fusion(f32[1538,3,1024]{0,2,1:T(8,128)} %maximum_convert_fusion, f32[3,1024]{1,0:T(4,128)S(1)} %get-tuple-element.19, f32[3,1024]{1,0:T(4,128)S(1)} %get-tuple-element.18, f32[3,1024]{1,0:T(4,128)S(1)} %get-tuple-element.17), kind=kLoop, calls=%fused_computation.6 | loop fusion | flops 23592960 | bytes 75534336 | tf_op jit(solution)/shard_map/add | solution.py:38
  562.3 13.2 %concatenate.11 = bf16[1664,1024]{1,0:T(8,128)(2,1)S(1)} concatenate(bf16[1,1024]{1,0:T(2,128)(2,1)S(1)} %broadcast_in_dim.116, bf16[127,1024]{1,0:T(8,128)(2,1)} %copy.61, bf16[1536,1024]{1,0:T(8,128)(2,1)} %bitcast.119), dimensions={0} | concatenate | bytes 6815744 | tf_op jit(solution)/shard_map/concatenate | solution.py:132
  585.6 4.3 slice.83
  589.9 4.7 fusion.18
  600.4 4.8 reshape.82
  605.1 13.1 %convolution_convert_fusion = bf16[768,4096]{1,0:T(8,128)(2,1)} fusion(bf16[1024,4096]{0,1:T(8,128)(2,1)} %bitcast.62, f32[768,1,1024]{0,2,1:T(8,128)} %reshape.82, f32[1536,1,1024]{0,2,1:T(8,128)} %get-tuple-element.5, s32[]{:T(128)S(6)} %select_n.269), kind=kOutput, calls=%fused_computation.20 | convolution fusion | flops 6447169536 | bytes 20971524 | tf_op jit(solution)/shard_map/dot_general | solution.py:150
  621.0 4.3 slice.77
  628.0 4.4 slice.79
  632.4 4.7 fusion.20
  645.9 12.6 %convolution_convert_fusion.1 = bf16[768,4096]{1,0:T(8,128)(2,1)} fusion(bf16[1024,4096]{0,1:T(8,128)(2,1)} %bitcast.62, f32[768,1,1024]{0,2,1:T(8,128)S(1)} %reshape.80, f32[1536,1,1024]{0,2,1:T(8,128)} %get-tuple-element.5, s32[]{:T(128)S(6)} %select_n.266), kind=kOutput, calls=%fused_computation.21 | convolution fusion | flops 6447169536 | bytes 20971524 | tf_op jit(solution)/shard_map/dot_general | solution.py:150
  660.3 13.2 %reduce-scatter.3.cloned.1.call-done = bf16[768,2048]{1,0:T(8,128)(2,1)} async-done(((bf16[768,4096]{1,0:T(8,128)(2,1)}), bf16[768,2048]{1,0:T(8,128)(2,1)}) %reduce-scatter.3.cloned.1.call-update) | async-done | bytes 3145744 | tf_op jit(solution)/shard_map/reduce_scatter | solution.py:151
  673.4 47.8 %collective-permute-done.33 = bf16[768,2048]{1,0:T(8,128)(2,1)} collective-permute-done((bf16[768,2048]{1,0:T(8,128)(2,1)}, bf16[768,2048]{1,0:T(8,128)(2,1)}, u32[]{:S(2)}, u32[]{:S(2)}) %collective-permute-start.33) | collective-permute-done | bytes 3145760 | tf_op jit(solution)/shard_map/ppermute | solution.py:15
  721.2 6.6 add_convert_fusion
  (169 shorter events, 198.3 us)
Async XLA Ops:
  6.5 426.5 %all-gather.2.cloned.1.call-start = ((), (), s32[]{:S(2)}) async-start(), calls=%async_computation.2 | async-start | bytes 18874368 | tf_op jit(solution)/shard_map/all_gather | solution.py:72
  6.5 72.2 %collective-permute-start = (bf16[768,2048]{1,0:T(8,128)(2,1)}, bf16[768,2048]{1,0:T(8,128)(2,1)}, u32[]{:S(2)}, u32[]{:S(2)}) collective-permute-start(bf16[768,2048]{1,0:T(8,128)(2,1)} %param.8), channel_id=1, source_target_pairs={{0,2},{2,0},{1,3},{3,1},{4,6},{6,4},{5,7},{7,5},{8,10},{10,8},{9,1... | collective-permute-start | bytes 9437192 | tf_op jit(solution)/shard_map/ppermute | solution.py:15
  16.4 95.2 %collective-permute-start.1 = (bf16[256,3,1024]{0,2,1:T(8,128)(2,1)}, bf16[256,3,1024]{0,2,1:T(8,128)(2,1)}, u32[]{:S(2)}, u32[]{:S(2)}) collective-permute-start(bf16[256,3,1024]{0,2,1:T(8,128)(2,1)} %copy.94), channel_id=1, source_target_pairs={{0,2},{2,0},{1,3},{3,1},{4,6},{6,4},{5,7},{7,5},{8,10},{10,8},{9,1... | collective-permute-start | bytes 4718600 | tf_op jit(solution)/shard_map/ppermute | solution.py:15
  19.0 94.4 %collective-permute-start.2 = (bf16[256,3072]{0,1:T(8,128)(2,1)}, bf16[256,3072]{0,1:T(8,128)(2,1)}, u32[]{:S(2)}, u32[]{:S(2)}) collective-permute-start(bf16[256,3072]{0,1:T(8,128)(2,1)} %bitcast.120), channel_id=1, source_target_pairs={{0,8},{8,16},{16,24},{24,28},{28,20},{20,12},{12,4},{4,0},{1,9},{9... | collective-permute-start | bytes 4718600 | tf_op jit(solution)/shard_map/ppermute | solution.py:106
  84.8 573.8 %reduce-scatter.5.cloned.1.call-start = ((), (), s32[]{:S(2)}) async-start(), calls=%async_computation.4 | async-start | bytes 9437184 | tf_op jit(solution)/shard_map/reduce_scatter | solution.py:151
  111.6 35.9 %collective-permute-start.3 = (bf16[256,3072]{0,1:T(8,128)(2,1)}, bf16[256,3072]{0,1:T(8,128)(2,1)}, u32[]{:S(2)}, u32[]{:S(2)}) collective-permute-start(bf16[256,3072]{0,1:T(8,128)(2,1)} %bitcast.8), channel_id=1, source_target_pairs={{8,0},{16,8},{24,16},{28,24},{20,28},{12,20},{4,12},{0,4},{9,1},{1... | collective-permute-start | bytes 4718600 | tf_op jit(solution)/shard_map/ppermute | solution.py:107
  113.4 35.6 %collective-permute-start.4 = (bf16[256,3072]{0,1:T(8,128)(2,1)}, bf16[256,3072]{0,1:T(8,128)(2,1)}, u32[]{:S(2)}, u32[]{:S(2)}) collective-permute-start(bf16[256,3072]{0,1:T(8,128)(2,1)} %collective-permute-done.2), channel_id=1, source_target_pairs={{0,8},{8,16},{16,24},{24,28},{28,20},{20,12},{12,4},{4,0},{1,9},{9... | collective-permute-start | bytes 4718600 | tf_op jit(solution)/shard_map/ppermute | solution.py:106
  147.5 35.0 %collective-permute-start.5 = (bf16[256,3072]{0,1:T(8,128)(2,1)}, bf16[256,3072]{0,1:T(8,128)(2,1)}, u32[]{:S(2)}, u32[]{:S(2)}) collective-permute-start(bf16[256,3072]{0,1:T(8,128)(2,1)} %collective-permute-done.3), channel_id=1, source_target_pairs={{8,0},{16,8},{24,16},{28,24},{20,28},{12,20},{4,12},{0,4},{9,1},{1... | collective-permute-start | bytes 4718600 | tf_op jit(solution)/shard_map/ppermute | solution.py:107
  149.0 83.4 %collective-permute-start.6 = (bf16[256,3072]{0,1:T(8,128)(2,1)}, bf16[256,3072]{0,1:T(8,128)(2,1)}, u32[]{:S(2)}, u32[]{:S(2)}) collective-permute-start(bf16[256,3072]{0,1:T(8,128)(2,1)} %collective-permute-done.4), channel_id=1, source_target_pairs={{0,8},{8,16},{16,24},{24,28},{28,20},{20,12},{12,4},{4,0},{1,9},{9... | collective-permute-start | bytes 4718600 | tf_op jit(solution)/shard_map/ppermute | solution.py:106
  151.8 34.5 %collective-permute-start.18 = (bf16[1024,256]{0,1:T(8,128)(2,1)}, bf16[1024,256]{0,1:T(8,128)(2,1)}, u32[]{:S(2)}, u32[]{:S(2)}) collective-permute-start(bf16[1024,256]{0,1:T(8,128)(2,1)} %copy.97), channel_id=1, source_target_pairs={{0,2},{2,0},{1,3},{3,1},{4,6},{6,4},{5,7},{7,5},{8,10},{10,8},{9,1... | collective-permute-start | bytes 1572872 | tf_op jit(solution)/shard_map/ppermute | solution.py:15
  154.2 40.5 %collective-permute-start.19 = (bf16[1024,256]{0,1:T(8,128)(2,1)}, bf16[1024,256]{0,1:T(8,128)(2,1)}, u32[]{:S(2)}, u32[]{:S(2)}) collective-permute-start(bf16[1024,256]{0,1:T(8,128)(2,1)} %copy.96), channel_id=1, source_target_pairs={{0,8},{8,16},{16,24},{24,28},{28,20},{20,12},{12,4},{4,0},{1,9},{9... | collective-permute-start | bytes 1572872 | tf_op jit(solution)/shard_map/ppermute | solution.py:108
  182.5 63.0 %collective-permute-start.7 = (bf16[256,3072]{0,1:T(8,128)(2,1)}, bf16[256,3072]{0,1:T(8,128)(2,1)}, u32[]{:S(2)}, u32[]{:S(2)}) collective-permute-start(bf16[256,3072]{0,1:T(8,128)(2,1)} %collective-permute-done.5), channel_id=1, source_target_pairs={{8,0},{16,8},{24,16},{28,24},{20,28},{12,20},{4,12},{0,4},{9,1},{1... | collective-permute-start | bytes 4718600 | tf_op jit(solution)/shard_map/ppermute | solution.py:107
  186.3 42.1 %collective-permute-start.20 = (bf16[1024,256]{0,1:T(8,128)(2,1)}, bf16[1024,256]{0,1:T(8,128)(2,1)S(1)}, u32[]{:S(2)}, u32[]{:S(2)}) collective-permute-start(bf16[1024,256]{0,1:T(8,128)(2,1)} %collective-permute-done.18), channel_id=1, source_target_pairs={{8,0},{16,8},{24,16},{28,24},{20,28},{12,20},{4,12},{0,4},{9,1},{1... | collective-permute-start | bytes 1572872 | tf_op jit(solution)/shard_map/ppermute | solution.py:109
  194.7 34.9 %collective-permute-start.21 = (bf16[1024,256]{0,1:T(8,128)(2,1)}, bf16[1024,256]{0,1:T(8,128)(2,1)S(1)}, u32[]{:S(2)}, u32[]{:S(2)}) collective-permute-start(bf16[1024,256]{0,1:T(8,128)(2,1)} %collective-permute-done.19), channel_id=1, source_target_pairs={{0,8},{8,16},{16,24},{24,28},{28,20},{20,12},{12,4},{4,0},{1,9},{9... | collective-permute-start | bytes 1572872 | tf_op jit(solution)/shard_map/ppermute | solution.py:108
  232.4 56.2 %collective-permute-start.8 = (bf16[256,3072]{0,1:T(8,128)(2,1)}, bf16[256,3072]{0,1:T(8,128)(2,1)}, u32[]{:S(2)}, u32[]{:S(2)}) collective-permute-start(bf16[256,3072]{0,1:T(8,128)(2,1)} %collective-permute-done.6), channel_id=1, source_target_pairs={{0,8},{8,16},{16,24},{24,28},{28,20},{20,12},{12,4},{4,0},{1,9},{9... | collective-permute-start | bytes 4718600 | tf_op jit(solution)/shard_map/ppermute | solution.py:106
  240.4 15.2 %collective-permute-start.24 = (bf16[1024,256]{0,1:T(8,128)(2,1)}, bf16[1024,256]{0,1:T(8,128)(2,1)}, u32[]{:S(2)}, u32[]{:S(2)}) collective-permute-start(bf16[1024,256]{0,1:T(8,128)(2,1)} %collective-permute-done.22), channel_id=1, source_target_pairs={{8,0},{16,8},{24,16},{28,24},{20,28},{12,20},{4,12},{0,4},{9,1},{1... | collective-permute-start | bytes 1572872 | tf_op jit(solution)/shard_map/ppermute | solution.py:109
  244.6 41.9 %collective-permute-start.25 = (bf16[1024,256]{0,1:T(8,128)(2,1)}, bf16[1024,256]{0,1:T(8,128)(2,1)}, u32[]{:S(2)}, u32[]{:S(2)}) collective-permute-start(bf16[1024,256]{0,1:T(8,128)(2,1)} %collective-permute-done.23), channel_id=1, source_target_pairs={{0,8},{8,16},{16,24},{24,28},{28,20},{20,12},{12,4},{4,0},{1,9},{9... | collective-permute-start | bytes 1572872 | tf_op jit(solution)/shard_map/ppermute | solution.py:108
  245.5 58.8 %collective-permute-start.9 = (bf16[256,3072]{0,1:T(8,128)(2,1)}, bf16[256,3072]{0,1:T(8,128)(2,1)}, u32[]{:S(2)}, u32[]{:S(2)}) collective-permute-start(bf16[256,3072]{0,1:T(8,128)(2,1)} %collective-permute-done.7), channel_id=1, source_target_pairs={{8,0},{16,8},{24,16},{28,24},{20,28},{12,20},{4,12},{0,4},{9,1},{1... | collective-permute-start | bytes 4718600 | tf_op jit(solution)/shard_map/ppermute | solution.py:107
  255.5 42.1 %collective-permute-start.26 = (bf16[1024,256]{0,1:T(8,128)(2,1)}, bf16[1024,256]{0,1:T(8,128)(2,1)S(1)}, u32[]{:S(2)}, u32[]{:S(2)}) collective-permute-start(bf16[1024,256]{0,1:T(8,128)(2,1)} %collective-permute-done.24), channel_id=1, source_target_pairs={{8,0},{16,8},{24,16},{28,24},{20,28},{12,20},{4,12},{0,4},{9,1},{1... | collective-permute-start | bytes 1572872 | tf_op jit(solution)/shard_map/ppermute | solution.py:109
  288.6 57.9 %collective-permute-start.10 = (bf16[256,3072]{0,1:T(8,128)(2,1)}, bf16[256,3072]{0,1:T(8,128)(2,1)}, u32[]{:S(2)}, u32[]{:S(2)}) collective-permute-start(bf16[256,3072]{0,1:T(8,128)(2,1)} %collective-permute-done.8), channel_id=1, source_target_pairs={{0,8},{8,16},{16,24},{24,28},{28,20},{20,12},{12,4},{4,0},{1,9},{9... | collective-permute-start | bytes 4718600 | tf_op jit(solution)/shard_map/ppermute | solution.py:106
  301.5 42.0 %collective-permute-start.29 = (bf16[1024,256]{0,1:T(8,128)(2,1)S(1)}, bf16[1024,256]{0,1:T(8,128)(2,1)}, u32[]{:S(2)}, u32[]{:S(2)}) collective-permute-start(bf16[1024,256]{0,1:T(8,128)(2,1)S(1)} %collective-permute-done.27), channel_id=1, source_target_pairs={{0,8},{8,16},{16,24},{24,28},{28,20},{20,12},{12,4},{4,0},{1,9},{9... | collective-permute-start | bytes 1572872 | tf_op jit(solution)/shard_map/ppermute | solution.py:108
  304.3 52.9 %collective-permute-start.11 = (bf16[256,3072]{0,1:T(8,128)(2,1)}, bf16[256,3072]{0,1:T(8,128)(2,1)}, u32[]{:S(2)}, u32[]{:S(2)}) collective-permute-start(bf16[256,3072]{0,1:T(8,128)(2,1)} %collective-permute-done.9), channel_id=1, source_target_pairs={{8,0},{16,8},{24,16},{28,24},{20,28},{12,20},{4,12},{0,4},{9,1},{1... | collective-permute-start | bytes 4718600 | tf_op jit(solution)/shard_map/ppermute | solution.py:107
  312.5 42.0 %collective-permute-start.30 = (bf16[1024,256]{0,1:T(8,128)(2,1)S(1)}, bf16[1024,256]{0,1:T(8,128)(2,1)}, u32[]{:S(2)}, u32[]{:S(2)}) collective-permute-start(bf16[1024,256]{0,1:T(8,128)(2,1)S(1)} %collective-permute-done.28), channel_id=1, source_target_pairs={{8,0},{16,8},{24,16},{28,24},{20,28},{12,20},{4,12},{0,4},{9,1},{1... | collective-permute-start | bytes 1572872 | tf_op jit(solution)/shard_map/ppermute | solution.py:109
  343.5 210.8 %collective-permute-start.31 = (bf16[1024,256]{0,1:T(8,128)(2,1)}, bf16[1024,256]{0,1:T(8,128)(2,1)}, u32[]{:S(2)}, u32[]{:S(2)}) collective-permute-start(bf16[1024,256]{0,1:T(8,128)(2,1)} %collective-permute-done.29), channel_id=1, source_target_pairs={{0,8},{8,16},{16,24},{24,28},{28,20},{20,12},{12,4},{4,0},{1,9},{9... | collective-permute-start | bytes 1572872 | tf_op jit(solution)/shard_map/ppermute | solution.py:108
  346.5 42.8 %collective-permute-start.12 = (bf16[256,3072]{0,1:T(8,128)(2,1)}, bf16[256,3072]{0,1:T(8,128)(2,1)}, u32[]{:S(2)}, u32[]{:S(2)}) collective-permute-start(bf16[256,3072]{0,1:T(8,128)(2,1)} %collective-permute-done.10), channel_id=1, source_target_pairs={{0,8},{8,16},{16,24},{24,28},{28,20},{20,12},{12,4},{4,0},{1,9},{9... | collective-permute-start | bytes 4718600 | tf_op jit(solution)/shard_map/ppermute | solution.py:106
  354.4 201.8 %collective-permute-start.32 = (bf16[1024,256]{0,1:T(8,128)(2,1)}, bf16[1024,256]{0,1:T(8,128)(2,1)}, u32[]{:S(2)}, u32[]{:S(2)}) collective-permute-start(bf16[1024,256]{0,1:T(8,128)(2,1)} %collective-permute-done.30), channel_id=1, source_target_pairs={{8,0},{16,8},{24,16},{28,24},{20,28},{12,20},{4,12},{0,4},{9,1},{1... | collective-permute-start | bytes 1572872 | tf_op jit(solution)/shard_map/ppermute | solution.py:109
  357.2 43.0 %collective-permute-start.13 = (bf16[256,3072]{0,1:T(8,128)(2,1)}, bf16[256,3072]{0,1:T(8,128)(2,1)}, u32[]{:S(2)}, u32[]{:S(2)}) collective-permute-start(bf16[256,3072]{0,1:T(8,128)(2,1)} %collective-permute-done.11), channel_id=1, source_target_pairs={{8,0},{16,8},{24,16},{28,24},{20,28},{12,20},{4,12},{0,4},{9,1},{1... | collective-permute-start | bytes 4718600 | tf_op jit(solution)/shard_map/ppermute | solution.py:107
  389.3 28.8 %collective-permute-start.14 = (bf16[256,3072]{0,1:T(8,128)(2,1)}, bf16[256,3072]{0,1:T(8,128)(2,1)}, u32[]{:S(2)}, u32[]{:S(2)}) collective-permute-start(bf16[256,3072]{0,1:T(8,128)(2,1)} %collective-permute-done.12), channel_id=1, source_target_pairs={{0,8},{8,16},{16,24},{24,28},{28,20},{20,12},{12,4},{4,0},{1,9},{9... | collective-permute-start | bytes 4718600 | tf_op jit(solution)/shard_map/ppermute | solution.py:106
  400.2 29.8 %collective-permute-start.15 = (bf16[256,3072]{0,1:T(8,128)(2,1)}, bf16[256,3072]{0,1:T(8,128)(2,1)}, u32[]{:S(2)}, u32[]{:S(2)}) collective-permute-start(bf16[256,3072]{0,1:T(8,128)(2,1)} %collective-permute-done.13), channel_id=1, source_target_pairs={{8,0},{16,8},{24,16},{28,24},{20,28},{12,20},{4,12},{0,4},{9,1},{1... | collective-permute-start | bytes 4718600 | tf_op jit(solution)/shard_map/ppermute | solution.py:107
  491.5 17.6 %collective-permute-start.16 = (bf16[2,3,1024]{2,1,0:T(4,128)(2,1)S(1)}, bf16[2,3,1024]{2,1,0:T(4,128)(2,1)S(1)}, u32[]{:S(2)}, u32[]{:S(2)}) collective-permute-start(bf16[2,3,1024]{2,1,0:T(4,128)(2,1)S(1)} %slice.65), channel_id=1, source_target_pairs={{0,4},{4,8},{8,12},{12,16},{16,20},{20,24},{24,28},{1,5},{5,9},{9,... | collective-permute-start | bytes 36872 | tf_op jit(solution)/shard_map/ppermute | solution.py:11
  618.2 55.2 %reduce-scatter.3.cloned.1.call-start = ((), (), s32[]{:S(2)}) async-start(), calls=%async_computation.3 | async-start | bytes 9437184 | tf_op jit(solution)/shard_map/reduce_scatter | solution.py:151
  658.6 62.7 %collective-permute-start.33 = (bf16[768,2048]{1,0:T(8,128)(2,1)}, bf16[768,2048]{1,0:T(8,128)(2,1)}, u32[]{:S(2)}, u32[]{:S(2)}) collective-permute-start(bf16[768,2048]{1,0:T(8,128)(2,1)} %reduce-scatter.5.cloned.1.call-done), channel_id=1, source_target_pairs={{0,2},{2,0},{1,3},{3,1},{4,6},{6,4},{5,7},{7,5},{8,10},{10,8},{9,1... | collective-permute-start | bytes 9437192 | tf_op jit(solution)/shard_map/ppermute | solution.py:15
  (18 other events, 728.9 us)
Sparse Core Ops, SparseCore 0:
  84.9 26.7 all-gather.1
  618.3 14.7 reduce-scatter.4
  658.7 14.7 reduce-scatter.2

commit v11 on v9

--- a/solution.py
+++ b/solution.py
@@ -68,13 +68,6 @@
     other = 1 - half
     half_width = local_width // 2
 
-    pair_tokens = pair_ordered(tokens, swap_pair(tokens), half, 0)
-    pair_tokens = lax.all_gather(pair_tokens, "tp", axis=1, tiled=True)
-    row_count = pair_tokens.shape[0]
-    wide_float = pair_tokens.astype(jnp.float32)
-    scale = lax.rsqrt(jnp.mean(wide_float * wide_float, axis=-1, keepdims=True) + 1e-06)
-    normed = (wide_float * scale * norm_gain).astype(jnp.bfloat16)
-
     own_piece = half_of(w_in, 2, half).reshape(w_rows, 3 * half_width)
     partner_piece = swap_pair(half_of(w_in, 2, other)).reshape(w_rows, 3 * half_width)
     order = ring_order(n_hi)
@@ -101,6 +94,9 @@
         return lax.dynamic_update_slice_in_dim(buffer, piece[:, None], ctx_index, axis=1)
 
     current, previous = toeplitz_pair(half_of(long_filter, 1, half))
+    late = min(2, n_hi - 1)
+    late_w = []
+    late_columns = []
     for step in range(n_hi):
         if step > 0:
             own_piece = lax.ppermute(own_piece, "hi", forward)
@@ -109,16 +105,33 @@
             partner_out = lax.ppermute(partner_out, "hi", backward)
         own_at = 2 * order_table[(here - step) % n_hi] + half
         partner_at = 2 * order_table[(here + step) % n_hi] + other
-        gathered_w = store(gathered_w, own_piece, own_at)
-        gathered_w = store(gathered_w, partner_piece, partner_at)
+        if step < n_hi - late:
+            gathered_w = store(gathered_w, own_piece, own_at)
+            gathered_w = store(gathered_w, partner_piece, partner_at)
+        else:
+            late_w += [own_piece, partner_piece]
+            late_columns += [own_at, partner_at]
         gathered_o = store_out(gathered_o, own_out, own_at)
         gathered_o = store_out(gathered_o, partner_out, partner_at)
     o_full = gathered_o.reshape(half_width, n_ctx * e_cols)
 
-    projected = jnp.dot(
+    pair_tokens = pair_ordered(tokens, swap_pair(tokens), half, 0)
+    pair_tokens = lax.all_gather(pair_tokens, "tp", axis=1, tiled=True)
+    row_count = pair_tokens.shape[0]
+    wide_float = pair_tokens.astype(jnp.float32)
+    scale = lax.rsqrt(jnp.mean(wide_float * wide_float, axis=-1, keepdims=True) + 1e-06)
+    normed = (wide_float * scale * norm_gain).astype(jnp.bfloat16)
+
+    early_part = jnp.dot(
         normed,
         gathered_w.reshape(n_ctx * w_rows, 3 * half_width),
         preferred_element_type=jnp.float32,
+    )
+    late_normed = jnp.concatenate(
+        [lax.dynamic_slice_in_dim(normed, at * w_rows, w_rows, axis=1) for at in late_columns], axis=1
+    )
+    projected = early_part + jnp.dot(
+        late_normed, jnp.concatenate(late_w, axis=0), preferred_element_type=jnp.float32
     )
     projected = projected.astype(jnp.bfloat16).reshape(row_count, 3, half_width)
 

time: 734 us -> 751 us (1.023)
  matrix products: 86.1 us -> 101 us
  other arithmetic: 64.4 us -> 72.3 us
    dot_general x0 -> x1, matrix products: none -> 17.2 us  [local(): jnp.dot(late_normed, jnp.concatenate(late_w, axis=0), preferred_element_t...]
    ppermute x7, waiting for transfers between devices: 72.5 us -> 56.7 us  [local(): own_out = lax.ppermute(own_out, 'hi', forward)]
    ppermute x4, waiting for transfers between devices: 137 us -> 153 us  [swap_pair(): return lax.ppermute(value, 'lo', [(0, 1), (1, 0)])]
    ppermute x7, waiting for transfers between devices: 29.4 us -> 43.1 us  [local(): own_piece = lax.ppermute(own_piece, 'hi', forward)]
    ppermute x7, waiting for transfers between devices: 48.3 us -> 39.8 us  [local(): partner_piece = lax.ppermute(partner_piece, 'hi', backward)]
    convert_element_type x1, local copies, waits for them, and re-layouts: 12.8 us -> 21.1 us  [local(): projected = projected.astype(jnp.bfloat16).reshape(row_count, 3, half_width)]
    convert_element_type x0 -> x1, other arithmetic: none -> 7.69 us  [local(): normed = (wide_float * scale * norm_gain).astype(jnp.bfloat16)]
    broadcast_in_dim x14 -> x10, local copies, waits for them, and re-layouts: 23.9 us -> 17.1 us  [store(): piece[None]]
  transfers between devices with their start and end apart: 37 -> 37, of which waited for: 22 -> 19; matrix products, arithmetic and copies ran while one was open for 33% -> 34% of each run, Pallas kernels for 0% -> 0%
where the time goes in v11:
time: 751 us; the launch traced here: 740 us
  waiting for transfers between devices  340 us (45%)
  local copies, waits for them, and re-layouts  151 us (20%)
  matrix products  101 us (13%)
  other arithmetic  72.3 us (10%)
  starting transfers between devices  40.6 us (5%)
  between operations  34.3 us (5%)
    ppermute x4, waiting for transfers between devices, swap_pair(): return lax.ppermute(value, 'lo', [(0, 1), (1, 0)])  153 us
    ppermute x7, waiting for transfers between devices, local(): own_out = lax.ppermute(own_out, 'hi', forward)  56.7 us
    dot_general x1, matrix products, local(): jnp.dot(normed, gathered_w.reshape(n_ctx * w_rows, 3 * half_width), prefe...  45.8 us
    ppermute x7, waiting for transfers between devices, local(): own_piece = lax.ppermute(own_piece, 'hi', forward)  43.1 us
    ppermute x7, waiting for transfers between devices, local(): partner_piece = lax.ppermute(partner_piece, 'hi', backward)  39.8 us
    ppermute x7, waiting for transfers between devices, local(): partner_out = lax.ppermute(partner_out, 'hi', backward)  29.6 us
    dynamic_update_slice x16, local copies, waits for them, and re-layouts, store_out(): lax.dynamic_update_slice_in_dim(buffer, piece[:, None], ctx_index, axis=1)  28 us
    dot_general x2, matrix products, out_terms(): jnp.dot(rows, o_full, preferred_element_type=jnp.float32)  24.8 us
  transfers between devices with their start and end apart: 37, of which 19 were waited for; matrix products, arithmetic and copies ran while one was open for 34% of the time, Pallas kernels for 0%

profile of v11, /device:TPU:0, one launch (start us, length us, event | category | flops | bytes accessed | tf_op | source)
XLA Modules:
  0.0 740.0 jit_solution(14533927110768063881)
XLA Ops:
  9.5 68.3 %collective-permute-done = bf16[768,2048]{1,0:T(8,128)(2,1)S(1)} collective-permute-done((bf16[768,2048]{1,0:T(8,128)(2,1)}, bf16[768,2048]{1,0:T(8,128)(2,1)S(1)}, u32[]{:S(2)}, u32[]{:S(2)}) %collective-permute-start) | collective-permute-done | bytes 3145760 | tf_op jit(solution)/shard_map/ppermute | solution.py:15
  91.8 31.8 %collective-permute-done.1 = bf16[256,3,1024]{0,2,1:T(8,128)(2,1)} collective-permute-done((bf16[256,3,1024]{0,2,1:T(8,128)(2,1)}, bf16[256,3,1024]{0,2,1:T(8,128)(2,1)}, u32[]{:S(2)}, u32[]{:S(2)}) %collective-permute-start.1) | collective-permute-done | bytes 1572896 | tf_op jit(solution)/shard_map/ppermute | solution.py:15
  126.9 31.7 %collective-permute-done.3 = bf16[256,3072]{0,1:T(8,128)(2,1)} collective-permute-done((bf16[256,3072]{0,1:T(8,128)(2,1)}, bf16[256,3072]{0,1:T(8,128)(2,1)}, u32[]{:S(2)}, u32[]{:S(2)}) %collective-permute-start.3) | collective-permute-done | bytes 1572896 | tf_op jit(solution)/shard_map/ppermute | solution.py:103
  191.1 8.6 %broadcast_in_dim.89 = bf16[16,256,3072]{2,1,0:T(8,128)(2,1)} broadcast(bf16[]{:T(256)} %constant.133.clone.1), dimensions={} | broadcast | bytes 25165826 | tf_op jit(solution)/shard_map/broadcast_in_dim | solution.py:87
  203.0 4.4 broadcast_in_dim.101
  222.8 7.7 %collective-permute-done.22 = bf16[1024,256]{0,1:T(8,128)(2,1)} collective-permute-done((bf16[1024,256]{0,1:T(8,128)(2,1)S(1)}, bf16[1024,256]{0,1:T(8,128)(2,1)}, u32[]{:S(2)}, u32[]{:S(2)}) %collective-permute-start.22) | collective-permute-done | bytes 524320 | tf_op jit(solution)/shard_map/ppermute | solution.py:105
  230.9 28.3 %collective-permute-done.23 = bf16[1024,256]{0,1:T(8,128)(2,1)} collective-permute-done((bf16[1024,256]{0,1:T(8,128)(2,1)S(1)}, bf16[1024,256]{0,1:T(8,128)(2,1)}, u32[]{:S(2)}, u32[]{:S(2)}) %collective-permute-start.23) | collective-permute-done | bytes 524320 | tf_op jit(solution)/shard_map/ppermute | solution.py:104
  278.9 8.6 %collective-permute-done.26 = bf16[1024,256]{0,1:T(8,128)(2,1)} collective-permute-done((bf16[1024,256]{0,1:T(8,128)(2,1)}, bf16[1024,256]{0,1:T(8,128)(2,1)}, u32[]{:S(2)}, u32[]{:S(2)}) %collective-permute-start.26) | collective-permute-done | bytes 524320 | tf_op jit(solution)/shard_map/ppermute | solution.py:105
  287.9 26.9 %collective-permute-done.27 = bf16[1024,256]{0,1:T(8,128)(2,1)} collective-permute-done((bf16[1024,256]{0,1:T(8,128)(2,1)}, bf16[1024,256]{0,1:T(8,128)(2,1)}, u32[]{:S(2)}, u32[]{:S(2)}) %collective-permute-start.27) | collective-permute-done | bytes 524320 | tf_op jit(solution)/shard_map/ppermute | solution.py:104
  323.9 5.0 collective-permute-done.28
  339.5 4.6 collective-permute-done.30
  349.1 25.7 %collective-permute-done.10 = bf16[256,3072]{0,1:T(8,128)(2,1)} collective-permute-done((bf16[256,3072]{0,1:T(8,128)(2,1)}, bf16[256,3072]{0,1:T(8,128)(2,1)}, u32[]{:S(2)}, u32[]{:S(2)}) %collective-permute-start.10) | collective-permute-done | bytes 1572896 | tf_op jit(solution)/shard_map/ppermute | solution.py:102
  392.1 17.1 %collective-permute-done.12 = bf16[256,3072]{0,1:T(8,128)(2,1)} collective-permute-done((bf16[256,3072]{0,1:T(8,128)(2,1)}, bf16[256,3072]{0,1:T(8,128)(2,1)}, u32[]{:S(2)}, u32[]{:S(2)}) %collective-permute-start.12) | collective-permute-done | bytes 1572896 | tf_op jit(solution)/shard_map/ppermute | solution.py:102
  411.6 8.1 %collective-permute-done.13 = bf16[256,3072]{0,1:T(8,128)(2,1)} collective-permute-done((bf16[256,3072]{0,1:T(8,128)(2,1)}, bf16[256,3072]{0,1:T(8,128)(2,1)}, u32[]{:S(2)}, u32[]{:S(2)}) %collective-permute-start.13) | collective-permute-done | bytes 1572896 | tf_op jit(solution)/shard_map/ppermute | solution.py:103
  420.0 7.1 fusion
  427.0 7.7 %fusion.2 = bf16[1536,4096]{1,0:T(8,128)(2,1)S(1)} fusion(bf16[1536,4096]{1,0:T(8,128)(2,1)} %all-gather.2.cloned.1.call-done, f32[4096]{0:T(1024)S(1)} %copy-done.12, f32[1536]{0:T(1024)S(1)} %add_rsqrt_fusion), kind=kLoop, calls=%fused_computation.4 | loop fusion | flops 25165824 | bytes 25188352 | tf_op jit(solution)/shard_map/convert_element_type | solution.py:123
  434.7 45.8 %fusion.47 = f32[1536,3072]{1,0:T(8,128)} fusion(bf16[1536,4096]{1,0:T(8,128)(2,1)S(1)} %fusion.2, bf16[4096,3072]{1,0:T(8,128)(2,1)} %bitcast.27), kind=kOutput, calls=%fused_computation.106 | convolution fusion | flops 38654705664 | bytes 56623104 | tf_op jit(solution)/shard_map/dot_general | solution.py:125
  480.9 17.2 %add_convert_fusion = bf16[1536,3072]{1,0:T(8,128)(2,1)} fusion(f32[1536,3072]{1,0:T(8,128)} %fusion.47, bf16[256,3072]{0,1:T(8,128)(2,1)} %collective-permute-done.15, bf16[256,3072]{0,1:T(8,128)(2,1)S(1)} %collective-permute-done.14, bf16[256,3072]{0,1:T(8,128)(2,1)} %collective-permute-done.13, bf16[256,3072]{0,1:T(8,128)(2,1)} %collective-permute-done.12, ...), kind=kOutput, calls=%fused_computation.10 | convolution fusion | flops 9710862336 | bytes 37748736 | tf_op jit(solution)/shard_map/dot_general | solution.py:133
  499.0 4.0 collective-permute-start.16
  504.9 21.1 %copy.36 = bf16[1536,3072]{0,1:T(8,128)(2,1)} copy(bf16[1536,3072]{1,0:T(8,128)(2,1)} %add_convert_fusion) | data formatting | bytes 18874368 | tf_op jit(solution)/shard_map/convert_element_type | solution.py:136
  526.4 15.1 %maximum_convert_fusion = f32[1538,3,1024]{0,2,1:T(8,128)} fusion(bf16[1536,3,1024]{0,2,1:T(8,128)(2,1)} %bitcast.107, bf16[2,3,1024]{0,2,1:T(8,128)(2,1)S(1)} %copy.37), kind=kLoop, calls=%fused_computation.11 | loop fusion | flops 18898944 | bytes 28348416 | tf_op jit(solution)/shard_map/convert_element_type | solution.py:34
  541.6 22.2 %fusion.3 = f32[1536,3,1024]{0,2,1:T(8,128)S(1)} fusion(f32[1538,3,1024]{0,2,1:T(8,128)} %maximum_convert_fusion, f32[3,1024]{1,0:T(4,128)S(1)} %copy-done.10, f32[3,1024]{1,0:T(4,128)S(1)} %copy-done.9, f32[3,1024]{1,0:T(4,128)S(1)} %copy-done.8), kind=kLoop, calls=%fused_computation.6 | loop fusion | flops 23592960 | bytes 75534336 | tf_op jit(solution)/shard_map/add | solution.py:38
  563.8 6.5 copy-done.2
  581.8 4.6 copy.41
  591.0 13.2 %concatenate.19 = bf16[1664,1024]{1,0:T(8,128)(2,1)S(1)} concatenate(bf16[1,1024]{1,0:T(2,128)(2,1)S(1)} %broadcast_in_dim.100, bf16[127,1024]{1,0:T(8,128)(2,1)} %copy.42, bf16[1536,1024]{1,0:T(8,128)(2,1)} %bitcast.109), dimensions={0} | concatenate | bytes 6815744 | tf_op jit(solution)/shard_map/concatenate | solution.py:145
  613.2 5.4 fusion.24
  624.0 4.8 fusion.7
  628.8 12.6 %convolution_convert_fusion = bf16[768,4096]{1,0:T(8,128)(2,1)} fusion(bf16[1024,4096]{0,1:T(8,128)(2,1)} %bitcast.58, bf16[1536,1024]{0,1:T(8,128)(2,1)S(1)} %fusion.7, s32[]{:T(128)S(6)} %select_n.274), kind=kOutput, calls=%fused_computation.17 | convolution fusion | flops 6445596672 | bytes 16252932 | tf_op jit(solution)/shard_map/dot_general | solution.py:160
  641.5 12.3 %convolution_convert_fusion.1 = bf16[768,4096]{1,0:T(8,128)(2,1)} fusion(bf16[1024,4096]{0,1:T(8,128)(2,1)} %bitcast.58, bf16[1536,1024]{0,1:T(8,128)(2,1)S(1)} %fusion.7, s32[]{:T(128)S(6)} %select_n.269), kind=kOutput, calls=%fused_computation.18 | convolution fusion | flops 6445596672 | bytes 16252932 | tf_op jit(solution)/shard_map/dot_general | solution.py:160
  657.5 16.4 %reduce-scatter.3.cloned.1.call-done = bf16[768,2048]{1,0:T(8,128)(2,1)} async-done(((bf16[768,4096]{1,0:T(8,128)(2,1)}), bf16[768,2048]{1,0:T(8,128)(2,1)}) %reduce-scatter.3.cloned.1.call-update) | async-done | bytes 3145744 | tf_op jit(solution)/shard_map/reduce_scatter | solution.py:161
  673.9 52.5 %collective-permute-done.33 = bf16[768,2048]{1,0:T(8,128)(2,1)} collective-permute-done((bf16[768,2048]{1,0:T(8,128)(2,1)}, bf16[768,2048]{1,0:T(8,128)(2,1)}, u32[]{:S(2)}, u32[]{:S(2)}) %collective-permute-start.33) | collective-permute-done | bytes 3145760 | tf_op jit(solution)/shard_map/ppermute | solution.py:15
  726.4 6.6 add_convert_fusion.1
  (157 shorter events, 153.6 us)
Async XLA Ops:
  6.5 413.4 %all-gather.2.cloned.1.call-start = ((), (), s32[]{:S(2)}) async-start(), calls=%async_computation.2 | async-start | bytes 18874368 | tf_op jit(solution)/shard_map/all_gather | solution.py:119
  6.5 71.2 %collective-permute-start = (bf16[768,2048]{1,0:T(8,128)(2,1)}, bf16[768,2048]{1,0:T(8,128)(2,1)S(1)}, u32[]{:S(2)}, u32[]{:S(2)}) collective-permute-start(bf16[768,2048]{1,0:T(8,128)(2,1)} %param.8), channel_id=1, source_target_pairs={{0,2},{2,0},{1,3},{3,1},{4,6},{6,4},{5,7},{7,5},{8,10},{10,8},{9,1... | collective-permute-start | bytes 9437192 | tf_op jit(solution)/shard_map/ppermute | solution.py:15
  83.9 571.9 %reduce-scatter.5.cloned.1.call-start = ((), (), s32[]{:S(2)}) async-start(), calls=%async_computation.4 | async-start | bytes 9437184 | tf_op jit(solution)/shard_map/reduce_scatter | solution.py:161
  87.8 35.9 %collective-permute-start.1 = (bf16[256,3,1024]{0,2,1:T(8,128)(2,1)}, bf16[256,3,1024]{0,2,1:T(8,128)(2,1)}, u32[]{:S(2)}, u32[]{:S(2)}) collective-permute-start(bf16[256,3,1024]{0,2,1:T(8,128)(2,1)} %copy.56), channel_id=1, source_target_pairs={{0,2},{2,0},{1,3},{3,1},{4,6},{6,4},{5,7},{7,5},{8,10},{10,8},{9,1... | collective-permute-start | bytes 4718600 | tf_op jit(solution)/shard_map/ppermute | solution.py:15
  90.2 35.1 %collective-permute-start.2 = (bf16[256,3072]{0,1:T(8,128)(2,1)S(1)}, bf16[256,3072]{0,1:T(8,128)(2,1)}, u32[]{:S(2)}, u32[]{:S(2)}) collective-permute-start(bf16[256,3072]{0,1:T(8,128)(2,1)S(1)} %bitcast.110), channel_id=1, source_target_pairs={{0,8},{8,16},{16,24},{24,28},{28,20},{20,12},{12,4},{4,0},{1,9},{9... | collective-permute-start | bytes 4718600 | tf_op jit(solution)/shard_map/ppermute | solution.py:102
  123.7 35.0 %collective-permute-start.3 = (bf16[256,3072]{0,1:T(8,128)(2,1)}, bf16[256,3072]{0,1:T(8,128)(2,1)}, u32[]{:S(2)}, u32[]{:S(2)}) collective-permute-start(bf16[256,3072]{0,1:T(8,128)(2,1)} %bitcast.8), channel_id=1, source_target_pairs={{8,0},{16,8},{24,16},{28,24},{20,28},{12,20},{4,12},{0,4},{9,1},{1... | collective-permute-start | bytes 4718600 | tf_op jit(solution)/shard_map/ppermute | solution.py:103
  125.3 84.0 %collective-permute-start.4 = (bf16[256,3072]{0,1:T(8,128)(2,1)}, bf16[256,3072]{0,1:T(8,128)(2,1)}, u32[]{:S(2)}, u32[]{:S(2)}) collective-permute-start(bf16[256,3072]{0,1:T(8,128)(2,1)} %collective-permute-done.2), channel_id=1, source_target_pairs={{0,8},{8,16},{16,24},{24,28},{28,20},{20,12},{12,4},{4,0},{1,9},{9... | collective-permute-start | bytes 4718600 | tf_op jit(solution)/shard_map/ppermute | solution.py:102
  158.6 58.9 %collective-permute-start.5 = (bf16[256,3072]{0,1:T(8,128)(2,1)}, bf16[256,3072]{0,1:T(8,128)(2,1)}, u32[]{:S(2)}, u32[]{:S(2)}) collective-permute-start(bf16[256,3072]{0,1:T(8,128)(2,1)} %collective-permute-done.3), channel_id=1, source_target_pairs={{8,0},{16,8},{24,16},{28,24},{20,28},{12,20},{4,12},{0,4},{9,1},{1... | collective-permute-start | bytes 4718600 | tf_op jit(solution)/shard_map/ppermute | solution.py:103
  162.1 38.9 %collective-permute-start.18 = (bf16[1024,256]{0,1:T(8,128)(2,1)}, bf16[1024,256]{0,1:T(8,128)(2,1)}, u32[]{:S(2)}, u32[]{:S(2)}) collective-permute-start(bf16[1024,256]{0,1:T(8,128)(2,1)} %copy.59), channel_id=1, source_target_pairs={{0,2},{2,0},{1,3},{3,1},{4,6},{6,4},{5,7},{7,5},{8,10},{10,8},{9,1... | collective-permute-start | bytes 1572872 | tf_op jit(solution)/shard_map/ppermute | solution.py:15
  164.6 37.9 %collective-permute-start.19 = (bf16[1024,256]{0,1:T(8,128)(2,1)}, bf16[1024,256]{0,1:T(8,128)(2,1)}, u32[]{:S(2)}, u32[]{:S(2)}) collective-permute-start(bf16[1024,256]{0,1:T(8,128)(2,1)} %copy.58), channel_id=1, source_target_pairs={{0,8},{8,16},{16,24},{24,28},{28,20},{20,12},{12,4},{4,0},{1,9},{9... | collective-permute-start | bytes 1572872 | tf_op jit(solution)/shard_map/ppermute | solution.py:104
  209.3 57.1 %collective-permute-start.6 = (bf16[256,3072]{0,1:T(8,128)(2,1)}, bf16[256,3072]{0,1:T(8,128)(2,1)}, u32[]{:S(2)}, u32[]{:S(2)}) collective-permute-start(bf16[256,3072]{0,1:T(8,128)(2,1)} %collective-permute-done.4), channel_id=1, source_target_pairs={{0,8},{8,16},{16,24},{24,28},{28,20},{20,12},{12,4},{4,0},{1,9},{9... | collective-permute-start | bytes 4718600 | tf_op jit(solution)/shard_map/ppermute | solution.py:102
  217.2 42.0 %collective-permute-start.23 = (bf16[1024,256]{0,1:T(8,128)(2,1)S(1)}, bf16[1024,256]{0,1:T(8,128)(2,1)}, u32[]{:S(2)}, u32[]{:S(2)}) collective-permute-start(bf16[1024,256]{0,1:T(8,128)(2,1)S(1)} %collective-permute-done.21), channel_id=1, source_target_pairs={{0,8},{8,16},{16,24},{24,28},{28,20},{20,12},{12,4},{4,0},{1,9},{9... | collective-permute-start | bytes 1572872 | tf_op jit(solution)/shard_map/ppermute | solution.py:104
  217.6 56.8 %collective-permute-start.7 = (bf16[256,3072]{0,1:T(8,128)(2,1)}, bf16[256,3072]{0,1:T(8,128)(2,1)}, u32[]{:S(2)}, u32[]{:S(2)}) collective-permute-start(bf16[256,3072]{0,1:T(8,128)(2,1)} %collective-permute-done.5), channel_id=1, source_target_pairs={{8,0},{16,8},{24,16},{28,24},{20,28},{12,20},{4,12},{0,4},{9,1},{1... | collective-permute-start | bytes 4718600 | tf_op jit(solution)/shard_map/ppermute | solution.py:103
  230.5 41.9 %collective-permute-start.24 = (bf16[1024,256]{0,1:T(8,128)(2,1)}, bf16[1024,256]{0,1:T(8,128)(2,1)}, u32[]{:S(2)}, u32[]{:S(2)}) collective-permute-start(bf16[1024,256]{0,1:T(8,128)(2,1)} %collective-permute-done.22), channel_id=1, source_target_pairs={{8,0},{16,8},{24,16},{28,24},{20,28},{12,20},{4,12},{0,4},{9,1},{1... | collective-permute-start | bytes 1572872 | tf_op jit(solution)/shard_map/ppermute | solution.py:105
  266.4 64.6 %collective-permute-start.8 = (bf16[256,3072]{0,1:T(8,128)(2,1)}, bf16[256,3072]{0,1:T(8,128)(2,1)}, u32[]{:S(2)}, u32[]{:S(2)}) collective-permute-start(bf16[256,3072]{0,1:T(8,128)(2,1)} %collective-permute-done.6), channel_id=1, source_target_pairs={{0,8},{8,16},{16,24},{24,28},{28,20},{20,12},{12,4},{4,0},{1,9},{9... | collective-permute-start | bytes 4718600 | tf_op jit(solution)/shard_map/ppermute | solution.py:102
  272.3 15.2 %collective-permute-start.26 = (bf16[1024,256]{0,1:T(8,128)(2,1)}, bf16[1024,256]{0,1:T(8,128)(2,1)}, u32[]{:S(2)}, u32[]{:S(2)}) collective-permute-start(bf16[1024,256]{0,1:T(8,128)(2,1)} %collective-permute-done.24), channel_id=1, source_target_pairs={{8,0},{16,8},{24,16},{28,24},{20,28},{12,20},{4,12},{0,4},{9,1},{1... | collective-permute-start | bytes 1572872 | tf_op jit(solution)/shard_map/ppermute | solution.py:105
  273.0 41.9 %collective-permute-start.27 = (bf16[1024,256]{0,1:T(8,128)(2,1)}, bf16[1024,256]{0,1:T(8,128)(2,1)}, u32[]{:S(2)}, u32[]{:S(2)}) collective-permute-start(bf16[1024,256]{0,1:T(8,128)(2,1)} %collective-permute-done.25), channel_id=1, source_target_pairs={{0,8},{8,16},{16,24},{24,28},{28,20},{20,12},{12,4},{4,0},{1,9},{9... | collective-permute-start | bytes 1572872 | tf_op jit(solution)/shard_map/ppermute | solution.py:104
  274.4 59.4 %collective-permute-start.9 = (bf16[256,3072]{0,1:T(8,128)(2,1)}, bf16[256,3072]{0,1:T(8,128)(2,1)}, u32[]{:S(2)}, u32[]{:S(2)}) collective-permute-start(bf16[256,3072]{0,1:T(8,128)(2,1)} %collective-permute-done.7), channel_id=1, source_target_pairs={{8,0},{16,8},{24,16},{28,24},{20,28},{12,20},{4,12},{0,4},{9,1},{1... | collective-permute-start | bytes 4718600 | tf_op jit(solution)/shard_map/ppermute | solution.py:103
  287.5 41.4 %collective-permute-start.28 = (bf16[1024,256]{0,1:T(8,128)(2,1)}, bf16[1024,256]{0,1:T(8,128)(2,1)}, u32[]{:S(2)}, u32[]{:S(2)}) collective-permute-start(bf16[1024,256]{0,1:T(8,128)(2,1)} %collective-permute-done.26), channel_id=1, source_target_pairs={{8,0},{16,8},{24,16},{28,24},{20,28},{12,20},{4,12},{0,4},{9,1},{1... | collective-permute-start | bytes 1572872 | tf_op jit(solution)/shard_map/ppermute | solution.py:105
  329.0 15.2 %collective-permute-start.30 = (bf16[1024,256]{0,1:T(8,128)(2,1)}, bf16[1024,256]{0,1:T(8,128)(2,1)}, u32[]{:S(2)}, u32[]{:S(2)}) collective-permute-start(bf16[1024,256]{0,1:T(8,128)(2,1)} %collective-permute-done.28), channel_id=1, source_target_pairs={{8,0},{16,8},{24,16},{28,24},{20,28},{12,20},{4,12},{0,4},{9,1},{1... | collective-permute-start | bytes 1572872 | tf_op jit(solution)/shard_map/ppermute | solution.py:105
  329.2 248.8 %collective-permute-start.31 = (bf16[1024,256]{0,1:T(8,128)(2,1)}, bf16[1024,256]{0,1:T(8,128)(2,1)}, u32[]{:S(2)}, u32[]{:S(2)}) collective-permute-start(bf16[1024,256]{0,1:T(8,128)(2,1)} %collective-permute-done.29), channel_id=1, source_target_pairs={{0,8},{8,16},{16,24},{24,28},{28,20},{20,12},{12,4},{4,0},{1,9},{9... | collective-permute-start | bytes 1572872 | tf_op jit(solution)/shard_map/ppermute | solution.py:104
  331.0 43.8 %collective-permute-start.10 = (bf16[256,3072]{0,1:T(8,128)(2,1)}, bf16[256,3072]{0,1:T(8,128)(2,1)}, u32[]{:S(2)}, u32[]{:S(2)}) collective-permute-start(bf16[256,3072]{0,1:T(8,128)(2,1)} %collective-permute-done.8), channel_id=1, source_target_pairs={{0,8},{8,16},{16,24},{24,28},{28,20},{20,12},{12,4},{4,0},{1,9},{9... | collective-permute-start | bytes 4718600 | tf_op jit(solution)/shard_map/ppermute | solution.py:102
  333.8 45.0 %collective-permute-start.11 = (bf16[256,3072]{0,1:T(8,128)(2,1)}, bf16[256,3072]{0,1:T(8,128)(2,1)}, u32[]{:S(2)}, u32[]{:S(2)}) collective-permute-start(bf16[256,3072]{0,1:T(8,128)(2,1)} %collective-permute-done.9), channel_id=1, source_target_pairs={{8,0},{16,8},{24,16},{28,24},{20,28},{12,20},{4,12},{0,4},{9,1},{1... | collective-permute-start | bytes 4718600 | tf_op jit(solution)/shard_map/ppermute | solution.py:103
  344.2 235.8 %collective-permute-start.32 = (bf16[1024,256]{0,1:T(8,128)(2,1)}, bf16[1024,256]{0,1:T(8,128)(2,1)}, u32[]{:S(2)}, u32[]{:S(2)}) collective-permute-start(bf16[1024,256]{0,1:T(8,128)(2,1)} %collective-permute-done.30), channel_id=1, source_target_pairs={{8,0},{16,8},{24,16},{28,24},{20,28},{12,20},{4,12},{0,4},{9,1},{1... | collective-permute-start | bytes 1572872 | tf_op jit(solution)/shard_map/ppermute | solution.py:105
  374.8 34.5 %collective-permute-start.12 = (bf16[256,3072]{0,1:T(8,128)(2,1)}, bf16[256,3072]{0,1:T(8,128)(2,1)}, u32[]{:S(2)}, u32[]{:S(2)}) collective-permute-start(bf16[256,3072]{0,1:T(8,128)(2,1)} %collective-permute-done.10), channel_id=1, source_target_pairs={{0,8},{8,16},{16,24},{24,28},{28,20},{20,12},{12,4},{4,0},{1,9},{9... | collective-permute-start | bytes 4718600 | tf_op jit(solution)/shard_map/ppermute | solution.py:102
  378.8 40.9 %collective-permute-start.13 = (bf16[256,3072]{0,1:T(8,128)(2,1)}, bf16[256,3072]{0,1:T(8,128)(2,1)}, u32[]{:S(2)}, u32[]{:S(2)}) collective-permute-start(bf16[256,3072]{0,1:T(8,128)(2,1)} %collective-permute-done.11), channel_id=1, source_target_pairs={{8,0},{16,8},{24,16},{28,24},{20,28},{12,20},{4,12},{0,4},{9,1},{1... | collective-permute-start | bytes 4718600 | tf_op jit(solution)/shard_map/ppermute | solution.py:103
  409.3 71.7 %collective-permute-start.14 = (bf16[256,3072]{0,1:T(8,128)(2,1)}, bf16[256,3072]{0,1:T(8,128)(2,1)S(1)}, u32[]{:S(2)}, u32[]{:S(2)}) collective-permute-start(bf16[256,3072]{0,1:T(8,128)(2,1)} %collective-permute-done.12), channel_id=1, source_target_pairs={{0,8},{8,16},{16,24},{24,28},{28,20},{20,12},{12,4},{4,0},{1,9},{9... | collective-permute-start | bytes 4718600 | tf_op jit(solution)/shard_map/ppermute | solution.py:102
  419.7 61.2 %collective-permute-start.15 = (bf16[256,3072]{0,1:T(8,128)(2,1)}, bf16[256,3072]{0,1:T(8,128)(2,1)}, u32[]{:S(2)}, u32[]{:S(2)}) collective-permute-start(bf16[256,3072]{0,1:T(8,128)(2,1)} %collective-permute-done.13), channel_id=1, source_target_pairs={{8,0},{16,8},{24,16},{28,24},{20,28},{12,20},{4,12},{0,4},{9,1},{1... | collective-permute-start | bytes 4718600 | tf_op jit(solution)/shard_map/ppermute | solution.py:103
  499.0 27.0 %collective-permute-start.16 = (bf16[2,3,1024]{2,1,0:T(4,128)(2,1)S(1)}, bf16[2,3,1024]{2,1,0:T(4,128)(2,1)S(1)}, u32[]{:S(2)}, u32[]{:S(2)}) collective-permute-start(bf16[2,3,1024]{2,1,0:T(4,128)(2,1)S(1)} %slice.49), channel_id=1, source_target_pairs={{0,4},{4,8},{8,12},{12,16},{16,20},{20,24},{24,28},{1,5},{5,9},{9,... | collective-permute-start | bytes 36872 | tf_op jit(solution)/shard_map/ppermute | solution.py:11
  574.9 15.1 %collective-permute-start.17 = (bf16[127,1024]{0,1:T(8,128)(2,1)}, bf16[127,1024]{0,1:T(8,128)(2,1)S(1)}, u32[]{:S(2)}, u32[]{:S(2)}) collective-permute-start(bf16[127,1024]{0,1:T(8,128)(2,1)} %slice_bitcast_fusion.1), channel_id=1, source_target_pairs={{0,4},{4,8},{8,12},{12,16},{16,20},{20,24},{24,28},{1,5},{5,9},{9,... | collective-permute-start | bytes 780296 | tf_op jit(solution)/shard_map/ppermute | solution.py:11
  641.4 32.5 %reduce-scatter.3.cloned.1.call-start = ((), (), s32[]{:S(2)}) async-start(), calls=%async_computation.3 | async-start | bytes 9437184 | tf_op jit(solution)/shard_map/reduce_scatter | solution.py:161
  655.8 70.6 %collective-permute-start.33 = (bf16[768,2048]{1,0:T(8,128)(2,1)}, bf16[768,2048]{1,0:T(8,128)(2,1)}, u32[]{:S(2)}, u32[]{:S(2)}) collective-permute-start(bf16[768,2048]{1,0:T(8,128)(2,1)} %reduce-scatter.5.cloned.1.call-done), channel_id=1, source_target_pairs={{0,2},{2,0},{1,3},{3,1},{4,6},{6,4},{5,7},{7,5},{8,10},{10,8},{9,1... | collective-permute-start | bytes 9437192 | tf_op jit(solution)/shard_map/ppermute | solution.py:15
  (19 other events, 773.2 us)
Sparse Core Ops, SparseCore 0:
  84.0 26.4 all-gather.1
  641.5 14.2 reduce-scatter.4
  658.2 15.6 reduce-scatter.2

commit v12 on v9

--- a/solution.py
+++ b/solution.py
@@ -68,13 +68,6 @@
     other = 1 - half
     half_width = local_width // 2
 
-    pair_tokens = pair_ordered(tokens, swap_pair(tokens), half, 0)
-    pair_tokens = lax.all_gather(pair_tokens, "tp", axis=1, tiled=True)
-    row_count = pair_tokens.shape[0]
-    wide_float = pair_tokens.astype(jnp.float32)
-    scale = lax.rsqrt(jnp.mean(wide_float * wide_float, axis=-1, keepdims=True) + 1e-06)
-    normed = (wide_float * scale * norm_gain).astype(jnp.bfloat16)
-
     own_piece = half_of(w_in, 2, half).reshape(w_rows, 3 * half_width)
     partner_piece = swap_pair(half_of(w_in, 2, other)).reshape(w_rows, 3 * half_width)
     order = ring_order(n_hi)
@@ -101,7 +94,15 @@
         return lax.dynamic_update_slice_in_dim(buffer, piece[:, None], ctx_index, axis=1)
 
     current, previous = toeplitz_pair(half_of(long_filter, 1, half))
+    chunks = max(c for c in range(1, min(n_hi - 1, 6) + 1) if own_rows % c == 0)
+    chunk_rows = own_rows // chunks
+    arrived_tokens = []
     for step in range(n_hi):
+        if 0 < step <= chunks:
+            sending, own_piece = lax.optimization_barrier(
+                (tokens[(step - 1) * chunk_rows : step * chunk_rows], own_piece)
+            )
+            arrived_tokens.append(swap_pair(sending))
         if step > 0:
             own_piece = lax.ppermute(own_piece, "hi", forward)
             partner_piece = lax.ppermute(partner_piece, "hi", backward)
@@ -114,6 +115,14 @@
         gathered_o = store_out(gathered_o, own_out, own_at)
         gathered_o = store_out(gathered_o, partner_out, partner_at)
     o_full = gathered_o.reshape(half_width, n_ctx * e_cols)
+
+    pair_tokens = pair_ordered(tokens, jnp.concatenate(arrived_tokens, axis=0), half, 0)
+    pair_tokens = lax.all_gather(pair_tokens, "tp", axis=1, tiled=True)
+    row_count = pair_tokens.shape[0]
+    wide_float = pair_tokens.astype(jnp.float32)
+    scale = lax.rsqrt(jnp.mean(wide_float * wide_float, axis=-1, keepdims=True) + 1e-06)
+    normed = (wide_float * scale * norm_gain).astype(jnp.bfloat16)
+
 
     projected = jnp.dot(
         normed,

time: 734 us -> 881 us (1.20)
  waiting for transfers between devices: 337 us -> 467 us
  starting transfers between devices: 43.2 us -> 55.9 us
    ppermute x7, waiting for transfers between devices: 29.4 us -> 138 us  [local(): own_piece = lax.ppermute(own_piece, 'hi', forward)]
    ppermute x7, waiting for transfers between devices: 30.9 us -> 104 us  [local(): partner_out = lax.ppermute(partner_out, 'hi', backward)]
    ppermute x7, waiting for transfers between devices: 72.5 us -> 0.02 us  [local(): own_out = lax.ppermute(own_out, 'hi', forward)]
    ppermute x7, waiting for transfers between devices: 48.3 us -> 72.3 us  [local(): partner_piece = lax.ppermute(partner_piece, 'hi', backward)]
    unnamed x32 -> x45, local copies, waits for them, and re-layouts: 17.4 us -> 21.8 us
    ppermute x4 -> x9, waiting for transfers between devices: 137 us -> 135 us  [swap_pair(): return lax.ppermute(value, 'lo', [(0, 1), (1, 0)])]
  transfers between devices with their start and end apart: 37 -> 42, of which waited for: 22 -> 24; matrix products, arithmetic and copies ran while one was open for 33% -> 27% of each run, Pallas kernels for 0% -> 0%
where the time goes in v12:
time: 881 us; the launch traced here: 871 us
  waiting for transfers between devices  467 us (53%)
  local copies, waits for them, and re-layouts  165 us (19%)
  matrix products  86 us (10%)
  other arithmetic  62.6 us (7%)
  starting transfers between devices  55.9 us (6%)
  between operations  34.7 us (4%)
    ppermute x7, waiting for transfers between devices, local(): own_piece = lax.ppermute(own_piece, 'hi', forward)  138 us
    ppermute x9, waiting for transfers between devices, swap_pair(): return lax.ppermute(value, 'lo', [(0, 1), (1, 0)])  135 us
    ppermute x7, waiting for transfers between devices, local(): partner_out = lax.ppermute(partner_out, 'hi', backward)  104 us
    ppermute x7, waiting for transfers between devices, local(): partner_piece = lax.ppermute(partner_piece, 'hi', backward)  72.3 us
    dot_general x1, matrix products, local(): jnp.dot(normed, gathered_w.reshape(n_ctx * w_rows, 3 * half_width), prefe...  47.9 us
    dynamic_update_slice x16, local copies, waits for them, and re-layouts, store_out(): lax.dynamic_update_slice_in_dim(buffer, piece[:, None], ctx_index, axis=1)  25.8 us
    dot_general x2, matrix products, out_terms(): jnp.dot(rows, o_full, preferred_element_type=jnp.float32)  24.8 us
    broadcast_in_dim x14, local copies, waits for them, and re-layouts, store(): piece[None]  23.1 us
  transfers between devices with their start and end apart: 42, of which 24 were waited for; matrix products, arithmetic and copies ran while one was open for 27% of the time, Pallas kernels for 0%

profile of v12, /device:TPU:0, one launch (start us, length us, event | category | flops | bytes accessed | tf_op | source)
XLA Modules:
  0.0 870.8 jit_solution(1440174648051330252)
XLA Ops:
  18.2 34.5 %collective-permute-done.1 = bf16[256,3072]{0,1:T(8,128)(2,1)S(1)} collective-permute-done((bf16[256,3072]{0,1:T(8,128)(2,1)}, bf16[256,3072]{0,1:T(8,128)(2,1)S(1)}, u32[]{:S(2)}, u32[]{:S(2)}) %collective-permute-start.1) | collective-permute-done | bytes 1572896 | tf_op jit(solution)/shard_map/ppermute | solution.py:107
  54.5 33.8 %collective-permute-done.3 = bf16[256,3072]{0,1:T(8,128)(2,1)S(1)} collective-permute-done((bf16[256,3072]{0,1:T(8,128)(2,1)S(1)}, bf16[256,3072]{0,1:T(8,128)(2,1)S(1)}, u32[]{:S(2)}, u32[]{:S(2)}) %collective-permute-start.3) | collective-permute-done | bytes 1572896 | tf_op jit(solution)/shard_map/ppermute | solution.py:107
  89.8 33.2 %collective-permute-done.5 = bf16[256,3072]{0,1:T(8,128)(2,1)S(1)} collective-permute-done((bf16[256,3072]{0,1:T(8,128)(2,1)S(1)}, bf16[256,3072]{0,1:T(8,128)(2,1)S(1)}, u32[]{:S(2)}, u32[]{:S(2)}) %collective-permute-start.5) | collective-permute-done | bytes 1572896 | tf_op jit(solution)/shard_map/ppermute | solution.py:107
  125.2 33.2 %collective-permute-done.7 = bf16[256,3072]{0,1:T(8,128)(2,1)} collective-permute-done((bf16[256,3072]{0,1:T(8,128)(2,1)S(1)}, bf16[256,3072]{0,1:T(8,128)(2,1)}, u32[]{:S(2)}, u32[]{:S(2)}) %collective-permute-start.7) | collective-permute-done | bytes 1572896 | tf_op jit(solution)/shard_map/ppermute | solution.py:107
  166.3 8.5 collective-permute-done
  177.3 8.7 collective-permute-done.2
  192.4 4.9 collective-permute-done.4
  198.3 43.7 %collective-permute-done.6 = bf16[128,2048]{1,0:T(8,128)(2,1)S(1)} collective-permute-done((bf16[128,2048]{1,0:T(8,128)(2,1)}, bf16[128,2048]{1,0:T(8,128)(2,1)S(1)}, u32[]{:S(2)}, u32[]{:S(2)}) %collective-permute-start.6) | collective-permute-done | bytes 524320 | tf_op jit(solution)/shard_map/ppermute | solution.py:15
  242.1 10.9 %collective-permute-done.8 = bf16[128,2048]{1,0:T(8,128)(2,1)S(1)} collective-permute-done((bf16[128,2048]{1,0:T(8,128)(2,1)}, bf16[128,2048]{1,0:T(8,128)(2,1)S(1)}, u32[]{:S(2)}, u32[]{:S(2)}) %collective-permute-start.8) | collective-permute-done | bytes 524320 | tf_op jit(solution)/shard_map/ppermute | solution.py:15
  253.0 5.6 collective-permute-done.10
  264.4 32.8 %collective-permute-done.12 = bf16[256,3072]{0,1:T(8,128)(2,1)} collective-permute-done((bf16[256,3072]{0,1:T(8,128)(2,1)}, bf16[256,3072]{0,1:T(8,128)(2,1)}, u32[]{:S(2)}, u32[]{:S(2)}) %collective-permute-start.12) | collective-permute-done | bytes 1572896 | tf_op jit(solution)/shard_map/ppermute | solution.py:108
  318.1 8.7 broadcast_in_dim.101
  358.3 19.4 %collective-permute-done.25 = bf16[1024,256]{0,1:T(8,128)(2,1)S(1)} collective-permute-done((bf16[1024,256]{0,1:T(8,128)(2,1)}, bf16[1024,256]{0,1:T(8,128)(2,1)S(1)}, u32[]{:S(2)}, u32[]{:S(2)}) %collective-permute-start.25) | collective-permute-done | bytes 524320 | tf_op jit(solution)/shard_map/ppermute | solution.py:110
  383.3 9.2 %collective-permute-done.27 = bf16[1024,256]{0,1:T(8,128)(2,1)} collective-permute-done((bf16[1024,256]{0,1:T(8,128)(2,1)S(1)}, bf16[1024,256]{0,1:T(8,128)(2,1)}, u32[]{:S(2)}, u32[]{:S(2)}) %collective-permute-start.27) | collective-permute-done | bytes 524320 | tf_op jit(solution)/shard_map/ppermute | solution.py:110
  412.8 36.8 %collective-permute-done.31 = bf16[1024,256]{0,1:T(8,128)(2,1)S(1)} collective-permute-done((bf16[1024,256]{0,1:T(8,128)(2,1)}, bf16[1024,256]{0,1:T(8,128)(2,1)S(1)}, u32[]{:S(2)}, u32[]{:S(2)}) %collective-permute-start.31) | collective-permute-done | bytes 524320 | tf_op jit(solution)/shard_map/ppermute | solution.py:110
  459.0 5.6 collective-permute-done.33
  476.4 30.0 %collective-permute-done.35 = bf16[1024,256]{0,1:T(8,128)(2,1)} collective-permute-done((bf16[1024,256]{0,1:T(8,128)(2,1)}, bf16[1024,256]{0,1:T(8,128)(2,1)}, u32[]{:S(2)}, u32[]{:S(2)}) %collective-permute-start.35) | collective-permute-done | bytes 524320 | tf_op jit(solution)/shard_map/ppermute | solution.py:110
  526.3 25.9 %collective-permute-done.18 = bf16[256,3072]{0,1:T(8,128)(2,1)} collective-permute-done((bf16[256,3072]{0,1:T(8,128)(2,1)}, bf16[256,3072]{0,1:T(8,128)(2,1)}, u32[]{:S(2)}, u32[]{:S(2)}) %collective-permute-start.18) | collective-permute-done | bytes 1572896 | tf_op jit(solution)/shard_map/ppermute | solution.py:108
  567.4 9.9 %collective-permute-done.20 = bf16[256,3072]{0,1:T(8,128)(2,1)} collective-permute-done((bf16[256,3072]{0,1:T(8,128)(2,1)}, bf16[256,3072]{0,1:T(8,128)(2,1)}, u32[]{:S(2)}, u32[]{:S(2)}) %collective-permute-start.20) | collective-permute-done | bytes 1572896 | tf_op jit(solution)/shard_map/ppermute | solution.py:108
  580.4 7.1 fusion
  587.4 47.9 %fusion.9 = bf16[1536,3072]{1,0:T(8,128)(2,1)S(1)} fusion(bf16[4096,3072]{1,0:T(8,128)(2,1)} %bitcast.35, bf16[1536,4096]{1,0:T(8,128)(2,1)} %all-gather.2.cloned.1.call-done, f32[4096]{0:T(1024)S(1)} %copy-done.16, f32[1536]{0:T(1024)S(1)} %add_rsqrt_fusion), kind=kOutput, calls=%fused_computation.13 | convolution fusion | flops 38684590080 | bytes 47208448 | tf_op jit(solution)/shard_map/dot_general | solution.py:127
  645.0 12.8 %copy.40 = bf16[1536,3072]{0,1:T(8,128)(2,1)} copy(bf16[1536,3072]{1,0:T(8,128)(2,1)} %copy-done.7) | data formatting | bytes 18874368 | tf_op jit(solution)/shard_map/convert_element_type | solution.py:132
  658.2 15.1 %maximum_convert_fusion = f32[1538,3,1024]{0,2,1:T(8,128)} fusion(bf16[1536,3,1024]{0,2,1:T(8,128)(2,1)} %bitcast.110, bf16[2,3,1024]{0,2,1:T(8,128)(2,1)S(1)} %copy.41), kind=kLoop, calls=%fused_computation.14 | loop fusion | flops 18898944 | bytes 28348416 | tf_op jit(solution)/shard_map/convert_element_type | solution.py:34
  673.4 22.2 %fusion.3 = f32[1536,3,1024]{0,2,1:T(8,128)S(1)} fusion(f32[1538,3,1024]{0,2,1:T(8,128)} %maximum_convert_fusion, f32[3,1024]{1,0:T(4,128)S(1)} %get-tuple-element.43, f32[3,1024]{1,0:T(4,128)S(1)} %get-tuple-element.42, f32[3,1024]{1,0:T(4,128)S(1)} %get-tuple-element.41), kind=kLoop, calls=%fused_computation.6 | loop fusion | flops 23592960 | bytes 75534336 | tf_op jit(solution)/shard_map/add | solution.py:38
  695.6 6.4 copy-done.2
  722.4 13.2 %concatenate.15 = bf16[1664,1024]{1,0:T(8,128)(2,1)S(1)} concatenate(bf16[1,1024]{1,0:T(2,128)(2,1)S(1)} %broadcast_in_dim.116, bf16[127,1024]{1,0:T(8,128)(2,1)} %copy.46, bf16[1536,1024]{1,0:T(8,128)(2,1)} %bitcast.112), dimensions={0} | concatenate | bytes 6815744 | tf_op jit(solution)/shard_map/concatenate | solution.py:141
  744.6 5.4 fusion.17
  760.3 12.5 %convolution_convert_fusion = bf16[768,4096]{1,0:T(8,128)(2,1)} fusion(bf16[1024,4096]{0,1:T(8,128)(2,1)} %bitcast.62, bf16[1536,1024]{0,1:T(8,128)(2,1)S(1)} %fusion.14, s32[]{:T(128)S(6)} %select_n.262), kind=kOutput, calls=%fused_computation.20 | convolution fusion | flops 6445596672 | bytes 16252932 | tf_op jit(solution)/shard_map/dot_general | solution.py:156
  772.9 12.3 %convolution_convert_fusion.1 = bf16[768,4096]{1,0:T(8,128)(2,1)} fusion(bf16[1024,4096]{0,1:T(8,128)(2,1)} %bitcast.62, bf16[1536,1024]{0,1:T(8,128)(2,1)S(1)} %fusion.14, s32[]{:T(128)S(6)} %select_n.261), kind=kOutput, calls=%fused_computation.21 | convolution fusion | flops 6445596672 | bytes 16252932 | tf_op jit(solution)/shard_map/dot_general | solution.py:156
  788.3 16.4 %reduce-scatter.3.cloned.1.call-done = bf16[768,2048]{1,0:T(8,128)(2,1)} async-done(((bf16[768,4096]{1,0:T(8,128)(2,1)}), bf16[768,2048]{1,0:T(8,128)(2,1)}) %reduce-scatter.3.cloned.1.call-update) | async-done | bytes 3145744 | tf_op jit(solution)/shard_map/reduce_scatter | solution.py:157
  804.7 52.5 %collective-permute-done.38 = bf16[768,2048]{1,0:T(8,128)(2,1)} collective-permute-done((bf16[768,2048]{1,0:T(8,128)(2,1)}, bf16[768,2048]{1,0:T(8,128)(2,1)}, u32[]{:S(2)}, u32[]{:S(2)}) %collective-permute-start.38) | collective-permute-done | bytes 3145760 | tf_op jit(solution)/shard_map/ppermute | solution.py:15
  857.2 6.6 add_convert_fusion
  (187 shorter events, 210.4 us)
Async XLA Ops:
  6.5 573.8 %all-gather.2.cloned.1.call-start = ((), (), s32[]{:S(2)}) async-start(), calls=%async_computation.2 | async-start | bytes 18874368 | tf_op jit(solution)/shard_map/all_gather | solution.py:120
  15.1 37.6 %collective-permute-start.1 = (bf16[256,3072]{0,1:T(8,128)(2,1)}, bf16[256,3072]{0,1:T(8,128)(2,1)S(1)}, u32[]{:S(2)}, u32[]{:S(2)}) collective-permute-start(bf16[256,3072]{0,1:T(8,128)(2,1)} %bitcast.113), channel_id=1, source_target_pairs={{0,8},{8,16},{16,24},{24,28},{28,20},{20,12},{12,4},{4,0},{1,9},{9... | collective-permute-start | bytes 4718600 | tf_op jit(solution)/shard_map/ppermute | solution.py:107
  52.7 35.6 %collective-permute-start.3 = (bf16[256,3072]{0,1:T(8,128)(2,1)S(1)}, bf16[256,3072]{0,1:T(8,128)(2,1)S(1)}, u32[]{:S(2)}, u32[]{:S(2)}) collective-permute-start(bf16[256,3072]{0,1:T(8,128)(2,1)S(1)} %collective-permute-done.1), channel_id=1, source_target_pairs={{0,8},{8,16},{16,24},{24,28},{28,20},{20,12},{12,4},{4,0},{1,9},{9... | collective-permute-start | bytes 4718600 | tf_op jit(solution)/shard_map/ppermute | solution.py:107
  88.3 34.7 %collective-permute-start.5 = (bf16[256,3072]{0,1:T(8,128)(2,1)S(1)}, bf16[256,3072]{0,1:T(8,128)(2,1)S(1)}, u32[]{:S(2)}, u32[]{:S(2)}) collective-permute-start(bf16[256,3072]{0,1:T(8,128)(2,1)S(1)} %collective-permute-done.3), channel_id=1, source_target_pairs={{0,8},{8,16},{16,24},{24,28},{28,20},{20,12},{12,4},{4,0},{1,9},{9... | collective-permute-start | bytes 4718600 | tf_op jit(solution)/shard_map/ppermute | solution.py:107
  124.1 34.3 %collective-permute-start.7 = (bf16[256,3072]{0,1:T(8,128)(2,1)S(1)}, bf16[256,3072]{0,1:T(8,128)(2,1)}, u32[]{:S(2)}, u32[]{:S(2)}) collective-permute-start(bf16[256,3072]{0,1:T(8,128)(2,1)S(1)} %collective-permute-done.5), channel_id=1, source_target_pairs={{0,8},{8,16},{16,24},{24,28},{28,20},{20,12},{12,4},{4,0},{1,9},{9... | collective-permute-start | bytes 4718600 | tf_op jit(solution)/shard_map/ppermute | solution.py:107
  158.4 33.2 %collective-permute-start.9 = (bf16[256,3072]{0,1:T(8,128)(2,1)}, bf16[256,3072]{0,1:T(8,128)(2,1)}, u32[]{:S(2)}, u32[]{:S(2)}) collective-permute-start(bf16[256,3072]{0,1:T(8,128)(2,1)} %collective-permute-done.7), channel_id=1, source_target_pairs={{0,8},{8,16},{16,24},{24,28},{28,20},{20,12},{12,4},{4,0},{1,9},{9... | collective-permute-start | bytes 4718600 | tf_op jit(solution)/shard_map/ppermute | solution.py:107
  161.6 35.6 %collective-permute-start.4 = (bf16[128,2048]{1,0:T(8,128)(2,1)}, bf16[128,2048]{1,0:T(8,128)(2,1)}, u32[]{:S(2)}, u32[]{:S(2)}) collective-permute-start(bf16[128,2048]{1,0:T(8,128)(2,1)} %get-tuple-element.21), channel_id=1, source_target_pairs={{0,2},{2,0},{1,3},{3,1},{4,6},{6,4},{5,7},{7,5},{8,10},{10,8},{9,1... | collective-permute-start | bytes 1572872 | tf_op jit(solution)/shard_map/ppermute | solution.py:15
  165.7 97.1 %collective-permute-start.11 = (bf16[256,3,1024]{0,2,1:T(8,128)(2,1)}, bf16[256,3,1024]{0,2,1:T(8,128)(2,1)}, u32[]{:S(2)}, u32[]{:S(2)}) collective-permute-start(bf16[256,3,1024]{0,2,1:T(8,128)(2,1)} %copy.60), channel_id=1, source_target_pairs={{0,2},{2,0},{1,3},{3,1},{4,6},{6,4},{5,7},{7,5},{8,10},{10,8},{9,1... | collective-permute-start | bytes 4718600 | tf_op jit(solution)/shard_map/ppermute | solution.py:15
  174.8 67.3 %collective-permute-start.6 = (bf16[128,2048]{1,0:T(8,128)(2,1)}, bf16[128,2048]{1,0:T(8,128)(2,1)S(1)}, u32[]{:S(2)}, u32[]{:S(2)}) collective-permute-start(bf16[128,2048]{1,0:T(8,128)(2,1)} %get-tuple-element.23), channel_id=1, source_target_pairs={{0,2},{2,0},{1,3},{3,1},{4,6},{6,4},{5,7},{7,5},{8,10},{10,8},{9,1... | collective-permute-start | bytes 1572872 | tf_op jit(solution)/shard_map/ppermute | solution.py:15
  186.0 67.0 %collective-permute-start.8 = (bf16[128,2048]{1,0:T(8,128)(2,1)}, bf16[128,2048]{1,0:T(8,128)(2,1)S(1)}, u32[]{:S(2)}, u32[]{:S(2)}) collective-permute-start(bf16[128,2048]{1,0:T(8,128)(2,1)} %get-tuple-element.25), channel_id=1, source_target_pairs={{0,2},{2,0},{1,3},{3,1},{4,6},{6,4},{5,7},{7,5},{8,10},{10,8},{9,1... | collective-permute-start | bytes 1572872 | tf_op jit(solution)/shard_map/ppermute | solution.py:15
  191.6 67.0 %collective-permute-start.10 = (bf16[128,2048]{1,0:T(8,128)(2,1)}, bf16[128,2048]{1,0:T(8,128)(2,1)S(1)}, u32[]{:S(2)}, u32[]{:S(2)}) collective-permute-start(bf16[128,2048]{1,0:T(8,128)(2,1)} %get-tuple-element.27), channel_id=1, source_target_pairs={{0,2},{2,0},{1,3},{3,1},{4,6},{6,4},{5,7},{7,5},{8,10},{10,8},{9,1... | collective-permute-start | bytes 1572872 | tf_op jit(solution)/shard_map/ppermute | solution.py:15
  262.8 523.8 %reduce-scatter.5.cloned.1.call-start = ((), (), s32[]{:S(2)}) async-start(), calls=%async_computation.4 | async-start | bytes 9437184 | tf_op jit(solution)/shard_map/reduce_scatter | solution.py:157
  262.9 34.3 %collective-permute-start.12 = (bf16[256,3072]{0,1:T(8,128)(2,1)}, bf16[256,3072]{0,1:T(8,128)(2,1)}, u32[]{:S(2)}, u32[]{:S(2)}) collective-permute-start(bf16[256,3072]{0,1:T(8,128)(2,1)} %bitcast.8), channel_id=1, source_target_pairs={{8,0},{16,8},{24,16},{28,24},{20,28},{12,20},{4,12},{0,4},{9,1},{1... | collective-permute-start | bytes 4718600 | tf_op jit(solution)/shard_map/ppermute | solution.py:108
  297.2 34.6 %collective-permute-start.13 = (bf16[256,3072]{0,1:T(8,128)(2,1)}, bf16[256,3072]{0,1:T(8,128)(2,1)}, u32[]{:S(2)}, u32[]{:S(2)}) collective-permute-start(bf16[256,3072]{0,1:T(8,128)(2,1)} %collective-permute-done.12), channel_id=1, source_target_pairs={{8,0},{16,8},{24,16},{28,24},{20,28},{12,20},{4,12},{0,4},{9,1},{1... | collective-permute-start | bytes 4718600 | tf_op jit(solution)/shard_map/ppermute | solution.py:108
  301.2 35.0 %collective-permute-start.23 = (bf16[1024,256]{0,1:T(8,128)(2,1)}, bf16[1024,256]{0,1:T(8,128)(2,1)}, u32[]{:S(2)}, u32[]{:S(2)}) collective-permute-start(bf16[1024,256]{0,1:T(8,128)(2,1)} %copy.63), channel_id=1, source_target_pairs={{0,2},{2,0},{1,3},{3,1},{4,6},{6,4},{5,7},{7,5},{8,10},{10,8},{9,1... | collective-permute-start | bytes 1572872 | tf_op jit(solution)/shard_map/ppermute | solution.py:15
  302.7 33.9 %collective-permute-start.24 = (bf16[1024,256]{0,1:T(8,128)(2,1)}, bf16[1024,256]{0,1:T(8,128)(2,1)}, u32[]{:S(2)}, u32[]{:S(2)}) collective-permute-start(bf16[1024,256]{0,1:T(8,128)(2,1)} %copy.62), channel_id=1, source_target_pairs={{0,8},{8,16},{16,24},{24,28},{28,20},{20,12},{12,4},{4,0},{1,9},{9... | collective-permute-start | bytes 1572872 | tf_op jit(solution)/shard_map/ppermute | solution.py:109
  331.7 62.8 %collective-permute-start.14 = (bf16[256,3072]{0,1:T(8,128)(2,1)}, bf16[256,3072]{0,1:T(8,128)(2,1)}, u32[]{:S(2)}, u32[]{:S(2)}) collective-permute-start(bf16[256,3072]{0,1:T(8,128)(2,1)} %collective-permute-done.13), channel_id=1, source_target_pairs={{8,0},{16,8},{24,16},{28,24},{20,28},{12,20},{4,12},{0,4},{9,1},{1... | collective-permute-start | bytes 4718600 | tf_op jit(solution)/shard_map/ppermute | solution.py:108
  336.3 41.4 %collective-permute-start.25 = (bf16[1024,256]{0,1:T(8,128)(2,1)}, bf16[1024,256]{0,1:T(8,128)(2,1)S(1)}, u32[]{:S(2)}, u32[]{:S(2)}) collective-permute-start(bf16[1024,256]{0,1:T(8,128)(2,1)} %collective-permute-done.23), channel_id=1, source_target_pairs={{8,0},{16,8},{24,16},{28,24},{20,28},{12,20},{4,12},{0,4},{9,1},{1... | collective-permute-start | bytes 1572872 | tf_op jit(solution)/shard_map/ppermute | solution.py:110
  336.5 42.9 %collective-permute-start.26 = (bf16[1024,256]{0,1:T(8,128)(2,1)}, bf16[1024,256]{0,1:T(8,128)(2,1)S(1)}, u32[]{:S(2)}, u32[]{:S(2)}) collective-permute-start(bf16[1024,256]{0,1:T(8,128)(2,1)} %collective-permute-done.24), channel_id=1, source_target_pairs={{0,8},{8,16},{16,24},{24,28},{28,20},{20,12},{12,4},{4,0},{1,9},{9... | collective-permute-start | bytes 1572872 | tf_op jit(solution)/shard_map/ppermute | solution.py:109
  394.5 59.0 %collective-permute-start.15 = (bf16[256,3072]{0,1:T(8,128)(2,1)}, bf16[256,3072]{0,1:T(8,128)(2,1)}, u32[]{:S(2)}, u32[]{:S(2)}) collective-permute-start(bf16[256,3072]{0,1:T(8,128)(2,1)} %collective-permute-done.14), channel_id=1, source_target_pairs={{8,0},{16,8},{24,16},{28,24},{20,28},{12,20},{4,12},{0,4},{9,1},{1... | collective-permute-start | bytes 4718600 | tf_op jit(solution)/shard_map/ppermute | solution.py:108
  407.7 42.0 %collective-permute-start.31 = (bf16[1024,256]{0,1:T(8,128)(2,1)}, bf16[1024,256]{0,1:T(8,128)(2,1)S(1)}, u32[]{:S(2)}, u32[]{:S(2)}) collective-permute-start(bf16[1024,256]{0,1:T(8,128)(2,1)} %collective-permute-done.29), channel_id=1, source_target_pairs={{8,0},{16,8},{24,16},{28,24},{20,28},{12,20},{4,12},{0,4},{9,1},{1... | collective-permute-start | bytes 1572872 | tf_op jit(solution)/shard_map/ppermute | solution.py:110
  409.5 42.0 %collective-permute-start.32 = (bf16[1024,256]{0,1:T(8,128)(2,1)}, bf16[1024,256]{0,1:T(8,128)(2,1)S(1)}, u32[]{:S(2)}, u32[]{:S(2)}) collective-permute-start(bf16[1024,256]{0,1:T(8,128)(2,1)} %collective-permute-done.30), channel_id=1, source_target_pairs={{0,8},{8,16},{16,24},{24,28},{28,20},{20,12},{12,4},{4,0},{1,9},{9... | collective-permute-start | bytes 1572872 | tf_op jit(solution)/shard_map/ppermute | solution.py:109
  453.5 56.5 %collective-permute-start.16 = (bf16[256,3072]{0,1:T(8,128)(2,1)}, bf16[256,3072]{0,1:T(8,128)(2,1)}, u32[]{:S(2)}, u32[]{:S(2)}) collective-permute-start(bf16[256,3072]{0,1:T(8,128)(2,1)} %collective-permute-done.15), channel_id=1, source_target_pairs={{8,0},{16,8},{24,16},{28,24},{20,28},{12,20},{4,12},{0,4},{9,1},{1... | collective-permute-start | bytes 4718600 | tf_op jit(solution)/shard_map/ppermute | solution.py:108
  464.6 41.9 %collective-permute-start.35 = (bf16[1024,256]{0,1:T(8,128)(2,1)}, bf16[1024,256]{0,1:T(8,128)(2,1)}, u32[]{:S(2)}, u32[]{:S(2)}) collective-permute-start(bf16[1024,256]{0,1:T(8,128)(2,1)} %collective-permute-done.33), channel_id=1, source_target_pairs={{8,0},{16,8},{24,16},{28,24},{20,28},{12,20},{4,12},{0,4},{9,1},{1... | collective-permute-start | bytes 1572872 | tf_op jit(solution)/shard_map/ppermute | solution.py:110
  466.4 243.0 %collective-permute-start.36 = (bf16[1024,256]{0,1:T(8,128)(2,1)}, bf16[1024,256]{0,1:T(8,128)(2,1)}, u32[]{:S(2)}, u32[]{:S(2)}) collective-permute-start(bf16[1024,256]{0,1:T(8,128)(2,1)} %collective-permute-done.34), channel_id=1, source_target_pairs={{0,8},{8,16},{16,24},{24,28},{28,20},{20,12},{12,4},{4,0},{1,9},{9... | collective-permute-start | bytes 1572872 | tf_op jit(solution)/shard_map/ppermute | solution.py:109
  469.8 48.7 %collective-permute-start.17 = (bf16[256,3072]{0,1:T(8,128)(2,1)}, bf16[256,3072]{0,1:T(8,128)(2,1)}, u32[]{:S(2)}, u32[]{:S(2)}) collective-permute-start(bf16[256,3072]{0,1:T(8,128)(2,1)} %collective-permute-done.9), channel_id=1, source_target_pairs={{0,8},{8,16},{16,24},{24,28},{28,20},{20,12},{12,4},{4,0},{1,9},{9... | collective-permute-start | bytes 4718600 | tf_op jit(solution)/shard_map/ppermute | solution.py:107
  506.5 204.9 %collective-permute-start.37 = (bf16[1024,256]{0,1:T(8,128)(2,1)}, bf16[1024,256]{0,1:T(8,128)(2,1)}, u32[]{:S(2)}, u32[]{:S(2)}) collective-permute-start(bf16[1024,256]{0,1:T(8,128)(2,1)} %collective-permute-done.35), channel_id=1, source_target_pairs={{8,0},{16,8},{24,16},{28,24},{20,28},{12,20},{4,12},{0,4},{9,1},{1... | collective-permute-start | bytes 1572872 | tf_op jit(solution)/shard_map/ppermute | solution.py:110
  510.0 42.2 %collective-permute-start.18 = (bf16[256,3072]{0,1:T(8,128)(2,1)}, bf16[256,3072]{0,1:T(8,128)(2,1)}, u32[]{:S(2)}, u32[]{:S(2)}) collective-permute-start(bf16[256,3072]{0,1:T(8,128)(2,1)} %collective-permute-done.16), channel_id=1, source_target_pairs={{8,0},{16,8},{24,16},{28,24},{20,28},{12,20},{4,12},{0,4},{9,1},{1... | collective-permute-start | bytes 4718600 | tf_op jit(solution)/shard_map/ppermute | solution.py:108
  518.5 44.5 %collective-permute-start.19 = (bf16[256,3072]{0,1:T(8,128)(2,1)}, bf16[256,3072]{0,1:T(8,128)(2,1)}, u32[]{:S(2)}, u32[]{:S(2)}) collective-permute-start(bf16[256,3072]{0,1:T(8,128)(2,1)} %collective-permute-done.17), channel_id=1, source_target_pairs={{0,8},{8,16},{16,24},{24,28},{28,20},{20,12},{12,4},{4,0},{1,9},{9... | collective-permute-start | bytes 4718600 | tf_op jit(solution)/shard_map/ppermute | solution.py:107
  552.2 25.1 %collective-permute-start.20 = (bf16[256,3072]{0,1:T(8,128)(2,1)}, bf16[256,3072]{0,1:T(8,128)(2,1)}, u32[]{:S(2)}, u32[]{:S(2)}) collective-permute-start(bf16[256,3072]{0,1:T(8,128)(2,1)} %collective-permute-done.18), channel_id=1, source_target_pairs={{8,0},{16,8},{24,16},{28,24},{20,28},{12,20},{4,12},{0,4},{9,1},{1... | collective-permute-start | bytes 4718600 | tf_op jit(solution)/shard_map/ppermute | solution.py:108
  772.9 31.9 %reduce-scatter.3.cloned.1.call-start = ((), (), s32[]{:S(2)}) async-start(), calls=%async_computation.3 | async-start | bytes 9437184 | tf_op jit(solution)/shard_map/reduce_scatter | solution.py:157
  786.6 70.6 %collective-permute-start.38 = (bf16[768,2048]{1,0:T(8,128)(2,1)}, bf16[768,2048]{1,0:T(8,128)(2,1)}, u32[]{:S(2)}, u32[]{:S(2)}) collective-permute-start(bf16[768,2048]{1,0:T(8,128)(2,1)} %reduce-scatter.5.cloned.1.call-done), channel_id=1, source_target_pairs={{0,2},{2,0},{1,3},{3,1},{4,6},{6,4},{5,7},{7,5},{8,10},{10,8},{9,1... | collective-permute-start | bytes 9437192 | tf_op jit(solution)/shard_map/ppermute | solution.py:15
  (28 other events, 1005.2 us)
Sparse Core Ops, SparseCore 0:
  262.9 25.1 all-gather.1
  773.0 13.5 reduce-scatter.4
  789.0 15.6 reduce-scatter.2

commit v13 on v9

--- a/solution.py
+++ b/solution.py
@@ -27,18 +27,6 @@
         return jnp.einsum("gm,mts->gts", table, hot.astype(table.dtype))
 
     return (spread(offset == tap), spread(offset + filter_len == tap))
-
-
-def featurize(extended, short_filter, count):
-    short_taps = short_filter.shape[0]
-    ext_float = extended.astype(jnp.float32)
-    featured = jnp.zeros((count,) + extended.shape[1:], jnp.float32)
-    for tap in range(short_taps):
-        featured = (
-            featured
-            + short_filter[tap] * ext_float[short_taps - 1 - tap : short_taps - 1 - tap + count]
-        )
-    return featured
 
 
 def half_of(value, axis, half):
@@ -124,10 +112,18 @@
 
     taps = half_of(short_filter, 2, half)
     prior_rows = shifted(projected[row_count - (short_taps - 1) :], "hi", 1)
-    featured = featurize(jnp.concatenate([prior_rows, projected], axis=0), taps, row_count)
-    mixed = (featured[:, 1] * featured[:, 2]).astype(jnp.bfloat16)
+    extended = jnp.concatenate([prior_rows, projected], axis=0)
+
+    def stream(index):
+        featured = jnp.zeros((row_count, half_width), jnp.float32)
+        for tap in range(short_taps):
+            rows = extended[short_taps - 1 - tap : short_taps - 1 - tap + row_count, index]
+            featured = featured + taps[tap, index] * rows.astype(jnp.float32)
+        return featured
+
+    mixed = (stream(1) * stream(2)).astype(jnp.bfloat16)
     mixed_prior = shifted(mixed[row_count - (filter_len - 1) :], "hi", 1)
-    query = featured[:, 0]
+    query = stream(0)
     zero_row = jnp.zeros((1, half_width), jnp.bfloat16)
     extended_mix = jnp.concatenate([zero_row, mixed_prior, mixed], axis=0)
     groups_here = long_filter.shape[1] // 2

time: 734 us -> 789 us (1.075)
  local copies, waits for them, and re-layouts: 158 us -> 189 us
  other arithmetic: 64.4 us -> 80.7 us
    ppermute x7, waiting for transfers between devices: 30.9 us -> 95.6 us  [local(): partner_out = lax.ppermute(partner_out, 'hi', backward)]
    ppermute x7, waiting for transfers between devices: 72.5 us -> 19.2 us  [local(): own_out = lax.ppermute(own_out, 'hi', forward)]
    convert_element_type x2 -> x6, local copies, waits for them, and re-layouts: 8.21 us -> 50.3 us  [stream(): featured = featured + taps[tap, index] * rows.astype(jnp.float32)]
    convert_element_type x2 -> x3, other arithmetic: 17.8 us -> 54.8 us  [the longest x2 37 us: local(): mixed = (stream(1) * stream(2)).astype(jnp.bfloat16)]
    add x1 -> x0, other arithmetic: 22.1 us -> none  [featurize(): featured + short_filter[tap] * ext_float[short_taps - 1 - tap:short_taps...]
    concatenate x1, local copies, waits for them, and re-layouts: 13.2 us -> 5.09 us  [local(): extended_mix = jnp.concatenate([zero_row, mixed_prior, mixed], axis=0)]
    unnamed x32 -> x68, local copies, waits for them, and re-layouts: 17.4 us -> 14.5 us
  transfers between devices with their start and end apart: 37 -> 37, of which waited for: 22 -> 16; matrix products, arithmetic and copies ran while one was open for 33% -> 28% of each run, Pallas kernels for 0% -> 0%
where the time goes in v13:
time: 789 us; the launch traced here: 777 us
  waiting for transfers between devices  340 us (43%)
  local copies, waits for them, and re-layouts  189 us (24%)
  matrix products  89.3 us (11%)
  other arithmetic  80.7 us (10%)
  starting transfers between devices  42.2 us (5%)
  between operations  35.6 us (5%)
    ppermute x4, waiting for transfers between devices, swap_pair(): return lax.ppermute(value, 'lo', [(0, 1), (1, 0)])  137 us
    ppermute x7, waiting for transfers between devices, local(): partner_out = lax.ppermute(partner_out, 'hi', backward)  95.6 us
    convert_element_type x6, local copies, waits for them, and re-layouts, stream(): featured = featured + taps[tap, index] * rows.astype(jnp.float32)  50.3 us
    dot_general x1, matrix products, local(): jnp.dot(normed, gathered_w.reshape(n_ctx * w_rows, 3 * half_width), prefe...  47.9 us
    ppermute x7, waiting for transfers between devices, local(): partner_piece = lax.ppermute(partner_piece, 'hi', backward)  43.9 us
    convert_element_type x2, other arithmetic, local(): mixed = (stream(1) * stream(2)).astype(jnp.bfloat16)  37 us
    ppermute x7, waiting for transfers between devices, local(): own_piece = lax.ppermute(own_piece, 'hi', forward)  28.8 us
    dot_general x2, matrix products, out_terms(): jnp.dot(rows, o_full, preferred_element_type=jnp.float32)  25.8 us
  transfers between devices with their start and end apart: 37, of which 16 were waited for; matrix products, arithmetic and copies ran while one was open for 28% of the time, Pallas kernels for 0%

profile of v13, /device:TPU:0, one launch (start us, length us, event | category | flops | bytes accessed | tf_op | source)
XLA Modules:
  0.0 776.9 jit_solution(9553126113503944621)
XLA Ops:
  21.1 57.6 %collective-permute-done = bf16[768,2048]{1,0:T(8,128)(2,1)} collective-permute-done((bf16[768,2048]{1,0:T(8,128)(2,1)}, bf16[768,2048]{1,0:T(8,128)(2,1)}, u32[]{:S(2)}, u32[]{:S(2)}) %collective-permute-start) | collective-permute-done | bytes 3145760 | tf_op jit(solution)/shard_map/ppermute | solution.py:15
  84.8 26.7 %collective-permute-done.1 = bf16[256,3,1024]{0,2,1:T(8,128)(2,1)} collective-permute-done((bf16[256,3,1024]{0,2,1:T(8,128)(2,1)}, bf16[256,3,1024]{0,2,1:T(8,128)(2,1)}, u32[]{:S(2)}, u32[]{:S(2)}) %collective-permute-start.1) | collective-permute-done | bytes 1572896 | tf_op jit(solution)/shard_map/ppermute | solution.py:15
  113.6 33.9 %collective-permute-done.3 = bf16[256,3072]{0,1:T(8,128)(2,1)} collective-permute-done((bf16[256,3072]{0,1:T(8,128)(2,1)}, bf16[256,3072]{0,1:T(8,128)(2,1)}, u32[]{:S(2)}, u32[]{:S(2)}) %collective-permute-start.3) | collective-permute-done | bytes 1572896 | tf_op jit(solution)/shard_map/ppermute | solution.py:95
  174.9 8.7 %broadcast_in_dim.101 = bf16[16,256,3072]{2,1,0:T(8,128)(2,1)} broadcast(bf16[]{:T(256)} %constant.131.clone.1), dimensions={} | broadcast | bytes 25165826 | tf_op jit(solution)/shard_map/broadcast_in_dim | solution.py:82
  214.2 16.6 %collective-permute-done.21 = bf16[1024,256]{0,1:T(8,128)(2,1)S(1)} collective-permute-done((bf16[1024,256]{0,1:T(8,128)(2,1)}, bf16[1024,256]{0,1:T(8,128)(2,1)S(1)}, u32[]{:S(2)}, u32[]{:S(2)}) %collective-permute-start.21) | collective-permute-done | bytes 524320 | tf_op jit(solution)/shard_map/ppermute | solution.py:96
  235.9 19.8 %collective-permute-done.22 = bf16[1024,256]{0,1:T(8,128)(2,1)} collective-permute-done((bf16[1024,256]{0,1:T(8,128)(2,1)S(1)}, bf16[1024,256]{0,1:T(8,128)(2,1)}, u32[]{:S(2)}, u32[]{:S(2)}) %collective-permute-start.22) | collective-permute-done | bytes 524320 | tf_op jit(solution)/shard_map/ppermute | solution.py:97
  278.0 34.5 %collective-permute-done.26 = bf16[1024,256]{0,1:T(8,128)(2,1)S(1)} collective-permute-done((bf16[1024,256]{0,1:T(8,128)(2,1)}, bf16[1024,256]{0,1:T(8,128)(2,1)S(1)}, u32[]{:S(2)}, u32[]{:S(2)}) %collective-permute-start.26) | collective-permute-done | bytes 524320 | tf_op jit(solution)/shard_map/ppermute | solution.py:97
  333.8 35.6 %collective-permute-done.30 = bf16[1024,256]{0,1:T(8,128)(2,1)} collective-permute-done((bf16[1024,256]{0,1:T(8,128)(2,1)}, bf16[1024,256]{0,1:T(8,128)(2,1)}, u32[]{:S(2)}, u32[]{:S(2)}) %collective-permute-start.30) | collective-permute-done | bytes 524320 | tf_op jit(solution)/shard_map/ppermute | solution.py:97
  385.2 18.3 %collective-permute-done.12 = bf16[256,3072]{0,1:T(8,128)(2,1)} collective-permute-done((bf16[256,3072]{0,1:T(8,128)(2,1)}, bf16[256,3072]{0,1:T(8,128)(2,1)}, u32[]{:S(2)}, u32[]{:S(2)}) %collective-permute-start.12) | collective-permute-done | bytes 1572896 | tf_op jit(solution)/shard_map/ppermute | solution.py:94
  424.3 10.5 %collective-permute-done.14 = bf16[256,3072]{0,1:T(8,128)(2,1)} collective-permute-done((bf16[256,3072]{0,1:T(8,128)(2,1)}, bf16[256,3072]{0,1:T(8,128)(2,1)}, u32[]{:S(2)}, u32[]{:S(2)}) %collective-permute-start.14) | collective-permute-done | bytes 1572896 | tf_op jit(solution)/shard_map/ppermute | solution.py:94
  439.2 7.1 collective-permute-done.15
  449.4 7.1 fusion
  456.5 47.9 %fusion.7 = bf16[1536,3072]{1,0:T(8,128)(2,1)S(1)} fusion(bf16[4096,3072]{1,0:T(8,128)(2,1)} %bitcast.35, bf16[1536,4096]{1,0:T(8,128)(2,1)} %all-gather.2.cloned.1.call-done, f32[4096]{0:T(1024)S(1)} %copy-done.27, f32[1536]{0:T(1024)S(1)} %add_rsqrt_fusion), kind=kOutput, calls=%fused_computation.13 | convolution fusion | flops 38684590080 | bytes 47208448 | tf_op jit(solution)/shard_map/dot_general | solution.py:106
  512.2 12.8 %copy.68 = bf16[1536,3072]{0,1:T(8,128)(2,1)} copy(bf16[1536,3072]{1,0:T(8,128)(2,1)} %copy-done.6) | data formatting | bytes 18874368 | tf_op jit(solution)/shard_map/convert_element_type | solution.py:111
  525.4 17.8 %fusion.29 = (f32[1536,1,1024]{0,2,1:T(8,128)}, f32[1536,1,1024]{0,2,1:T(8,128)}, f32[1536,1,1024]{0,2,1:T(8,128)}, f32[1536,1,1024]{0,2,1:T(8,128)}, f32[1536,1,1024]{0,2,1:T(8,128)}) fusion(bf16[1536,3,1024]{0,2,1:T(8,128)(2,1)} %bitcast.166, bf16[2,3,1024]{0,2,1:T(8,128)(2,1)S(1)} %copy.70), kind=kLoop, calls=%fused_computation.57 | loop fusion | flops 22020096 | bytes 47198208 | tf_op jit(solution)/shard_map/convert_element_type | solution.py:121
  543.2 8.4 %reshape.145 = f32[12,128,64,16]{1,0,3,2:T(8,128)} reshape(f32[1536,1,1024]{0,2,1:T(8,128)} %get-tuple-element.22) | data formatting | bytes 12582912 | tf_op jit(solution)/shard_map/convert_element_type | solution.py:121
  551.6 8.3 %reshape.146 = f32[12,128,64,16]{1,0,3,2:T(8,128)} reshape(f32[1536,1,1024]{0,2,1:T(8,128)} %get-tuple-element.19) | data formatting | bytes 12582912 | tf_op jit(solution)/shard_map/convert_element_type | solution.py:121
  560.0 8.4 %reshape.147 = f32[12,128,64,16]{1,0,3,2:T(8,128)} reshape(f32[1536,1,1024]{0,2,1:T(8,128)} %get-tuple-element.20) | data formatting | bytes 12582912 | tf_op jit(solution)/shard_map/convert_element_type | solution.py:121
  568.3 8.4 %reshape.148 = f32[12,128,64,16]{1,0,3,2:T(8,128)} reshape(f32[1536,1,1024]{0,2,1:T(8,128)} %get-tuple-element.23) | data formatting | bytes 12582912 | tf_op jit(solution)/shard_map/convert_element_type | solution.py:121
  576.8 8.4 %reshape.149 = f32[12,128,64,16]{1,0,3,2:T(8,128)} reshape(f32[1536,1,1024]{0,2,1:T(8,128)} %get-tuple-element.21) | data formatting | bytes 12582912 | tf_op jit(solution)/shard_map/convert_element_type | solution.py:121
  585.2 17.8 %fusion.17 = (bf16[1536,1024]{0,1:T(8,128)(2,1)S(1)}, f32[1536,1,1024]{0,2,1:T(8,128)}) fusion(f32[1024]{0:T(1024)S(1)} %bitcast.182, f32[1024]{0:T(1024)S(1)} %bitcast.181, f32[1024]{0:T(1024)S(1)} %bitcast.180, f32[1024]{0:T(1024)S(1)} %bitcast.179, f32[1024]{0:T(1024)S(1)} %bitcast.178, f32[1024]{0:T(1024)S(1)} %bitcast.177, ...), kind=kLoop, calls=%fused_computation.38 | loop fusion | flops 47185920 | bytes 25976832 | tf_op jit(solution)/shard_map/convert_element_type | solution.py:124
  603.0 8.4 %reshape.150 = f32[12,128,64,16]{1,0,3,2:T(8,128)} reshape(f32[1536,1,1024]{0,2,1:T(8,128)} %get-tuple-element.18) | data formatting | bytes 12582912 | tf_op jit(solution)/shard_map/convert_element_type | solution.py:121
  611.6 5.1 collective-permute-start.17
  616.7 19.3 %multiply_convert_fusion = bf16[12,128,64,16]{1,0,3,2:T(8,128)(2,1)} fusion(f32[12,128,64,16]{1,0,3,2:T(8,128)} %reshape.150, f32[12,128,64,16]{1,0,3,2:T(8,128)} %reshape.149, f32[12,128,64,16]{1,0,3,2:T(8,128)} %reshape.148, f32[12,128,64,16]{1,0,3,2:T(8,128)} %reshape.147, f32[12,128,64,16]{1,0,3,2:T(8,128)} %reshape.146, ...), kind=kLoop, calls=%fused_computation.17 | loop fusion | flops 18874368 | bytes 40919040 | tf_op jit(solution)/shard_map/convert_element_type | solution.py:124
  636.0 5.1 concatenate.11
  646.6 5.3 fusion.33
  659.9 6.2 fusion.12
  667.8 12.5 %convolution_convert_fusion = bf16[768,4096]{1,0:T(8,128)(2,1)} fusion(bf16[1024,4096]{0,1:T(8,128)(2,1)} %bitcast.75, bf16[1536,1024]{0,1:T(8,128)(2,1)S(1)} %fusion.12, s32[]{:T(128)S(6)} %select_n.262), kind=kOutput, calls=%fused_computation.25 | convolution fusion | flops 6445596672 | bytes 16252932 | tf_op jit(solution)/shard_map/dot_general | solution.py:143
  682.2 13.3 %convolution_convert_fusion.1 = bf16[768,4096]{1,0:T(8,128)(2,1)} fusion(bf16[1024,4096]{0,1:T(8,128)(2,1)} %bitcast.75, bf16[1536,1024]{0,1:T(8,128)(2,1)S(1)} %copy-done.9, s32[]{:T(128)S(6)} %select_n.261), kind=kOutput, calls=%fused_computation.26 | convolution fusion | flops 6445596672 | bytes 16252932 | tf_op jit(solution)/shard_map/dot_general | solution.py:143
  695.6 15.1 %reduce-scatter.3.cloned.1.call-done = bf16[768,2048]{1,0:T(8,128)(2,1)} async-done(((bf16[768,4096]{1,0:T(8,128)(2,1)}), bf16[768,2048]{1,0:T(8,128)(2,1)}) %reduce-scatter.3.cloned.1.call-update) | async-done | bytes 3145744 | tf_op jit(solution)/shard_map/reduce_scatter | solution.py:144
  710.8 52.5 %collective-permute-done.33 = bf16[768,2048]{1,0:T(8,128)(2,1)} collective-permute-done((bf16[768,2048]{1,0:T(8,128)(2,1)}, bf16[768,2048]{1,0:T(8,128)(2,1)}, u32[]{:S(2)}, u32[]{:S(2)}) %collective-permute-start.33) | collective-permute-done | bytes 3145760 | tf_op jit(solution)/shard_map/ppermute | solution.py:15
  763.3 6.6 add_convert_fusion
  (208 shorter events, 177.4 us)
Async XLA Ops:
  6.5 442.8 %all-gather.2.cloned.1.call-start = ((), (), s32[]{:S(2)}) async-start(), calls=%async_computation.2 | async-start | bytes 18874368 | tf_op jit(solution)/shard_map/all_gather | solution.py:60
  6.5 72.2 %collective-permute-start = (bf16[768,2048]{1,0:T(8,128)(2,1)}, bf16[768,2048]{1,0:T(8,128)(2,1)}, u32[]{:S(2)}, u32[]{:S(2)}) collective-permute-start(bf16[768,2048]{1,0:T(8,128)(2,1)} %param.8), channel_id=1, source_target_pairs={{0,2},{2,0},{1,3},{3,1},{4,6},{6,4},{5,7},{7,5},{8,10},{10,8},{9,1... | collective-permute-start | bytes 9437192 | tf_op jit(solution)/shard_map/ppermute | solution.py:15
  16.4 95.2 %collective-permute-start.1 = (bf16[256,3,1024]{0,2,1:T(8,128)(2,1)}, bf16[256,3,1024]{0,2,1:T(8,128)(2,1)}, u32[]{:S(2)}, u32[]{:S(2)}) collective-permute-start(bf16[256,3,1024]{0,2,1:T(8,128)(2,1)} %copy.86), channel_id=1, source_target_pairs={{0,2},{2,0},{1,3},{3,1},{4,6},{6,4},{5,7},{7,5},{8,10},{10,8},{9,1... | collective-permute-start | bytes 4718600 | tf_op jit(solution)/shard_map/ppermute | solution.py:15
  19.0 94.4 %collective-permute-start.2 = (bf16[256,3072]{0,1:T(8,128)(2,1)}, bf16[256,3072]{0,1:T(8,128)(2,1)}, u32[]{:S(2)}, u32[]{:S(2)}) collective-permute-start(bf16[256,3072]{0,1:T(8,128)(2,1)} %bitcast.172), channel_id=1, source_target_pairs={{0,8},{8,16},{16,24},{24,28},{28,20},{20,12},{12,4},{4,0},{1,9},{9... | collective-permute-start | bytes 4718600 | tf_op jit(solution)/shard_map/ppermute | solution.py:94
  84.8 610.7 %reduce-scatter.5.cloned.1.call-start = ((), (), s32[]{:S(2)}) async-start(), calls=%async_computation.4 | async-start | bytes 9437184 | tf_op jit(solution)/shard_map/reduce_scatter | solution.py:144
  111.6 35.9 %collective-permute-start.3 = (bf16[256,3072]{0,1:T(8,128)(2,1)}, bf16[256,3072]{0,1:T(8,128)(2,1)}, u32[]{:S(2)}, u32[]{:S(2)}) collective-permute-start(bf16[256,3072]{0,1:T(8,128)(2,1)} %bitcast.8), channel_id=1, source_target_pairs={{8,0},{16,8},{24,16},{28,24},{20,28},{12,20},{4,12},{0,4},{9,1},{1... | collective-permute-start | bytes 4718600 | tf_op jit(solution)/shard_map/ppermute | solution.py:95
  113.4 71.5 %collective-permute-start.4 = (bf16[256,3072]{0,1:T(8,128)(2,1)}, bf16[256,3072]{0,1:T(8,128)(2,1)}, u32[]{:S(2)}, u32[]{:S(2)}) collective-permute-start(bf16[256,3072]{0,1:T(8,128)(2,1)} %collective-permute-done.2), channel_id=1, source_target_pairs={{0,8},{8,16},{16,24},{24,28},{28,20},{20,12},{12,4},{4,0},{1,9},{9... | collective-permute-start | bytes 4718600 | tf_op jit(solution)/shard_map/ppermute | solution.py:94
  147.5 60.1 %collective-permute-start.5 = (bf16[256,3072]{0,1:T(8,128)(2,1)}, bf16[256,3072]{0,1:T(8,128)(2,1)}, u32[]{:S(2)}, u32[]{:S(2)}) collective-permute-start(bf16[256,3072]{0,1:T(8,128)(2,1)} %collective-permute-done.3), channel_id=1, source_target_pairs={{8,0},{16,8},{24,16},{28,24},{20,28},{12,20},{4,12},{0,4},{9,1},{1... | collective-permute-start | bytes 4718600 | tf_op jit(solution)/shard_map/ppermute | solution.py:95
  151.2 48.1 %collective-permute-start.18 = (bf16[1024,256]{0,1:T(8,128)(2,1)}, bf16[1024,256]{0,1:T(8,128)(2,1)}, u32[]{:S(2)}, u32[]{:S(2)}) collective-permute-start(bf16[1024,256]{0,1:T(8,128)(2,1)} %copy.89), channel_id=1, source_target_pairs={{0,2},{2,0},{1,3},{3,1},{4,6},{6,4},{5,7},{7,5},{8,10},{10,8},{9,1... | collective-permute-start | bytes 1572872 | tf_op jit(solution)/shard_map/ppermute | solution.py:15
  153.7 46.0 %collective-permute-start.19 = (bf16[1024,256]{0,1:T(8,128)(2,1)}, bf16[1024,256]{0,1:T(8,128)(2,1)}, u32[]{:S(2)}, u32[]{:S(2)}) collective-permute-start(bf16[1024,256]{0,1:T(8,128)(2,1)} %copy.88), channel_id=1, source_target_pairs={{0,8},{8,16},{16,24},{24,28},{28,20},{20,12},{12,4},{4,0},{1,9},{9... | collective-permute-start | bytes 1572872 | tf_op jit(solution)/shard_map/ppermute | solution.py:96
  184.8 72.9 %collective-permute-start.6 = (bf16[256,3072]{0,1:T(8,128)(2,1)}, bf16[256,3072]{0,1:T(8,128)(2,1)}, u32[]{:S(2)}, u32[]{:S(2)}) collective-permute-start(bf16[256,3072]{0,1:T(8,128)(2,1)} %collective-permute-done.4), channel_id=1, source_target_pairs={{0,8},{8,16},{16,24},{24,28},{28,20},{20,12},{12,4},{4,0},{1,9},{9... | collective-permute-start | bytes 4718600 | tf_op jit(solution)/shard_map/ppermute | solution.py:94
  199.7 31.0 %collective-permute-start.21 = (bf16[1024,256]{0,1:T(8,128)(2,1)}, bf16[1024,256]{0,1:T(8,128)(2,1)S(1)}, u32[]{:S(2)}, u32[]{:S(2)}) collective-permute-start(bf16[1024,256]{0,1:T(8,128)(2,1)} %collective-permute-done.19), channel_id=1, source_target_pairs={{0,8},{8,16},{16,24},{24,28},{28,20},{20,12},{12,4},{4,0},{1,9},{9... | collective-permute-start | bytes 1572872 | tf_op jit(solution)/shard_map/ppermute | solution.py:96
  207.6 58.9 %collective-permute-start.7 = (bf16[256,3072]{0,1:T(8,128)(2,1)}, bf16[256,3072]{0,1:T(8,128)(2,1)}, u32[]{:S(2)}, u32[]{:S(2)}) collective-permute-start(bf16[256,3072]{0,1:T(8,128)(2,1)} %collective-permute-done.5), channel_id=1, source_target_pairs={{8,0},{16,8},{24,16},{28,24},{20,28},{12,20},{4,12},{0,4},{9,1},{1... | collective-permute-start | bytes 4718600 | tf_op jit(solution)/shard_map/ppermute | solution.py:95
  213.8 42.0 %collective-permute-start.22 = (bf16[1024,256]{0,1:T(8,128)(2,1)S(1)}, bf16[1024,256]{0,1:T(8,128)(2,1)}, u32[]{:S(2)}, u32[]{:S(2)}) collective-permute-start(bf16[1024,256]{0,1:T(8,128)(2,1)S(1)} %collective-permute-done.20), channel_id=1, source_target_pairs={{8,0},{16,8},{24,16},{28,24},{20,28},{12,20},{4,12},{0,4},{9,1},{1... | collective-permute-start | bytes 1572872 | tf_op jit(solution)/shard_map/ppermute | solution.py:97
  230.7 25.4 %collective-permute-start.23 = (bf16[1024,256]{0,1:T(8,128)(2,1)S(1)}, bf16[1024,256]{0,1:T(8,128)(2,1)}, u32[]{:S(2)}, u32[]{:S(2)}) collective-permute-start(bf16[1024,256]{0,1:T(8,128)(2,1)S(1)} %collective-permute-done.21), channel_id=1, source_target_pairs={{0,8},{8,16},{16,24},{24,28},{28,20},{20,12},{12,4},{4,0},{1,9},{9... | collective-permute-start | bytes 1572872 | tf_op jit(solution)/shard_map/ppermute | solution.py:96
  257.8 56.8 %collective-permute-start.8 = (bf16[256,3072]{0,1:T(8,128)(2,1)}, bf16[256,3072]{0,1:T(8,128)(2,1)}, u32[]{:S(2)}, u32[]{:S(2)}) collective-permute-start(bf16[256,3072]{0,1:T(8,128)(2,1)} %collective-permute-done.6), channel_id=1, source_target_pairs={{0,8},{8,16},{16,24},{24,28},{28,20},{20,12},{12,4},{4,0},{1,9},{9... | collective-permute-start | bytes 4718600 | tf_op jit(solution)/shard_map/ppermute | solution.py:94
  266.4 53.1 %collective-permute-start.9 = (bf16[256,3072]{0,1:T(8,128)(2,1)}, bf16[256,3072]{0,1:T(8,128)(2,1)}, u32[]{:S(2)}, u32[]{:S(2)}) collective-permute-start(bf16[256,3072]{0,1:T(8,128)(2,1)} %collective-permute-done.7), channel_id=1, source_target_pairs={{8,0},{16,8},{24,16},{28,24},{20,28},{12,20},{4,12},{0,4},{9,1},{1... | collective-permute-start | bytes 4718600 | tf_op jit(solution)/shard_map/ppermute | solution.py:95
  268.3 44.2 %collective-permute-start.26 = (bf16[1024,256]{0,1:T(8,128)(2,1)}, bf16[1024,256]{0,1:T(8,128)(2,1)S(1)}, u32[]{:S(2)}, u32[]{:S(2)}) collective-permute-start(bf16[1024,256]{0,1:T(8,128)(2,1)} %collective-permute-done.24), channel_id=1, source_target_pairs={{8,0},{16,8},{24,16},{28,24},{20,28},{12,20},{4,12},{0,4},{9,1},{1... | collective-permute-start | bytes 1572872 | tf_op jit(solution)/shard_map/ppermute | solution.py:97
  271.3 41.5 %collective-permute-start.27 = (bf16[1024,256]{0,1:T(8,128)(2,1)}, bf16[1024,256]{0,1:T(8,128)(2,1)S(1)}, u32[]{:S(2)}, u32[]{:S(2)}) collective-permute-start(bf16[1024,256]{0,1:T(8,128)(2,1)} %collective-permute-done.25), channel_id=1, source_target_pairs={{0,8},{8,16},{16,24},{24,28},{28,20},{20,12},{12,4},{4,0},{1,9},{9... | collective-permute-start | bytes 1572872 | tf_op jit(solution)/shard_map/ppermute | solution.py:96
  314.5 55.1 %collective-permute-start.10 = (bf16[256,3072]{0,1:T(8,128)(2,1)}, bf16[256,3072]{0,1:T(8,128)(2,1)}, u32[]{:S(2)}, u32[]{:S(2)}) collective-permute-start(bf16[256,3072]{0,1:T(8,128)(2,1)} %collective-permute-done.8), channel_id=1, source_target_pairs={{0,8},{8,16},{16,24},{24,28},{28,20},{20,12},{12,4},{4,0},{1,9},{9... | collective-permute-start | bytes 4718600 | tf_op jit(solution)/shard_map/ppermute | solution.py:94
  319.5 56.3 %collective-permute-start.11 = (bf16[256,3072]{0,1:T(8,128)(2,1)}, bf16[256,3072]{0,1:T(8,128)(2,1)}, u32[]{:S(2)}, u32[]{:S(2)}) collective-permute-start(bf16[256,3072]{0,1:T(8,128)(2,1)} %collective-permute-done.9), channel_id=1, source_target_pairs={{8,0},{16,8},{24,16},{28,24},{20,28},{12,20},{4,12},{0,4},{9,1},{1... | collective-permute-start | bytes 4718600 | tf_op jit(solution)/shard_map/ppermute | solution.py:95
  327.5 41.9 %collective-permute-start.30 = (bf16[1024,256]{0,1:T(8,128)(2,1)}, bf16[1024,256]{0,1:T(8,128)(2,1)}, u32[]{:S(2)}, u32[]{:S(2)}) collective-permute-start(bf16[1024,256]{0,1:T(8,128)(2,1)} %collective-permute-done.28), channel_id=1, source_target_pairs={{8,0},{16,8},{24,16},{28,24},{20,28},{12,20},{4,12},{0,4},{9,1},{1... | collective-permute-start | bytes 1572872 | tf_op jit(solution)/shard_map/ppermute | solution.py:97
  329.0 44.2 %collective-permute-start.31 = (bf16[1024,256]{0,1:T(8,128)(2,1)S(1)}, bf16[1024,256]{0,1:T(8,128)(2,1)S(1)}, u32[]{:S(2)}, u32[]{:S(2)}) collective-permute-start(bf16[1024,256]{0,1:T(8,128)(2,1)S(1)} %collective-permute-done.29), channel_id=1, source_target_pairs={{0,8},{8,16},{16,24},{24,28},{28,20},{20,12},{12,4},{4,0},{1,9},{9... | collective-permute-start | bytes 1572872 | tf_op jit(solution)/shard_map/ppermute | solution.py:96
  369.3 141.0 %collective-permute-start.32 = (bf16[1024,256]{0,1:T(8,128)(2,1)}, bf16[1024,256]{0,1:T(8,128)(2,1)}, u32[]{:S(2)}, u32[]{:S(2)}) collective-permute-start(bf16[1024,256]{0,1:T(8,128)(2,1)} %collective-permute-done.30), channel_id=1, source_target_pairs={{8,0},{16,8},{24,16},{28,24},{20,28},{12,20},{4,12},{0,4},{9,1},{1... | collective-permute-start | bytes 1572872 | tf_op jit(solution)/shard_map/ppermute | solution.py:97
  369.6 33.8 %collective-permute-start.12 = (bf16[256,3072]{0,1:T(8,128)(2,1)}, bf16[256,3072]{0,1:T(8,128)(2,1)}, u32[]{:S(2)}, u32[]{:S(2)}) collective-permute-start(bf16[256,3072]{0,1:T(8,128)(2,1)} %collective-permute-done.10), channel_id=1, source_target_pairs={{0,8},{8,16},{16,24},{24,28},{28,20},{20,12},{12,4},{4,0},{1,9},{9... | collective-permute-start | bytes 4718600 | tf_op jit(solution)/shard_map/ppermute | solution.py:94
  375.8 39.0 %collective-permute-start.13 = (bf16[256,3072]{0,1:T(8,128)(2,1)}, bf16[256,3072]{0,1:T(8,128)(2,1)}, u32[]{:S(2)}, u32[]{:S(2)}) collective-permute-start(bf16[256,3072]{0,1:T(8,128)(2,1)} %collective-permute-done.11), channel_id=1, source_target_pairs={{8,0},{16,8},{24,16},{28,24},{20,28},{12,20},{4,12},{0,4},{9,1},{1... | collective-permute-start | bytes 4718600 | tf_op jit(solution)/shard_map/ppermute | solution.py:95
  403.4 31.4 %collective-permute-start.14 = (bf16[256,3072]{0,1:T(8,128)(2,1)}, bf16[256,3072]{0,1:T(8,128)(2,1)}, u32[]{:S(2)}, u32[]{:S(2)}) collective-permute-start(bf16[256,3072]{0,1:T(8,128)(2,1)} %collective-permute-done.12), channel_id=1, source_target_pairs={{0,8},{8,16},{16,24},{24,28},{28,20},{20,12},{12,4},{4,0},{1,9},{9... | collective-permute-start | bytes 4718600 | tf_op jit(solution)/shard_map/ppermute | solution.py:94
  414.8 31.5 %collective-permute-start.15 = (bf16[256,3072]{0,1:T(8,128)(2,1)}, bf16[256,3072]{0,1:T(8,128)(2,1)}, u32[]{:S(2)}, u32[]{:S(2)}) collective-permute-start(bf16[256,3072]{0,1:T(8,128)(2,1)} %collective-permute-done.13), channel_id=1, source_target_pairs={{8,0},{16,8},{24,16},{28,24},{20,28},{12,20},{4,12},{0,4},{9,1},{1... | collective-permute-start | bytes 4718600 | tf_op jit(solution)/shard_map/ppermute | solution.py:95
  508.0 17.0 %collective-permute-start.16 = (bf16[2,3,1024]{2,0,1:T(2,128)(2,1)S(1)}, bf16[2,3,1024]{2,0,1:T(2,128)(2,1)S(1)}, u32[]{:S(2)}, u32[]{:S(2)}) collective-permute-start(bf16[2,3,1024]{2,0,1:T(2,128)(2,1)S(1)} %bitcast.183), channel_id=1, source_target_pairs={{0,4},{4,8},{8,12},{12,16},{16,20},{20,24},{24,28},{1,5},{5,9},{9,... | collective-permute-start | bytes 36872 | tf_op jit(solution)/shard_map/ppermute | solution.py:11
  611.6 24.4 %collective-permute-start.17 = (bf16[127,1024]{0,1:T(8,128)(2,1)S(1)}, bf16[127,1024]{0,1:T(8,128)(2,1)}, u32[]{:S(2)}, u32[]{:S(2)}) collective-permute-start(bf16[127,1024]{0,1:T(8,128)(2,1)S(1)} %slice.108), channel_id=1, source_target_pairs={{0,4},{4,8},{8,12},{12,16},{16,20},{20,24},{24,28},{1,5},{5,9},{9,... | collective-permute-start | bytes 780296 | tf_op jit(solution)/shard_map/ppermute | solution.py:11
  680.3 30.4 %reduce-scatter.3.cloned.1.call-start = ((), (), s32[]{:S(2)}) async-start(), calls=%async_computation.3 | async-start | bytes 9437184 | tf_op jit(solution)/shard_map/reduce_scatter | solution.py:144
  695.5 67.8 %collective-permute-start.33 = (bf16[768,2048]{1,0:T(8,128)(2,1)}, bf16[768,2048]{1,0:T(8,128)(2,1)}, u32[]{:S(2)}, u32[]{:S(2)}) collective-permute-start(bf16[768,2048]{1,0:T(8,128)(2,1)} %reduce-scatter.5.cloned.1.call-done), channel_id=1, source_target_pairs={{0,2},{2,0},{1,3},{3,1},{4,6},{6,4},{5,7},{7,5},{8,10},{10,8},{9,1... | collective-permute-start | bytes 9437192 | tf_op jit(solution)/shard_map/ppermute | solution.py:15
  (38 other events, 918.9 us)
Sparse Core Ops, SparseCore 0:
  84.9 26.7 all-gather.1
  680.5 12.1 reduce-scatter.4
  695.6 15.1 reduce-scatter.2

commit v14 on v9

--- a/solution.py
+++ b/solution.py
@@ -129,17 +129,18 @@
     mixed_prior = shifted(mixed[row_count - (filter_len - 1) :], "hi", 1)
     query = featured[:, 0]
     zero_row = jnp.zeros((1, half_width), jnp.bfloat16)
-    extended_mix = jnp.concatenate([zero_row, mixed_prior, mixed], axis=0)
     groups_here = long_filter.shape[1] // 2
     group_size = half_width // groups_here
-    mix_blocks = extended_mix.reshape(
-        row_count // filter_len + 1, filter_len, groups_here, group_size
-    )
-    filtered = jnp.einsum(
-        "gts,bsgc->btgc", current, mix_blocks[1:], preferred_element_type=jnp.float32
-    )
-    filtered = filtered + jnp.einsum(
-        "gts,bsgc->btgc", previous, mix_blocks[:-1], preferred_element_type=jnp.float32
+    block_shape = (filter_len, groups_here, group_size)
+    mix_blocks = mixed.reshape((row_count // filter_len,) + block_shape)
+    halo_block = jnp.concatenate([zero_row, mixed_prior], axis=0).reshape((1,) + block_shape)
+
+    def apply(table, blocks):
+        return jnp.einsum("gts,bsgc->btgc", table, blocks, preferred_element_type=jnp.float32)
+
+    filtered = apply(current, mix_blocks)
+    filtered = filtered + jnp.concatenate(
+        [apply(previous, halo_block), apply(previous, mix_blocks[:-1])], axis=0
     )
     gated = (query * filtered.reshape(row_count, half_width)).astype(jnp.bfloat16)
 

time: 734 us -> 724 us (0.986)
  local copies, waits for them, and re-layouts: 158 us -> 138 us
  matrix products: 86.1 us -> 94.8 us
    ppermute x7, waiting for transfers between devices: 30.9 us -> 90.7 us  [local(): partner_out = lax.ppermute(partner_out, 'hi', backward)]
    ppermute x7, waiting for transfers between devices: 72.5 us -> 20.5 us  [local(): own_out = lax.ppermute(own_out, 'hi', forward)]
    concatenate x1, local copies, waits for them, and re-layouts: 13.2 us -> 0.14 us  [local(): jnp.concatenate([zero_row, mixed_prior], axis=0).reshape((1,) + block_shape)]
    dot_general x2 -> x3, matrix products: 7.93 us -> 16.9 us  [apply(): jnp.einsum('gts,bsgc->btgc', table, blocks, preferred_element_type=jnp.fl...]
    unnamed x32 -> x29, local copies, waits for them, and re-layouts: 17.4 us -> 17.5 us
  transfers between devices with their start and end apart: 37 -> 37, of which waited for: 22 -> 16; matrix products, arithmetic and copies ran while one was open for 33% -> 28% of each run, Pallas kernels for 0% -> 0%
where the time goes in v14:
time: 724 us; the launch traced here: 714 us
  waiting for transfers between devices  337 us (47%)
  local copies, waits for them, and re-layouts  138 us (19%)
  matrix products  94.8 us (13%)
  other arithmetic  64.8 us (9%)
  starting transfers between devices  44.8 us (6%)
  between operations  34.4 us (5%)
    ppermute x4, waiting for transfers between devices, swap_pair(): return lax.ppermute(value, 'lo', [(0, 1), (1, 0)])  137 us
    ppermute x7, waiting for transfers between devices, local(): partner_out = lax.ppermute(partner_out, 'hi', backward)  90.7 us
    dot_general x1, matrix products, local(): jnp.dot(normed, gathered_w.reshape(n_ctx * w_rows, 3 * half_width), prefe...  47.9 us
    ppermute x7, waiting for transfers between devices, local(): partner_piece = lax.ppermute(partner_piece, 'hi', backward)  44.9 us
    ppermute x7, waiting for transfers between devices, local(): own_piece = lax.ppermute(own_piece, 'hi', forward)  26.7 us
    dot_general x2, matrix products, out_terms(): jnp.dot(rows, o_full, preferred_element_type=jnp.float32)  24.5 us
    broadcast_in_dim x14, local copies, waits for them, and re-layouts, store(): piece[None]  23.9 us
    dynamic_update_slice x16, local copies, waits for them, and re-layouts, store_out(): lax.dynamic_update_slice_in_dim(buffer, piece[:, None], ctx_index, axis=1)  23.8 us
  transfers between devices with their start and end apart: 37, of which 16 were waited for; matrix products, arithmetic and copies ran while one was open for 28% of the time, Pallas kernels for 0%

profile of v14, /device:TPU:0, one launch (start us, length us, event | category | flops | bytes accessed | tf_op | source)
XLA Modules:
  0.0 713.6 jit_solution(17882903978000441418)
XLA Ops:
  9.5 4.1 constant_dynamic-slice_fusion.2
  21.1 57.6 %collective-permute-done = bf16[768,2048]{1,0:T(8,128)(2,1)} collective-permute-done((bf16[768,2048]{1,0:T(8,128)(2,1)}, bf16[768,2048]{1,0:T(8,128)(2,1)}, u32[]{:S(2)}, u32[]{:S(2)}) %collective-permute-start) | collective-permute-done | bytes 3145760 | tf_op jit(solution)/shard_map/ppermute | solution.py:15
  81.1 3.7 pad_maximum_fusion
  84.8 26.8 %collective-permute-done.1 = bf16[256,3,1024]{0,2,1:T(8,128)(2,1)} collective-permute-done((bf16[256,3,1024]{0,2,1:T(8,128)(2,1)}, bf16[256,3,1024]{0,2,1:T(8,128)(2,1)}, u32[]{:S(2)}, u32[]{:S(2)}) %collective-permute-start.1) | collective-permute-done | bytes 1572896 | tf_op jit(solution)/shard_map/ppermute | solution.py:15
  113.7 33.9 %collective-permute-done.3 = bf16[256,3072]{0,1:T(8,128)(2,1)} collective-permute-done((bf16[256,3072]{0,1:T(8,128)(2,1)}, bf16[256,3072]{0,1:T(8,128)(2,1)}, u32[]{:S(2)}, u32[]{:S(2)}) %collective-permute-start.3) | collective-permute-done | bytes 1572896 | tf_op jit(solution)/shard_map/ppermute | solution.py:107
  168.2 8.6 %broadcast_in_dim.99 = bf16[16,256,3072]{2,1,0:T(8,128)(2,1)} broadcast(bf16[]{:T(256)} %constant.131.clone.1), dimensions={} | broadcast | bytes 25165826 | tf_op jit(solution)/shard_map/broadcast_in_dim | solution.py:94
  179.7 4.3 broadcast_in_dim.114
  206.1 17.9 %collective-permute-done.21 = bf16[1024,256]{0,1:T(8,128)(2,1)S(1)} collective-permute-done((bf16[1024,256]{0,1:T(8,128)(2,1)}, bf16[1024,256]{0,1:T(8,128)(2,1)S(1)}, u32[]{:S(2)}, u32[]{:S(2)}) %collective-permute-start.21) | collective-permute-done | bytes 524320 | tf_op jit(solution)/shard_map/ppermute | solution.py:108
  229.2 16.1 %collective-permute-done.22 = bf16[1024,256]{0,1:T(8,128)(2,1)} collective-permute-done((bf16[1024,256]{0,1:T(8,128)(2,1)S(1)}, bf16[1024,256]{0,1:T(8,128)(2,1)}, u32[]{:S(2)}, u32[]{:S(2)}) %collective-permute-start.22) | collective-permute-done | bytes 524320 | tf_op jit(solution)/shard_map/ppermute | solution.py:109
  267.6 34.5 %collective-permute-done.26 = bf16[1024,256]{0,1:T(8,128)(2,1)S(1)} collective-permute-done((bf16[1024,256]{0,1:T(8,128)(2,1)}, bf16[1024,256]{0,1:T(8,128)(2,1)S(1)}, u32[]{:S(2)}, u32[]{:S(2)}) %collective-permute-start.26) | collective-permute-done | bytes 524320 | tf_op jit(solution)/shard_map/ppermute | solution.py:109
  312.7 4.4 collective-permute-done.28
  323.1 35.6 %collective-permute-done.30 = bf16[1024,256]{0,1:T(8,128)(2,1)} collective-permute-done((bf16[1024,256]{0,1:T(8,128)(2,1)}, bf16[1024,256]{0,1:T(8,128)(2,1)}, u32[]{:S(2)}, u32[]{:S(2)}) %collective-permute-start.30) | collective-permute-done | bytes 524320 | tf_op jit(solution)/shard_map/ppermute | solution.py:109
  374.7 18.4 %collective-permute-done.12 = bf16[256,3072]{0,1:T(8,128)(2,1)} collective-permute-done((bf16[256,3072]{0,1:T(8,128)(2,1)}, bf16[256,3072]{0,1:T(8,128)(2,1)}, u32[]{:S(2)}, u32[]{:S(2)}) %collective-permute-start.12) | collective-permute-done | bytes 1572896 | tf_op jit(solution)/shard_map/ppermute | solution.py:106
  413.8 8.3 %collective-permute-done.14 = bf16[256,3072]{0,1:T(8,128)(2,1)} collective-permute-done((bf16[256,3072]{0,1:T(8,128)(2,1)}, bf16[256,3072]{0,1:T(8,128)(2,1)}, u32[]{:S(2)}, u32[]{:S(2)}) %collective-permute-start.14) | collective-permute-done | bytes 1572896 | tf_op jit(solution)/shard_map/ppermute | solution.py:106
  426.5 8.3 %collective-permute-done.15 = bf16[256,3072]{0,1:T(8,128)(2,1)} collective-permute-done((bf16[256,3072]{0,1:T(8,128)(2,1)}, bf16[256,3072]{0,1:T(8,128)(2,1)}, u32[]{:S(2)}, u32[]{:S(2)}) %collective-permute-start.15) | collective-permute-done | bytes 1572896 | tf_op jit(solution)/shard_map/ppermute | solution.py:107
  437.8 7.1 fusion
  444.8 47.9 %fusion.9 = bf16[1536,3072]{1,0:T(8,128)(2,1)S(1)} fusion(bf16[4096,3072]{1,0:T(8,128)(2,1)} %bitcast.35, bf16[1536,4096]{1,0:T(8,128)(2,1)} %all-gather.2.cloned.1.call-done, f32[4096]{0:T(1024)S(1)} %copy-done.10, f32[1536]{0:T(1024)S(1)} %add_rsqrt_fusion), kind=kOutput, calls=%fused_computation.13 | convolution fusion | flops 38684590080 | bytes 47208448 | tf_op jit(solution)/shard_map/dot_general | solution.py:118
  492.7 3.7 copy-done.5
  500.7 12.8 %copy.45 = bf16[1536,3072]{0,1:T(8,128)(2,1)} copy(bf16[1536,3072]{1,0:T(8,128)(2,1)} %copy-done.5) | data formatting | bytes 18874368 | tf_op jit(solution)/shard_map/convert_element_type | solution.py:123
  514.0 15.1 %maximum_convert_fusion = f32[1538,3,1024]{0,2,1:T(8,128)} fusion(bf16[1536,3,1024]{0,2,1:T(8,128)(2,1)} %bitcast.115, bf16[2,3,1024]{0,2,1:T(8,128)(2,1)S(1)} %copy.46), kind=kLoop, calls=%fused_computation.14 | loop fusion | flops 18898944 | bytes 28348416 | tf_op jit(solution)/shard_map/convert_element_type | solution.py:34
  529.1 22.3 %fusion.3 = f32[1536,3,1024]{0,2,1:T(8,128)S(1)} fusion(f32[1538,3,1024]{0,2,1:T(8,128)} %maximum_convert_fusion, f32[3,1024]{1,0:T(4,128)S(1)} %get-tuple-element.13, f32[3,1024]{1,0:T(4,128)S(1)} %get-tuple-element.12, f32[3,1024]{1,0:T(4,128)S(1)} %get-tuple-element.11), kind=kLoop, calls=%fused_computation.6 | loop fusion | flops 23592960 | bytes 75534336 | tf_op jit(solution)/shard_map/add | solution.py:38
  551.4 6.5 copy-done.2
  562.6 6.9 convert_element_type.49
  574.2 4.6 collective-permute-start.17
  578.8 8.0 %fusion.23 = f32[11,128,64,16]{1,3,0,2:T(8,128)} fusion(bf16[11,128,64,16]{1,0,3,2:T(8,128)(2,1)} %slice.60, bf16[64,128,128,1]{2,0,1,3:T(8,128)(2,1)} %bitcast.117), kind=kOutput, calls=%fused_computation.37 | convolution fusion | flops 369098752 | bytes 10747904 | tf_op jit(solution)/shard_map/gts,bsgc->btgc/dot_general | solution.py:139
  589.0 7.1 maximum_add_fusion
  598.9 5.1 fusion.14
  604.0 12.3 %convolution_convert_fusion = bf16[768,4096]{1,0:T(8,128)(2,1)} fusion(bf16[1024,4096]{0,1:T(8,128)(2,1)} %bitcast.65, bf16[1536,1024]{0,1:T(8,128)(2,1)S(1)} %fusion.14, s32[]{:T(128)S(6)} %select_n.262), kind=kOutput, calls=%fused_computation.20 | convolution fusion | flops 6445596672 | bytes 16252932 | tf_op jit(solution)/shard_map/dot_general | solution.py:148
  616.4 12.2 %convolution_convert_fusion.1 = bf16[768,4096]{1,0:T(8,128)(2,1)} fusion(bf16[1024,4096]{0,1:T(8,128)(2,1)} %bitcast.65, bf16[1536,1024]{0,1:T(8,128)(2,1)S(1)} %fusion.14, s32[]{:T(128)S(6)} %select_n.261), kind=kOutput, calls=%fused_computation.21 | convolution fusion | flops 6445596672 | bytes 16252932 | tf_op jit(solution)/shard_map/dot_general | solution.py:148
  631.1 16.4 %reduce-scatter.3.cloned.1.call-done = bf16[768,2048]{1,0:T(8,128)(2,1)} async-done(((bf16[768,4096]{1,0:T(8,128)(2,1)}), bf16[768,2048]{1,0:T(8,128)(2,1)}) %reduce-scatter.3.cloned.1.call-update) | async-done | bytes 3145744 | tf_op jit(solution)/shard_map/reduce_scatter | solution.py:149
  647.5 52.5 %collective-permute-done.33 = bf16[768,2048]{1,0:T(8,128)(2,1)} collective-permute-done((bf16[768,2048]{1,0:T(8,128)(2,1)}, bf16[768,2048]{1,0:T(8,128)(2,1)}, u32[]{:S(2)}, u32[]{:S(2)}) %collective-permute-start.33) | collective-permute-done | bytes 3145760 | tf_op jit(solution)/shard_map/ppermute | solution.py:15
  700.0 6.6 add_convert_fusion
  (157 shorter events, 149.6 us)
Async XLA Ops:
  6.5 431.2 %all-gather.2.cloned.1.call-start = ((), (), s32[]{:S(2)}) async-start(), calls=%async_computation.2 | async-start | bytes 18874368 | tf_op jit(solution)/shard_map/all_gather | solution.py:72
  6.5 72.2 %collective-permute-start = (bf16[768,2048]{1,0:T(8,128)(2,1)}, bf16[768,2048]{1,0:T(8,128)(2,1)}, u32[]{:S(2)}, u32[]{:S(2)}) collective-permute-start(bf16[768,2048]{1,0:T(8,128)(2,1)} %param.8), channel_id=1, source_target_pairs={{0,2},{2,0},{1,3},{3,1},{4,6},{6,4},{5,7},{7,5},{8,10},{10,8},{9,1... | collective-permute-start | bytes 9437192 | tf_op jit(solution)/shard_map/ppermute | solution.py:15
  16.2 95.5 %collective-permute-start.1 = (bf16[256,3,1024]{0,2,1:T(8,128)(2,1)}, bf16[256,3,1024]{0,2,1:T(8,128)(2,1)}, u32[]{:S(2)}, u32[]{:S(2)}) collective-permute-start(bf16[256,3,1024]{0,2,1:T(8,128)(2,1)} %copy.65), channel_id=1, source_target_pairs={{0,2},{2,0},{1,3},{3,1},{4,6},{6,4},{5,7},{7,5},{8,10},{10,8},{9,1... | collective-permute-start | bytes 4718600 | tf_op jit(solution)/shard_map/ppermute | solution.py:15
  18.9 94.5 %collective-permute-start.2 = (bf16[256,3072]{0,1:T(8,128)(2,1)}, bf16[256,3072]{0,1:T(8,128)(2,1)}, u32[]{:S(2)}, u32[]{:S(2)}) collective-permute-start(bf16[256,3072]{0,1:T(8,128)(2,1)} %bitcast.118), channel_id=1, source_target_pairs={{0,8},{8,16},{16,24},{24,28},{28,20},{20,12},{12,4},{4,0},{1,9},{9... | collective-permute-start | bytes 4718600 | tf_op jit(solution)/shard_map/ppermute | solution.py:106
  84.8 544.6 %reduce-scatter.5.cloned.1.call-start = ((), (), s32[]{:S(2)}) async-start(), calls=%async_computation.4 | async-start | bytes 9437184 | tf_op jit(solution)/shard_map/reduce_scatter | solution.py:149
  111.6 35.9 %collective-permute-start.3 = (bf16[256,3072]{0,1:T(8,128)(2,1)}, bf16[256,3072]{0,1:T(8,128)(2,1)}, u32[]{:S(2)}, u32[]{:S(2)}) collective-permute-start(bf16[256,3072]{0,1:T(8,128)(2,1)} %bitcast.8), channel_id=1, source_target_pairs={{8,0},{16,8},{24,16},{28,24},{20,28},{12,20},{4,12},{0,4},{9,1},{1... | collective-permute-start | bytes 4718600 | tf_op jit(solution)/shard_map/ppermute | solution.py:107
  113.4 64.7 %collective-permute-start.4 = (bf16[256,3072]{0,1:T(8,128)(2,1)}, bf16[256,3072]{0,1:T(8,128)(2,1)}, u32[]{:S(2)}, u32[]{:S(2)}) collective-permute-start(bf16[256,3072]{0,1:T(8,128)(2,1)} %collective-permute-done.2), channel_id=1, source_target_pairs={{0,8},{8,16},{16,24},{24,28},{28,20},{20,12},{12,4},{4,0},{1,9},{9... | collective-permute-start | bytes 4718600 | tf_op jit(solution)/shard_map/ppermute | solution.py:106
  147.5 52.0 %collective-permute-start.5 = (bf16[256,3072]{0,1:T(8,128)(2,1)}, bf16[256,3072]{0,1:T(8,128)(2,1)}, u32[]{:S(2)}, u32[]{:S(2)}) collective-permute-start(bf16[256,3072]{0,1:T(8,128)(2,1)} %collective-permute-done.3), channel_id=1, source_target_pairs={{8,0},{16,8},{24,16},{28,24},{20,28},{12,20},{4,12},{0,4},{9,1},{1... | collective-permute-start | bytes 4718600 | tf_op jit(solution)/shard_map/ppermute | solution.py:107
  151.2 34.7 %collective-permute-start.18 = (bf16[1024,256]{0,1:T(8,128)(2,1)}, bf16[1024,256]{0,1:T(8,128)(2,1)}, u32[]{:S(2)}, u32[]{:S(2)}) collective-permute-start(bf16[1024,256]{0,1:T(8,128)(2,1)} %copy.68), channel_id=1, source_target_pairs={{0,2},{2,0},{1,3},{3,1},{4,6},{6,4},{5,7},{7,5},{8,10},{10,8},{9,1... | collective-permute-start | bytes 1572872 | tf_op jit(solution)/shard_map/ppermute | solution.py:15
  153.7 32.6 %collective-permute-start.19 = (bf16[1024,256]{0,1:T(8,128)(2,1)}, bf16[1024,256]{0,1:T(8,128)(2,1)}, u32[]{:S(2)}, u32[]{:S(2)}) collective-permute-start(bf16[1024,256]{0,1:T(8,128)(2,1)} %copy.67), channel_id=1, source_target_pairs={{0,8},{8,16},{16,24},{24,28},{28,20},{20,12},{12,4},{4,0},{1,9},{9... | collective-permute-start | bytes 1572872 | tf_op jit(solution)/shard_map/ppermute | solution.py:108
  178.1 69.2 %collective-permute-start.6 = (bf16[256,3072]{0,1:T(8,128)(2,1)}, bf16[256,3072]{0,1:T(8,128)(2,1)}, u32[]{:S(2)}, u32[]{:S(2)}) collective-permute-start(bf16[256,3072]{0,1:T(8,128)(2,1)} %collective-permute-done.4), channel_id=1, source_target_pairs={{0,8},{8,16},{16,24},{24,28},{28,20},{20,12},{12,4},{4,0},{1,9},{9... | collective-permute-start | bytes 4718600 | tf_op jit(solution)/shard_map/ppermute | solution.py:106
  185.9 18.6 %collective-permute-start.20 = (bf16[1024,256]{0,1:T(8,128)(2,1)}, bf16[1024,256]{0,1:T(8,128)(2,1)S(1)}, u32[]{:S(2)}, u32[]{:S(2)}) collective-permute-start(bf16[1024,256]{0,1:T(8,128)(2,1)} %collective-permute-done.18), channel_id=1, source_target_pairs={{8,0},{16,8},{24,16},{28,24},{20,28},{12,20},{4,12},{0,4},{9,1},{1... | collective-permute-start | bytes 1572872 | tf_op jit(solution)/shard_map/ppermute | solution.py:109
  186.3 37.7 %collective-permute-start.21 = (bf16[1024,256]{0,1:T(8,128)(2,1)}, bf16[1024,256]{0,1:T(8,128)(2,1)S(1)}, u32[]{:S(2)}, u32[]{:S(2)}) collective-permute-start(bf16[1024,256]{0,1:T(8,128)(2,1)} %collective-permute-done.19), channel_id=1, source_target_pairs={{0,8},{8,16},{16,24},{24,28},{28,20},{20,12},{12,4},{4,0},{1,9},{9... | collective-permute-start | bytes 1572872 | tf_op jit(solution)/shard_map/ppermute | solution.py:108
  199.5 56.5 %collective-permute-start.7 = (bf16[256,3072]{0,1:T(8,128)(2,1)}, bf16[256,3072]{0,1:T(8,128)(2,1)}, u32[]{:S(2)}, u32[]{:S(2)}) collective-permute-start(bf16[256,3072]{0,1:T(8,128)(2,1)} %collective-permute-done.5), channel_id=1, source_target_pairs={{8,0},{16,8},{24,16},{28,24},{20,28},{12,20},{4,12},{0,4},{9,1},{1... | collective-permute-start | bytes 4718600 | tf_op jit(solution)/shard_map/ppermute | solution.py:107
  204.5 40.8 %collective-permute-start.22 = (bf16[1024,256]{0,1:T(8,128)(2,1)S(1)}, bf16[1024,256]{0,1:T(8,128)(2,1)}, u32[]{:S(2)}, u32[]{:S(2)}) collective-permute-start(bf16[1024,256]{0,1:T(8,128)(2,1)S(1)} %collective-permute-done.20), channel_id=1, source_target_pairs={{8,0},{16,8},{24,16},{28,24},{20,28},{12,20},{4,12},{0,4},{9,1},{1... | collective-permute-start | bytes 1572872 | tf_op jit(solution)/shard_map/ppermute | solution.py:109
  224.0 21.7 %collective-permute-start.23 = (bf16[1024,256]{0,1:T(8,128)(2,1)S(1)}, bf16[1024,256]{0,1:T(8,128)(2,1)}, u32[]{:S(2)}, u32[]{:S(2)}) collective-permute-start(bf16[1024,256]{0,1:T(8,128)(2,1)S(1)} %collective-permute-done.21), channel_id=1, source_target_pairs={{0,8},{8,16},{16,24},{24,28},{28,20},{20,12},{12,4},{4,0},{1,9},{9... | collective-permute-start | bytes 1572872 | tf_op jit(solution)/shard_map/ppermute | solution.py:108
  247.4 56.8 %collective-permute-start.8 = (bf16[256,3072]{0,1:T(8,128)(2,1)}, bf16[256,3072]{0,1:T(8,128)(2,1)}, u32[]{:S(2)}, u32[]{:S(2)}) collective-permute-start(bf16[256,3072]{0,1:T(8,128)(2,1)} %collective-permute-done.6), channel_id=1, source_target_pairs={{0,8},{8,16},{16,24},{24,28},{28,20},{20,12},{12,4},{4,0},{1,9},{9... | collective-permute-start | bytes 4718600 | tf_op jit(solution)/shard_map/ppermute | solution.py:106
  256.0 53.0 %collective-permute-start.9 = (bf16[256,3072]{0,1:T(8,128)(2,1)}, bf16[256,3072]{0,1:T(8,128)(2,1)}, u32[]{:S(2)}, u32[]{:S(2)}) collective-permute-start(bf16[256,3072]{0,1:T(8,128)(2,1)} %collective-permute-done.7), channel_id=1, source_target_pairs={{8,0},{16,8},{24,16},{28,24},{20,28},{12,20},{4,12},{0,4},{9,1},{1... | collective-permute-start | bytes 4718600 | tf_op jit(solution)/shard_map/ppermute | solution.py:107
  257.9 44.2 %collective-permute-start.26 = (bf16[1024,256]{0,1:T(8,128)(2,1)}, bf16[1024,256]{0,1:T(8,128)(2,1)S(1)}, u32[]{:S(2)}, u32[]{:S(2)}) collective-permute-start(bf16[1024,256]{0,1:T(8,128)(2,1)} %collective-permute-done.24), channel_id=1, source_target_pairs={{8,0},{16,8},{24,16},{28,24},{20,28},{12,20},{4,12},{0,4},{9,1},{1... | collective-permute-start | bytes 1572872 | tf_op jit(solution)/shard_map/ppermute | solution.py:109
  260.9 41.4 %collective-permute-start.27 = (bf16[1024,256]{0,1:T(8,128)(2,1)}, bf16[1024,256]{0,1:T(8,128)(2,1)S(1)}, u32[]{:S(2)}, u32[]{:S(2)}) collective-permute-start(bf16[1024,256]{0,1:T(8,128)(2,1)} %collective-permute-done.25), channel_id=1, source_target_pairs={{0,8},{8,16},{16,24},{24,28},{28,20},{20,12},{12,4},{4,0},{1,9},{9... | collective-permute-start | bytes 1572872 | tf_op jit(solution)/shard_map/ppermute | solution.py:108
  304.1 55.0 %collective-permute-start.10 = (bf16[256,3072]{0,1:T(8,128)(2,1)}, bf16[256,3072]{0,1:T(8,128)(2,1)}, u32[]{:S(2)}, u32[]{:S(2)}) collective-permute-start(bf16[256,3072]{0,1:T(8,128)(2,1)} %collective-permute-done.8), channel_id=1, source_target_pairs={{0,8},{8,16},{16,24},{24,28},{28,20},{20,12},{12,4},{4,0},{1,9},{9... | collective-permute-start | bytes 4718600 | tf_op jit(solution)/shard_map/ppermute | solution.py:106
  309.1 56.3 %collective-permute-start.11 = (bf16[256,3072]{0,1:T(8,128)(2,1)}, bf16[256,3072]{0,1:T(8,128)(2,1)}, u32[]{:S(2)}, u32[]{:S(2)}) collective-permute-start(bf16[256,3072]{0,1:T(8,128)(2,1)} %collective-permute-done.9), channel_id=1, source_target_pairs={{8,0},{16,8},{24,16},{28,24},{20,28},{12,20},{4,12},{0,4},{9,1},{1... | collective-permute-start | bytes 4718600 | tf_op jit(solution)/shard_map/ppermute | solution.py:107
  317.1 41.7 %collective-permute-start.30 = (bf16[1024,256]{0,1:T(8,128)(2,1)}, bf16[1024,256]{0,1:T(8,128)(2,1)}, u32[]{:S(2)}, u32[]{:S(2)}) collective-permute-start(bf16[1024,256]{0,1:T(8,128)(2,1)} %collective-permute-done.28), channel_id=1, source_target_pairs={{8,0},{16,8},{24,16},{28,24},{20,28},{12,20},{4,12},{0,4},{9,1},{1... | collective-permute-start | bytes 1572872 | tf_op jit(solution)/shard_map/ppermute | solution.py:109
  318.5 44.3 %collective-permute-start.31 = (bf16[1024,256]{0,1:T(8,128)(2,1)S(1)}, bf16[1024,256]{0,1:T(8,128)(2,1)S(1)}, u32[]{:S(2)}, u32[]{:S(2)}) collective-permute-start(bf16[1024,256]{0,1:T(8,128)(2,1)S(1)} %collective-permute-done.29), channel_id=1, source_target_pairs={{0,8},{8,16},{16,24},{24,28},{28,20},{20,12},{12,4},{4,0},{1,9},{9... | collective-permute-start | bytes 1572872 | tf_op jit(solution)/shard_map/ppermute | solution.py:108
  358.7 140.1 %collective-permute-start.32 = (bf16[1024,256]{0,1:T(8,128)(2,1)}, bf16[1024,256]{0,1:T(8,128)(2,1)}, u32[]{:S(2)}, u32[]{:S(2)}) collective-permute-start(bf16[1024,256]{0,1:T(8,128)(2,1)} %collective-permute-done.30), channel_id=1, source_target_pairs={{8,0},{16,8},{24,16},{28,24},{20,28},{12,20},{4,12},{0,4},{9,1},{1... | collective-permute-start | bytes 1572872 | tf_op jit(solution)/shard_map/ppermute | solution.py:109
  359.1 33.9 %collective-permute-start.12 = (bf16[256,3072]{0,1:T(8,128)(2,1)}, bf16[256,3072]{0,1:T(8,128)(2,1)}, u32[]{:S(2)}, u32[]{:S(2)}) collective-permute-start(bf16[256,3072]{0,1:T(8,128)(2,1)} %collective-permute-done.10), channel_id=1, source_target_pairs={{0,8},{8,16},{16,24},{24,28},{28,20},{20,12},{12,4},{4,0},{1,9},{9... | collective-permute-start | bytes 4718600 | tf_op jit(solution)/shard_map/ppermute | solution.py:106
  365.4 38.9 %collective-permute-start.13 = (bf16[256,3072]{0,1:T(8,128)(2,1)}, bf16[256,3072]{0,1:T(8,128)(2,1)}, u32[]{:S(2)}, u32[]{:S(2)}) collective-permute-start(bf16[256,3072]{0,1:T(8,128)(2,1)} %collective-permute-done.11), channel_id=1, source_target_pairs={{8,0},{16,8},{24,16},{28,24},{20,28},{12,20},{4,12},{0,4},{9,1},{1... | collective-permute-start | bytes 4718600 | tf_op jit(solution)/shard_map/ppermute | solution.py:107
  393.0 29.1 %collective-permute-start.14 = (bf16[256,3072]{0,1:T(8,128)(2,1)}, bf16[256,3072]{0,1:T(8,128)(2,1)}, u32[]{:S(2)}, u32[]{:S(2)}) collective-permute-start(bf16[256,3072]{0,1:T(8,128)(2,1)} %collective-permute-done.12), channel_id=1, source_target_pairs={{0,8},{8,16},{16,24},{24,28},{28,20},{20,12},{12,4},{4,0},{1,9},{9... | collective-permute-start | bytes 4718600 | tf_op jit(solution)/shard_map/ppermute | solution.py:106
  404.3 30.5 %collective-permute-start.15 = (bf16[256,3072]{0,1:T(8,128)(2,1)}, bf16[256,3072]{0,1:T(8,128)(2,1)}, u32[]{:S(2)}, u32[]{:S(2)}) collective-permute-start(bf16[256,3072]{0,1:T(8,128)(2,1)} %collective-permute-done.13), channel_id=1, source_target_pairs={{8,0},{16,8},{24,16},{28,24},{20,28},{12,20},{4,12},{0,4},{9,1},{1... | collective-permute-start | bytes 4718600 | tf_op jit(solution)/shard_map/ppermute | solution.py:107
  496.4 17.1 %collective-permute-start.16 = (bf16[2,3,1024]{2,1,0:T(4,128)(2,1)S(1)}, bf16[2,3,1024]{2,1,0:T(4,128)(2,1)S(1)}, u32[]{:S(2)}, u32[]{:S(2)}) collective-permute-start(bf16[2,3,1024]{2,1,0:T(4,128)(2,1)S(1)} %slice.48), channel_id=1, source_target_pairs={{0,4},{4,8},{8,12},{12,16},{16,20},{20,24},{24,28},{1,5},{5,9},{9,... | collective-permute-start | bytes 36872 | tf_op jit(solution)/shard_map/ppermute | solution.py:11
  616.3 31.1 %reduce-scatter.3.cloned.1.call-start = ((), (), s32[]{:S(2)}) async-start(), calls=%async_computation.3 | async-start | bytes 9437184 | tf_op jit(solution)/shard_map/reduce_scatter | solution.py:149
  629.4 70.6 %collective-permute-start.33 = (bf16[768,2048]{1,0:T(8,128)(2,1)}, bf16[768,2048]{1,0:T(8,128)(2,1)}, u32[]{:S(2)}, u32[]{:S(2)}) collective-permute-start(bf16[768,2048]{1,0:T(8,128)(2,1)} %reduce-scatter.5.cloned.1.call-done), channel_id=1, source_target_pairs={{0,2},{2,0},{1,3},{3,1},{4,6},{6,4},{5,7},{7,5},{8,10},{10,8},{9,1... | collective-permute-start | bytes 9437192 | tf_op jit(solution)/shard_map/ppermute | solution.py:15
  (17 other events, 759.4 us)
Sparse Core Ops, SparseCore 0:
  84.9 26.6 all-gather.1
  616.5 12.8 reduce-scatter.4
  631.8 15.6 reduce-scatter.2

commit v15 on v14

--- a/solution.py
+++ b/solution.py
@@ -27,18 +27,6 @@
         return jnp.einsum("gm,mts->gts", table, hot.astype(table.dtype))
 
     return (spread(offset == tap), spread(offset + filter_len == tap))
-
-
-def featurize(extended, short_filter, count):
-    short_taps = short_filter.shape[0]
-    ext_float = extended.astype(jnp.float32)
-    featured = jnp.zeros((count,) + extended.shape[1:], jnp.float32)
-    for tap in range(short_taps):
-        featured = (
-            featured
-            + short_filter[tap] * ext_float[short_taps - 1 - tap : short_taps - 1 - tap + count]
-        )
-    return featured
 
 
 def half_of(value, axis, half):
@@ -124,7 +112,12 @@
 
     taps = half_of(short_filter, 2, half)
     prior_rows = shifted(projected[row_count - (short_taps - 1) :], "hi", 1)
-    featured = featurize(jnp.concatenate([prior_rows, projected], axis=0), taps, row_count)
+    featured = jnp.zeros((row_count,) + projected.shape[1:], jnp.float32)
+    for tap in range(short_taps):
+        shifted_rows = jnp.concatenate(
+            [prior_rows[short_taps - 1 - tap :], projected[: row_count - tap]], axis=0
+        )
+        featured = featured + taps[tap] * shifted_rows.astype(jnp.float32)
     mixed = (featured[:, 1] * featured[:, 2]).astype(jnp.bfloat16)
     mixed_prior = shifted(mixed[row_count - (filter_len - 1) :], "hi", 1)
     query = featured[:, 0]

time: 724 us -> 734 us (1.014)
  local copies, waits for them, and re-layouts: 138 us -> 166 us
  other arithmetic: 64.8 us -> 46 us
    slice x0 -> x4, local copies, waits for them, and re-layouts: none -> 26.5 us  [the longest x2 25.3 us: local(): projected[:row_count - tap]]
    convert_element_type x1 -> x0, other arithmetic: 15.1 us -> none  [featurize(): ext_float = extended.astype(jnp.float32)]
  transfers between devices with their start and end apart: 37 -> 37, of which waited for: 16 -> 16; matrix products, arithmetic and copies ran while one was open for 28% -> 31% of each run, Pallas kernels for 0% -> 0%
where the time goes in v15:
time: 734 us; the launch traced here: 722 us
  waiting for transfers between devices  336 us (46%)
  local copies, waits for them, and re-layouts  166 us (23%)
  matrix products  94.5 us (13%)
  other arithmetic  46 us (6%)
  starting transfers between devices  45.4 us (6%)
  between operations  34.2 us (5%)
    ppermute x4, waiting for transfers between devices, swap_pair(): return lax.ppermute(value, 'lo', [(0, 1), (1, 0)])  137 us
    ppermute x7, waiting for transfers between devices, local(): partner_out = lax.ppermute(partner_out, 'hi', backward)  90.5 us
    dot_general x1, matrix products, local(): jnp.dot(normed, gathered_w.reshape(n_ctx * w_rows, 3 * half_width), prefe...  47.7 us
    ppermute x7, waiting for transfers between devices, local(): partner_piece = lax.ppermute(partner_piece, 'hi', backward)  44.8 us
    ppermute x7, waiting for transfers between devices, local(): own_piece = lax.ppermute(own_piece, 'hi', forward)  26.5 us
    slice x2, local copies, waits for them, and re-layouts, local(): projected[:row_count - tap]  25.3 us
    dot_general x2, matrix products, out_terms(): jnp.dot(rows, o_full, preferred_element_type=jnp.float32)  24.5 us
    broadcast_in_dim x14, local copies, waits for them, and re-layouts, store(): piece[None]  23.9 us
  transfers between devices with their start and end apart: 37, of which 16 were waited for; matrix products, arithmetic and copies ran while one was open for 31% of the time, Pallas kernels for 0%

profile of v15, /device:TPU:0, one launch (start us, length us, event | category | flops | bytes accessed | tf_op | source)
XLA Modules:
  0.0 722.5 jit_solution(13651857745462837375)
XLA Ops:
  9.5 4.2 constant_dynamic-slice_fusion.2
  21.2 57.6 %collective-permute-done = bf16[768,2048]{1,0:T(8,128)(2,1)} collective-permute-done((bf16[768,2048]{1,0:T(8,128)(2,1)}, bf16[768,2048]{1,0:T(8,128)(2,1)}, u32[]{:S(2)}, u32[]{:S(2)}) %collective-permute-start) | collective-permute-done | bytes 3145760 | tf_op jit(solution)/shard_map/ppermute | solution.py:15
  81.1 3.8 pad_maximum_fusion
  84.9 26.7 %collective-permute-done.1 = bf16[256,3,1024]{0,2,1:T(8,128)(2,1)} collective-permute-done((bf16[256,3,1024]{0,2,1:T(8,128)(2,1)}, bf16[256,3,1024]{0,2,1:T(8,128)(2,1)}, u32[]{:S(2)}, u32[]{:S(2)}) %collective-permute-start.1) | collective-permute-done | bytes 1572896 | tf_op jit(solution)/shard_map/ppermute | solution.py:15
  113.7 33.9 %collective-permute-done.3 = bf16[256,3072]{0,1:T(8,128)(2,1)} collective-permute-done((bf16[256,3072]{0,1:T(8,128)(2,1)}, bf16[256,3072]{0,1:T(8,128)(2,1)}, u32[]{:S(2)}, u32[]{:S(2)}) %collective-permute-start.3) | collective-permute-done | bytes 1572896 | tf_op jit(solution)/shard_map/ppermute | solution.py:95
  168.2 8.6 %broadcast_in_dim.99 = bf16[16,256,3072]{2,1,0:T(8,128)(2,1)} broadcast(bf16[]{:T(256)} %constant.131.clone.1), dimensions={} | broadcast | bytes 25165826 | tf_op jit(solution)/shard_map/broadcast_in_dim | solution.py:82
  179.7 4.3 broadcast_in_dim.114
  206.1 18.0 %collective-permute-done.21 = bf16[1024,256]{0,1:T(8,128)(2,1)S(1)} collective-permute-done((bf16[1024,256]{0,1:T(8,128)(2,1)}, bf16[1024,256]{0,1:T(8,128)(2,1)S(1)}, u32[]{:S(2)}, u32[]{:S(2)}) %collective-permute-start.21) | collective-permute-done | bytes 524320 | tf_op jit(solution)/shard_map/ppermute | solution.py:96
  229.2 16.1 %collective-permute-done.22 = bf16[1024,256]{0,1:T(8,128)(2,1)} collective-permute-done((bf16[1024,256]{0,1:T(8,128)(2,1)S(1)}, bf16[1024,256]{0,1:T(8,128)(2,1)}, u32[]{:S(2)}, u32[]{:S(2)}) %collective-permute-start.22) | collective-permute-done | bytes 524320 | tf_op jit(solution)/shard_map/ppermute | solution.py:97
  267.4 34.6 %collective-permute-done.26 = bf16[1024,256]{0,1:T(8,128)(2,1)S(1)} collective-permute-done((bf16[1024,256]{0,1:T(8,128)(2,1)}, bf16[1024,256]{0,1:T(8,128)(2,1)S(1)}, u32[]{:S(2)}, u32[]{:S(2)}) %collective-permute-start.26) | collective-permute-done | bytes 524320 | tf_op jit(solution)/shard_map/ppermute | solution.py:97
  312.6 4.5 collective-permute-done.28
  323.0 35.4 %collective-permute-done.30 = bf16[1024,256]{0,1:T(8,128)(2,1)} collective-permute-done((bf16[1024,256]{0,1:T(8,128)(2,1)}, bf16[1024,256]{0,1:T(8,128)(2,1)}, u32[]{:S(2)}, u32[]{:S(2)}) %collective-permute-start.30) | collective-permute-done | bytes 524320 | tf_op jit(solution)/shard_map/ppermute | solution.py:97
  374.6 18.3 %collective-permute-done.12 = bf16[256,3072]{0,1:T(8,128)(2,1)} collective-permute-done((bf16[256,3072]{0,1:T(8,128)(2,1)}, bf16[256,3072]{0,1:T(8,128)(2,1)}, u32[]{:S(2)}, u32[]{:S(2)}) %collective-permute-start.12) | collective-permute-done | bytes 1572896 | tf_op jit(solution)/shard_map/ppermute | solution.py:94
  413.8 8.1 %collective-permute-done.14 = bf16[256,3072]{0,1:T(8,128)(2,1)} collective-permute-done((bf16[256,3072]{0,1:T(8,128)(2,1)}, bf16[256,3072]{0,1:T(8,128)(2,1)}, u32[]{:S(2)}, u32[]{:S(2)}) %collective-permute-start.14) | collective-permute-done | bytes 1572896 | tf_op jit(solution)/shard_map/ppermute | solution.py:94
  426.3 8.3 %collective-permute-done.15 = bf16[256,3072]{0,1:T(8,128)(2,1)} collective-permute-done((bf16[256,3072]{0,1:T(8,128)(2,1)}, bf16[256,3072]{0,1:T(8,128)(2,1)}, u32[]{:S(2)}, u32[]{:S(2)}) %collective-permute-start.15) | collective-permute-done | bytes 1572896 | tf_op jit(solution)/shard_map/ppermute | solution.py:95
  437.6 7.1 fusion
  444.7 47.7 %fusion.7 = bf16[1536,3072]{1,0:T(8,128)(2,1)S(1)} fusion(bf16[4096,3072]{1,0:T(8,128)(2,1)} %bitcast.35, bf16[1536,4096]{1,0:T(8,128)(2,1)} %all-gather.2.cloned.1.call-done, f32[4096]{0:T(1024)S(1)} %copy-done.10, f32[1536]{0:T(1024)S(1)} %add_rsqrt_fusion), kind=kOutput, calls=%fused_computation.9 | convolution fusion | flops 38684590080 | bytes 47208448 | tf_op jit(solution)/shard_map/dot_general | solution.py:106
  500.4 13.7 %copy.80 = f32[1536,3072]{0,1:T(8,128)} copy(bf16[1536,3072]{1,0:T(8,128)(2,1)} %copy-done.2) | data formatting | bytes 28311552 | tf_op jit(solution)/shard_map/convert_element_type | solution.py:120
  514.1 12.6 %copy.82 = bf16[1535,3072]{0,1:T(8,128)(2,1)} copy(bf16[1535,3072]{1,0:T(8,128)(2,1)} %bitcast.120) | data formatting | bytes 18862080 | tf_op jit(solution)/shard_map/slice | solution.py:118
  526.8 12.6 %copy.84 = bf16[1534,3072]{0,1:T(8,128)(2,1)} copy(bf16[1534,3072]{1,0:T(8,128)(2,1)} %bitcast.121) | data formatting | bytes 18849792 | tf_op jit(solution)/shard_map/slice | solution.py:118
  541.9 18.6 %multiply_add_fusion = f32[1536,3,1024]{0,2,1:T(8,128)S(1)} fusion(f32[1536,3,1024]{0,2,1:T(8,128)} %bitcast.122, bf16[1535,3,1024]{0,2,1:T(8,128)(2,1)} %bitcast.123, bf16[1,3,1024]{0,2,1:T(8,128)(2,1)} %copy.83, bf16[1534,3,1024]{0,2,1:T(8,128)(2,1)} %bitcast.124, bf16[2,3,1024]{0,2,1:T(8,128)(2,1)} %copy.85, f32[3,1024]{1,0:T(4,128)S(1)} %get-tuple-element.13, ...), kind=kLoop, calls=%fused_computation.5 | loop fusion | flops 61341696 | bytes 56659968 | tf_op jit(solution)/shard_map/add | solution.py:120
  560.5 6.5 copy-done.3
  571.7 6.9 convert_element_type.61
  583.3 4.8 collective-permute-start.17
  588.1 8.0 %fusion.21 = f32[11,128,64,16]{1,3,0,2:T(8,128)} fusion(bf16[11,128,64,16]{1,0,3,2:T(8,128)(2,1)} %slice.68, bf16[64,128,128,1]{2,0,1,3:T(8,128)(2,1)} %bitcast.126), kind=kOutput, calls=%fused_computation.32 | convolution fusion | flops 369098752 | bytes 10747904 | tf_op jit(solution)/shard_map/gts,bsgc->btgc/dot_general | solution.py:132
  598.2 7.1 maximum_add_fusion
  608.2 5.0 fusion.12
  613.2 12.3 %convolution_convert_fusion = bf16[768,4096]{1,0:T(8,128)(2,1)} fusion(bf16[1024,4096]{0,1:T(8,128)(2,1)} %bitcast.68, bf16[1536,1024]{0,1:T(8,128)(2,1)S(1)} %fusion.12, s32[]{:T(128)S(6)} %select_n.262), kind=kOutput, calls=%fused_computation.15 | convolution fusion | flops 6445596672 | bytes 16252932 | tf_op jit(solution)/shard_map/dot_general | solution.py:141
  625.6 12.2 %convolution_convert_fusion.1 = bf16[768,4096]{1,0:T(8,128)(2,1)} fusion(bf16[1024,4096]{0,1:T(8,128)(2,1)} %bitcast.68, bf16[1536,1024]{0,1:T(8,128)(2,1)S(1)} %fusion.12, s32[]{:T(128)S(6)} %select_n.261), kind=kOutput, calls=%fused_computation.16 | convolution fusion | flops 6445596672 | bytes 16252932 | tf_op jit(solution)/shard_map/dot_general | solution.py:141
  640.3 16.4 %reduce-scatter.3.cloned.1.call-done = bf16[768,2048]{1,0:T(8,128)(2,1)} async-done(((bf16[768,4096]{1,0:T(8,128)(2,1)}), bf16[768,2048]{1,0:T(8,128)(2,1)}) %reduce-scatter.3.cloned.1.call-update) | async-done | bytes 3145744 | tf_op jit(solution)/shard_map/reduce_scatter | solution.py:142
  656.7 52.5 %collective-permute-done.33 = bf16[768,2048]{1,0:T(8,128)(2,1)} collective-permute-done((bf16[768,2048]{1,0:T(8,128)(2,1)}, bf16[768,2048]{1,0:T(8,128)(2,1)}, u32[]{:S(2)}, u32[]{:S(2)}) %collective-permute-start.33) | collective-permute-done | bytes 3145760 | tf_op jit(solution)/shard_map/ppermute | solution.py:15
  709.2 6.6 add_convert_fusion
  (159 shorter events, 155.5 us)
Async XLA Ops:
  6.5 431.1 %all-gather.2.cloned.1.call-start = ((), (), s32[]{:S(2)}) async-start(), calls=%async_computation.2 | async-start | bytes 18874368 | tf_op jit(solution)/shard_map/all_gather | solution.py:60
  6.5 72.2 %collective-permute-start = (bf16[768,2048]{1,0:T(8,128)(2,1)}, bf16[768,2048]{1,0:T(8,128)(2,1)}, u32[]{:S(2)}, u32[]{:S(2)}) collective-permute-start(bf16[768,2048]{1,0:T(8,128)(2,1)} %param.8), channel_id=1, source_target_pairs={{0,2},{2,0},{1,3},{3,1},{4,6},{6,4},{5,7},{7,5},{8,10},{10,8},{9,1... | collective-permute-start | bytes 9437192 | tf_op jit(solution)/shard_map/ppermute | solution.py:15
  16.2 95.4 %collective-permute-start.1 = (bf16[256,3,1024]{0,2,1:T(8,128)(2,1)}, bf16[256,3,1024]{0,2,1:T(8,128)(2,1)}, u32[]{:S(2)}, u32[]{:S(2)}) collective-permute-start(bf16[256,3,1024]{0,2,1:T(8,128)(2,1)} %copy.104), channel_id=1, source_target_pairs={{0,2},{2,0},{1,3},{3,1},{4,6},{6,4},{5,7},{7,5},{8,10},{10,8},{9,1... | collective-permute-start | bytes 4718600 | tf_op jit(solution)/shard_map/ppermute | solution.py:15
  19.0 94.4 %collective-permute-start.2 = (bf16[256,3072]{0,1:T(8,128)(2,1)}, bf16[256,3072]{0,1:T(8,128)(2,1)}, u32[]{:S(2)}, u32[]{:S(2)}) collective-permute-start(bf16[256,3072]{0,1:T(8,128)(2,1)} %bitcast.127), channel_id=1, source_target_pairs={{0,8},{8,16},{16,24},{24,28},{28,20},{20,12},{12,4},{4,0},{1,9},{9... | collective-permute-start | bytes 4718600 | tf_op jit(solution)/shard_map/ppermute | solution.py:94
  84.8 553.7 %reduce-scatter.5.cloned.1.call-start = ((), (), s32[]{:S(2)}) async-start(), calls=%async_computation.4 | async-start | bytes 9437184 | tf_op jit(solution)/shard_map/reduce_scatter | solution.py:142
  111.6 35.9 %collective-permute-start.3 = (bf16[256,3072]{0,1:T(8,128)(2,1)}, bf16[256,3072]{0,1:T(8,128)(2,1)}, u32[]{:S(2)}, u32[]{:S(2)}) collective-permute-start(bf16[256,3072]{0,1:T(8,128)(2,1)} %bitcast.8), channel_id=1, source_target_pairs={{8,0},{16,8},{24,16},{28,24},{20,28},{12,20},{4,12},{0,4},{9,1},{1... | collective-permute-start | bytes 4718600 | tf_op jit(solution)/shard_map/ppermute | solution.py:95
  113.4 64.7 %collective-permute-start.4 = (bf16[256,3072]{0,1:T(8,128)(2,1)}, bf16[256,3072]{0,1:T(8,128)(2,1)}, u32[]{:S(2)}, u32[]{:S(2)}) collective-permute-start(bf16[256,3072]{0,1:T(8,128)(2,1)} %collective-permute-done.2), channel_id=1, source_target_pairs={{0,8},{8,16},{16,24},{24,28},{28,20},{20,12},{12,4},{4,0},{1,9},{9... | collective-permute-start | bytes 4718600 | tf_op jit(solution)/shard_map/ppermute | solution.py:94
  147.5 51.9 %collective-permute-start.5 = (bf16[256,3072]{0,1:T(8,128)(2,1)}, bf16[256,3072]{0,1:T(8,128)(2,1)}, u32[]{:S(2)}, u32[]{:S(2)}) collective-permute-start(bf16[256,3072]{0,1:T(8,128)(2,1)} %collective-permute-done.3), channel_id=1, source_target_pairs={{8,0},{16,8},{24,16},{28,24},{20,28},{12,20},{4,12},{0,4},{9,1},{1... | collective-permute-start | bytes 4718600 | tf_op jit(solution)/shard_map/ppermute | solution.py:95
  151.2 34.7 %collective-permute-start.18 = (bf16[1024,256]{0,1:T(8,128)(2,1)}, bf16[1024,256]{0,1:T(8,128)(2,1)}, u32[]{:S(2)}, u32[]{:S(2)}) collective-permute-start(bf16[1024,256]{0,1:T(8,128)(2,1)} %copy.107), channel_id=1, source_target_pairs={{0,2},{2,0},{1,3},{3,1},{4,6},{6,4},{5,7},{7,5},{8,10},{10,8},{9,1... | collective-permute-start | bytes 1572872 | tf_op jit(solution)/shard_map/ppermute | solution.py:15
  153.7 32.6 %collective-permute-start.19 = (bf16[1024,256]{0,1:T(8,128)(2,1)}, bf16[1024,256]{0,1:T(8,128)(2,1)}, u32[]{:S(2)}, u32[]{:S(2)}) collective-permute-start(bf16[1024,256]{0,1:T(8,128)(2,1)} %copy.106), channel_id=1, source_target_pairs={{0,8},{8,16},{16,24},{24,28},{28,20},{20,12},{12,4},{4,0},{1,9},{9... | collective-permute-start | bytes 1572872 | tf_op jit(solution)/shard_map/ppermute | solution.py:96
  178.1 69.1 %collective-permute-start.6 = (bf16[256,3072]{0,1:T(8,128)(2,1)}, bf16[256,3072]{0,1:T(8,128)(2,1)}, u32[]{:S(2)}, u32[]{:S(2)}) collective-permute-start(bf16[256,3072]{0,1:T(8,128)(2,1)} %collective-permute-done.4), channel_id=1, source_target_pairs={{0,8},{8,16},{16,24},{24,28},{28,20},{20,12},{12,4},{4,0},{1,9},{9... | collective-permute-start | bytes 4718600 | tf_op jit(solution)/shard_map/ppermute | solution.py:94
  185.9 18.5 %collective-permute-start.20 = (bf16[1024,256]{0,1:T(8,128)(2,1)}, bf16[1024,256]{0,1:T(8,128)(2,1)S(1)}, u32[]{:S(2)}, u32[]{:S(2)}) collective-permute-start(bf16[1024,256]{0,1:T(8,128)(2,1)} %collective-permute-done.18), channel_id=1, source_target_pairs={{8,0},{16,8},{24,16},{28,24},{20,28},{12,20},{4,12},{0,4},{9,1},{1... | collective-permute-start | bytes 1572872 | tf_op jit(solution)/shard_map/ppermute | solution.py:97
  186.3 37.7 %collective-permute-start.21 = (bf16[1024,256]{0,1:T(8,128)(2,1)}, bf16[1024,256]{0,1:T(8,128)(2,1)S(1)}, u32[]{:S(2)}, u32[]{:S(2)}) collective-permute-start(bf16[1024,256]{0,1:T(8,128)(2,1)} %collective-permute-done.19), channel_id=1, source_target_pairs={{0,8},{8,16},{16,24},{24,28},{28,20},{20,12},{12,4},{4,0},{1,9},{9... | collective-permute-start | bytes 1572872 | tf_op jit(solution)/shard_map/ppermute | solution.py:96
  199.4 56.5 %collective-permute-start.7 = (bf16[256,3072]{0,1:T(8,128)(2,1)}, bf16[256,3072]{0,1:T(8,128)(2,1)}, u32[]{:S(2)}, u32[]{:S(2)}) collective-permute-start(bf16[256,3072]{0,1:T(8,128)(2,1)} %collective-permute-done.5), channel_id=1, source_target_pairs={{8,0},{16,8},{24,16},{28,24},{20,28},{12,20},{4,12},{0,4},{9,1},{1... | collective-permute-start | bytes 4718600 | tf_op jit(solution)/shard_map/ppermute | solution.py:95
  204.5 40.8 %collective-permute-start.22 = (bf16[1024,256]{0,1:T(8,128)(2,1)S(1)}, bf16[1024,256]{0,1:T(8,128)(2,1)}, u32[]{:S(2)}, u32[]{:S(2)}) collective-permute-start(bf16[1024,256]{0,1:T(8,128)(2,1)S(1)} %collective-permute-done.20), channel_id=1, source_target_pairs={{8,0},{16,8},{24,16},{28,24},{20,28},{12,20},{4,12},{0,4},{9,1},{1... | collective-permute-start | bytes 1572872 | tf_op jit(solution)/shard_map/ppermute | solution.py:97
  224.0 21.6 %collective-permute-start.23 = (bf16[1024,256]{0,1:T(8,128)(2,1)S(1)}, bf16[1024,256]{0,1:T(8,128)(2,1)}, u32[]{:S(2)}, u32[]{:S(2)}) collective-permute-start(bf16[1024,256]{0,1:T(8,128)(2,1)S(1)} %collective-permute-done.21), channel_id=1, source_target_pairs={{0,8},{8,16},{16,24},{24,28},{28,20},{20,12},{12,4},{4,0},{1,9},{9... | collective-permute-start | bytes 1572872 | tf_op jit(solution)/shard_map/ppermute | solution.py:96
  247.2 56.8 %collective-permute-start.8 = (bf16[256,3072]{0,1:T(8,128)(2,1)}, bf16[256,3072]{0,1:T(8,128)(2,1)}, u32[]{:S(2)}, u32[]{:S(2)}) collective-permute-start(bf16[256,3072]{0,1:T(8,128)(2,1)} %collective-permute-done.6), channel_id=1, source_target_pairs={{0,8},{8,16},{16,24},{24,28},{28,20},{20,12},{12,4},{4,0},{1,9},{9... | collective-permute-start | bytes 4718600 | tf_op jit(solution)/shard_map/ppermute | solution.py:94
  256.0 53.1 %collective-permute-start.9 = (bf16[256,3072]{0,1:T(8,128)(2,1)}, bf16[256,3072]{0,1:T(8,128)(2,1)}, u32[]{:S(2)}, u32[]{:S(2)}) collective-permute-start(bf16[256,3072]{0,1:T(8,128)(2,1)} %collective-permute-done.7), channel_id=1, source_target_pairs={{8,0},{16,8},{24,16},{28,24},{20,28},{12,20},{4,12},{0,4},{9,1},{1... | collective-permute-start | bytes 4718600 | tf_op jit(solution)/shard_map/ppermute | solution.py:95
  257.8 44.3 %collective-permute-start.26 = (bf16[1024,256]{0,1:T(8,128)(2,1)}, bf16[1024,256]{0,1:T(8,128)(2,1)S(1)}, u32[]{:S(2)}, u32[]{:S(2)}) collective-permute-start(bf16[1024,256]{0,1:T(8,128)(2,1)} %collective-permute-done.24), channel_id=1, source_target_pairs={{8,0},{16,8},{24,16},{28,24},{20,28},{12,20},{4,12},{0,4},{9,1},{1... | collective-permute-start | bytes 1572872 | tf_op jit(solution)/shard_map/ppermute | solution.py:97
  260.8 41.5 %collective-permute-start.27 = (bf16[1024,256]{0,1:T(8,128)(2,1)}, bf16[1024,256]{0,1:T(8,128)(2,1)S(1)}, u32[]{:S(2)}, u32[]{:S(2)}) collective-permute-start(bf16[1024,256]{0,1:T(8,128)(2,1)} %collective-permute-done.25), channel_id=1, source_target_pairs={{0,8},{8,16},{16,24},{24,28},{28,20},{20,12},{12,4},{4,0},{1,9},{9... | collective-permute-start | bytes 1572872 | tf_op jit(solution)/shard_map/ppermute | solution.py:96
  304.1 55.1 %collective-permute-start.10 = (bf16[256,3072]{0,1:T(8,128)(2,1)}, bf16[256,3072]{0,1:T(8,128)(2,1)}, u32[]{:S(2)}, u32[]{:S(2)}) collective-permute-start(bf16[256,3072]{0,1:T(8,128)(2,1)} %collective-permute-done.8), channel_id=1, source_target_pairs={{0,8},{8,16},{16,24},{24,28},{28,20},{20,12},{12,4},{4,0},{1,9},{9... | collective-permute-start | bytes 4718600 | tf_op jit(solution)/shard_map/ppermute | solution.py:94
  309.1 56.3 %collective-permute-start.11 = (bf16[256,3072]{0,1:T(8,128)(2,1)}, bf16[256,3072]{0,1:T(8,128)(2,1)}, u32[]{:S(2)}, u32[]{:S(2)}) collective-permute-start(bf16[256,3072]{0,1:T(8,128)(2,1)} %collective-permute-done.9), channel_id=1, source_target_pairs={{8,0},{16,8},{24,16},{28,24},{20,28},{12,20},{4,12},{0,4},{9,1},{1... | collective-permute-start | bytes 4718600 | tf_op jit(solution)/shard_map/ppermute | solution.py:95
  317.0 41.4 %collective-permute-start.30 = (bf16[1024,256]{0,1:T(8,128)(2,1)}, bf16[1024,256]{0,1:T(8,128)(2,1)}, u32[]{:S(2)}, u32[]{:S(2)}) collective-permute-start(bf16[1024,256]{0,1:T(8,128)(2,1)} %collective-permute-done.28), channel_id=1, source_target_pairs={{8,0},{16,8},{24,16},{28,24},{20,28},{12,20},{4,12},{0,4},{9,1},{1... | collective-permute-start | bytes 1572872 | tf_op jit(solution)/shard_map/ppermute | solution.py:97
  318.5 44.2 %collective-permute-start.31 = (bf16[1024,256]{0,1:T(8,128)(2,1)S(1)}, bf16[1024,256]{0,1:T(8,128)(2,1)S(1)}, u32[]{:S(2)}, u32[]{:S(2)}) collective-permute-start(bf16[1024,256]{0,1:T(8,128)(2,1)S(1)} %collective-permute-done.29), channel_id=1, source_target_pairs={{0,8},{8,16},{16,24},{24,28},{28,20},{20,12},{12,4},{4,0},{1,9},{9... | collective-permute-start | bytes 1572872 | tf_op jit(solution)/shard_map/ppermute | solution.py:96
  358.4 140.1 %collective-permute-start.32 = (bf16[1024,256]{0,1:T(8,128)(2,1)}, bf16[1024,256]{0,1:T(8,128)(2,1)}, u32[]{:S(2)}, u32[]{:S(2)}) collective-permute-start(bf16[1024,256]{0,1:T(8,128)(2,1)} %collective-permute-done.30), channel_id=1, source_target_pairs={{8,0},{16,8},{24,16},{28,24},{20,28},{12,20},{4,12},{0,4},{9,1},{1... | collective-permute-start | bytes 1572872 | tf_op jit(solution)/shard_map/ppermute | solution.py:97
  359.1 33.8 %collective-permute-start.12 = (bf16[256,3072]{0,1:T(8,128)(2,1)}, bf16[256,3072]{0,1:T(8,128)(2,1)}, u32[]{:S(2)}, u32[]{:S(2)}) collective-permute-start(bf16[256,3072]{0,1:T(8,128)(2,1)} %collective-permute-done.10), channel_id=1, source_target_pairs={{0,8},{8,16},{16,24},{24,28},{28,20},{20,12},{12,4},{4,0},{1,9},{9... | collective-permute-start | bytes 4718600 | tf_op jit(solution)/shard_map/ppermute | solution.py:94
  365.3 38.8 %collective-permute-start.13 = (bf16[256,3072]{0,1:T(8,128)(2,1)}, bf16[256,3072]{0,1:T(8,128)(2,1)}, u32[]{:S(2)}, u32[]{:S(2)}) collective-permute-start(bf16[256,3072]{0,1:T(8,128)(2,1)} %collective-permute-done.11), channel_id=1, source_target_pairs={{8,0},{16,8},{24,16},{28,24},{20,28},{12,20},{4,12},{0,4},{9,1},{1... | collective-permute-start | bytes 4718600 | tf_op jit(solution)/shard_map/ppermute | solution.py:95
  393.0 29.0 %collective-permute-start.14 = (bf16[256,3072]{0,1:T(8,128)(2,1)}, bf16[256,3072]{0,1:T(8,128)(2,1)}, u32[]{:S(2)}, u32[]{:S(2)}) collective-permute-start(bf16[256,3072]{0,1:T(8,128)(2,1)} %collective-permute-done.12), channel_id=1, source_target_pairs={{0,8},{8,16},{16,24},{24,28},{28,20},{20,12},{12,4},{4,0},{1,9},{9... | collective-permute-start | bytes 4718600 | tf_op jit(solution)/shard_map/ppermute | solution.py:94
  404.1 30.5 %collective-permute-start.15 = (bf16[256,3072]{0,1:T(8,128)(2,1)}, bf16[256,3072]{0,1:T(8,128)(2,1)}, u32[]{:S(2)}, u32[]{:S(2)}) collective-permute-start(bf16[256,3072]{0,1:T(8,128)(2,1)} %collective-permute-done.13), channel_id=1, source_target_pairs={{8,0},{16,8},{24,16},{28,24},{20,28},{12,20},{4,12},{0,4},{9,1},{1... | collective-permute-start | bytes 4718600 | tf_op jit(solution)/shard_map/ppermute | solution.py:95
  496.1 43.3 %collective-permute-start.16 = (bf16[2,3,1024]{2,0,1:T(2,128)(2,1)S(1)}, bf16[2,3,1024]{2,0,1:T(2,128)(2,1)S(1)}, u32[]{:S(2)}, u32[]{:S(2)}) collective-permute-start(bf16[2,3,1024]{2,0,1:T(2,128)(2,1)S(1)} %bitcast.131), channel_id=1, source_target_pairs={{0,4},{4,8},{8,12},{12,16},{16,20},{20,24},{24,28},{1,5},{5,9},{9,... | collective-permute-start | bytes 36872 | tf_op jit(solution)/shard_map/ppermute | solution.py:11
  625.5 31.1 %reduce-scatter.3.cloned.1.call-start = ((), (), s32[]{:S(2)}) async-start(), calls=%async_computation.3 | async-start | bytes 9437184 | tf_op jit(solution)/shard_map/reduce_scatter | solution.py:142
  638.6 70.6 %collective-permute-start.33 = (bf16[768,2048]{1,0:T(8,128)(2,1)}, bf16[768,2048]{1,0:T(8,128)(2,1)}, u32[]{:S(2)}, u32[]{:S(2)}) collective-permute-start(bf16[768,2048]{1,0:T(8,128)(2,1)} %reduce-scatter.5.cloned.1.call-done), channel_id=1, source_target_pairs={{0,2},{2,0},{1,3},{3,1},{4,6},{6,4},{5,7},{7,5},{8,10},{10,8},{9,1... | collective-permute-start | bytes 9437192 | tf_op jit(solution)/shard_map/ppermute | solution.py:15
  (17 other events, 759.5 us)
Sparse Core Ops, SparseCore 0:
  85.0 26.6 all-gather.1
  625.6 12.8 reduce-scatter.4
  641.0 15.6 reduce-scatter.2
